TPU v7x, 32 devices: a whole 2x2x4 slice. The times are simulated.
32 devices in a mesh: gx: 4 (over z), gy: 2 (over y), gz: 4 (over x, core).
Axes of the slice: x: 2, y: 2, z: 4, core: 2. Of those that a mesh axis runs over, the one named last changes fastest.
Arguments:
- positions: float32 [3, 4, 2, 8, 128], P(None, 'gx', 'gy', 'gz'), may hold values from 0 to 8, as said below
- velocity: float32 [3, 4, 2, 8, 128], P(None, 'gx', 'gy', 'gz'), may hold values from -16 to 16
- counts: int32 [4, 2, 8], P('gx', 'gy', 'gz'), may hold values from 0 to 128, as said below
Outputs:
- velocity_new: float32 [3, 4, 2, 8, 128], P(None, 'gx', 'gy', 'gz')
- pressure: float32 [4, 2, 8, 128], P('gx', 'gy', 'gz')
Inputs may be any that keep to these rules, and one draw needn't show every extreme that they name: `positions`: component k of the position of any slot of tile (a, b, c) lies in [t, t + 1), where t is a, b or c for k = 0, 1, 2. A tile's particles fill its first counts[a, b, c] slots. In every column of tiles the bottom tile is full, the tiles below one topmost wet tile hold 96 or more particles, and the tiles above it are empty.
All inputs are finite; a program needn't handle non-finite values.
Results may differ from a plain program's by a relative error of at most 0.0003.
Values sent between devices are 32-bit elements; how exact they have to be, the bound alone decides.
No kernel may reach another device: no remote copies, remote signals or barrier semaphores. Data moves between devices by JAX's collectives and lax.ppermute only.
A program may use at most 64 MiB of HBM per device.

v0:
```python
import jax
import jax.numpy as jnp
from jax import lax
from jax.sharding import PartitionSpec as P

P_SIZE = 128
ITERS = 3


DIAG_SHIFT = 0.05
VISCOSITY = 0.5
GRAVITY = 0.1
GRADIENT_GAIN = 32.0


def with_halo(cells, sides, width):
    for axis, dim in sides:
        count = lax.axis_size(axis)
        ends = count - 1
        head = lax.slice_in_dim(cells, 0, width, axis=dim)
        tail = lax.slice_in_dim(cells, cells.shape[dim] - width, cells.shape[dim], axis=dim)
        cells = jnp.concatenate(
            [
                lax.ppermute(tail, axis, [(i, (i + 1) % count) for i in range(ends)]),
                cells,
                lax.ppermute(head, axis, [((i + 1) % count, i) for i in range(ends)]),
            ],
            axis=dim,
        )
    return cells


def tile_pairs(rim_positions, rim_valid, rim_field, fold_step, totals):
    size_x = rim_positions.shape[1] - 2
    size_y = rim_positions.shape[2] - 2
    size_z = rim_positions.shape[3] - 2
    slab_tiles = size_y * size_z
    tile_width = rim_positions.shape[4]

    def near_block(source_array, x_start, y_start, z_start):
        zero_start = jnp.zeros((), jnp.int32)
        window = lax.dynamic_slice(
            source_array,
            (zero_start, x_start, y_start, z_start, zero_start),
            (source_array.shape[0], 1, size_y, size_z, tile_width),
        )
        return window.reshape(source_array.shape[0], slab_tiles, tile_width)

    def slab_totals(x_index):
        unit_step = jnp.ones((), jnp.int32)
        own_positions = near_block(rim_positions, x_index + unit_step, unit_step, unit_step)
        own_valid = near_block(rim_valid, x_index + unit_step, unit_step, unit_step)[0]
        start_totals = jax.tree.map(
            lambda item: jnp.zeros((item.shape[0], slab_tiles, item.shape[2]), jnp.float32), totals
        )

        def one_offset(offset_index, carry):
            offset_code = jnp.asarray(offset_index).astype(jnp.int32)
            step_x = offset_code // 9
            step_y = offset_code // 3 % 3
            step_z = offset_code % 3
            near_positions = near_block(rim_positions, x_index + step_x, step_y, step_z)
            near_valid = near_block(rim_valid, x_index + step_x, step_y, step_z)[0]
            near_field = near_block(rim_field, x_index + step_x, step_y, step_z)
            offset = own_positions[:, :, :, None] - near_positions[:, :, None, :]
            distance = offset[0] * offset[0] + offset[1] * offset[1] + offset[2] * offset[2]
            closeness = jnp.maximum(1.0 - distance, 0.0)
            weight = closeness * closeness * own_valid[:, :, None] * near_valid[:, None, :]
            return fold_step(carry, weight, offset, near_field)

        return lax.fori_loop(0, 27, one_offset, start_totals)

    stacked = lax.map(slab_totals, jnp.arange(size_x, dtype=jnp.int32))
    return jax.tree.map(
        lambda block_out: jnp.moveaxis(block_out, 0, 1).reshape(
            block_out.shape[1], size_x * slab_tiles, block_out.shape[3]
        ),
        stacked,
    )


def flat_zeros(rim_positions, components):
    tile_count = (
        (rim_positions.shape[1] - 2) * (rim_positions.shape[2] - 2) * (rim_positions.shape[3] - 2)
    )
    return jnp.zeros((components, tile_count, rim_positions.shape[4]), jnp.float32)


def unflat(flat_values, rim_positions):
    return flat_values.reshape(
        flat_values.shape[0],
        rim_positions.shape[1] - 2,
        rim_positions.shape[2] - 2,
        rim_positions.shape[3] - 2,
        flat_values.shape[2],
    )


def viscous_fold(totals, weight, offset, near_field):
    near_sums, row_sums = totals
    near_sums = near_sums + jnp.einsum(
        "tij,ctj->cti", weight, near_field, precision=lax.Precision.HIGHEST
    )
    return (near_sums, row_sums + jnp.sum(weight, axis=2)[None])


def divergence_fold(totals, weight, offset, near_field):
    lever_sums, flux_sums = totals
    levered = weight[None] * offset
    flux_sums = (
        flux_sums
        + jnp.einsum("ctij,ctj->ti", levered, near_field, precision=lax.Precision.HIGHEST)[None]
    )
    return (lever_sums + jnp.sum(levered, axis=3), flux_sums)


def laplace_fold(totals, weight, offset, near_field):
    return totals + jnp.einsum("tij,ctj->cti", weight, near_field, precision=lax.Precision.HIGHEST)


def gradient_fold(totals, weight, offset, near_field):
    levered = weight[None] * offset
    return totals + jnp.einsum(
        "ctij,tj->cti", levered, near_field[0], precision=lax.Precision.HIGHEST
    )


def viscous_pass(rim_positions, rim_valid, rim_field):
    near_sums, row_sums = tile_pairs(
        rim_positions,
        rim_valid,
        rim_field,
        viscous_fold,
        (flat_zeros(rim_positions, 3), flat_zeros(rim_positions, 1)),
    )
    return (unflat(near_sums, rim_positions), unflat(row_sums, rim_positions))


def divergence_pass(rim_positions, rim_valid, rim_field):
    lever_sums, flux_sums = tile_pairs(
        rim_positions,
        rim_valid,
        rim_field,
        divergence_fold,
        (flat_zeros(rim_positions, 3), flat_zeros(rim_positions, 1)),
    )
    return (unflat(lever_sums, rim_positions), unflat(flux_sums, rim_positions))


def laplace_pass(rim_positions, rim_valid, rim_field):
    return unflat(
        tile_pairs(rim_positions, rim_valid, rim_field, laplace_fold, flat_zeros(rim_positions, 1)),
        rim_positions,
    )


def gradient_pass(rim_positions, rim_valid, rim_field):
    return unflat(
        tile_pairs(
            rim_positions, rim_valid, rim_field, gradient_fold, flat_zeros(rim_positions, 3)
        ),
        rim_positions,
    )


def advance(velocity, valid_mask, near_sums, row_sums):
    gravity_pull = jnp.array([0.0, 0.0, -GRAVITY], jnp.float32).reshape(3, 1, 1, 1, 1)
    return valid_mask * (
        velocity + VISCOSITY / P_SIZE * (near_sums - row_sums * velocity) + gravity_pull
    )


def operate(direction, rim_positions, rim_valid, diagonal):
    rim_direction = with_halo(direction, (("gx", 1), ("gy", 2), ("gz", 3)), 1)
    return (
        rim_direction,
        diagonal * direction - laplace_pass(rim_positions, rim_valid, rim_direction) / P_SIZE,
    )


def paired_sums(residual, precond, applied):
    return lax.psum((jnp.sum(residual * precond), jnp.sum(precond * applied)), ("gx", "gy", "gz"))


def on_device(positions, velocity, counts):
    slot_ids = jnp.arange(positions.shape[4], dtype=jnp.int32)
    valid_mask = (slot_ids[None, None, None, :] < counts[:, :, :, None]).astype(jnp.float32)[None]
    rim_positions, rim_valid, rim_velocity = (
        with_halo(positions, (("gx", 1), ("gy", 2), ("gz", 3)), 1),
        with_halo(valid_mask, (("gx", 1), ("gy", 2), ("gz", 3)), 1),
        with_halo(velocity, (("gx", 1), ("gy", 2), ("gz", 3)), 1),
    )
    near_sums, row_sums = viscous_pass(rim_positions, rim_valid, rim_velocity)
    predicted = advance(velocity, valid_mask, near_sums, row_sums)
    rim_predicted = with_halo(predicted, (("gx", 1), ("gy", 2), ("gz", 3)), 1)
    diagonal = DIAG_SHIFT + row_sums / P_SIZE
    lever_sums, flux_sums = divergence_pass(rim_positions, rim_valid, rim_predicted)
    source = -(GRADIENT_GAIN / P_SIZE) * (
        jnp.sum(predicted * lever_sums, axis=0, keepdims=True) - flux_sums
    )
    pressure = jnp.zeros_like(source)
    residual = source
    precond = residual / diagonal
    rim_search, applied = operate(precond, rim_positions, rim_valid, diagonal)
    norm_now, curvature_sum = paired_sums(residual, precond, applied)
    step_size = norm_now / curvature_sum
    direction = precond
    along = applied
    for iteration in range(ITERS):
        pressure = pressure + step_size * direction
        residual = residual - step_size * along
        if iteration + 1 < ITERS:
            precond = residual / diagonal
            rim_fresh, applied = operate(precond, rim_positions, rim_valid, diagonal)
            norm_next, curvature_sum = paired_sums(residual, precond, applied)
            blend = norm_next / norm_now
            step_size = norm_next / (curvature_sum - blend * norm_next / step_size)
            direction = precond + blend * direction
            along = applied + blend * along
            norm_now = norm_next
    rim_pressure = with_halo(pressure, (("gx", 1), ("gy", 2), ("gz", 3)), 1)
    moments = gradient_pass(rim_positions, rim_valid, rim_pressure)
    velocity_new = predicted - GRADIENT_GAIN / P_SIZE * (pressure * lever_sums - moments)
    return (velocity_new, pressure[0])


def solution(mesh):
    in_specs = (
        P(None, "gx", "gy", "gz", None),
        P(None, "gx", "gy", "gz", None),
        P("gx", "gy", "gz"),
    )
    out_specs = (P(None, "gx", "gy", "gz", None), P("gx", "gy", "gz", None))
    return jax.shard_map(
        on_device, mesh=mesh, in_specs=in_specs, out_specs=out_specs, check_vma=False
    )
```

profile of v0, /device:TPU:0, one launch (start us, length us, event | category | flops | bytes accessed | tf_op | source)
XLA Modules:
  0.0 469.5 jit_solution(9429154291890890409)
XLA Ops:
  1.4 5.0 %collective-permute-start.12 = (f32[1,1,1,2,128]{4,3,2,1,0:T(2,128)S(1)}, f32[1,1,1,2,128]{4,3,2,1,0:T(2,128)S(1)}, u32[]{:S(2)}, u32[]{:S(2)}) collective-permute-start(f32[1,1,1,2,128]{4,3,2,1,0:T(2,128)S(1)} %compare_convert_fusion.6), channel_id=1, source_target_pairs={{0,8},{8,16},{16,24},{1,9},{9,17},{17,25},{2,10},{10,18},{18,26},{... | collective-permute-start | bytes 3080 | tf_op jit(solution)/shard_map/ppermute | solution.py:24
  7.7 4.5 collective-permute-start
  13.6 4.5 collective-permute-start.6
  24.3 4.5 collective-permute-start.2
  32.9 4.5 collective-permute-start.8
  38.8 4.2 collective-permute-done.9
  47.7 5.7 %collective-permute-start.4 = (f32[3,3,3,1,128]{4,0,3,2,1:T(4,128)S(1)}, f32[3,3,3,1,128]{4,0,3,2,1:T(4,128)S(1)}, u32[]{:S(2)}, u32[]{:S(2)}) collective-permute-start(f32[3,3,3,1,128]{4,0,3,2,1:T(4,128)S(1)} %get-tuple-element.1885), channel_id=1, source_target_pairs={{0,1},{1,2},{2,3},{4,5},{5,6},{6,7},{8,9},{9,10},{10,11},{12,13},{... | collective-permute-start | bytes 41480 | tf_op jit(solution)/shard_map/ppermute | solution.py:24
  57.8 24.4 %while.152 = (s32[]{:T(128)}, f32[3,2,128]{2,0,1:T(4,128)S(1)}, f32[1,2,128]{2,1,0:T(2,128)S(1)}, f32[3,3,3,4,128]{4,0,3,2,1:T(4,128)S(1)}, f32[3,1,1,2,128]{4,3...) while((s32[]{:T(128)}, f32[3,2,128]{2,0,1:T(4,128)S(1)}, ...), condition=%wide.region_2.3_spmd.clone, body=%wide.region_0.2_spmd.clone.sunk | while | flops 1640740 | bytes 1081868 | solution.py:71
  83.0 4.5 collective-permute-start.18
  88.8 4.2 collective-permute-done.19
  96.0 4.2 collective-permute-done.21
  103.1 4.1 collective-permute-done.23
  107.3 40.3 %while.153 = (s32[]{:T(128)}, f32[3,2,128]{2,1,0:T(2,128)S(1)}, f32[1,2,128]{2,1,0:T(2,128)S(1)}, f32[3,1,1,2,128]{4,3,0,2,1:T(2,128)S(1)}, f32[3,3,3,4,128]{4,3...) while((s32[]{:T(128)}, f32[3,2,128]{2,1,0:T(2,128)S(1)}, ...), condition=%wide.region_5.6_spmd.clone, body=%wide.region_3.5_spmd.clone.sunk | while | flops 2098980 | bytes 1235468 | solution.py:71
  152.4 4.2 collective-permute-done.25
  159.5 4.2 collective-permute-done.27
  166.5 4.1 collective-permute-done.29
  170.7 21.0 %while.154 = (s32[]{:T(128)}, f32[1,2,128]{2,1,0:T(2,128)S(1)}, f32[1,3,3,4,128]{4,3,2,1,0:T(4,128)S(1)}, f32[3,1,1,2,128]{4,3,2,1,0:T(2,128)S(1)}, f32[3,3,3,4,...) while((s32[]{:T(128)}, f32[1,2,128]{2,1,0:T(2,128)S(1)}, ...), condition=%wide.region_10.11_spmd.clone, body=%wide.region_9.10_spmd.clone.sunk | while | flops 820260 | bytes 811523 | solution.py:71
  192.3 39.9 %all-reduce.2 = (f32[]{:T(128)}, f32[]{:T(128)}) all-reduce(f32[]{:T(128)} %get-tuple-element.1783, f32[]{:T(128)} %get-tuple-element.1782), channel_id=1, replica_groups=mesh['gx'=4,'gy'=2,'gz'=4] {'gx','gy','gz'}, use_global_device_ids=true, to_apply=%region_8.9 | all-reduce | flops 2 | bytes 16 | tf_op jit(solution)/shard_map/psum | solution.py:182
  237.3 4.2 collective-permute-done.31
  241.5 4.4 collective-permute-start.32
  247.2 4.2 collective-permute-done.33
  254.0 4.0 collective-permute-done.35
  258.0 21.0 %while.155 = (s32[]{:T(128)}, f32[1,2,128]{2,1,0:T(2,128)S(1)}, f32[1,3,3,4,128]{4,3,2,1,0:T(4,128)S(1)}, f32[3,1,1,2,128]{4,3,2,1,0:T(2,128)S(1)}, f32[3,3,3,4,...) while((s32[]{:T(128)}, f32[1,2,128]{2,1,0:T(2,128)S(1)}, ...), condition=%wide.region_16.17_spmd.clone, body=%wide.region_15.16_spmd.clone.sunk | while | flops 820260 | bytes 811523 | solution.py:71
  279.6 39.2 %all-reduce.1 = (f32[]{:T(128)}, f32[]{:T(128)}) all-reduce(f32[]{:T(128)} %get-tuple-element.1781, f32[]{:T(128)} %get-tuple-element.1780), channel_id=1, replica_groups=mesh['gx'=4,'gy'=2,'gz'=4] {'gx','gy','gz'}, use_global_device_ids=true, to_apply=%region_14.15 | all-reduce | flops 2 | bytes 16 | tf_op jit(solution)/shard_map/psum | solution.py:182
  327.6 4.2 collective-permute-done.37
  331.8 4.4 collective-permute-start.38
  337.5 4.2 collective-permute-done.39
  348.3 21.0 %while.156 = (s32[]{:T(128)}, f32[1,2,128]{2,1,0:T(2,128)S(1)}, f32[1,3,3,4,128]{4,3,2,1,0:T(4,128)S(1)}, f32[3,1,1,2,128]{4,3,2,1,0:T(2,128)S(1)}, f32[3,3,3,4,...) while((s32[]{:T(128)}, f32[1,2,128]{2,1,0:T(2,128)S(1)}, ...), condition=%wide.region_22.23_spmd.clone, body=%wide.region_21.22_spmd.clone.sunk | while | flops 820260 | bytes 811523 | solution.py:71
  369.9 39.2 %all-reduce = (f32[]{:T(128)}, f32[]{:T(128)}) all-reduce(f32[]{:T(128)} %get-tuple-element.1779, f32[]{:T(128)} %get-tuple-element.1778), channel_id=1, replica_groups=mesh['gx'=4,'gy'=2,'gz'=4] {'gx','gy','gz'}, use_global_device_ids=true, to_apply=%region_20.21 | all-reduce | flops 2 | bytes 16 | tf_op jit(solution)/shard_map/psum | solution.py:182
  417.3 4.1 collective-permute-done.43
  421.5 4.4 collective-permute-start.44
  437.9 31.0 %while.157 = (s32[]{:T(128)}, f32[3,2,128]{2,1,0:T(2,128)S(1)}, f32[1,3,3,4,128]{4,3,2,1,0:T(4,128)S(1)}, f32[3,1,1,2,128]{4,3,2,1,0:T(2,128)S(1)}, f32[3,3,3,4,...) while((s32[]{:T(128)}, f32[3,2,128]{2,1,0:T(2,128)S(1)}, ...), condition=%wide.region_26.27_spmd.clone, body=%wide.region_25.26_spmd.clone.sunk | while | flops 1804324 | bytes 1088003 | solution.py:71
  (1383 shorter events, 219.8 us)
Async XLA Ops:
  1.4 16.9 %collective-permute-start.12 = (f32[1,1,1,2,128]{4,3,2,1,0:T(2,128)S(1)}, f32[1,1,1,2,128]{4,3,2,1,0:T(2,128)S(1)}, u32[]{:S(2)}, u32[]{:S(2)}) collective-permute-start(f32[1,1,1,2,128]{4,3,2,1,0:T(2,128)S(1)} %compare_convert_fusion.6), channel_id=1, source_target_pairs={{0,8},{8,16},{16,24},{1,9},{9,17},{17,25},{2,10},{10,18},{18,26},{... | collective-permute-start | bytes 3080 | tf_op jit(solution)/shard_map/ppermute | solution.py:24
  6.4 13.1 %collective-permute-start.13 = (f32[1,1,1,2,128]{4,3,2,1,0:T(2,128)S(1)}, f32[1,1,1,2,128]{4,3,2,1,0:T(2,128)S(1)}, u32[]{:S(2)}, u32[]{:S(2)}) collective-permute-start(f32[1,1,1,2,128]{4,3,2,1,0:T(2,128)S(1)} %compare_convert_fusion.6), channel_id=1, source_target_pairs={{8,0},{16,8},{24,16},{9,1},{17,9},{25,17},{10,2},{18,10},{26,18},{... | collective-permute-start | bytes 3080 | tf_op jit(solution)/shard_map/ppermute | solution.py:26
  7.7 15.2 %collective-permute-start = (f32[3,1,1,2,128]{4,0,3,2,1:T(4,128)S(1)}, f32[3,1,1,2,128]{4,0,3,2,1:T(4,128)S(1)}, u32[]{:S(2)}, u32[]{:S(2)}) collective-permute-start(f32[3,1,1,2,128]{4,0,3,2,1:T(4,128)S(1)} %copy.12), channel_id=1, source_target_pairs={{0,8},{8,16},{16,24},{1,9},{9,17},{17,25},{2,10},{10,18},{18,26},{... | collective-permute-start | bytes 9224 | tf_op jit(solution)/shard_map/ppermute | solution.py:24
  12.3 12.0 %collective-permute-start.1 = (f32[3,1,1,2,128]{4,0,3,2,1:T(4,128)S(1)}, f32[3,1,1,2,128]{4,0,3,2,1:T(4,128)S(1)}, u32[]{:S(2)}, u32[]{:S(2)}) collective-permute-start(f32[3,1,1,2,128]{4,0,3,2,1:T(4,128)S(1)} %copy.12), channel_id=1, source_target_pairs={{8,0},{16,8},{24,16},{9,1},{17,9},{25,17},{10,2},{18,10},{26,18},{... | collective-permute-start | bytes 9224 | tf_op jit(solution)/shard_map/ppermute | solution.py:26
  13.6 15.3 %collective-permute-start.6 = (f32[3,1,1,2,128]{4,3,2,1,0:T(2,128)S(1)}, f32[3,1,1,2,128]{4,3,2,1,0:T(2,128)S(1)}, u32[]{:S(2)}, u32[]{:S(2)}) collective-permute-start(f32[3,1,1,2,128]{4,3,2,1,0:T(2,128)S(1)} %copy-done), channel_id=1, source_target_pairs={{0,8},{8,16},{16,24},{1,9},{9,17},{17,25},{2,10},{10,18},{18,26},{... | collective-permute-start | bytes 9224 | tf_op jit(solution)/shard_map/ppermute | solution.py:24
  18.2 14.6 %collective-permute-start.7 = (f32[3,1,1,2,128]{4,3,2,1,0:T(2,128)S(1)}, f32[3,1,1,2,128]{4,3,2,1,0:T(2,128)S(1)}, u32[]{:S(2)}, u32[]{:S(2)}) collective-permute-start(f32[3,1,1,2,128]{4,3,2,1,0:T(2,128)S(1)} %copy-done), channel_id=1, source_target_pairs={{8,0},{16,8},{24,16},{9,1},{17,9},{25,17},{10,2},{18,10},{26,18},{... | collective-permute-start | bytes 9224 | tf_op jit(solution)/shard_map/ppermute | solution.py:26
  19.5 10.7 %collective-permute-start.14 = (f32[1,3,1,2,128]{4,3,2,1,0:T(2,128)S(1)}, f32[1,3,1,2,128]{4,3,2,1,0:T(2,128)S(1)}, u32[]{:S(2)}, u32[]{:S(2)}) collective-permute-start(f32[1,3,1,2,128]{4,3,2,1,0:T(2,128)S(1)} %pad_maximum_fusion.17), channel_id=1, source_target_pairs={{0,4},{1,5},{2,6},{3,7},{8,12},{9,13},{10,14},{11,15},{16,20},{17,... | collective-permute-start | bytes 9224 | tf_op jit(solution)/shard_map/ppermute | solution.py:24
  23.0 7.2 %collective-permute-start.15 = (f32[1,3,1,2,128]{4,3,2,1,0:T(2,128)S(1)}, f32[1,3,1,2,128]{4,3,2,1,0:T(2,128)S(1)}, u32[]{:S(2)}, u32[]{:S(2)}) collective-permute-start(f32[1,3,1,2,128]{4,3,2,1,0:T(2,128)S(1)} %pad_maximum_fusion.17), channel_id=1, source_target_pairs={{4,0},{5,1},{6,2},{7,3},{12,8},{13,9},{14,10},{15,11},{20,16},{21,... | collective-permute-start | bytes 9224 | tf_op jit(solution)/shard_map/ppermute | solution.py:26
  24.3 23.4 %collective-permute-start.2 = (f32[3,3,1,2,128]{4,0,3,2,1:T(4,128)S(1)}, f32[3,3,1,2,128]{4,0,3,2,1:T(4,128)S(1)}, u32[]{:S(2)}, u32[]{:S(2)}) collective-permute-start(f32[3,3,1,2,128]{4,0,3,2,1:T(4,128)S(1)} %constant_dynamic-update-slice_fusion), channel_id=1, source_target_pairs={{0,4},{1,5},{2,6},{3,7},{8,12},{9,13},{10,14},{11,15},{16,20},{17,... | collective-permute-start | bytes 27656 | tf_op jit(solution)/shard_map/ppermute | solution.py:24
  28.9 18.8 %collective-permute-start.3 = (f32[3,3,1,2,128]{4,0,3,2,1:T(4,128)S(1)}, f32[3,3,1,2,128]{4,0,3,2,1:T(4,128)S(1)}, u32[]{:S(2)}, u32[]{:S(2)}) collective-permute-start(f32[3,3,1,2,128]{4,0,3,2,1:T(4,128)S(1)} %constant_dynamic-update-slice_fusion), channel_id=1, source_target_pairs={{4,0},{5,1},{6,2},{7,3},{12,8},{13,9},{14,10},{15,11},{20,16},{21,... | collective-permute-start | bytes 27656 | tf_op jit(solution)/shard_map/ppermute | solution.py:26
  30.3 7.2 %collective-permute-start.16 = (f32[1,3,3,1,128]{4,3,2,1,0:T(1,128)S(1)}, f32[1,3,3,1,128]{4,3,2,1,0:T(1,128)S(1)}, u32[]{:S(2)}, u32[]{:S(2)}) collective-permute-start(f32[1,3,3,1,128]{4,3,2,1,0:T(1,128)S(1)} %get-tuple-element.1899), channel_id=1, source_target_pairs={{0,1},{1,2},{2,3},{4,5},{5,6},{6,7},{8,9},{9,10},{10,11},{12,13},{... | collective-permute-start | bytes 13832 | tf_op jit(solution)/shard_map/ppermute | solution.py:24
  31.6 7.2 %collective-permute-start.17 = (f32[1,3,3,1,128]{4,3,2,1,0:T(1,128)S(1)}, f32[1,3,3,1,128]{4,3,2,1,0:T(1,128)S(1)}, u32[]{:S(2)}, u32[]{:S(2)}) collective-permute-start(f32[1,3,3,1,128]{4,3,2,1,0:T(1,128)S(1)} %get-tuple-element.1900), channel_id=1, source_target_pairs={{1,0},{2,1},{3,2},{5,4},{6,5},{7,6},{9,8},{10,9},{11,10},{13,12},{... | collective-permute-start | bytes 13832 | tf_op jit(solution)/shard_map/ppermute | solution.py:26
  32.9 5.9 %collective-permute-start.8 = (f32[3,3,1,2,128]{4,3,2,1,0:T(2,128)S(1)}, f32[3,3,1,2,128]{4,3,2,1,0:T(2,128)S(1)}, u32[]{:S(2)}, u32[]{:S(2)}) collective-permute-start(f32[3,3,1,2,128]{4,3,2,1,0:T(2,128)S(1)} %constant_dynamic-update-slice_fusion.3), channel_id=1, source_target_pairs={{0,4},{1,5},{2,6},{3,7},{8,12},{9,13},{10,14},{11,15},{16,20},{17,... | collective-permute-start | bytes 27656 | tf_op jit(solution)/shard_map/ppermute | solution.py:24
  37.5 5.6 %collective-permute-start.9 = (f32[3,3,1,2,128]{4,3,2,1,0:T(2,128)S(1)}, f32[3,3,1,2,128]{4,3,2,1,0:T(2,128)S(1)}, u32[]{:S(2)}, u32[]{:S(2)}) collective-permute-start(f32[3,3,1,2,128]{4,3,2,1,0:T(2,128)S(1)} %constant_dynamic-update-slice_fusion.3), channel_id=1, source_target_pairs={{4,0},{5,1},{6,2},{7,3},{12,8},{13,9},{14,10},{15,11},{20,16},{21,... | collective-permute-start | bytes 27656 | tf_op jit(solution)/shard_map/ppermute | solution.py:26
  43.1 11.7 %collective-permute-start.10 = (f32[3,3,3,1,128]{4,3,2,1,0:T(1,128)S(1)}, f32[3,3,3,1,128]{4,3,2,1,0:T(1,128)S(1)}, u32[]{:S(2)}, u32[]{:S(2)}) collective-permute-start(f32[3,3,3,1,128]{4,3,2,1,0:T(1,128)S(1)} %get-tuple-element.1889), channel_id=1, source_target_pairs={{0,1},{1,2},{2,3},{4,5},{5,6},{6,7},{8,9},{9,10},{10,11},{12,13},{... | collective-permute-start | bytes 41480 | tf_op jit(solution)/shard_map/ppermute | solution.py:24
  46.4 8.4 %collective-permute-start.11 = (f32[3,3,3,1,128]{4,3,2,1,0:T(1,128)S(1)}, f32[3,3,3,1,128]{4,3,2,1,0:T(1,128)S(1)}, u32[]{:S(2)}, u32[]{:S(2)}) collective-permute-start(f32[3,3,3,1,128]{4,3,2,1,0:T(1,128)S(1)} %get-tuple-element.1890), channel_id=1, source_target_pairs={{1,0},{2,1},{3,2},{5,4},{6,5},{7,6},{9,8},{10,9},{11,10},{13,12},{... | collective-permute-start | bytes 41480 | tf_op jit(solution)/shard_map/ppermute | solution.py:26
  47.7 7.1 %collective-permute-start.4 = (f32[3,3,3,1,128]{4,0,3,2,1:T(4,128)S(1)}, f32[3,3,3,1,128]{4,0,3,2,1:T(4,128)S(1)}, u32[]{:S(2)}, u32[]{:S(2)}) collective-permute-start(f32[3,3,3,1,128]{4,0,3,2,1:T(4,128)S(1)} %get-tuple-element.1885), channel_id=1, source_target_pairs={{0,1},{1,2},{2,3},{4,5},{5,6},{6,7},{8,9},{9,10},{10,11},{12,13},{... | collective-permute-start | bytes 41480 | tf_op jit(solution)/shard_map/ppermute | solution.py:24
  83.0 5.8 %collective-permute-start.18 = (f32[3,1,1,2,128]{4,3,2,1,0:T(2,128)S(1)}, f32[3,1,1,2,128]{4,3,2,1,0:T(2,128)S(1)}, u32[]{:S(2)}, u32[]{:S(2)}) collective-permute-start(f32[3,1,1,2,128]{4,3,2,1,0:T(2,128)S(1)} %fusion.106), channel_id=1, source_target_pairs={{0,8},{8,16},{16,24},{1,9},{9,17},{17,25},{2,10},{10,18},{18,26},{... | collective-permute-start | bytes 9224 | tf_op jit(solution)/shard_map/ppermute | solution.py:24
  87.5 5.5 %collective-permute-start.19 = (f32[3,1,1,2,128]{4,3,2,1,0:T(2,128)S(1)}, f32[3,1,1,2,128]{4,3,2,1,0:T(2,128)S(1)}, u32[]{:S(2)}, u32[]{:S(2)}) collective-permute-start(f32[3,1,1,2,128]{4,3,2,1,0:T(2,128)S(1)} %fusion.106), channel_id=1, source_target_pairs={{8,0},{16,8},{24,16},{9,1},{17,9},{25,17},{10,2},{18,10},{26,18},{... | collective-permute-start | bytes 9224 | tf_op jit(solution)/shard_map/ppermute | solution.py:26
  94.6 5.6 %collective-permute-start.21 = (f32[3,3,1,2,128]{4,3,2,1,0:T(2,128)S(1)}, f32[3,3,1,2,128]{4,3,2,1,0:T(2,128)S(1)}, u32[]{:S(2)}, u32[]{:S(2)}) collective-permute-start(f32[3,3,1,2,128]{4,3,2,1,0:T(2,128)S(1)} %pad_maximum_fusion.12), channel_id=1, source_target_pairs={{4,0},{5,1},{6,2},{7,3},{12,8},{13,9},{14,10},{15,11},{20,16},{21,... | collective-permute-start | bytes 27656 | tf_op jit(solution)/shard_map/ppermute | solution.py:26
  101.8 5.5 %collective-permute-start.23 = (f32[3,3,3,1,128]{4,3,2,1,0:T(1,128)S(1)}, f32[3,3,3,1,128]{4,3,2,1,0:T(1,128)S(1)}, u32[]{:S(2)}, u32[]{:S(2)}) collective-permute-start(f32[3,3,3,1,128]{4,3,2,1,0:T(1,128)S(1)} %get-tuple-element.1888), channel_id=1, source_target_pairs={{1,0},{2,1},{3,2},{5,4},{6,5},{7,6},{9,8},{10,9},{11,10},{13,12},{... | collective-permute-start | bytes 41480 | tf_op jit(solution)/shard_map/ppermute | solution.py:26
  151.1 5.5 %collective-permute-start.25 = (f32[1,1,1,2,128]{4,3,2,1,0:T(2,128)S(1)}, f32[1,1,1,2,128]{4,3,2,1,0:T(2,128)S(1)}, u32[]{:S(2)}, u32[]{:S(2)}) collective-permute-start(f32[1,1,1,2,128]{4,3,2,1,0:T(2,128)S(1)} %bitcast_divide_fusion.3), channel_id=1, source_target_pairs={{8,0},{16,8},{24,16},{9,1},{17,9},{25,17},{10,2},{18,10},{26,18},{... | collective-permute-start | bytes 3080 | tf_op jit(solution)/shard_map/ppermute | solution.py:26
  158.2 5.5 %collective-permute-start.27 = (f32[1,3,1,2,128]{4,3,2,1,0:T(2,128)S(1)}, f32[1,3,1,2,128]{4,3,2,1,0:T(2,128)S(1)}, u32[]{:S(2)}, u32[]{:S(2)}) collective-permute-start(f32[1,3,1,2,128]{4,3,2,1,0:T(2,128)S(1)} %pad_maximum_fusion.18), channel_id=1, source_target_pairs={{4,0},{5,1},{6,2},{7,3},{12,8},{13,9},{14,10},{15,11},{20,16},{21,... | collective-permute-start | bytes 9224 | tf_op jit(solution)/shard_map/ppermute | solution.py:26
  236.0 5.5 %collective-permute-start.31 = (f32[1,1,1,2,128]{4,3,2,1,0:T(2,128)S(1)}, f32[1,1,1,2,128]{4,3,2,1,0:T(2,128)S(1)}, u32[]{:S(2)}, u32[]{:S(2)}) collective-permute-start(f32[1,1,1,2,128]{4,3,2,1,0:T(2,128)S(1)} %bitcast_divide_fusion.2), channel_id=1, source_target_pairs={{8,0},{16,8},{24,16},{9,1},{17,9},{25,17},{10,2},{18,10},{26,18},{... | collective-permute-start | bytes 3080 | tf_op jit(solution)/shard_map/ppermute | solution.py:26
  241.5 5.7 %collective-permute-start.32 = (f32[1,3,1,2,128]{4,3,2,1,0:T(2,128)S(1)}, f32[1,3,1,2,128]{4,3,2,1,0:T(2,128)S(1)}, u32[]{:S(2)}, u32[]{:S(2)}) collective-permute-start(f32[1,3,1,2,128]{4,3,2,1,0:T(2,128)S(1)} %pad_maximum_fusion.19), channel_id=1, source_target_pairs={{0,4},{1,5},{2,6},{3,7},{8,12},{9,13},{10,14},{11,15},{16,20},{17,... | collective-permute-start | bytes 9224 | tf_op jit(solution)/shard_map/ppermute | solution.py:24
  245.9 5.5 %collective-permute-start.33 = (f32[1,3,1,2,128]{4,3,2,1,0:T(2,128)S(1)}, f32[1,3,1,2,128]{4,3,2,1,0:T(2,128)S(1)}, u32[]{:S(2)}, u32[]{:S(2)}) collective-permute-start(f32[1,3,1,2,128]{4,3,2,1,0:T(2,128)S(1)} %pad_maximum_fusion.19), channel_id=1, source_target_pairs={{4,0},{5,1},{6,2},{7,3},{12,8},{13,9},{14,10},{15,11},{20,16},{21,... | collective-permute-start | bytes 9224 | tf_op jit(solution)/shard_map/ppermute | solution.py:26
  326.3 5.5 %collective-permute-start.37 = (f32[1,1,1,2,128]{4,3,2,1,0:T(2,128)S(1)}, f32[1,1,1,2,128]{4,3,2,1,0:T(2,128)S(1)}, u32[]{:S(2)}, u32[]{:S(2)}) collective-permute-start(f32[1,1,1,2,128]{4,3,2,1,0:T(2,128)S(1)} %fusion.117), channel_id=1, source_target_pairs={{8,0},{16,8},{24,16},{9,1},{17,9},{25,17},{10,2},{18,10},{26,18},{... | collective-permute-start | bytes 3080 | tf_op jit(solution)/shard_map/ppermute | solution.py:26
  331.8 5.7 %collective-permute-start.38 = (f32[1,3,1,2,128]{4,3,2,1,0:T(2,128)S(1)}, f32[1,3,1,2,128]{4,3,2,1,0:T(2,128)S(1)}, u32[]{:S(2)}, u32[]{:S(2)}) collective-permute-start(f32[1,3,1,2,128]{4,3,2,1,0:T(2,128)S(1)} %pad_maximum_fusion.20), channel_id=1, source_target_pairs={{0,4},{1,5},{2,6},{3,7},{8,12},{9,13},{10,14},{11,15},{16,20},{17,... | collective-permute-start | bytes 9224 | tf_op jit(solution)/shard_map/ppermute | solution.py:24
  336.2 5.5 %collective-permute-start.39 = (f32[1,3,1,2,128]{4,3,2,1,0:T(2,128)S(1)}, f32[1,3,1,2,128]{4,3,2,1,0:T(2,128)S(1)}, u32[]{:S(2)}, u32[]{:S(2)}) collective-permute-start(f32[1,3,1,2,128]{4,3,2,1,0:T(2,128)S(1)} %pad_maximum_fusion.20), channel_id=1, source_target_pairs={{4,0},{5,1},{6,2},{7,3},{12,8},{13,9},{14,10},{15,11},{20,16},{21,... | collective-permute-start | bytes 9224 | tf_op jit(solution)/shard_map/ppermute | solution.py:26
  416.0 5.5 %collective-permute-start.43 = (f32[1,1,1,2,128]{4,3,2,1,0:T(2,128)S(1)}, f32[1,1,1,2,128]{4,3,2,1,0:T(2,128)S(1)}, u32[]{:S(2)}, u32[]{:S(2)}) collective-permute-start(f32[1,1,1,2,128]{4,3,2,1,0:T(2,128)S(1)} %multiply_add_fusion.1), channel_id=1, source_target_pairs={{8,0},{16,8},{24,16},{9,1},{17,9},{25,17},{10,2},{18,10},{26,18},{... | collective-permute-start | bytes 3080 | tf_op jit(solution)/shard_map/ppermute | solution.py:26
  421.5 6.3 %collective-permute-start.44 = (f32[1,3,1,2,128]{4,3,2,1,0:T(2,128)S(1)}, f32[1,3,1,2,128]{4,3,2,1,0:T(2,128)S(1)}, u32[]{:S(2)}, u32[]{:S(2)}) collective-permute-start(f32[1,3,1,2,128]{4,3,2,1,0:T(2,128)S(1)} %pad_maximum_fusion.21), channel_id=1, source_target_pairs={{0,4},{1,5},{2,6},{3,7},{8,12},{9,13},{10,14},{11,15},{16,20},{17,... | collective-permute-start | bytes 9224 | tf_op jit(solution)/shard_map/ppermute | solution.py:24
  425.8 5.5 %collective-permute-start.45 = (f32[1,3,1,2,128]{4,3,2,1,0:T(2,128)S(1)}, f32[1,3,1,2,128]{4,3,2,1,0:T(2,128)S(1)}, u32[]{:S(2)}, u32[]{:S(2)}) collective-permute-start(f32[1,3,1,2,128]{4,3,2,1,0:T(2,128)S(1)} %pad_maximum_fusion.21), channel_id=1, source_target_pairs={{4,0},{5,1},{6,2},{7,3},{12,8},{13,9},{14,10},{15,11},{20,16},{21,... | collective-permute-start | bytes 9224 | tf_op jit(solution)/shard_map/ppermute | solution.py:26
  (20 other events, 83.0 us)
where the time goes:
time: 473 us; the launch traced here: 470 us
  blocking collectives  118 us (25%)
  starting transfers between devices  108 us (23%)
  matrix products  72 us (15%)
  waiting for transfers between devices  68.5 us (14%)
  other arithmetic  63.7 us (13%)
  loops' own time  19.8 us (4%)
  between operations  11.1 us (2%)
  local copies, waits for them, and re-layouts  8.18 us (2%)
    psum x3, blocking collectives, paired_sums(): lax.psum((jnp.sum(residual * precond), jnp.sum(precond * applied)), ('gx'...  118 us
    ppermute x24, starting transfers between devices, with_halo(): lax.ppermute(tail, axis, [(i, (i + 1) % count) for i in range(ends)])  76.9 us
    ppermute x24, waiting for transfers between devices, with_halo(): lax.ppermute(head, axis, [((i + 1) % count, i) for i in range(ends)])  68.4 us
    ppermute x24, starting transfers between devices, with_halo(): lax.ppermute(head, axis, [((i + 1) % count, i) for i in range(ends)])  31 us
    dot_general x81, matrix products, laplace_fold(): jnp.einsum('tij,ctj->cti', weight, near_field, precision=lax.Precision.HI...  30.4 us
    sub x162, other arithmetic, one_offset(): offset = own_positions[:, :, :, None] - near_positions[:, :, None, :]  26.4 us
    another operation x6, loops' own time, slab_totals(): return lax.fori_loop(0, 27, one_offset, start_totals)  19.8 us
    dot_general x27, matrix products, divergence_fold(): jnp.einsum('ctij,ctj->ti', levered, near_field, precision=lax.Precision.H...  16.7 us
  transfers between devices with their start and end apart: 48, of which 18 were waited for; matrix products, arithmetic and copies ran while one was open for 0% of the time, Pallas kernels for 0%

commit v1 on v0

v1 whole, which is shorter than its diff:
```python
import jax
import jax.numpy as jnp
from jax import lax
from jax.sharding import PartitionSpec as P

ITERS = 3

DIAG_SHIFT = 0.05
VISCOSITY = 0.5
GRAVITY = 0.1
GRADIENT_GAIN = 32.0

AXES = (("gx", 1), ("gy", 2), ("gz", 3))


def with_halo(cells, sides, width):
    for axis, dim in sides:
        count = lax.axis_size(axis)
        ends = count - 1
        head = lax.slice_in_dim(cells, 0, width, axis=dim)
        tail = lax.slice_in_dim(cells, cells.shape[dim] - width, cells.shape[dim], axis=dim)
        cells = jnp.concatenate(
            [
                lax.ppermute(tail, axis, [(i, (i + 1) % count) for i in range(ends)]),
                cells,
                lax.ppermute(head, axis, [((i + 1) % count, i) for i in range(ends)]),
            ],
            axis=dim,
        )
    return cells


def neighbours(rim):
    comps, size_x, size_y, size_z, width = rim.shape
    blocks = []
    for ax in range(size_x - 2):
        for ay in range(size_y - 2):
            for az in range(size_z - 2):
                window = rim[:, ax:ax + 3, ay:ay + 3, az:az + 3, :]
                blocks.append(window.reshape(comps, 27 * width))
    return jnp.stack(blocks, axis=1)


def flat(cells):
    return cells.reshape(cells.shape[0], -1, cells.shape[4])


def wsum(weight, near):
    return jnp.sum(weight[None] * near[:, :, None, :], axis=-1)


def tile_corners(block_shape):
    _, size_x, size_y, size_z, _ = block_shape
    base = (
        lax.axis_index("gx") * size_x,
        lax.axis_index("gy") * size_y,
        lax.axis_index("gz") * size_z,
    )
    corners = []
    for ax in range(size_x):
        for ay in range(size_y):
            for az in range(size_z):
                corners.append(jnp.stack([base[0] + ax, base[1] + ay, base[2] + az]))
    return jnp.stack(corners, axis=1).astype(jnp.float32)


def on_device(positions, velocity, counts):
    block_shape = positions.shape
    width = positions.shape[4]
    slot_ids = jnp.arange(width, dtype=jnp.int32)
    valid_mask = (slot_ids[None, None, None, :] < counts[:, :, :, None]).astype(jnp.float32)[None]
    packed = jnp.concatenate([positions, valid_mask, velocity], axis=0)
    near_all = neighbours(with_halo(packed, AXES, 1))
    near_x = near_all[0:3]
    near_valid = near_all[3]
    near_v = near_all[4:7]
    own_x = flat(positions)
    own_valid = flat(valid_mask)[0]
    own_v = flat(velocity)

    offset = own_x[:, :, :, None] - near_x[:, :, None, :]
    distance = offset[0] * offset[0] + offset[1] * offset[1] + offset[2] * offset[2]
    closeness = jnp.maximum(1.0 - distance, 0.0)
    weight = closeness * closeness * own_valid[:, :, None] * near_valid[:, None, :]

    corner = tile_corners(block_shape)[:, :, None]
    local_own = own_x - corner
    local_near = near_x - corner

    row = jnp.sum(weight, axis=-1)[None]
    sums = wsum(weight, jnp.concatenate([near_v, local_near], axis=0))
    near_sums = sums[0:3]
    lever = local_own * row - sums[3:6]

    gravity_pull = jnp.array([0.0, 0.0, -GRAVITY], jnp.float32).reshape(3, 1, 1)
    predicted = own_valid[None] * (
        own_v + VISCOSITY / width * (near_sums - row * own_v) + gravity_pull
    )
    diagonal = DIAG_SHIFT + row / width

    def shaped(values):
        return values.reshape(values.shape[0], *block_shape[1:])

    near_pred = neighbours(with_halo(shaped(predicted), AXES, 1))
    dotted = jnp.sum(near_pred * local_near, axis=0, keepdims=True)
    psums = wsum(weight, jnp.concatenate([near_pred, dotted], axis=0))
    flux = jnp.sum(local_own * psums[0:3], axis=0, keepdims=True) - psums[3:4]
    source = -(GRADIENT_GAIN / width) * (
        jnp.sum(predicted * lever, axis=0, keepdims=True) - flux
    )

    def operate(field):
        near_field = neighbours(with_halo(shaped(field), AXES, 1))
        return near_field, diagonal * field - wsum(weight, near_field) / width

    def paired_sums(residual, precond, applied):
        pair = jnp.stack([jnp.sum(residual * precond), jnp.sum(precond * applied)])
        total = lax.psum(pair, ("gx", "gy", "gz"))
        return total[0], total[1]

    pressure = jnp.zeros_like(source)
    residual = source
    precond = residual / diagonal
    near_dir, applied = operate(precond)
    norm_now, curvature_sum = paired_sums(residual, precond, applied)
    step_size = norm_now / curvature_sum
    direction = precond
    along = applied
    near_pressure = jnp.zeros_like(near_dir)
    for iteration in range(ITERS):
        pressure = pressure + step_size * direction
        near_pressure = near_pressure + step_size * near_dir
        residual = residual - step_size * along
        if iteration + 1 < ITERS:
            precond = residual / diagonal
            near_fresh, applied = operate(precond)
            norm_next, curvature_sum = paired_sums(residual, precond, applied)
            blend = norm_next / norm_now
            step_size = norm_next / (curvature_sum - blend * norm_next / step_size)
            direction = precond + blend * direction
            near_dir = near_fresh + blend * near_dir
            along = applied + blend * along
            norm_now = norm_next

    grads = wsum(weight, jnp.concatenate([near_pressure, near_pressure * local_near], axis=0))
    moments = local_own * grads[0:1] - grads[1:4]
    velocity_new = predicted - GRADIENT_GAIN / width * (pressure * lever - moments)
    return (shaped(velocity_new), shaped(pressure)[0])


def solution(mesh):
    in_specs = (
        P(None, "gx", "gy", "gz", None),
        P(None, "gx", "gy", "gz", None),
        P("gx", "gy", "gz"),
    )
    out_specs = (P(None, "gx", "gy", "gz", None), P("gx", "gy", "gz", None))
    return jax.shard_map(
        on_device, mesh=mesh, in_specs=in_specs, out_specs=out_specs, check_vma=False
    )
```

time: 473 us -> 322 us (0.68)
  matrix products: 72 us -> 0 us
  waiting for transfers between devices: 68.5 us -> 25.9 us
  starting transfers between devices: 108 us -> 76 us
  local copies, waits for them, and re-layouts: 8.18 us -> 32.6 us
  other arithmetic: 63.7 us -> 41.9 us
  loops' own time: 19.8 us -> 0 us
  blocking collectives: 118 us -> 132 us
    dot_general x162 -> x0, matrix products: 72 us -> none  [the longest x81 30.4 us: laplace_fold(): jnp.einsum('tij,ctj->cti', weight, near_field, precision=lax.Precision.HI...]
    ppermute x24 -> x15, waiting for transfers between devices: 68.4 us -> 13.5 us  [with_halo(): lax.ppermute(head, axis, [((i + 1) % count, i) for i in range(ends)])]
    sub x163 -> x2, other arithmetic: 27 us -> 1.58 us  [the longest x1 1.5 us: on_device(): offset = own_x[:, :, :, None] - near_x[:, :, None, :]]
    ppermute x24 -> x15, starting transfers between devices: 76.9 us -> 56.6 us  [with_halo(): lax.ppermute(tail, axis, [(i, (i + 1) % count) for i in range(ends)])]
    another operation x6 -> x0, loops' own time: 19.8 us -> none  [slab_totals(): return lax.fori_loop(0, 27, one_offset, start_totals)]
    another operation x0 -> x15, local copies, waits for them, and re-layouts: none -> 19.3 us  [neighbours(): return jnp.stack(blocks, axis=1)]
    mul x217 -> x3, other arithmetic: 17.1 us -> 1.37 us  [the longest x1 0.93 us: on_device(): near_pressure * local_near]
    psum x3, blocking collectives: 118 us -> 132 us  [paired_sums(): total = lax.psum(pair, ('gx', 'gy', 'gz'))]
  transfers between devices with their start and end apart: 48 -> 30, of which waited for: 18 -> 13; matrix products, arithmetic and copies ran while one was open for 0% -> 2% of each run, Pallas kernels for 0% -> 0%
where the time goes in v1:
time: 322 us; the launch traced here: 319 us
  blocking collectives  132 us (41%)
  starting transfers between devices  76 us (24%)
  other arithmetic  41.9 us (13%)
  local copies, waits for them, and re-layouts  32.6 us (10%)
  waiting for transfers between devices  25.9 us (8%)
  between operations  11.2 us (3%)
    psum x3, blocking collectives, paired_sums(): total = lax.psum(pair, ('gx', 'gy', 'gz'))  132 us
    ppermute x15, starting transfers between devices, with_halo(): lax.ppermute(tail, axis, [(i, (i + 1) % count) for i in range(ends)])  56.6 us
    ppermute x15, starting transfers between devices, with_halo(): lax.ppermute(head, axis, [((i + 1) % count, i) for i in range(ends)])  19.5 us
    another operation x15, local copies, waits for them, and re-layouts, neighbours(): return jnp.stack(blocks, axis=1)  19.3 us
    ppermute x15, waiting for transfers between devices, with_halo(): lax.ppermute(head, axis, [((i + 1) % count, i) for i in range(ends)])  13.5 us
    reduce_sum x6, other arithmetic, wsum(): return jnp.sum(weight[None] * near[:, :, None, :], axis=-1)  12.6 us
    ppermute x15, waiting for transfers between devices, with_halo(): lax.ppermute(tail, axis, [(i, (i + 1) % count) for i in range(ends)])  12.3 us
  transfers between devices with their start and end apart: 30, of which 13 were waited for; matrix products, arithmetic and copies ran while one was open for 2% of the time, Pallas kernels for 0%

profile of v1, /device:TPU:0, one launch (start us, length us, event | category | flops | bytes accessed | tf_op | source)
XLA Modules:
  0.0 319.3 jit_solution(7614055411883678423)
XLA Ops:
  4.0 5.6 %collective-permute-start = (f32[7,1,1,2,128]{4,0,3,2,1:T(8,128)S(1)}, f32[7,1,1,2,128]{4,0,3,2,1:T(8,128)S(1)}, u32[]{:S(2)}, u32[]{:S(2)}) collective-permute-start(f32[7,1,1,2,128]{4,0,3,2,1:T(8,128)S(1)} %pad_maximum_fusion.19), channel_id=1, source_target_pairs={{0,8},{8,16},{16,24},{1,9},{9,17},{17,25},{2,10},{10,18},{18,26},{... | collective-permute-start | bytes 21512 | tf_op jit(solution)/shard_map/ppermute | solution.py:24
  12.3 4.5 %collective-permute-start.2 = (f32[7,3,1,2,128]{4,0,3,2,1:T(8,128)S(1)}, f32[7,3,1,2,128]{4,0,3,2,1:T(8,128)S(1)}, u32[]{:S(2)}, u32[]{:S(2)}) collective-permute-start(f32[7,3,1,2,128]{4,0,3,2,1:T(8,128)S(1)} %pad_maximum_fusion.11), channel_id=1, source_target_pairs={{0,4},{1,5},{2,6},{3,7},{8,12},{9,13},{10,14},{11,15},{16,20},{17,... | collective-permute-start | bytes 64520 | tf_op jit(solution)/shard_map/ppermute | solution.py:24
  21.0 3.9 %collective-permute-done.5 = f32[7,3,3,1,128]{4,0,3,2,1:T(8,128)S(1)} collective-permute-done((f32[7,3,3,1,128]{4,0,3,2,1:T(8,128)S(1)}, f32[7,3,3,1,128]{4,0,3,2,1:T(8,128)S(1)}, u32[]{:S(2)}, u32[]{:S(2)}) %collective-permute-start.5) | collective-permute-done | bytes 32288 | tf_op jit(solution)/shard_map/ppermute | solution.py:26
  25.7 1.5 broadcast_subtract_fusion
  27.2 1.6 fusion.6
  29.3 1.7 copy-done
  31.0 1.8 multiply_reduce_fusion
  34.2 4.8 %collective-permute-start.6 = (f32[3,1,1,2,128]{4,3,0,2,1:T(2,128)S(1)}, f32[3,1,1,2,128]{4,3,0,2,1:T(2,128)S(1)}, u32[]{:S(2)}, u32[]{:S(2)}) collective-permute-start(f32[3,1,1,2,128]{4,3,0,2,1:T(2,128)S(1)} %bitcast.144), channel_id=1, source_target_pairs={{0,8},{8,16},{16,24},{1,9},{9,17},{17,25},{2,10},{10,18},{18,26},{... | collective-permute-start | bytes 9224 | tf_op jit(solution)/shard_map/ppermute | solution.py:24
  41.7 4.5 %collective-permute-start.8 = (f32[3,3,1,2,128]{4,3,0,2,1:T(2,128)S(1)}, f32[3,3,1,2,128]{4,3,0,2,1:T(2,128)S(1)}, u32[]{:S(2)}, u32[]{:S(2)}) collective-permute-start(f32[3,3,1,2,128]{4,3,0,2,1:T(2,128)S(1)} %pad_maximum_fusion.15), channel_id=1, source_target_pairs={{0,4},{1,5},{2,6},{3,7},{8,12},{9,13},{10,14},{11,15},{16,20},{17,... | collective-permute-start | bytes 27656 | tf_op jit(solution)/shard_map/ppermute | solution.py:24
  49.5 3.8 %collective-permute-start.10 = (f32[3,3,3,1,128]{4,3,0,2,1:T(1,128)}, f32[3,3,3,1,128]{4,3,0,2,1:T(1,128)}, u32[]{:S(2)}, u32[]{:S(2)}) collective-permute-start(f32[3,3,3,1,128]{4,3,0,2,1:T(1,128)} %get-tuple-element.28), channel_id=1, source_target_pairs={{0,1},{1,2},{2,3},{4,5},{5,6},{6,7},{8,9},{9,10},{10,11},{12,13},{... | collective-permute-start | bytes 41480 | tf_op jit(solution)/shard_map/ppermute | solution.py:24
  54.7 1.5 pad_maximum_fusion.5
  56.8 1.5 stack_reshape.32
  61.1 1.5 stack_reshape.33
  62.6 1.4 constant_dynamic-update-slice_fusion
  66.1 3.3 %multiply_reduce_fusion.2 = f32[4,2,128]{2,1,0:T(2,128)S(1)} fusion(f32[4,2,3456]{2,1,0:T(2,128)S(1)} %copy.34, f32[2,128,3456]{2,1,0:T(8,128)} %copy-done), kind=kLoop, calls=%fused_computation.2 | loop fusion | flops 7076864 | bytes 3653632 | tf_op jit(solution)/shard_map/reduce_sum | solution.py:49
  71.4 4.6 %collective-permute-start.12 = (f32[1,1,1,2,128]{4,3,2,1,0:T(2,128)S(1)}, f32[1,1,1,2,128]{4,3,2,1,0:T(2,128)S(1)}, u32[]{:S(2)}, u32[]{:S(2)}) collective-permute-start(f32[1,1,1,2,128]{4,3,2,1,0:T(2,128)S(1)} %bitcast.160), channel_id=1, source_target_pairs={{0,8},{8,16},{16,24},{1,9},{9,17},{17,25},{2,10},{10,18},{18,26},{... | collective-permute-start | bytes 3080 | tf_op jit(solution)/shard_map/ppermute | solution.py:24
  78.6 4.5 %collective-permute-start.14 = (f32[1,3,1,2,128]{4,3,2,1,0:T(2,128)S(1)}, f32[1,3,1,2,128]{4,3,2,1,0:T(2,128)S(1)}, u32[]{:S(2)}, u32[]{:S(2)}) collective-permute-start(f32[1,3,1,2,128]{4,3,2,1,0:T(2,128)S(1)} %pad_maximum_fusion.20), channel_id=1, source_target_pairs={{0,4},{1,5},{2,6},{3,7},{8,12},{9,13},{10,14},{11,15},{16,20},{17,... | collective-permute-start | bytes 9224 | tf_op jit(solution)/shard_map/ppermute | solution.py:24
  84.5 1.5 collective-permute-start.16
  87.3 5.3 %collective-permute-done.17 = f32[1,3,3,1,128]{4,3,2,1,0:T(1,128)S(1)} collective-permute-done((f32[1,3,3,1,128]{4,3,2,1,0:T(1,128)S(1)}, f32[1,3,3,1,128]{4,3,2,1,0:T(1,128)S(1)}, u32[]{:S(2)}, u32[]{:S(2)}) %collective-permute-start.17) | collective-permute-done | bytes 4640 | tf_op jit(solution)/shard_map/ppermute | solution.py:26
  98.8 1.8 pad_maximum_fusion.23
  100.6 43.4 %psum.21 = f32[2]{0:T(128)} all-reduce(f32[2]{0:T(128)} %pad_maximum_fusion.23), channel_id=1, replica_groups=mesh['gx'=4,'gy'=2,'gz'=4] {'gx','gy','gz'}, use_global_device_ids=true, to_apply=%region_9.0 | all-reduce | flops 2 | bytes 16 | tf_op jit(solution)/shard_map/psum | solution.py:118
  148.7 4.5 %collective-permute-start.18 = (f32[1,1,1,2,128]{4,3,2,1,0:T(2,128)S(1)}, f32[1,1,1,2,128]{4,3,2,1,0:T(2,128)S(1)}, u32[]{:S(2)}, u32[]{:S(2)}) collective-permute-start(f32[1,1,1,2,128]{4,3,2,1,0:T(2,128)S(1)} %bitcast.149), channel_id=1, source_target_pairs={{0,8},{8,16},{16,24},{1,9},{9,17},{17,25},{2,10},{10,18},{18,26},{... | collective-permute-start | bytes 3080 | tf_op jit(solution)/shard_map/ppermute | solution.py:24
  155.9 4.5 %collective-permute-start.20 = (f32[1,3,1,2,128]{4,3,2,1,0:T(2,128)S(1)}, f32[1,3,1,2,128]{4,3,2,1,0:T(2,128)S(1)}, u32[]{:S(2)}, u32[]{:S(2)}) collective-permute-start(f32[1,3,1,2,128]{4,3,2,1,0:T(2,128)S(1)} %pad_maximum_fusion.21), channel_id=1, source_target_pairs={{0,4},{1,5},{2,6},{3,7},{8,12},{9,13},{10,14},{11,15},{16,20},{17,... | collective-permute-start | bytes 9224 | tf_op jit(solution)/shard_map/ppermute | solution.py:24
  164.4 4.3 %collective-permute-done.23 = f32[1,3,3,1,128]{4,3,2,1,0:T(1,128)S(1)} collective-permute-done((f32[1,3,3,1,128]{4,3,2,1,0:T(1,128)S(1)}, f32[1,3,3,1,128]{4,3,2,1,0:T(1,128)S(1)}, u32[]{:S(2)}, u32[]{:S(2)}) %collective-permute-start.23) | collective-permute-done | bytes 4640 | tf_op jit(solution)/shard_map/ppermute | solution.py:26
  175.5 1.8 pad_maximum_fusion.24
  177.4 43.4 %psum.22 = f32[2]{0:T(128)} all-reduce(f32[2]{0:T(128)} %pad_maximum_fusion.24), channel_id=1, replica_groups=mesh['gx'=4,'gy'=2,'gz'=4] {'gx','gy','gz'}, use_global_device_ids=true, to_apply=%region_13.0 | all-reduce | flops 2 | bytes 16 | tf_op jit(solution)/shard_map/psum | solution.py:118
  229.1 4.5 %collective-permute-start.24 = (f32[1,1,1,2,128]{4,3,2,1,0:T(2,128)S(1)}, f32[1,1,1,2,128]{4,3,2,1,0:T(2,128)S(1)}, u32[]{:S(2)}, u32[]{:S(2)}) collective-permute-start(f32[1,1,1,2,128]{4,3,2,1,0:T(2,128)S(1)} %bitcast.155), channel_id=1, source_target_pairs={{0,8},{8,16},{16,24},{1,9},{9,17},{17,25},{2,10},{10,18},{18,26},{... | collective-permute-start | bytes 3080 | tf_op jit(solution)/shard_map/ppermute | solution.py:24
  236.3 4.5 %collective-permute-start.26 = (f32[1,3,1,2,128]{4,3,2,1,0:T(2,128)S(1)}, f32[1,3,1,2,128]{4,3,2,1,0:T(2,128)S(1)}, u32[]{:S(2)}, u32[]{:S(2)}) collective-permute-start(f32[1,3,1,2,128]{4,3,2,1,0:T(2,128)S(1)} %pad_maximum_fusion.22), channel_id=1, source_target_pairs={{0,4},{1,5},{2,6},{3,7},{8,12},{9,13},{10,14},{11,15},{16,20},{17,... | collective-permute-start | bytes 9224 | tf_op jit(solution)/shard_map/ppermute | solution.py:24
  242.7 1.9 collective-permute-start.28
  244.6 1.5 collective-permute-start.29
  262.5 45.0 %psum.23 = f32[2]{0:T(128)S(1)} all-reduce(f32[2]{0:T(128)S(1)} %pad_maximum_fusion.25), channel_id=1, replica_groups=mesh['gx'=4,'gy'=2,'gz'=4] {'gx','gy','gz'}, use_global_device_ids=true, to_apply=%region_17.0 | all-reduce | flops 2 | bytes 16 | tf_op jit(solution)/shard_map/psum | solution.py:118
  315.3 3.3 %multiply_reduce_fusion.1 = f32[4,2,128]{2,1,0:T(2,128)S(1)} fusion(f32[4,2,3456]{2,1,0:T(2,128)S(1)} %copy.41, f32[2,128,3456]{2,1,0:T(8,128)} %copy-done), kind=kLoop, calls=%fused_computation.1 | loop fusion | flops 7076864 | bytes 3653632 | tf_op jit(solution)/shard_map/reduce_sum | solution.py:49
  (198 shorter events, 84.8 us)
Async XLA Ops:
  2.7 7.6 %collective-permute-start.1 = (f32[7,1,1,2,128]{4,0,3,2,1:T(8,128)S(1)}, f32[7,1,1,2,128]{4,0,3,2,1:T(8,128)S(1)}, u32[]{:S(2)}, u32[]{:S(2)}) collective-permute-start(f32[7,1,1,2,128]{4,0,3,2,1:T(8,128)S(1)} %pad_maximum_fusion.19), channel_id=1, source_target_pairs={{8,0},{16,8},{24,16},{9,1},{17,9},{25,17},{10,2},{18,10},{26,18},{... | collective-permute-start | bytes 21512 | tf_op jit(solution)/shard_map/ppermute | solution.py:26
  4.0 6.9 %collective-permute-start = (f32[7,1,1,2,128]{4,0,3,2,1:T(8,128)S(1)}, f32[7,1,1,2,128]{4,0,3,2,1:T(8,128)S(1)}, u32[]{:S(2)}, u32[]{:S(2)}) collective-permute-start(f32[7,1,1,2,128]{4,0,3,2,1:T(8,128)S(1)} %pad_maximum_fusion.19), channel_id=1, source_target_pairs={{0,8},{8,16},{16,24},{1,9},{9,17},{17,25},{2,10},{10,18},{18,26},{... | collective-permute-start | bytes 21512 | tf_op jit(solution)/shard_map/ppermute | solution.py:24
  11.0 5.9 %collective-permute-start.3 = (f32[7,3,1,2,128]{4,0,3,2,1:T(8,128)S(1)}, f32[7,3,1,2,128]{4,0,3,2,1:T(8,128)S(1)}, u32[]{:S(2)}, u32[]{:S(2)}) collective-permute-start(f32[7,3,1,2,128]{4,0,3,2,1:T(8,128)S(1)} %pad_maximum_fusion.11), channel_id=1, source_target_pairs={{4,0},{5,1},{6,2},{7,3},{12,8},{13,9},{14,10},{15,11},{20,16},{21,... | collective-permute-start | bytes 64520 | tf_op jit(solution)/shard_map/ppermute | solution.py:26
  12.3 6.1 %collective-permute-start.2 = (f32[7,3,1,2,128]{4,0,3,2,1:T(8,128)S(1)}, f32[7,3,1,2,128]{4,0,3,2,1:T(8,128)S(1)}, u32[]{:S(2)}, u32[]{:S(2)}) collective-permute-start(f32[7,3,1,2,128]{4,0,3,2,1:T(8,128)S(1)} %pad_maximum_fusion.11), channel_id=1, source_target_pairs={{0,4},{1,5},{2,6},{3,7},{8,12},{9,13},{10,14},{11,15},{16,20},{17,... | collective-permute-start | bytes 64520 | tf_op jit(solution)/shard_map/ppermute | solution.py:24
  18.3 2.6 collective-permute-start.4
  19.6 5.3 %collective-permute-start.5 = (f32[7,3,3,1,128]{4,0,3,2,1:T(8,128)S(1)}, f32[7,3,3,1,128]{4,0,3,2,1:T(8,128)S(1)}, u32[]{:S(2)}, u32[]{:S(2)}) collective-permute-start(f32[7,3,3,1,128]{4,0,3,2,1:T(8,128)S(1)} %get-tuple-element.24), channel_id=1, source_target_pairs={{1,0},{2,1},{3,2},{5,4},{6,5},{7,6},{9,8},{10,9},{11,10},{13,12},{... | collective-permute-start | bytes 96776 | tf_op jit(solution)/shard_map/ppermute | solution.py:26
  32.9 60.3 %copy-start.3 = (f32[3,2,128]{2,1,0:T(2,128)}, f32[3,2,128]{2,1,0:T(2,128)S(1)}, u32[]{:S(2)}) copy-start(f32[3,2,128]{2,1,0:T(2,128)S(1)} %fusion.20) | copy-start | bytes 9220
  32.9 6.1 %collective-permute-start.7 = (f32[3,1,1,2,128]{4,3,0,2,1:T(2,128)S(1)}, f32[3,1,1,2,128]{4,3,0,2,1:T(2,128)S(1)}, u32[]{:S(2)}, u32[]{:S(2)}) collective-permute-start(f32[3,1,1,2,128]{4,3,0,2,1:T(2,128)S(1)} %bitcast.143), channel_id=1, source_target_pairs={{8,0},{16,8},{24,16},{9,1},{17,9},{25,17},{10,2},{18,10},{26,18},{... | collective-permute-start | bytes 9224 | tf_op jit(solution)/shard_map/ppermute | solution.py:26
  34.2 6.1 %collective-permute-start.6 = (f32[3,1,1,2,128]{4,3,0,2,1:T(2,128)S(1)}, f32[3,1,1,2,128]{4,3,0,2,1:T(2,128)S(1)}, u32[]{:S(2)}, u32[]{:S(2)}) collective-permute-start(f32[3,1,1,2,128]{4,3,0,2,1:T(2,128)S(1)} %bitcast.144), channel_id=1, source_target_pairs={{0,8},{8,16},{16,24},{1,9},{9,17},{17,25},{2,10},{10,18},{18,26},{... | collective-permute-start | bytes 9224 | tf_op jit(solution)/shard_map/ppermute | solution.py:24
  40.4 5.9 %collective-permute-start.9 = (f32[3,3,1,2,128]{4,3,0,2,1:T(2,128)S(1)}, f32[3,3,1,2,128]{4,3,0,2,1:T(2,128)S(1)}, u32[]{:S(2)}, u32[]{:S(2)}) collective-permute-start(f32[3,3,1,2,128]{4,3,0,2,1:T(2,128)S(1)} %pad_maximum_fusion.15), channel_id=1, source_target_pairs={{4,0},{5,1},{6,2},{7,3},{12,8},{13,9},{14,10},{15,11},{20,16},{21,... | collective-permute-start | bytes 27656 | tf_op jit(solution)/shard_map/ppermute | solution.py:26
  41.7 5.9 %collective-permute-start.8 = (f32[3,3,1,2,128]{4,3,0,2,1:T(2,128)S(1)}, f32[3,3,1,2,128]{4,3,0,2,1:T(2,128)S(1)}, u32[]{:S(2)}, u32[]{:S(2)}) collective-permute-start(f32[3,3,1,2,128]{4,3,0,2,1:T(2,128)S(1)} %pad_maximum_fusion.15), channel_id=1, source_target_pairs={{0,4},{1,5},{2,6},{3,7},{8,12},{9,13},{10,14},{11,15},{16,20},{17,... | collective-permute-start | bytes 27656 | tf_op jit(solution)/shard_map/ppermute | solution.py:24
  48.2 6.5 %collective-permute-start.11 = (f32[3,3,3,1,128]{4,3,0,2,1:T(1,128)}, f32[3,3,3,1,128]{4,3,0,2,1:T(1,128)}, u32[]{:S(2)}, u32[]{:S(2)}) collective-permute-start(f32[3,3,3,1,128]{4,3,0,2,1:T(1,128)} %get-tuple-element.27), channel_id=1, source_target_pairs={{1,0},{2,1},{3,2},{5,4},{6,5},{7,6},{9,8},{10,9},{11,10},{13,12},{... | collective-permute-start | bytes 41480 | tf_op jit(solution)/shard_map/ppermute | solution.py:26
  49.5 5.2 %collective-permute-start.10 = (f32[3,3,3,1,128]{4,3,0,2,1:T(1,128)}, f32[3,3,3,1,128]{4,3,0,2,1:T(1,128)}, u32[]{:S(2)}, u32[]{:S(2)}) collective-permute-start(f32[3,3,3,1,128]{4,3,0,2,1:T(1,128)} %get-tuple-element.28), channel_id=1, source_target_pairs={{0,1},{1,2},{2,3},{4,5},{5,6},{6,7},{8,9},{9,10},{10,11},{12,13},{... | collective-permute-start | bytes 41480 | tf_op jit(solution)/shard_map/ppermute | solution.py:24
  70.1 5.9 %collective-permute-start.13 = (f32[1,1,1,2,128]{4,3,2,1,0:T(2,128)S(1)}, f32[1,1,1,2,128]{4,3,2,1,0:T(2,128)S(1)}, u32[]{:S(2)}, u32[]{:S(2)}) collective-permute-start(f32[1,1,1,2,128]{4,3,2,1,0:T(2,128)S(1)} %bitcast.159), channel_id=1, source_target_pairs={{8,0},{16,8},{24,16},{9,1},{17,9},{25,17},{10,2},{18,10},{26,18},{... | collective-permute-start | bytes 3080 | tf_op jit(solution)/shard_map/ppermute | solution.py:26
  71.4 5.9 %collective-permute-start.12 = (f32[1,1,1,2,128]{4,3,2,1,0:T(2,128)S(1)}, f32[1,1,1,2,128]{4,3,2,1,0:T(2,128)S(1)}, u32[]{:S(2)}, u32[]{:S(2)}) collective-permute-start(f32[1,1,1,2,128]{4,3,2,1,0:T(2,128)S(1)} %bitcast.160), channel_id=1, source_target_pairs={{0,8},{8,16},{16,24},{1,9},{9,17},{17,25},{2,10},{10,18},{18,26},{... | collective-permute-start | bytes 3080 | tf_op jit(solution)/shard_map/ppermute | solution.py:24
  77.3 5.8 %collective-permute-start.15 = (f32[1,3,1,2,128]{4,3,2,1,0:T(2,128)S(1)}, f32[1,3,1,2,128]{4,3,2,1,0:T(2,128)S(1)}, u32[]{:S(2)}, u32[]{:S(2)}) collective-permute-start(f32[1,3,1,2,128]{4,3,2,1,0:T(2,128)S(1)} %pad_maximum_fusion.20), channel_id=1, source_target_pairs={{4,0},{5,1},{6,2},{7,3},{12,8},{13,9},{14,10},{15,11},{20,16},{21,... | collective-permute-start | bytes 9224 | tf_op jit(solution)/shard_map/ppermute | solution.py:26
  78.6 5.9 %collective-permute-start.14 = (f32[1,3,1,2,128]{4,3,2,1,0:T(2,128)S(1)}, f32[1,3,1,2,128]{4,3,2,1,0:T(2,128)S(1)}, u32[]{:S(2)}, u32[]{:S(2)}) collective-permute-start(f32[1,3,1,2,128]{4,3,2,1,0:T(2,128)S(1)} %pad_maximum_fusion.20), channel_id=1, source_target_pairs={{0,4},{1,5},{2,6},{3,7},{8,12},{9,13},{10,14},{11,15},{16,20},{17,... | collective-permute-start | bytes 9224 | tf_op jit(solution)/shard_map/ppermute | solution.py:24
  84.5 2.8 collective-permute-start.16
  86.0 6.6 %collective-permute-start.17 = (f32[1,3,3,1,128]{4,3,2,1,0:T(1,128)S(1)}, f32[1,3,3,1,128]{4,3,2,1,0:T(1,128)S(1)}, u32[]{:S(2)}, u32[]{:S(2)}) collective-permute-start(f32[1,3,3,1,128]{4,3,2,1,0:T(1,128)S(1)} %get-tuple-element.40), channel_id=1, source_target_pairs={{1,0},{2,1},{3,2},{5,4},{6,5},{7,6},{9,8},{10,9},{11,10},{13,12},{... | collective-permute-start | bytes 13832 | tf_op jit(solution)/shard_map/ppermute | solution.py:26
  147.5 5.8 %collective-permute-start.19 = (f32[1,1,1,2,128]{4,3,2,1,0:T(2,128)S(1)}, f32[1,1,1,2,128]{4,3,2,1,0:T(2,128)S(1)}, u32[]{:S(2)}, u32[]{:S(2)}) collective-permute-start(f32[1,1,1,2,128]{4,3,2,1,0:T(2,128)S(1)} %bitcast.148), channel_id=1, source_target_pairs={{8,0},{16,8},{24,16},{9,1},{17,9},{25,17},{10,2},{18,10},{26,18},{... | collective-permute-start | bytes 3080 | tf_op jit(solution)/shard_map/ppermute | solution.py:26
  148.7 5.8 %collective-permute-start.18 = (f32[1,1,1,2,128]{4,3,2,1,0:T(2,128)S(1)}, f32[1,1,1,2,128]{4,3,2,1,0:T(2,128)S(1)}, u32[]{:S(2)}, u32[]{:S(2)}) collective-permute-start(f32[1,1,1,2,128]{4,3,2,1,0:T(2,128)S(1)} %bitcast.149), channel_id=1, source_target_pairs={{0,8},{8,16},{16,24},{1,9},{9,17},{17,25},{2,10},{10,18},{18,26},{... | collective-permute-start | bytes 3080 | tf_op jit(solution)/shard_map/ppermute | solution.py:24
  154.6 5.8 %collective-permute-start.21 = (f32[1,3,1,2,128]{4,3,2,1,0:T(2,128)S(1)}, f32[1,3,1,2,128]{4,3,2,1,0:T(2,128)S(1)}, u32[]{:S(2)}, u32[]{:S(2)}) collective-permute-start(f32[1,3,1,2,128]{4,3,2,1,0:T(2,128)S(1)} %pad_maximum_fusion.21), channel_id=1, source_target_pairs={{4,0},{5,1},{6,2},{7,3},{12,8},{13,9},{14,10},{15,11},{20,16},{21,... | collective-permute-start | bytes 9224 | tf_op jit(solution)/shard_map/ppermute | solution.py:26
  155.9 5.9 %collective-permute-start.20 = (f32[1,3,1,2,128]{4,3,2,1,0:T(2,128)S(1)}, f32[1,3,1,2,128]{4,3,2,1,0:T(2,128)S(1)}, u32[]{:S(2)}, u32[]{:S(2)}) collective-permute-start(f32[1,3,1,2,128]{4,3,2,1,0:T(2,128)S(1)} %pad_maximum_fusion.21), channel_id=1, source_target_pairs={{0,4},{1,5},{2,6},{3,7},{8,12},{9,13},{10,14},{11,15},{16,20},{17,... | collective-permute-start | bytes 9224 | tf_op jit(solution)/shard_map/ppermute | solution.py:24
  161.7 2.6 collective-permute-start.22
  163.0 5.6 %collective-permute-start.23 = (f32[1,3,3,1,128]{4,3,2,1,0:T(1,128)S(1)}, f32[1,3,3,1,128]{4,3,2,1,0:T(1,128)S(1)}, u32[]{:S(2)}, u32[]{:S(2)}) collective-permute-start(f32[1,3,3,1,128]{4,3,2,1,0:T(1,128)S(1)} %get-tuple-element.36), channel_id=1, source_target_pairs={{1,0},{2,1},{3,2},{5,4},{6,5},{7,6},{9,8},{10,9},{11,10},{13,12},{... | collective-permute-start | bytes 13832 | tf_op jit(solution)/shard_map/ppermute | solution.py:26
  227.9 5.8 %collective-permute-start.25 = (f32[1,1,1,2,128]{4,3,2,1,0:T(2,128)S(1)}, f32[1,1,1,2,128]{4,3,2,1,0:T(2,128)S(1)}, u32[]{:S(2)}, u32[]{:S(2)}) collective-permute-start(f32[1,1,1,2,128]{4,3,2,1,0:T(2,128)S(1)} %bitcast.154), channel_id=1, source_target_pairs={{8,0},{16,8},{24,16},{9,1},{17,9},{25,17},{10,2},{18,10},{26,18},{... | collective-permute-start | bytes 3080 | tf_op jit(solution)/shard_map/ppermute | solution.py:26
  229.1 5.8 %collective-permute-start.24 = (f32[1,1,1,2,128]{4,3,2,1,0:T(2,128)S(1)}, f32[1,1,1,2,128]{4,3,2,1,0:T(2,128)S(1)}, u32[]{:S(2)}, u32[]{:S(2)}) collective-permute-start(f32[1,1,1,2,128]{4,3,2,1,0:T(2,128)S(1)} %bitcast.155), channel_id=1, source_target_pairs={{0,8},{8,16},{16,24},{1,9},{9,17},{17,25},{2,10},{10,18},{18,26},{... | collective-permute-start | bytes 3080 | tf_op jit(solution)/shard_map/ppermute | solution.py:24
  235.0 5.8 %collective-permute-start.27 = (f32[1,3,1,2,128]{4,3,2,1,0:T(2,128)S(1)}, f32[1,3,1,2,128]{4,3,2,1,0:T(2,128)S(1)}, u32[]{:S(2)}, u32[]{:S(2)}) collective-permute-start(f32[1,3,1,2,128]{4,3,2,1,0:T(2,128)S(1)} %pad_maximum_fusion.22), channel_id=1, source_target_pairs={{4,0},{5,1},{6,2},{7,3},{12,8},{13,9},{14,10},{15,11},{20,16},{21,... | collective-permute-start | bytes 9224 | tf_op jit(solution)/shard_map/ppermute | solution.py:26
  236.3 5.9 %collective-permute-start.26 = (f32[1,3,1,2,128]{4,3,2,1,0:T(2,128)S(1)}, f32[1,3,1,2,128]{4,3,2,1,0:T(2,128)S(1)}, u32[]{:S(2)}, u32[]{:S(2)}) collective-permute-start(f32[1,3,1,2,128]{4,3,2,1,0:T(2,128)S(1)} %pad_maximum_fusion.22), channel_id=1, source_target_pairs={{0,4},{1,5},{2,6},{3,7},{8,12},{9,13},{10,14},{11,15},{16,20},{17,... | collective-permute-start | bytes 9224 | tf_op jit(solution)/shard_map/ppermute | solution.py:24
  242.7 8.7 %collective-permute-start.28 = (f32[1,3,3,1,128]{4,3,2,1,0:T(1,128)}, f32[1,3,3,1,128]{4,3,2,1,0:T(1,128)}, u32[]{:S(2)}, u32[]{:S(2)}) collective-permute-start(f32[1,3,3,1,128]{4,3,2,1,0:T(1,128)} %get-tuple-element.31), channel_id=1, source_target_pairs={{0,1},{1,2},{2,3},{4,5},{5,6},{6,7},{8,9},{9,10},{10,11},{12,13},{... | collective-permute-start | bytes 13832 | tf_op jit(solution)/shard_map/ppermute | solution.py:24
  244.6 6.8 %collective-permute-start.29 = (f32[1,3,3,1,128]{4,3,2,1,0:T(1,128)}, f32[1,3,3,1,128]{4,3,2,1,0:T(1,128)}, u32[]{:S(2)}, u32[]{:S(2)}) collective-permute-start(f32[1,3,3,1,128]{4,3,2,1,0:T(1,128)} %get-tuple-element.32), channel_id=1, source_target_pairs={{1,0},{2,1},{3,2},{5,4},{6,5},{7,6},{9,8},{10,9},{11,10},{13,12},{... | collective-permute-start | bytes 13832 | tf_op jit(solution)/shard_map/ppermute | solution.py:26
  259.1 59.5 %copy-start.4 = (f32[3,2,128]{2,1,0:T(2,128)S(1)}, f32[3,2,128]{2,1,0:T(2,128)}, u32[]{:S(2)}) copy-start(f32[3,2,128]{2,1,0:T(2,128)} %copy-done.3) | copy-start | bytes 9220
  (35 other events, 506.8 us)

commit v2 on v1

--- a/solution.py
+++ b/solution.py
@@ -19,6 +19,14 @@
         ends = count - 1
         head = lax.slice_in_dim(cells, 0, width, axis=dim)
         tail = lax.slice_in_dim(cells, cells.shape[dim] - width, cells.shape[dim], axis=dim)
+        if count == 2:
+            first = lax.axis_index(axis) == 0
+            got = lax.ppermute(jnp.where(first, tail, head), axis, [(0, 1), (1, 0)])
+            empty = jnp.zeros_like(got)
+            cells = jnp.concatenate(
+                [jnp.where(first, empty, got), cells, jnp.where(first, got, empty)], axis=dim
+            )
+            continue
         cells = jnp.concatenate(
             [
                 lax.ppermute(tail, axis, [(i, (i + 1) % count) for i in range(ends)]),
@@ -28,6 +36,19 @@
             axis=dim,
         )
     return cells
+
+
+def total(values):
+    for axis in ("gx", "gy", "gz"):
+        count = lax.axis_size(axis)
+        if count & (count - 1):
+            values = lax.psum(values, axis)
+            continue
+        step = 1
+        while step < count:
+            values = values + lax.ppermute(values, axis, [(i, i ^ step) for i in range(count)])
+            step *= 2
+    return values
 
 
 def neighbours(rim):
@@ -109,38 +130,44 @@
         jnp.sum(predicted * lever, axis=0, keepdims=True) - flux
     )
 
-    def operate(field):
+    def spread(field):
         near_field = neighbours(with_halo(shaped(field), AXES, 1))
-        return near_field, diagonal * field - wsum(weight, near_field) / width
+        return near_field, -(wsum(weight, near_field) / width) / diagonal
 
-    def paired_sums(residual, precond, applied):
-        pair = jnp.stack([jnp.sum(residual * precond), jnp.sum(precond * applied)])
-        total = lax.psum(pair, ("gx", "gy", "gz"))
-        return total[0], total[1]
+    basis = [source / diagonal]
+    near_basis = []
+    for _ in range(ITERS):
+        near_field, following = spread(basis[-1])
+        near_basis.append(near_field)
+        basis.append(following)
+    stacked = jnp.concatenate(basis, axis=0)
+    weighted = stacked * diagonal
+    gram = total(jnp.sum(weighted[:, None] * stacked[None, :], axis=(2, 3)))
+    size = ITERS + 1
 
-    pressure = jnp.zeros_like(source)
-    residual = source
-    precond = residual / diagonal
-    near_dir, applied = operate(precond)
-    norm_now, curvature_sum = paired_sums(residual, precond, applied)
-    step_size = norm_now / curvature_sum
-    direction = precond
-    along = applied
-    near_pressure = jnp.zeros_like(near_dir)
+    def shift_add(coords):
+        return coords + jnp.concatenate([jnp.zeros((1,), coords.dtype), coords[:-1]])
+
+    def quad(left, right):
+        return jnp.sum(left * jnp.sum(gram * right[None, :], axis=1))
+
+    resid = jnp.zeros((size,), jnp.float32).at[0].set(1.0)
+    along = resid
+    coords = jnp.zeros((size,), jnp.float32)
+    norm_now = quad(resid, resid)
     for iteration in range(ITERS):
-        pressure = pressure + step_size * direction
-        near_pressure = near_pressure + step_size * near_dir
-        residual = residual - step_size * along
+        applied = shift_add(along)
+        step_size = norm_now / quad(along, applied)
+        coords = coords + step_size * along
+        resid = resid - step_size * applied
         if iteration + 1 < ITERS:
-            precond = residual / diagonal
-            near_fresh, applied = operate(precond)
-            norm_next, curvature_sum = paired_sums(residual, precond, applied)
-            blend = norm_next / norm_now
-            step_size = norm_next / (curvature_sum - blend * norm_next / step_size)
-            direction = precond + blend * direction
-            near_dir = near_fresh + blend * near_dir
-            along = applied + blend * along
+            norm_next = quad(resid, resid)
+            along = resid + (norm_next / norm_now) * along
             norm_now = norm_next
+    pressure = jnp.sum(coords[:ITERS, None, None] * stacked[:ITERS], axis=0, keepdims=True)
+    near_pressure = coords[0] * near_basis[0]
+    for k in range(1, ITERS):
+        near_pressure = near_pressure + coords[k] * near_basis[k]
 
     grads = wsum(weight, jnp.concatenate([near_pressure, near_pressure * local_near], axis=0))
     moments = local_own * grads[0:1] - grads[1:4]

time: 322 us -> 186 us (0.58)
  blocking collectives: 132 us -> 0 us
  starting transfers between devices: 76 us -> 67 us
  waiting for transfers between devices: 25.9 us -> 34.2 us
  local copies, waits for them, and re-layouts: 32.6 us -> 27.6 us
  other arithmetic: 41.9 us -> 46.4 us
  between operations: 11.2 us -> 7.95 us
    psum x3 -> x0, blocking collectives: 132 us -> none  [paired_sums(): total = lax.psum(pair, ('gx', 'gy', 'gz'))]
    ppermute x15 -> x10, starting transfers between devices: 56.6 us -> 36.3 us  [with_halo(): lax.ppermute(tail, axis, [(i, (i + 1) % count) for i in range(ends)])]
    ppermute x0 -> x10, starting transfers between devices: none -> 17.7 us  [the longest x5 9.5 us: total(): lax.ppermute(values, axis, [(i, i ^ step) for i in range(count)])]
    ppermute x0 -> x10, waiting for transfers between devices: none -> 14.3 us  [the longest x5 10.2 us: with_halo(): got = lax.ppermute(jnp.where(first, tail, head), axis, [(0, 1), (1, 0)])]
    ppermute x15 -> x10, waiting for transfers between devices: 12.3 us -> 5.71 us  [with_halo(): lax.ppermute(tail, axis, [(i, (i + 1) % count) for i in range(ends)])]
    ppermute x15 -> x10, starting transfers between devices: 19.5 us -> 13.1 us  [with_halo(): lax.ppermute(head, axis, [((i + 1) % count, i) for i in range(ends)])]
    add x3 -> x12, other arithmetic: 2.45 us -> 8.14 us  [the longest x2 5.37 us: on_device(): near_pressure = near_pressure + coords[k] * near_basis[k]]
    another operation x3 -> x0, other arithmetic: 4.92 us -> none  [paired_sums(): pair = jnp.stack([jnp.sum(residual * precond), jnp.sum(precond * applied)])]
  transfers between devices with their start and end apart: 30 -> 30, of which waited for: 13 -> 19; matrix products, arithmetic and copies ran while one was open for 2% -> 4% of each run, Pallas kernels for 0% -> 0%
where the time goes in v2:
time: 186 us; the launch traced here: 183 us
  starting transfers between devices  67 us (36%)
  other arithmetic  46.4 us (25%)
  waiting for transfers between devices  34.2 us (18%)
  local copies, waits for them, and re-layouts  27.6 us (15%)
  between operations  7.95 us (4%)
    ppermute x10, starting transfers between devices, with_halo(): lax.ppermute(tail, axis, [(i, (i + 1) % count) for i in range(ends)])  36.3 us
    another operation x15, local copies, waits for them, and re-layouts, neighbours(): return jnp.stack(blocks, axis=1)  16.9 us
    ppermute x10, waiting for transfers between devices, with_halo(): lax.ppermute(head, axis, [((i + 1) % count, i) for i in range(ends)])  14.2 us
    ppermute x10, starting transfers between devices, with_halo(): lax.ppermute(head, axis, [((i + 1) % count, i) for i in range(ends)])  13.1 us
    reduce_sum x6, other arithmetic, wsum(): return jnp.sum(weight[None] * near[:, :, None, :], axis=-1)  12.6 us
    ppermute x5, waiting for transfers between devices, with_halo(): got = lax.ppermute(jnp.where(first, tail, head), axis, [(0, 1), (1, 0)])  10.2 us
    ppermute x5, starting transfers between devices, total(): lax.ppermute(values, axis, [(i, i ^ step) for i in range(count)])  9.5 us
    ppermute x5, starting transfers between devices, with_halo(): got = lax.ppermute(jnp.where(first, tail, head), axis, [(0, 1), (1, 0)])  8.16 us
  transfers between devices with their start and end apart: 30, of which 19 were waited for; matrix products, arithmetic and copies ran while one was open for 4% of the time, Pallas kernels for 0%

profile of v2, /device:TPU:0, one launch (start us, length us, event | category | flops | bytes accessed | tf_op | source)
XLA Modules:
  0.0 183.2 jit_solution(11234952964922651653)
XLA Ops:
  4.0 5.6 %collective-permute-start = (f32[7,1,1,2,128]{4,0,3,2,1:T(8,128)S(1)}, f32[7,1,1,2,128]{4,0,3,2,1:T(8,128)S(1)}, u32[]{:S(2)}, u32[]{:S(2)}) collective-permute-start(f32[7,1,1,2,128]{4,0,3,2,1:T(8,128)S(1)} %pad_maximum_fusion.18), channel_id=1, source_target_pairs={{0,8},{8,16},{16,24},{1,9},{9,17},{17,25},{2,10},{10,18},{18,26},{... | collective-permute-start | bytes 21512 | tf_op jit(solution)/shard_map/ppermute | solution.py:32
  11.0 2.0 %collective-permute-start.2 = (f32[7,3,1,2,128]{4,0,3,2,1:T(8,128)S(1)}, f32[7,3,1,2,128]{4,0,3,2,1:T(8,128)S(1)}, u32[]{:S(2)}, u32[]{:S(2)}) collective-permute-start(f32[7,3,1,2,128]{4,0,3,2,1:T(8,128)S(1)} %pad_maximum_fusion.10), channel_id=1, source_target_pairs={{0,4},{4,0},{1,5},{5,1},{2,6},{6,2},{3,7},{7,3},{8,12},{12,8},{9,1... | collective-permute-start | bytes 64520 | tf_op jit(solution)/shard_map/ppermute | solution.py:24
  13.1 1.8 collective-permute-done.2
  17.5 3.9 %collective-permute-done.4 = f32[7,3,3,1,128]{4,0,3,2,1:T(8,128)S(1)} collective-permute-done((f32[7,3,3,1,128]{4,0,3,2,1:T(8,128)S(1)}, f32[7,3,3,1,128]{4,0,3,2,1:T(8,128)S(1)}, u32[]{:S(2)}, u32[]{:S(2)}) %collective-permute-start.4) | collective-permute-done | bytes 32288 | tf_op jit(solution)/shard_map/ppermute | solution.py:34
  23.8 1.6 fusion.6
  25.8 1.7 copy-done
  27.6 1.8 multiply_reduce_fusion
  30.8 4.8 %collective-permute-start.5 = (f32[3,1,1,2,128]{4,3,0,2,1:T(2,128)S(1)}, f32[3,1,1,2,128]{4,3,0,2,1:T(2,128)S(1)}, u32[]{:S(2)}, u32[]{:S(2)}) collective-permute-start(f32[3,1,1,2,128]{4,3,0,2,1:T(2,128)S(1)} %bitcast.113), channel_id=1, source_target_pairs={{0,8},{8,16},{16,24},{1,9},{9,17},{17,25},{2,10},{10,18},{18,26},{... | collective-permute-start | bytes 9224 | tf_op jit(solution)/shard_map/ppermute | solution.py:32
  36.9 1.6 collective-permute-start.7
  38.5 2.1 %collective-permute-done.7 = f32[3,3,1,2,128]{4,3,0,2,1:T(2,128)S(1)} collective-permute-done((f32[3,3,1,2,128]{4,3,0,2,1:T(2,128)S(1)}, f32[3,3,1,2,128]{4,3,0,2,1:T(2,128)S(1)}, u32[]{:S(2)}, u32[]{:S(2)}) %collective-permute-start.7) | collective-permute-done | bytes 9248 | tf_op jit(solution)/shard_map/ppermute | solution.py:24
  42.6 3.8 %collective-permute-start.8 = (f32[3,3,3,1,128]{4,3,0,2,1:T(1,128)}, f32[3,3,3,1,128]{4,3,0,2,1:T(1,128)}, u32[]{:S(2)}, u32[]{:S(2)}) collective-permute-start(f32[3,3,3,1,128]{4,3,0,2,1:T(1,128)} %get-tuple-element.36), channel_id=1, source_target_pairs={{0,1},{1,2},{2,3},{4,5},{5,6},{6,7},{8,9},{9,10},{10,11},{12,13},{... | collective-permute-start | bytes 41480 | tf_op jit(solution)/shard_map/ppermute | solution.py:32
  59.2 3.3 %multiply_reduce_fusion.2 = f32[4,2,128]{2,1,0:T(2,128)S(1)} fusion(f32[4,2,3456]{2,1,0:T(2,128)S(1)} %copy.34, f32[2,128,3456]{2,1,0:T(8,128)} %copy-done), kind=kLoop, calls=%fused_computation.2 | loop fusion | flops 7076864 | bytes 3653632 | tf_op jit(solution)/shard_map/reduce_sum | solution.py:70
  64.6 4.6 %collective-permute-start.10 = (f32[1,1,1,2,128]{4,3,2,1,0:T(2,128)S(1)}, f32[1,1,1,2,128]{4,3,2,1,0:T(2,128)S(1)}, u32[]{:S(2)}, u32[]{:S(2)}) collective-permute-start(f32[1,1,1,2,128]{4,3,2,1,0:T(2,128)S(1)} %bitcast.119), channel_id=1, source_target_pairs={{0,8},{8,16},{16,24},{1,9},{9,17},{17,25},{2,10},{10,18},{18,26},{... | collective-permute-start | bytes 3080 | tf_op jit(solution)/shard_map/ppermute | solution.py:32
  70.5 1.5 collective-permute-start.12
  72.1 2.1 %collective-permute-done.12 = f32[1,3,1,2,128]{4,3,2,1,0:T(2,128)S(1)} collective-permute-done((f32[1,3,1,2,128]{4,3,2,1,0:T(2,128)S(1)}, f32[1,3,1,2,128]{4,3,2,1,0:T(2,128)S(1)}, u32[]{:S(2)}, u32[]{:S(2)}) %collective-permute-start.12) | collective-permute-done | bytes 3104 | tf_op jit(solution)/shard_map/ppermute | solution.py:24
  77.0 5.3 %collective-permute-done.14 = f32[1,3,3,1,128]{4,3,2,1,0:T(1,128)S(1)} collective-permute-done((f32[1,3,3,1,128]{4,3,2,1,0:T(1,128)S(1)}, f32[1,3,3,1,128]{4,3,2,1,0:T(1,128)S(1)}, u32[]{:S(2)}, u32[]{:S(2)}) %collective-permute-start.14) | collective-permute-done | bytes 4640 | tf_op jit(solution)/shard_map/ppermute | solution.py:34
  89.8 4.8 %collective-permute-start.15 = (f32[1,1,1,2,128]{4,3,2,1,0:T(2,128)S(1)}, f32[1,1,1,2,128]{4,3,2,1,0:T(2,128)S(1)}, u32[]{:S(2)}, u32[]{:S(2)}) collective-permute-start(f32[1,1,1,2,128]{4,3,2,1,0:T(2,128)S(1)} %get-tuple-element.63), channel_id=1, source_target_pairs={{0,8},{8,16},{16,24},{1,9},{9,17},{17,25},{2,10},{10,18},{18,26},{... | collective-permute-start | bytes 3080 | tf_op jit(solution)/shard_map/ppermute | solution.py:32
  95.9 1.5 collective-permute-start.17
  97.4 2.1 %collective-permute-done.17 = f32[1,3,1,2,128]{4,3,2,1,0:T(2,128)S(1)} collective-permute-done((f32[1,3,1,2,128]{4,3,2,1,0:T(2,128)S(1)}, f32[1,3,1,2,128]{4,3,2,1,0:T(2,128)S(1)}, u32[]{:S(2)}, u32[]{:S(2)}) %collective-permute-start.17) | collective-permute-done | bytes 3104 | tf_op jit(solution)/shard_map/ppermute | solution.py:24
  99.5 2.3 %collective-permute-start.18 = (f32[1,3,3,1,128]{4,3,2,1,0:T(1,128)S(1)}, f32[1,3,3,1,128]{4,3,2,1,0:T(1,128)S(1)}, u32[]{:S(2)}, u32[]{:S(2)}) collective-permute-start(f32[1,3,3,1,128]{4,3,2,1,0:T(1,128)S(1)} %get-tuple-element.45), channel_id=1, source_target_pairs={{0,1},{1,2},{2,3},{4,5},{5,6},{6,7},{8,9},{9,10},{10,11},{12,13},{... | collective-permute-start | bytes 13832 | tf_op jit(solution)/shard_map/ppermute | solution.py:32
  103.1 3.3 %collective-permute-done.19 = f32[1,3,3,1,128]{4,3,2,1,0:T(1,128)S(1)} collective-permute-done((f32[1,3,3,1,128]{4,3,2,1,0:T(1,128)S(1)}, f32[1,3,3,1,128]{4,3,2,1,0:T(1,128)S(1)}, u32[]{:S(2)}, u32[]{:S(2)}) %collective-permute-start.19) | collective-permute-done | bytes 4640 | tf_op jit(solution)/shard_map/ppermute | solution.py:34
  113.9 4.8 %collective-permute-start.20 = (f32[1,1,1,2,128]{4,3,2,1,0:T(2,128)S(1)}, f32[1,1,1,2,128]{4,3,2,1,0:T(2,128)S(1)}, u32[]{:S(2)}, u32[]{:S(2)}) collective-permute-start(f32[1,1,1,2,128]{4,3,2,1,0:T(2,128)S(1)} %divide_bitcast_fusion), channel_id=1, source_target_pairs={{0,8},{8,16},{16,24},{1,9},{9,17},{17,25},{2,10},{10,18},{18,26},{... | collective-permute-start | bytes 3080 | tf_op jit(solution)/shard_map/ppermute | solution.py:32
  120.0 1.5 collective-permute-start.22
  121.6 2.1 %collective-permute-done.22 = f32[1,3,1,2,128]{4,3,2,1,0:T(2,128)S(1)} collective-permute-done((f32[1,3,1,2,128]{4,3,2,1,0:T(2,128)S(1)}, f32[1,3,1,2,128]{4,3,2,1,0:T(2,128)S(1)}, u32[]{:S(2)}, u32[]{:S(2)}) %collective-permute-start.22) | collective-permute-done | bytes 3104 | tf_op jit(solution)/shard_map/ppermute | solution.py:24
  124.3 2.8 %collective-permute-start.23 = (f32[1,3,3,1,128]{4,3,2,1,0:T(1,128)}, f32[1,3,3,1,128]{4,3,2,1,0:T(1,128)}, u32[]{:S(2)}, u32[]{:S(2)}) collective-permute-start(f32[1,3,3,1,128]{4,3,2,1,0:T(1,128)} %get-tuple-element.41), channel_id=1, source_target_pairs={{0,1},{1,2},{2,3},{4,5},{5,6},{6,7},{8,9},{9,10},{10,11},{12,13},{... | collective-permute-start | bytes 13832 | tf_op jit(solution)/shard_map/ppermute | solution.py:32
  130.0 1.6 collective-permute-done.24
  139.4 2.3 %collective-permute-start.25 = (f32[4,4]{1,0:T(4,128)S(1)}, f32[4,4]{1,0:T(4,128)S(1)}, u32[]{:S(2)}, u32[]{:S(2)}) collective-permute-start(f32[4,4]{1,0:T(4,128)S(1)} %multiply_reduce_fusion.7), channel_id=1, source_target_pairs={{0,8},{8,0},{16,24},{24,16},{1,9},{9,1},{17,25},{25,17},{2,10},{10... | collective-permute-start | bytes 200 | tf_op jit(solution)/shard_map/ppermute | solution.py:49
  143.3 3.5 %collective-permute-start.26 = (f32[4,4]{1,0:T(4,128)S(1)}, f32[4,4]{1,0:T(4,128)S(1)}, u32[]{:S(2)}, u32[]{:S(2)}) collective-permute-start(f32[4,4]{1,0:T(4,128)S(1)} %add.152), channel_id=1, source_target_pairs={{0,16},{8,24},{16,0},{24,8},{1,17},{9,25},{17,1},{25,9},{2,18},{10... | collective-permute-start | bytes 200 | tf_op jit(solution)/shard_map/ppermute | solution.py:49
  153.1 2.2 %collective-permute-start.29 = (f32[4,4]{1,0:T(4,128)S(1)}, f32[4,4]{1,0:T(4,128)S(1)}, u32[]{:S(2)}, u32[]{:S(2)}) collective-permute-start(f32[4,4]{1,0:T(4,128)S(1)} %add.155), channel_id=1, source_target_pairs={{0,2},{1,3},{2,0},{3,1},{4,6},{5,7},{6,4},{7,5},{8,10},{9,11},{10,... | collective-permute-start | bytes 200 | tf_op jit(solution)/shard_map/ppermute | solution.py:49
  172.7 2.7 %multiply_add_fusion = f32[1,2,3456]{2,0,1:T(1,128)S(1)} fusion(f32[]{:T(128)} %bitcast.31, f32[]{:T(128)} %bitcast.30, f32[]{:T(128)} %bitcast.29, f32[1,1,3456]{2,0,1:T(1,128)} %bitcast.106, f32[1,1,3456]{2,0,1:T(1,128)} %bitcast.108, f32[1,1,3456]{2,0,1:T(1,128)} %bitcast.102, f32[1,1,3456]{2,0,1:T(1,128)} %bitcast.104, f32[1,1,3456]{2,0,1:T(1,128)S(1)} %bitcast.98, ...), kind=kLoop, calls=%fused_computation.51 | loop fusion | flops 55296 | bytes 110604 | tf_op jit(solution)/shard_map/add | solution.py:170
  175.4 2.7 %fusion.12 = f32[2,3456]{1,0:T(2,128)S(1)} fusion(f32[1,3456]{1,0:T(1,128)} %stack.77, f32[1,3456]{1,0:T(1,128)S(1)} %stack.76, f32[1,3456]{1,0:T(1,128)S(1)} %stack.80, f32[1,3456]{1,0:T(1,128)S(1)} %stack.79, f32[1,3456]{1,0:T(1,128)S(1)} %stack.83, f32[1,3456]{1,0:T(1,128)S(1)} %stack.82, f32[]{:T(128)} %bitcast.31, f32[]{:T(128)} %bitcast.30, f32[]{:T(128)} %bitcast.29), kind=kLoop, calls=%fused_computation.44 | loop fusion | flops 55296 | bytes 110604 | tf_op jit(solution)/shard_map/add | solution.py:170
  179.1 3.3 %multiply_reduce_fusion.1 = f32[4,2,128]{2,1,0:T(2,128)S(1)} fusion(f32[4,2,3456]{2,1,0:T(2,128)S(1)} %copy.42, f32[2,128,3456]{2,1,0:T(8,128)} %copy-done), kind=kLoop, calls=%fused_computation.1 | loop fusion | flops 7076864 | bytes 3653632 | tf_op jit(solution)/shard_map/reduce_sum | solution.py:70
  (207 shorter events, 84.2 us)
Async XLA Ops:
  2.7 7.6 %collective-permute-start.1 = (f32[7,1,1,2,128]{4,0,3,2,1:T(8,128)S(1)}, f32[7,1,1,2,128]{4,0,3,2,1:T(8,128)S(1)}, u32[]{:S(2)}, u32[]{:S(2)}) collective-permute-start(f32[7,1,1,2,128]{4,0,3,2,1:T(8,128)S(1)} %pad_maximum_fusion.18), channel_id=1, source_target_pairs={{8,0},{16,8},{24,16},{9,1},{17,9},{25,17},{10,2},{18,10},{26,18},{... | collective-permute-start | bytes 21512 | tf_op jit(solution)/shard_map/ppermute | solution.py:34
  4.0 6.9 %collective-permute-start = (f32[7,1,1,2,128]{4,0,3,2,1:T(8,128)S(1)}, f32[7,1,1,2,128]{4,0,3,2,1:T(8,128)S(1)}, u32[]{:S(2)}, u32[]{:S(2)}) collective-permute-start(f32[7,1,1,2,128]{4,0,3,2,1:T(8,128)S(1)} %pad_maximum_fusion.18), channel_id=1, source_target_pairs={{0,8},{8,16},{16,24},{1,9},{9,17},{17,25},{2,10},{10,18},{18,26},{... | collective-permute-start | bytes 21512 | tf_op jit(solution)/shard_map/ppermute | solution.py:32
  11.0 3.9 %collective-permute-start.2 = (f32[7,3,1,2,128]{4,0,3,2,1:T(8,128)S(1)}, f32[7,3,1,2,128]{4,0,3,2,1:T(8,128)S(1)}, u32[]{:S(2)}, u32[]{:S(2)}) collective-permute-start(f32[7,3,1,2,128]{4,0,3,2,1:T(8,128)S(1)} %pad_maximum_fusion.10), channel_id=1, source_target_pairs={{0,4},{4,0},{1,5},{5,1},{2,6},{6,2},{3,7},{7,3},{8,12},{12,8},{9,1... | collective-permute-start | bytes 64520 | tf_op jit(solution)/shard_map/ppermute | solution.py:24
  14.9 2.6 %collective-permute-start.3 = (f32[7,3,3,1,128]{4,0,3,2,1:T(8,128)S(1)}, f32[7,3,3,1,128]{4,0,3,2,1:T(8,128)S(1)}, u32[]{:S(2)}, u32[]{:S(2)}) collective-permute-start(f32[7,3,3,1,128]{4,0,3,2,1:T(8,128)S(1)} %get-tuple-element.31), channel_id=1, source_target_pairs={{0,1},{1,2},{2,3},{4,5},{5,6},{6,7},{8,9},{9,10},{10,11},{12,13},{... | collective-permute-start | bytes 96776 | tf_op jit(solution)/shard_map/ppermute | solution.py:32
  16.2 5.3 %collective-permute-start.4 = (f32[7,3,3,1,128]{4,0,3,2,1:T(8,128)S(1)}, f32[7,3,3,1,128]{4,0,3,2,1:T(8,128)S(1)}, u32[]{:S(2)}, u32[]{:S(2)}) collective-permute-start(f32[7,3,3,1,128]{4,0,3,2,1:T(8,128)S(1)} %get-tuple-element.32), channel_id=1, source_target_pairs={{1,0},{2,1},{3,2},{5,4},{6,5},{7,6},{9,8},{10,9},{11,10},{13,12},{... | collective-permute-start | bytes 96776 | tf_op jit(solution)/shard_map/ppermute | solution.py:34
  29.5 53.5 %copy-start.3 = (f32[3,2,128]{2,1,0:T(2,128)}, f32[3,2,128]{2,1,0:T(2,128)S(1)}, u32[]{:S(2)}) copy-start(f32[3,2,128]{2,1,0:T(2,128)S(1)} %fusion.21) | copy-start | bytes 9220
  29.5 6.1 %collective-permute-start.6 = (f32[3,1,1,2,128]{4,3,0,2,1:T(2,128)S(1)}, f32[3,1,1,2,128]{4,3,0,2,1:T(2,128)S(1)}, u32[]{:S(2)}, u32[]{:S(2)}) collective-permute-start(f32[3,1,1,2,128]{4,3,0,2,1:T(2,128)S(1)} %bitcast.112), channel_id=1, source_target_pairs={{8,0},{16,8},{24,16},{9,1},{17,9},{25,17},{10,2},{18,10},{26,18},{... | collective-permute-start | bytes 9224 | tf_op jit(solution)/shard_map/ppermute | solution.py:34
  30.8 6.1 %collective-permute-start.5 = (f32[3,1,1,2,128]{4,3,0,2,1:T(2,128)S(1)}, f32[3,1,1,2,128]{4,3,0,2,1:T(2,128)S(1)}, u32[]{:S(2)}, u32[]{:S(2)}) collective-permute-start(f32[3,1,1,2,128]{4,3,0,2,1:T(2,128)S(1)} %bitcast.113), channel_id=1, source_target_pairs={{0,8},{8,16},{16,24},{1,9},{9,17},{17,25},{2,10},{10,18},{18,26},{... | collective-permute-start | bytes 9224 | tf_op jit(solution)/shard_map/ppermute | solution.py:32
  36.9 3.7 %collective-permute-start.7 = (f32[3,3,1,2,128]{4,3,0,2,1:T(2,128)S(1)}, f32[3,3,1,2,128]{4,3,0,2,1:T(2,128)S(1)}, u32[]{:S(2)}, u32[]{:S(2)}) collective-permute-start(f32[3,3,1,2,128]{4,3,0,2,1:T(2,128)S(1)} %pad_maximum_fusion.14), channel_id=1, source_target_pairs={{0,4},{4,0},{1,5},{5,1},{2,6},{6,2},{3,7},{7,3},{8,12},{12,8},{9,1... | collective-permute-start | bytes 27656 | tf_op jit(solution)/shard_map/ppermute | solution.py:24
  41.3 6.4 %collective-permute-start.9 = (f32[3,3,3,1,128]{4,3,0,2,1:T(1,128)}, f32[3,3,3,1,128]{4,3,0,2,1:T(1,128)}, u32[]{:S(2)}, u32[]{:S(2)}) collective-permute-start(f32[3,3,3,1,128]{4,3,0,2,1:T(1,128)} %get-tuple-element.35), channel_id=1, source_target_pairs={{1,0},{2,1},{3,2},{5,4},{6,5},{7,6},{9,8},{10,9},{11,10},{13,12},{... | collective-permute-start | bytes 41480 | tf_op jit(solution)/shard_map/ppermute | solution.py:34
  42.6 5.1 %collective-permute-start.8 = (f32[3,3,3,1,128]{4,3,0,2,1:T(1,128)}, f32[3,3,3,1,128]{4,3,0,2,1:T(1,128)}, u32[]{:S(2)}, u32[]{:S(2)}) collective-permute-start(f32[3,3,3,1,128]{4,3,0,2,1:T(1,128)} %get-tuple-element.36), channel_id=1, source_target_pairs={{0,1},{1,2},{2,3},{4,5},{5,6},{6,7},{8,9},{9,10},{10,11},{12,13},{... | collective-permute-start | bytes 41480 | tf_op jit(solution)/shard_map/ppermute | solution.py:32
  63.3 6.0 %collective-permute-start.11 = (f32[1,1,1,2,128]{4,3,2,1,0:T(2,128)S(1)}, f32[1,1,1,2,128]{4,3,2,1,0:T(2,128)S(1)}, u32[]{:S(2)}, u32[]{:S(2)}) collective-permute-start(f32[1,1,1,2,128]{4,3,2,1,0:T(2,128)S(1)} %bitcast.118), channel_id=1, source_target_pairs={{8,0},{16,8},{24,16},{9,1},{17,9},{25,17},{10,2},{18,10},{26,18},{... | collective-permute-start | bytes 3080 | tf_op jit(solution)/shard_map/ppermute | solution.py:34
  64.6 5.9 %collective-permute-start.10 = (f32[1,1,1,2,128]{4,3,2,1,0:T(2,128)S(1)}, f32[1,1,1,2,128]{4,3,2,1,0:T(2,128)S(1)}, u32[]{:S(2)}, u32[]{:S(2)}) collective-permute-start(f32[1,1,1,2,128]{4,3,2,1,0:T(2,128)S(1)} %bitcast.119), channel_id=1, source_target_pairs={{0,8},{8,16},{16,24},{1,9},{9,17},{17,25},{2,10},{10,18},{18,26},{... | collective-permute-start | bytes 3080 | tf_op jit(solution)/shard_map/ppermute | solution.py:32
  70.5 3.6 %collective-permute-start.12 = (f32[1,3,1,2,128]{4,3,2,1,0:T(2,128)S(1)}, f32[1,3,1,2,128]{4,3,2,1,0:T(2,128)S(1)}, u32[]{:S(2)}, u32[]{:S(2)}) collective-permute-start(f32[1,3,1,2,128]{4,3,2,1,0:T(2,128)S(1)} %pad_maximum_fusion.20), channel_id=1, source_target_pairs={{0,4},{4,0},{1,5},{5,1},{2,6},{6,2},{3,7},{7,3},{8,12},{12,8},{9,1... | collective-permute-start | bytes 9224 | tf_op jit(solution)/shard_map/ppermute | solution.py:24
  74.2 2.8 %collective-permute-start.13 = (f32[1,3,3,1,128]{4,3,2,1,0:T(1,128)S(1)}, f32[1,3,3,1,128]{4,3,2,1,0:T(1,128)S(1)}, u32[]{:S(2)}, u32[]{:S(2)}) collective-permute-start(f32[1,3,3,1,128]{4,3,2,1,0:T(1,128)S(1)} %get-tuple-element.49), channel_id=1, source_target_pairs={{0,1},{1,2},{2,3},{4,5},{5,6},{6,7},{8,9},{9,10},{10,11},{12,13},{... | collective-permute-start | bytes 13832 | tf_op jit(solution)/shard_map/ppermute | solution.py:32
  75.7 6.7 %collective-permute-start.14 = (f32[1,3,3,1,128]{4,3,2,1,0:T(1,128)S(1)}, f32[1,3,3,1,128]{4,3,2,1,0:T(1,128)S(1)}, u32[]{:S(2)}, u32[]{:S(2)}) collective-permute-start(f32[1,3,3,1,128]{4,3,2,1,0:T(1,128)S(1)} %get-tuple-element.50), channel_id=1, source_target_pairs={{1,0},{2,1},{3,2},{5,4},{6,5},{7,6},{9,8},{10,9},{11,10},{13,12},{... | collective-permute-start | bytes 13832 | tf_op jit(solution)/shard_map/ppermute | solution.py:34
  88.5 6.1 %collective-permute-start.16 = (f32[1,1,1,2,128]{4,3,2,1,0:T(2,128)S(1)}, f32[1,1,1,2,128]{4,3,2,1,0:T(2,128)S(1)}, u32[]{:S(2)}, u32[]{:S(2)}) collective-permute-start(f32[1,1,1,2,128]{4,3,2,1,0:T(2,128)S(1)} %get-tuple-element.63), channel_id=1, source_target_pairs={{8,0},{16,8},{24,16},{9,1},{17,9},{25,17},{10,2},{18,10},{26,18},{... | collective-permute-start | bytes 3080 | tf_op jit(solution)/shard_map/ppermute | solution.py:34
  89.8 6.1 %collective-permute-start.15 = (f32[1,1,1,2,128]{4,3,2,1,0:T(2,128)S(1)}, f32[1,1,1,2,128]{4,3,2,1,0:T(2,128)S(1)}, u32[]{:S(2)}, u32[]{:S(2)}) collective-permute-start(f32[1,1,1,2,128]{4,3,2,1,0:T(2,128)S(1)} %get-tuple-element.63), channel_id=1, source_target_pairs={{0,8},{8,16},{16,24},{1,9},{9,17},{17,25},{2,10},{10,18},{18,26},{... | collective-permute-start | bytes 3080 | tf_op jit(solution)/shard_map/ppermute | solution.py:32
  95.9 3.6 %collective-permute-start.17 = (f32[1,3,1,2,128]{4,3,2,1,0:T(2,128)S(1)}, f32[1,3,1,2,128]{4,3,2,1,0:T(2,128)S(1)}, u32[]{:S(2)}, u32[]{:S(2)}) collective-permute-start(f32[1,3,1,2,128]{4,3,2,1,0:T(2,128)S(1)} %pad_maximum_fusion.21), channel_id=1, source_target_pairs={{0,4},{4,0},{1,5},{5,1},{2,6},{6,2},{3,7},{7,3},{8,12},{12,8},{9,1... | collective-permute-start | bytes 9224 | tf_op jit(solution)/shard_map/ppermute | solution.py:24
  99.5 3.6 %collective-permute-start.18 = (f32[1,3,3,1,128]{4,3,2,1,0:T(1,128)S(1)}, f32[1,3,3,1,128]{4,3,2,1,0:T(1,128)S(1)}, u32[]{:S(2)}, u32[]{:S(2)}) collective-permute-start(f32[1,3,3,1,128]{4,3,2,1,0:T(1,128)S(1)} %get-tuple-element.45), channel_id=1, source_target_pairs={{0,1},{1,2},{2,3},{4,5},{5,6},{6,7},{8,9},{9,10},{10,11},{12,13},{... | collective-permute-start | bytes 13832 | tf_op jit(solution)/shard_map/ppermute | solution.py:32
  101.8 4.6 %collective-permute-start.19 = (f32[1,3,3,1,128]{4,3,2,1,0:T(1,128)S(1)}, f32[1,3,3,1,128]{4,3,2,1,0:T(1,128)S(1)}, u32[]{:S(2)}, u32[]{:S(2)}) collective-permute-start(f32[1,3,3,1,128]{4,3,2,1,0:T(1,128)S(1)} %get-tuple-element.46), channel_id=1, source_target_pairs={{1,0},{2,1},{3,2},{5,4},{6,5},{7,6},{9,8},{10,9},{11,10},{13,12},{... | collective-permute-start | bytes 13832 | tf_op jit(solution)/shard_map/ppermute | solution.py:34
  112.7 6.1 %collective-permute-start.21 = (f32[1,1,1,2,128]{4,3,2,1,0:T(2,128)S(1)}, f32[1,1,1,2,128]{4,3,2,1,0:T(2,128)S(1)}, u32[]{:S(2)}, u32[]{:S(2)}) collective-permute-start(f32[1,1,1,2,128]{4,3,2,1,0:T(2,128)S(1)} %divide_bitcast_fusion), channel_id=1, source_target_pairs={{8,0},{16,8},{24,16},{9,1},{17,9},{25,17},{10,2},{18,10},{26,18},{... | collective-permute-start | bytes 3080 | tf_op jit(solution)/shard_map/ppermute | solution.py:34
  113.9 6.1 %collective-permute-start.20 = (f32[1,1,1,2,128]{4,3,2,1,0:T(2,128)S(1)}, f32[1,1,1,2,128]{4,3,2,1,0:T(2,128)S(1)}, u32[]{:S(2)}, u32[]{:S(2)}) collective-permute-start(f32[1,1,1,2,128]{4,3,2,1,0:T(2,128)S(1)} %divide_bitcast_fusion), channel_id=1, source_target_pairs={{0,8},{8,16},{16,24},{1,9},{9,17},{17,25},{2,10},{10,18},{18,26},{... | collective-permute-start | bytes 3080 | tf_op jit(solution)/shard_map/ppermute | solution.py:32
  120.0 3.6 %collective-permute-start.22 = (f32[1,3,1,2,128]{4,3,2,1,0:T(2,128)S(1)}, f32[1,3,1,2,128]{4,3,2,1,0:T(2,128)S(1)}, u32[]{:S(2)}, u32[]{:S(2)}) collective-permute-start(f32[1,3,1,2,128]{4,3,2,1,0:T(2,128)S(1)} %pad_maximum_fusion.22), channel_id=1, source_target_pairs={{0,4},{4,0},{1,5},{5,1},{2,6},{6,2},{3,7},{7,3},{8,12},{12,8},{9,1... | collective-permute-start | bytes 9224 | tf_op jit(solution)/shard_map/ppermute | solution.py:24
  124.3 5.7 %collective-permute-start.23 = (f32[1,3,3,1,128]{4,3,2,1,0:T(1,128)}, f32[1,3,3,1,128]{4,3,2,1,0:T(1,128)}, u32[]{:S(2)}, u32[]{:S(2)}) collective-permute-start(f32[1,3,3,1,128]{4,3,2,1,0:T(1,128)} %get-tuple-element.41), channel_id=1, source_target_pairs={{0,1},{1,2},{2,3},{4,5},{5,6},{6,7},{8,9},{9,10},{10,11},{12,13},{... | collective-permute-start | bytes 13832 | tf_op jit(solution)/shard_map/ppermute | solution.py:32
  127.1 4.4 %collective-permute-start.24 = (f32[1,3,3,1,128]{4,3,2,1,0:T(1,128)}, f32[1,3,3,1,128]{4,3,2,1,0:T(1,128)}, u32[]{:S(2)}, u32[]{:S(2)}) collective-permute-start(f32[1,3,3,1,128]{4,3,2,1,0:T(1,128)} %get-tuple-element.42), channel_id=1, source_target_pairs={{1,0},{2,1},{3,2},{5,4},{6,5},{7,6},{9,8},{10,9},{11,10},{13,12},{... | collective-permute-start | bytes 13832 | tf_op jit(solution)/shard_map/ppermute | solution.py:34
  137.9 44.6 %copy-start.4 = (f32[3,2,128]{2,1,0:T(2,128)S(1)}, f32[3,2,128]{2,1,0:T(2,128)}, u32[]{:S(2)}) copy-start(f32[3,2,128]{2,1,0:T(2,128)} %copy-done.3) | copy-start | bytes 9220
  139.4 3.9 %collective-permute-start.25 = (f32[4,4]{1,0:T(4,128)S(1)}, f32[4,4]{1,0:T(4,128)S(1)}, u32[]{:S(2)}, u32[]{:S(2)}) collective-permute-start(f32[4,4]{1,0:T(4,128)S(1)} %multiply_reduce_fusion.7), channel_id=1, source_target_pairs={{0,8},{8,0},{16,24},{24,16},{1,9},{9,1},{17,25},{25,17},{2,10},{10... | collective-permute-start | bytes 200 | tf_op jit(solution)/shard_map/ppermute | solution.py:49
  143.3 5.0 %collective-permute-start.26 = (f32[4,4]{1,0:T(4,128)S(1)}, f32[4,4]{1,0:T(4,128)S(1)}, u32[]{:S(2)}, u32[]{:S(2)}) collective-permute-start(f32[4,4]{1,0:T(4,128)S(1)} %add.152), channel_id=1, source_target_pairs={{0,16},{8,24},{16,0},{24,8},{1,17},{9,25},{17,1},{25,9},{2,18},{10... | collective-permute-start | bytes 200 | tf_op jit(solution)/shard_map/ppermute | solution.py:49
  148.3 3.6 %collective-permute-start.27 = (f32[4,4]{1,0:T(4,128)S(1)}, f32[4,4]{1,0:T(4,128)S(1)}, u32[]{:S(2)}, u32[]{:S(2)}) collective-permute-start(f32[4,4]{1,0:T(4,128)S(1)} %add.153), channel_id=1, source_target_pairs={{0,4},{4,0},{1,5},{5,1},{2,6},{6,2},{3,7},{7,3},{8,12},{12,8},{9,1... | collective-permute-start | bytes 200 | tf_op jit(solution)/shard_map/ppermute | solution.py:49
  151.9 1.2 collective-permute-start.28
  153.1 3.7 %collective-permute-start.29 = (f32[4,4]{1,0:T(4,128)S(1)}, f32[4,4]{1,0:T(4,128)S(1)}, u32[]{:S(2)}, u32[]{:S(2)}) collective-permute-start(f32[4,4]{1,0:T(4,128)S(1)} %add.155), channel_id=1, source_target_pairs={{0,2},{1,3},{2,0},{3,1},{4,6},{5,7},{6,4},{7,5},{8,10},{9,11},{10,... | collective-permute-start | bytes 200 | tf_op jit(solution)/shard_map/ppermute | solution.py:49
  (30 other events, 409.3 us)

commit v3 on v2

--- a/solution.py
+++ b/solution.py
@@ -1,4 +1,5 @@
 import jax
+import numpy as np
 import jax.numpy as jnp
 from jax import lax
 from jax.sharding import PartitionSpec as P
@@ -85,31 +86,72 @@
     return jnp.stack(corners, axis=1).astype(jnp.float32)
 
 
+def adjacency(block_shape):
+    _, size_x, size_y, size_z, width = block_shape
+    rows = []
+    for ax in range(size_x):
+        for ay in range(size_y):
+            for az in range(size_z):
+                near = np.zeros((size_x + 2, size_y + 2, size_z + 2), np.float32)
+                near[ax:ax + 3, ay:ay + 3, az:az + 3] = 1.0
+                rows.append(np.repeat(near.reshape(-1), width))
+    return np.stack(rows)
+
+
+def solve3(matrix, rhs):
+    h = [[matrix[i, j] for j in range(3)] for i in range(3)]
+    g = [rhs[i] for i in range(3)]
+    m1 = h[1][0] / h[0][0]
+    m2 = h[2][0] / h[0][0]
+    a11 = h[1][1] - m1 * h[0][1]
+    a12 = h[1][2] - m1 * h[0][2]
+    b1 = g[1] - m1 * g[0]
+    a21 = h[2][1] - m2 * h[0][1]
+    a22 = h[2][2] - m2 * h[0][2]
+    b2 = g[2] - m2 * g[0]
+    m3 = a21 / a11
+    y2 = (b2 - m3 * b1) / (a22 - m3 * a12)
+    y1 = (b1 - a12 * y2) / a11
+    y0 = (g[0] - h[0][1] * y1 - h[0][2] * y2) / h[0][0]
+    return (y0, y1, y2)
+
+
 def on_device(positions, velocity, counts):
     block_shape = positions.shape
     width = positions.shape[4]
     slot_ids = jnp.arange(width, dtype=jnp.int32)
     valid_mask = (slot_ids[None, None, None, :] < counts[:, :, :, None]).astype(jnp.float32)[None]
     packed = jnp.concatenate([positions, valid_mask, velocity], axis=0)
-    near_all = neighbours(with_halo(packed, AXES, 1))
+
+    def rim_flat(cells):
+        rim = with_halo(cells, AXES, 1)
+        return rim.reshape(rim.shape[0], 1, -1)
+
+    near_all = rim_flat(packed)
     near_x = near_all[0:3]
     near_valid = near_all[3]
     near_v = near_all[4:7]
     own_x = flat(positions)
     own_valid = flat(valid_mask)[0]
     own_v = flat(velocity)
+    tiles = own_x.shape[1]
 
     offset = own_x[:, :, :, None] - near_x[:, :, None, :]
     distance = offset[0] * offset[0] + offset[1] * offset[1] + offset[2] * offset[2]
     closeness = jnp.maximum(1.0 - distance, 0.0)
-    weight = closeness * closeness * own_valid[:, :, None] * near_valid[:, None, :]
+    weight = (
+        closeness * closeness * own_valid[:, :, None] * near_valid[:, None, :]
+    ) * jnp.asarray(adjacency(block_shape))[:, None, :]
 
     corner = tile_corners(block_shape)[:, :, None]
     local_own = own_x - corner
     local_near = near_x - corner
 
+    def spread_t(near_field):
+        return jnp.broadcast_to(near_field, (near_field.shape[0], tiles, near_field.shape[2]))
+
     row = jnp.sum(weight, axis=-1)[None]
-    sums = wsum(weight, jnp.concatenate([near_v, local_near], axis=0))
+    sums = wsum(weight, jnp.concatenate([spread_t(near_v), local_near], axis=0))
     near_sums = sums[0:3]
     lever = local_own * row - sums[3:6]
 
@@ -122,55 +164,36 @@
     def shaped(values):
         return values.reshape(values.shape[0], *block_shape[1:])
 
-    near_pred = neighbours(with_halo(shaped(predicted), AXES, 1))
+    near_pred = rim_flat(shaped(predicted))
     dotted = jnp.sum(near_pred * local_near, axis=0, keepdims=True)
-    psums = wsum(weight, jnp.concatenate([near_pred, dotted], axis=0))
+    psums = wsum(weight, jnp.concatenate([spread_t(near_pred), dotted], axis=0))
     flux = jnp.sum(local_own * psums[0:3], axis=0, keepdims=True) - psums[3:4]
     source = -(GRADIENT_GAIN / width) * (
         jnp.sum(predicted * lever, axis=0, keepdims=True) - flux
     )
 
-    def spread(field):
-        near_field = neighbours(with_halo(shaped(field), AXES, 1))
-        return near_field, -(wsum(weight, near_field) / width) / diagonal
-
     basis = [source / diagonal]
-    near_basis = []
+    near_w = []
+    near_wx = []
     for _ in range(ITERS):
-        near_field, following = spread(basis[-1])
-        near_basis.append(near_field)
-        basis.append(following)
+        near_u = rim_flat(shaped(basis[-1]))
+        out = wsum(weight, jnp.concatenate([spread_t(near_u), near_u * local_near], axis=0))
+        near_w.append(out[0:1])
+        near_wx.append(out[1:4])
+        basis.append(-(out[0:1] / width) / diagonal)
     stacked = jnp.concatenate(basis, axis=0)
-    weighted = stacked * diagonal
+    weighted = stacked[:ITERS] * diagonal
     gram = total(jnp.sum(weighted[:, None] * stacked[None, :], axis=(2, 3)))
-    size = ITERS + 1
-
-    def shift_add(coords):
-        return coords + jnp.concatenate([jnp.zeros((1,), coords.dtype), coords[:-1]])
-
-    def quad(left, right):
-        return jnp.sum(left * jnp.sum(gram * right[None, :], axis=1))
-
-    resid = jnp.zeros((size,), jnp.float32).at[0].set(1.0)
-    along = resid
-    coords = jnp.zeros((size,), jnp.float32)
-    norm_now = quad(resid, resid)
-    for iteration in range(ITERS):
-        applied = shift_add(along)
-        step_size = norm_now / quad(along, applied)
-        coords = coords + step_size * along
-        resid = resid - step_size * applied
-        if iteration + 1 < ITERS:
-            norm_next = quad(resid, resid)
-            along = resid + (norm_next / norm_now) * along
-            norm_now = norm_next
-    pressure = jnp.sum(coords[:ITERS, None, None] * stacked[:ITERS], axis=0, keepdims=True)
-    near_pressure = coords[0] * near_basis[0]
+    coords = solve3(gram[:, :ITERS] + gram[:, 1:], gram[:, 0])
+
+    pressure = coords[0] * basis[0]
+    applied = coords[0] * near_w[0]
+    applied_x = coords[0] * near_wx[0]
     for k in range(1, ITERS):
-        near_pressure = near_pressure + coords[k] * near_basis[k]
-
-    grads = wsum(weight, jnp.concatenate([near_pressure, near_pressure * local_near], axis=0))
-    moments = local_own * grads[0:1] - grads[1:4]
+        pressure = pressure + coords[k] * basis[k]
+        applied = applied + coords[k] * near_w[k]
+        applied_x = applied_x + coords[k] * near_wx[k]
+    moments = local_own * applied - applied_x
     velocity_new = predicted - GRADIENT_GAIN / width * (pressure * lever - moments)
     return (shaped(velocity_new), shaped(pressure)[0])
 

time: 186 us -> 164 us (0.88)
  waiting for transfers between devices: 34.2 us -> 61.9 us
  local copies, waits for them, and re-layouts: 27.6 us -> 1.83 us
  starting transfers between devices: 67 us -> 49 us
  other arithmetic: 46.4 us -> 35.7 us
  between operations: 7.95 us -> 14.3 us
    ppermute x10, waiting for transfers between devices: 14.2 us -> 38.5 us  [with_halo(): lax.ppermute(head, axis, [((i + 1) % count, i) for i in range(ends)])]
    another operation x15 -> x0, local copies, waits for them, and re-layouts: 16.9 us -> none  [neighbours(): return jnp.stack(blocks, axis=1)]
    ppermute x10, starting transfers between devices: 36.3 us -> 24.4 us  [with_halo(): lax.ppermute(tail, axis, [(i, (i + 1) % count) for i in range(ends)])]
    ppermute x5, waiting for transfers between devices: 4.17 us -> 12.8 us  [total(): lax.ppermute(values, axis, [(i, i ^ step) for i in range(count)])]
    reduce_sum x6 -> x5, other arithmetic: 12.6 us -> 21.1 us  [wsum(): return jnp.sum(weight[None] * near[:, :, None, :], axis=-1)]
    add x7 -> x2, other arithmetic: 6.88 us -> 0.08 us  [the longest x1 0.08 us: on_device(): coords = solve3(gram[:, :ITERS] + gram[:, 1:], gram[:, 0])]
    reduce_sum x11 -> x0, other arithmetic: 5.88 us -> none  [the longest x10 5.8 us: quad(): return jnp.sum(left * jnp.sum(gram * right[None, :], axis=1))]
    ppermute x10, waiting for transfers between devices: 5.71 us -> 0.03 us  [with_halo(): lax.ppermute(tail, axis, [(i, (i + 1) % count) for i in range(ends)])]
  transfers between devices with their start and end apart: 30 -> 30, of which waited for: 19 -> 20; matrix products, arithmetic and copies ran while one was open for 4% -> 1% of each run, Pallas kernels for 0% -> 0%
where the time goes in v3:
time: 164 us; the launch traced here: 163 us
  waiting for transfers between devices  61.9 us (38%)
  starting transfers between devices  49 us (30%)
  other arithmetic  35.7 us (22%)
  between operations  14.3 us (9%)
  local copies, waits for them, and re-layouts  1.83 us (1%)
    ppermute x10, waiting for transfers between devices, with_halo(): lax.ppermute(head, axis, [((i + 1) % count, i) for i in range(ends)])  38.5 us
    ppermute x10, starting transfers between devices, with_halo(): lax.ppermute(tail, axis, [(i, (i + 1) % count) for i in range(ends)])  24.4 us
    reduce_sum x5, other arithmetic, wsum(): return jnp.sum(weight[None] * near[:, :, None, :], axis=-1)  21.1 us
    ppermute x10, starting transfers between devices, with_halo(): lax.ppermute(head, axis, [((i + 1) % count, i) for i in range(ends)])  13.1 us
    ppermute x5, waiting for transfers between devices, total(): lax.ppermute(values, axis, [(i, i ^ step) for i in range(count)])  12.8 us
    ppermute x5, waiting for transfers between devices, with_halo(): got = lax.ppermute(jnp.where(first, tail, head), axis, [(0, 1), (1, 0)])  10.6 us
    ppermute x5, starting transfers between devices, with_halo(): got = lax.ppermute(jnp.where(first, tail, head), axis, [(0, 1), (1, 0)])  7.66 us
    ppermute x5, starting transfers between devices, total(): lax.ppermute(values, axis, [(i, i ^ step) for i in range(count)])  3.84 us
  transfers between devices with their start and end apart: 30, of which 20 were waited for; matrix products, arithmetic and copies ran while one was open for 1% of the time, Pallas kernels for 0%

profile of v3, /device:TPU:0, one launch (start us, length us, event | category | flops | bytes accessed | tf_op | source)
XLA Modules:
  0.0 162.8 jit_solution(3570551702384358545)
XLA Ops:
  2.1 4.9 %collective-permute-start = (f32[7,1,1,2,128]{4,3,2,1,0:T(2,128)S(1)}, f32[7,1,1,2,128]{4,3,2,1,0:T(2,128)S(1)}, u32[]{:S(2)}, u32[]{:S(2)}) collective-permute-start(f32[7,1,1,2,128]{4,3,2,1,0:T(2,128)S(1)} %pad_maximum_fusion.17), channel_id=1, source_target_pairs={{0,8},{8,16},{16,24},{1,9},{9,17},{17,25},{2,10},{10,18},{18,26},{... | collective-permute-start | bytes 21512 | tf_op jit(solution)/shard_map/ppermute | solution.py:33
  9.0 3.5 %collective-permute-done.1 = f32[7,1,1,2,128]{4,3,2,1,0:T(2,128)S(1)} collective-permute-done((f32[7,1,1,2,128]{4,3,2,1,0:T(2,128)S(1)}, f32[7,1,1,2,128]{4,3,2,1,0:T(2,128)S(1)}, u32[]{:S(2)}, u32[]{:S(2)}) %collective-permute-start.1) | collective-permute-done | bytes 7200 | tf_op jit(solution)/shard_map/ppermute | solution.py:35
  14.9 2.2 %collective-permute-done.2 = f32[7,3,1,2,128]{4,3,2,1,0:T(2,128)S(1)} collective-permute-done((f32[7,3,1,2,128]{4,3,2,1,0:T(2,128)S(1)}, f32[7,3,1,2,128]{4,3,2,1,0:T(2,128)S(1)}, u32[]{:S(2)}, u32[]{:S(2)}) %collective-permute-start.2) | collective-permute-done | bytes 21536 | tf_op jit(solution)/shard_map/ppermute | solution.py:25
  20.6 3.4 %collective-permute-done.4 = f32[7,3,3,1,128]{4,3,2,1,0:T(1,128)S(1)} collective-permute-done((f32[7,3,3,1,128]{4,3,2,1,0:T(1,128)S(1)}, f32[7,3,3,1,128]{4,3,2,1,0:T(1,128)S(1)}, u32[]{:S(2)}, u32[]{:S(2)}) %collective-permute-start.4) | collective-permute-done | bytes 32288 | tf_op jit(solution)/shard_map/ppermute | solution.py:35
  24.9 2.4 %broadcast_subtract_fusion = f32[3,2,128,4608]{3,2,1,0:T(8,128)S(1)} fusion(f32[3,4608]{1,0:T(4,128)S(1)} %sub.105, f32[3,2,128]{2,1,0:T(2,128)} %bitcast.76), kind=kLoop, calls=%fused_computation.5 | loop fusion | flops 3538944 | bytes 14214144 | tf_op jit(solution)/shard_map/sub | solution.py:139
  27.4 2.5 %fusion.7 = (f32[2,128]{1,0:T(2,128)S(1)}, f32[1,2,128,4608]{3,2,1,0:T(8,128)S(1)}) fusion(f32[2,4608]{1,0:T(2,128)S(1)} %copy-done.1, f32[4608]{0:T(1024)S(1)} %mul.331, f32[2,128]{1,0:T(2,128)S(1)} %compare_convert_fusion.1, f32[3,2,128,4608]{3,2,1,0:T(8,128)S(1)} %broadcast_subtract_fusion), kind=kLoop, calls=%fused_computation.17 | loop fusion | flops 14155520 | bytes 18931712 | tf_op jit(solution)/shard_map/reduce_sum | solution.py:153
  29.9 2.9 %multiply_bitcast_fusion = f32[2,128,4608]{2,1,0:T(8,128)} fusion(f32[1,2,128,4608]{3,2,1,0:T(8,128)S(1)} %get-tuple-element.7, f32[2,4608]{1,0:T(2,128)S(1)} %copy-done.1, f32[4608]{0:T(1024)S(1)} %mul.331, f32[2,128]{1,0:T(2,128)S(1)} %compare_convert_fusion.1), kind=kLoop, calls=%fused_computation.18 | loop fusion | flops 3538944 | bytes 9493504 | tf_op jit(solution)/shard_map/mul | solution.py:71
  33.1 4.9 %multiply_reduce_fusion = f32[6,2,128]{2,1,0:T(2,128)S(1)} fusion(f32[6,2,4608]{2,1,0:T(2,128)S(1)} %pad_maximum_fusion, f32[2,128,4608]{2,1,0:T(8,128)} %multiply_bitcast_fusion), kind=kLoop, calls=%fused_computation | loop fusion | flops 14154240 | bytes 4945920 | tf_op jit(solution)/shard_map/reduce_sum | solution.py:71
  38.1 3.5 %collective-permute-start.5 = (f32[3,1,1,2,128]{4,3,0,2,1:T(2,128)S(1)}, f32[3,1,1,2,128]{4,3,0,2,1:T(2,128)S(1)}, u32[]{:S(2)}, u32[]{:S(2)}) collective-permute-start(f32[3,1,1,2,128]{4,3,0,2,1:T(2,128)S(1)} %bitcast.78), channel_id=1, source_target_pairs={{0,8},{8,16},{16,24},{1,9},{9,17},{17,25},{2,10},{10,18},{18,26},{... | collective-permute-start | bytes 9224 | tf_op jit(solution)/shard_map/ppermute | solution.py:33
  42.9 4.2 %collective-permute-done.6 = f32[3,1,1,2,128]{4,3,0,2,1:T(2,128)S(1)} collective-permute-done((f32[3,1,1,2,128]{4,3,0,2,1:T(2,128)S(1)}, f32[3,1,1,2,128]{4,3,0,2,1:T(2,128)S(1)}, u32[]{:S(2)}, u32[]{:S(2)}) %collective-permute-start.6) | collective-permute-done | bytes 3104 | tf_op jit(solution)/shard_map/ppermute | solution.py:35
  48.6 2.1 %collective-permute-done.7 = f32[3,3,1,2,128]{4,3,0,2,1:T(2,128)S(1)} collective-permute-done((f32[3,3,1,2,128]{4,3,0,2,1:T(2,128)S(1)}, f32[3,3,1,2,128]{4,3,0,2,1:T(2,128)S(1)}, u32[]{:S(2)}, u32[]{:S(2)}) %collective-permute-start.7) | collective-permute-done | bytes 9248 | tf_op jit(solution)/shard_map/ppermute | solution.py:25
  50.8 2.0 %collective-permute-start.8 = (f32[3,3,3,1,128]{4,3,0,2,1:T(1,128)S(1)}, f32[3,3,3,1,128]{4,3,0,2,1:T(1,128)S(1)}, u32[]{:S(2)}, u32[]{:S(2)}) collective-permute-start(f32[3,3,3,1,128]{4,3,0,2,1:T(1,128)S(1)} %get-tuple-element.12), channel_id=1, source_target_pairs={{0,1},{1,2},{2,3},{4,5},{5,6},{6,7},{8,9},{9,10},{10,11},{12,13},{... | collective-permute-start | bytes 41480 | tf_op jit(solution)/shard_map/ppermute | solution.py:33
  54.2 3.8 %collective-permute-done.9 = f32[3,3,3,1,128]{4,3,0,2,1:T(1,128)S(1)} collective-permute-done((f32[3,3,3,1,128]{4,3,0,2,1:T(1,128)S(1)}, f32[3,3,3,1,128]{4,3,0,2,1:T(1,128)S(1)}, u32[]{:S(2)}, u32[]{:S(2)}) %collective-permute-start.9) | collective-permute-done | bytes 13856 | tf_op jit(solution)/shard_map/ppermute | solution.py:35
  58.3 4.1 %multiply_reduce_fusion.4 = f32[4,2,128]{2,1,0:T(2,128)S(1)} fusion(f32[4,2,4608]{2,1,0:T(2,128)S(1)} %pad_maximum_fusion.1, f32[2,128,4608]{2,1,0:T(8,128)} %multiply_bitcast_fusion), kind=kLoop, calls=%fused_computation.4 | loop fusion | flops 9436160 | bytes 4870144 | tf_op jit(solution)/shard_map/reduce_sum | solution.py:71
  62.5 3.5 %collective-permute-start.10 = (f32[1,1,1,2,128]{4,3,2,1,0:T(2,128)S(1)}, f32[1,1,1,2,128]{4,3,2,1,0:T(2,128)S(1)}, u32[]{:S(2)}, u32[]{:S(2)}) collective-permute-start(f32[1,1,1,2,128]{4,3,2,1,0:T(2,128)S(1)} %bitcast.83), channel_id=1, source_target_pairs={{0,8},{8,16},{16,24},{1,9},{9,17},{17,25},{2,10},{10,18},{18,26},{... | collective-permute-start | bytes 3080 | tf_op jit(solution)/shard_map/ppermute | solution.py:33
  67.3 4.2 %collective-permute-done.11 = f32[1,1,1,2,128]{4,3,2,1,0:T(2,128)S(1)} collective-permute-done((f32[1,1,1,2,128]{4,3,2,1,0:T(2,128)S(1)}, f32[1,1,1,2,128]{4,3,2,1,0:T(2,128)S(1)}, u32[]{:S(2)}, u32[]{:S(2)}) %collective-permute-start.11) | collective-permute-done | bytes 1056 | tf_op jit(solution)/shard_map/ppermute | solution.py:35
  73.0 2.1 %collective-permute-done.12 = f32[1,3,1,2,128]{4,3,2,1,0:T(2,128)S(1)} collective-permute-done((f32[1,3,1,2,128]{4,3,2,1,0:T(2,128)S(1)}, f32[1,3,1,2,128]{4,3,2,1,0:T(2,128)S(1)}, u32[]{:S(2)}, u32[]{:S(2)}) %collective-permute-start.12) | collective-permute-done | bytes 3104 | tf_op jit(solution)/shard_map/ppermute | solution.py:25
  75.1 2.0 %collective-permute-start.13 = (f32[1,3,3,1,128]{4,3,2,1,0:T(1,128)S(1)}, f32[1,3,3,1,128]{4,3,2,1,0:T(1,128)S(1)}, u32[]{:S(2)}, u32[]{:S(2)}) collective-permute-start(f32[1,3,3,1,128]{4,3,2,1,0:T(1,128)S(1)} %get-tuple-element.20), channel_id=1, source_target_pairs={{0,1},{1,2},{2,3},{4,5},{5,6},{6,7},{8,9},{9,10},{10,11},{12,13},{... | collective-permute-start | bytes 13832 | tf_op jit(solution)/shard_map/ppermute | solution.py:33
  78.4 3.6 %collective-permute-done.14 = f32[1,3,3,1,128]{4,3,2,1,0:T(1,128)S(1)} collective-permute-done((f32[1,3,3,1,128]{4,3,2,1,0:T(1,128)S(1)}, f32[1,3,3,1,128]{4,3,2,1,0:T(1,128)S(1)}, u32[]{:S(2)}, u32[]{:S(2)}) %collective-permute-start.14) | collective-permute-done | bytes 4640 | tf_op jit(solution)/shard_map/ppermute | solution.py:35
  82.3 4.1 %multiply_reduce_fusion.3 = f32[4,2,128]{2,1,0:T(2,128)S(1)} fusion(f32[4,2,4608]{2,1,0:T(2,128)S(1)} %pad_maximum_fusion.2, f32[2,128,4608]{2,1,0:T(8,128)} %multiply_bitcast_fusion), kind=kLoop, calls=%fused_computation.3 | loop fusion | flops 9436160 | bytes 4870144 | tf_op jit(solution)/shard_map/reduce_sum | solution.py:71
  89.6 4.2 %collective-permute-done.16 = f32[1,1,1,2,128]{4,3,2,1,0:T(2,128)S(1)} collective-permute-done((f32[1,1,1,2,128]{4,3,2,1,0:T(2,128)S(1)}, f32[1,1,1,2,128]{4,3,2,1,0:T(2,128)S(1)}, u32[]{:S(2)}, u32[]{:S(2)}) %collective-permute-start.16) | collective-permute-done | bytes 1056 | tf_op jit(solution)/shard_map/ppermute | solution.py:35
  95.3 2.1 %collective-permute-done.17 = f32[1,3,1,2,128]{4,3,2,1,0:T(2,128)S(1)} collective-permute-done((f32[1,3,1,2,128]{4,3,2,1,0:T(2,128)S(1)}, f32[1,3,1,2,128]{4,3,2,1,0:T(2,128)S(1)}, u32[]{:S(2)}, u32[]{:S(2)}) %collective-permute-start.17) | collective-permute-done | bytes 3104 | tf_op jit(solution)/shard_map/ppermute | solution.py:25
  100.6 3.7 %collective-permute-done.19 = f32[1,3,3,1,128]{4,3,2,1,0:T(1,128)S(1)} collective-permute-done((f32[1,3,3,1,128]{4,3,2,1,0:T(1,128)S(1)}, f32[1,3,3,1,128]{4,3,2,1,0:T(1,128)S(1)}, u32[]{:S(2)}, u32[]{:S(2)}) %collective-permute-start.19) | collective-permute-done | bytes 4640 | tf_op jit(solution)/shard_map/ppermute | solution.py:35
  104.5 4.1 %multiply_reduce_fusion.2 = f32[4,2,128]{2,1,0:T(2,128)S(1)} fusion(f32[4,2,4608]{2,1,0:T(2,128)S(1)} %pad_maximum_fusion.3, f32[2,128,4608]{2,1,0:T(8,128)} %multiply_bitcast_fusion), kind=kLoop, calls=%fused_computation.2 | loop fusion | flops 9436160 | bytes 4870144 | tf_op jit(solution)/shard_map/reduce_sum | solution.py:71
  111.8 4.2 %collective-permute-done.21 = f32[1,1,1,2,128]{4,3,2,1,0:T(2,128)S(1)} collective-permute-done((f32[1,1,1,2,128]{4,3,2,1,0:T(2,128)S(1)}, f32[1,1,1,2,128]{4,3,2,1,0:T(2,128)S(1)}, u32[]{:S(2)}, u32[]{:S(2)}) %collective-permute-start.21) | collective-permute-done | bytes 1056 | tf_op jit(solution)/shard_map/ppermute | solution.py:35
  117.5 2.1 %collective-permute-done.22 = f32[1,3,1,2,128]{4,3,2,1,0:T(2,128)S(1)} collective-permute-done((f32[1,3,1,2,128]{4,3,2,1,0:T(2,128)S(1)}, f32[1,3,1,2,128]{4,3,2,1,0:T(2,128)S(1)}, u32[]{:S(2)}, u32[]{:S(2)}) %collective-permute-start.22) | collective-permute-done | bytes 3104 | tf_op jit(solution)/shard_map/ppermute | solution.py:25
  122.6 3.9 %collective-permute-done.24 = f32[1,3,3,1,128]{4,3,2,1,0:T(1,128)S(1)} collective-permute-done((f32[1,3,3,1,128]{4,3,2,1,0:T(1,128)S(1)}, f32[1,3,3,1,128]{4,3,2,1,0:T(1,128)S(1)}, u32[]{:S(2)}, u32[]{:S(2)}) %collective-permute-start.24) | collective-permute-done | bytes 4640 | tf_op jit(solution)/shard_map/ppermute | solution.py:35
  126.7 4.1 %multiply_reduce_fusion.1 = f32[4,2,128]{2,1,0:T(2,128)S(1)} fusion(f32[4,2,4608]{2,1,0:T(2,128)S(1)} %pad_maximum_fusion.4, f32[2,128,4608]{2,1,0:T(8,128)} %multiply_bitcast_fusion), kind=kLoop, calls=%fused_computation.1 | loop fusion | flops 9436160 | bytes 4870144 | tf_op jit(solution)/shard_map/reduce_sum | solution.py:71
  130.9 3.6 %collective-permute-done.25 = f32[3,4]{1,0:T(4,128)S(1)} collective-permute-done((f32[3,4]{1,0:T(4,128)S(1)}, f32[3,4]{1,0:T(4,128)S(1)}, u32[]{:S(2)}, u32[]{:S(2)}) %collective-permute-start.25) | collective-permute-done | bytes 80 | tf_op jit(solution)/shard_map/ppermute | solution.py:50
  134.5 4.5 %collective-permute-done.26 = f32[3,4]{1,0:T(4,128)S(1)} collective-permute-done((f32[3,4]{1,0:T(4,128)S(1)}, f32[3,4]{1,0:T(4,128)S(1)}, u32[]{:S(2)}, u32[]{:S(2)}) %collective-permute-start.26) | collective-permute-done | bytes 80 | tf_op jit(solution)/shard_map/ppermute | solution.py:50
  140.5 2.1 %collective-permute-done.27 = f32[3,4]{1,0:T(4,128)S(1)} collective-permute-done((f32[3,4]{1,0:T(4,128)S(1)}, f32[3,4]{1,0:T(4,128)S(1)}, u32[]{:S(2)}, u32[]{:S(2)}) %collective-permute-start.27) | collective-permute-done | bytes 80 | tf_op jit(solution)/shard_map/ppermute | solution.py:50
  143.8 2.3 %collective-permute-start.29 = (f32[3,4]{1,0:T(4,128)S(1)}, f32[3,4]{1,0:T(4,128)S(1)}, u32[]{:S(2)}, u32[]{:S(2)}) collective-permute-start(f32[3,4]{1,0:T(4,128)S(1)} %add.90), channel_id=1, source_target_pairs={{0,2},{1,3},{2,0},{3,1},{4,6},{5,7},{6,4},{7,5},{8,10},{9,11},{10,... | collective-permute-start | bytes 152 | tf_op jit(solution)/shard_map/ppermute | solution.py:50
  (124 shorter events, 42.1 us)
Async XLA Ops:
  2.1 7.0 %collective-permute-start = (f32[7,1,1,2,128]{4,3,2,1,0:T(2,128)S(1)}, f32[7,1,1,2,128]{4,3,2,1,0:T(2,128)S(1)}, u32[]{:S(2)}, u32[]{:S(2)}) collective-permute-start(f32[7,1,1,2,128]{4,3,2,1,0:T(2,128)S(1)} %pad_maximum_fusion.17), channel_id=1, source_target_pairs={{0,8},{8,16},{16,24},{1,9},{9,17},{17,25},{2,10},{10,18},{18,26},{... | collective-permute-start | bytes 21512 | tf_op jit(solution)/shard_map/ppermute | solution.py:33
  7.0 5.5 %collective-permute-start.1 = (f32[7,1,1,2,128]{4,3,2,1,0:T(2,128)S(1)}, f32[7,1,1,2,128]{4,3,2,1,0:T(2,128)S(1)}, u32[]{:S(2)}, u32[]{:S(2)}) collective-permute-start(f32[7,1,1,2,128]{4,3,2,1,0:T(2,128)S(1)} %pad_maximum_fusion.17), channel_id=1, source_target_pairs={{8,0},{16,8},{24,16},{9,1},{17,9},{25,17},{10,2},{18,10},{26,18},{... | collective-permute-start | bytes 21512 | tf_op jit(solution)/shard_map/ppermute | solution.py:35
  13.2 3.9 %collective-permute-start.2 = (f32[7,3,1,2,128]{4,3,2,1,0:T(2,128)S(1)}, f32[7,3,1,2,128]{4,3,2,1,0:T(2,128)S(1)}, u32[]{:S(2)}, u32[]{:S(2)}) collective-permute-start(f32[7,3,1,2,128]{4,3,2,1,0:T(2,128)S(1)} %pad_maximum_fusion.9), channel_id=1, source_target_pairs={{0,4},{4,0},{1,5},{5,1},{2,6},{6,2},{3,7},{7,3},{8,12},{12,8},{9,1... | collective-permute-start | bytes 64520 | tf_op jit(solution)/shard_map/ppermute | solution.py:25
  17.9 2.7 %collective-permute-start.3 = (f32[7,3,3,1,128]{4,3,2,1,0:T(1,128)S(1)}, f32[7,3,3,1,128]{4,3,2,1,0:T(1,128)S(1)}, u32[]{:S(2)}, u32[]{:S(2)}) collective-permute-start(f32[7,3,3,1,128]{4,3,2,1,0:T(1,128)S(1)} %get-tuple-element.10), channel_id=1, source_target_pairs={{0,1},{1,2},{2,3},{4,5},{5,6},{6,7},{8,9},{9,10},{10,11},{12,13},{... | collective-permute-start | bytes 96776 | tf_op jit(solution)/shard_map/ppermute | solution.py:33
  19.2 4.8 %collective-permute-start.4 = (f32[7,3,3,1,128]{4,3,2,1,0:T(1,128)S(1)}, f32[7,3,3,1,128]{4,3,2,1,0:T(1,128)S(1)}, u32[]{:S(2)}, u32[]{:S(2)}) collective-permute-start(f32[7,3,3,1,128]{4,3,2,1,0:T(1,128)S(1)} %get-tuple-element.11), channel_id=1, source_target_pairs={{1,0},{2,1},{3,2},{5,4},{6,5},{7,6},{9,8},{10,9},{11,10},{13,12},{... | collective-permute-start | bytes 96776 | tf_op jit(solution)/shard_map/ppermute | solution.py:35
  32.8 5.2 %copy-start.4 = (f32[3]{0:T(128)S(1)}, f32[3]{0:T(128)}, u32[]{:S(2)}) copy-start(f32[3]{0:T(128)} %constant.45.clone) | copy-start | bytes 40
  33.1 29.3 %copy-start = (f32[3,1,1,2,128]{4,3,2,1,0:T(2,128)S(1)}, f32[3,1,1,2,128]{4,3,2,1,0:T(2,128)}, u32[]{:S(2)}) copy-start(f32[3,1,1,2,128]{4,3,2,1,0:T(2,128)} %param.5) | copy-start | bytes 9220
  38.1 4.8 %collective-permute-start.5 = (f32[3,1,1,2,128]{4,3,0,2,1:T(2,128)S(1)}, f32[3,1,1,2,128]{4,3,0,2,1:T(2,128)S(1)}, u32[]{:S(2)}, u32[]{:S(2)}) collective-permute-start(f32[3,1,1,2,128]{4,3,0,2,1:T(2,128)S(1)} %bitcast.78), channel_id=1, source_target_pairs={{0,8},{8,16},{16,24},{1,9},{9,17},{17,25},{2,10},{10,18},{18,26},{... | collective-permute-start | bytes 9224 | tf_op jit(solution)/shard_map/ppermute | solution.py:33
  41.6 5.5 %collective-permute-start.6 = (f32[3,1,1,2,128]{4,3,0,2,1:T(2,128)S(1)}, f32[3,1,1,2,128]{4,3,0,2,1:T(2,128)S(1)}, u32[]{:S(2)}, u32[]{:S(2)}) collective-permute-start(f32[3,1,1,2,128]{4,3,0,2,1:T(2,128)S(1)} %bitcast.79), channel_id=1, source_target_pairs={{8,0},{16,8},{24,16},{9,1},{17,9},{25,17},{10,2},{18,10},{26,18},{... | collective-permute-start | bytes 9224 | tf_op jit(solution)/shard_map/ppermute | solution.py:35
  47.1 3.7 %collective-permute-start.7 = (f32[3,3,1,2,128]{4,3,0,2,1:T(2,128)S(1)}, f32[3,3,1,2,128]{4,3,0,2,1:T(2,128)S(1)}, u32[]{:S(2)}, u32[]{:S(2)}) collective-permute-start(f32[3,3,1,2,128]{4,3,0,2,1:T(2,128)S(1)} %pad_maximum_fusion.13), channel_id=1, source_target_pairs={{0,4},{4,0},{1,5},{5,1},{2,6},{6,2},{3,7},{7,3},{8,12},{12,8},{9,1... | collective-permute-start | bytes 27656 | tf_op jit(solution)/shard_map/ppermute | solution.py:25
  50.8 3.3 %collective-permute-start.8 = (f32[3,3,3,1,128]{4,3,0,2,1:T(1,128)S(1)}, f32[3,3,3,1,128]{4,3,0,2,1:T(1,128)S(1)}, u32[]{:S(2)}, u32[]{:S(2)}) collective-permute-start(f32[3,3,3,1,128]{4,3,0,2,1:T(1,128)S(1)} %get-tuple-element.12), channel_id=1, source_target_pairs={{0,1},{1,2},{2,3},{4,5},{5,6},{6,7},{8,9},{9,10},{10,11},{12,13},{... | collective-permute-start | bytes 41480 | tf_op jit(solution)/shard_map/ppermute | solution.py:33
  52.9 5.1 %collective-permute-start.9 = (f32[3,3,3,1,128]{4,3,0,2,1:T(1,128)S(1)}, f32[3,3,3,1,128]{4,3,0,2,1:T(1,128)S(1)}, u32[]{:S(2)}, u32[]{:S(2)}) collective-permute-start(f32[3,3,3,1,128]{4,3,0,2,1:T(1,128)S(1)} %get-tuple-element.13), channel_id=1, source_target_pairs={{1,0},{2,1},{3,2},{5,4},{6,5},{7,6},{9,8},{10,9},{11,10},{13,12},{... | collective-permute-start | bytes 41480 | tf_op jit(solution)/shard_map/ppermute | solution.py:35
  62.5 4.8 %collective-permute-start.10 = (f32[1,1,1,2,128]{4,3,2,1,0:T(2,128)S(1)}, f32[1,1,1,2,128]{4,3,2,1,0:T(2,128)S(1)}, u32[]{:S(2)}, u32[]{:S(2)}) collective-permute-start(f32[1,1,1,2,128]{4,3,2,1,0:T(2,128)S(1)} %bitcast.83), channel_id=1, source_target_pairs={{0,8},{8,16},{16,24},{1,9},{9,17},{17,25},{2,10},{10,18},{18,26},{... | collective-permute-start | bytes 3080 | tf_op jit(solution)/shard_map/ppermute | solution.py:33
  66.0 5.5 %collective-permute-start.11 = (f32[1,1,1,2,128]{4,3,2,1,0:T(2,128)S(1)}, f32[1,1,1,2,128]{4,3,2,1,0:T(2,128)S(1)}, u32[]{:S(2)}, u32[]{:S(2)}) collective-permute-start(f32[1,1,1,2,128]{4,3,2,1,0:T(2,128)S(1)} %bitcast.84), channel_id=1, source_target_pairs={{8,0},{16,8},{24,16},{9,1},{17,9},{25,17},{10,2},{18,10},{26,18},{... | collective-permute-start | bytes 3080 | tf_op jit(solution)/shard_map/ppermute | solution.py:35
  71.5 3.6 %collective-permute-start.12 = (f32[1,3,1,2,128]{4,3,2,1,0:T(2,128)S(1)}, f32[1,3,1,2,128]{4,3,2,1,0:T(2,128)S(1)}, u32[]{:S(2)}, u32[]{:S(2)}) collective-permute-start(f32[1,3,1,2,128]{4,3,2,1,0:T(2,128)S(1)} %pad_maximum_fusion.19), channel_id=1, source_target_pairs={{0,4},{4,0},{1,5},{5,1},{2,6},{6,2},{3,7},{7,3},{8,12},{12,8},{9,1... | collective-permute-start | bytes 9224 | tf_op jit(solution)/shard_map/ppermute | solution.py:25
  75.1 3.3 %collective-permute-start.13 = (f32[1,3,3,1,128]{4,3,2,1,0:T(1,128)S(1)}, f32[1,3,3,1,128]{4,3,2,1,0:T(1,128)S(1)}, u32[]{:S(2)}, u32[]{:S(2)}) collective-permute-start(f32[1,3,3,1,128]{4,3,2,1,0:T(1,128)S(1)} %get-tuple-element.20), channel_id=1, source_target_pairs={{0,1},{1,2},{2,3},{4,5},{5,6},{6,7},{8,9},{9,10},{10,11},{12,13},{... | collective-permute-start | bytes 13832 | tf_op jit(solution)/shard_map/ppermute | solution.py:33
  77.1 4.9 %collective-permute-start.14 = (f32[1,3,3,1,128]{4,3,2,1,0:T(1,128)S(1)}, f32[1,3,3,1,128]{4,3,2,1,0:T(1,128)S(1)}, u32[]{:S(2)}, u32[]{:S(2)}) collective-permute-start(f32[1,3,3,1,128]{4,3,2,1,0:T(1,128)S(1)} %get-tuple-element.21), channel_id=1, source_target_pairs={{1,0},{2,1},{3,2},{5,4},{6,5},{7,6},{9,8},{10,9},{11,10},{13,12},{... | collective-permute-start | bytes 13832 | tf_op jit(solution)/shard_map/ppermute | solution.py:35
  86.4 3.2 %collective-permute-start.15 = (f32[1,1,1,2,128]{4,3,2,1,0:T(2,128)S(1)}, f32[1,1,1,2,128]{4,3,2,1,0:T(2,128)S(1)}, u32[]{:S(2)}, u32[]{:S(2)}) collective-permute-start(f32[1,1,1,2,128]{4,3,2,1,0:T(2,128)S(1)} %bitcast.88), channel_id=1, source_target_pairs={{0,8},{8,16},{16,24},{1,9},{9,17},{17,25},{2,10},{10,18},{18,26},{... | collective-permute-start | bytes 3080 | tf_op jit(solution)/shard_map/ppermute | solution.py:33
  88.3 5.5 %collective-permute-start.16 = (f32[1,1,1,2,128]{4,3,2,1,0:T(2,128)S(1)}, f32[1,1,1,2,128]{4,3,2,1,0:T(2,128)S(1)}, u32[]{:S(2)}, u32[]{:S(2)}) collective-permute-start(f32[1,1,1,2,128]{4,3,2,1,0:T(2,128)S(1)} %bitcast.89), channel_id=1, source_target_pairs={{8,0},{16,8},{24,16},{9,1},{17,9},{25,17},{10,2},{18,10},{26,18},{... | collective-permute-start | bytes 3080 | tf_op jit(solution)/shard_map/ppermute | solution.py:35
  93.8 3.6 %collective-permute-start.17 = (f32[1,3,1,2,128]{4,3,2,1,0:T(2,128)S(1)}, f32[1,3,1,2,128]{4,3,2,1,0:T(2,128)S(1)}, u32[]{:S(2)}, u32[]{:S(2)}) collective-permute-start(f32[1,3,1,2,128]{4,3,2,1,0:T(2,128)S(1)} %pad_maximum_fusion.20), channel_id=1, source_target_pairs={{0,4},{4,0},{1,5},{5,1},{2,6},{6,2},{3,7},{7,3},{8,12},{12,8},{9,1... | collective-permute-start | bytes 9224 | tf_op jit(solution)/shard_map/ppermute | solution.py:25
  97.4 3.2 %collective-permute-start.18 = (f32[1,3,3,1,128]{4,3,2,1,0:T(1,128)S(1)}, f32[1,3,3,1,128]{4,3,2,1,0:T(1,128)S(1)}, u32[]{:S(2)}, u32[]{:S(2)}) collective-permute-start(f32[1,3,3,1,128]{4,3,2,1,0:T(1,128)S(1)} %get-tuple-element.18), channel_id=1, source_target_pairs={{0,1},{1,2},{2,3},{4,5},{5,6},{6,7},{8,9},{9,10},{10,11},{12,13},{... | collective-permute-start | bytes 13832 | tf_op jit(solution)/shard_map/ppermute | solution.py:33
  99.1 5.2 %collective-permute-start.19 = (f32[1,3,3,1,128]{4,3,2,1,0:T(1,128)S(1)}, f32[1,3,3,1,128]{4,3,2,1,0:T(1,128)S(1)}, u32[]{:S(2)}, u32[]{:S(2)}) collective-permute-start(f32[1,3,3,1,128]{4,3,2,1,0:T(1,128)S(1)} %get-tuple-element.19), channel_id=1, source_target_pairs={{1,0},{2,1},{3,2},{5,4},{6,5},{7,6},{9,8},{10,9},{11,10},{13,12},{... | collective-permute-start | bytes 13832 | tf_op jit(solution)/shard_map/ppermute | solution.py:35
  108.6 3.2 %collective-permute-start.20 = (f32[1,1,1,2,128]{4,3,2,1,0:T(2,128)S(1)}, f32[1,1,1,2,128]{4,3,2,1,0:T(2,128)S(1)}, u32[]{:S(2)}, u32[]{:S(2)}) collective-permute-start(f32[1,1,1,2,128]{4,3,2,1,0:T(2,128)S(1)} %bitcast.93), channel_id=1, source_target_pairs={{0,8},{8,16},{16,24},{1,9},{9,17},{17,25},{2,10},{10,18},{18,26},{... | collective-permute-start | bytes 3080 | tf_op jit(solution)/shard_map/ppermute | solution.py:33
  110.5 5.5 %collective-permute-start.21 = (f32[1,1,1,2,128]{4,3,2,1,0:T(2,128)S(1)}, f32[1,1,1,2,128]{4,3,2,1,0:T(2,128)S(1)}, u32[]{:S(2)}, u32[]{:S(2)}) collective-permute-start(f32[1,1,1,2,128]{4,3,2,1,0:T(2,128)S(1)} %bitcast.94), channel_id=1, source_target_pairs={{8,0},{16,8},{24,16},{9,1},{17,9},{25,17},{10,2},{18,10},{26,18},{... | collective-permute-start | bytes 3080 | tf_op jit(solution)/shard_map/ppermute | solution.py:35
  116.0 3.6 %collective-permute-start.22 = (f32[1,3,1,2,128]{4,3,2,1,0:T(2,128)S(1)}, f32[1,3,1,2,128]{4,3,2,1,0:T(2,128)S(1)}, u32[]{:S(2)}, u32[]{:S(2)}) collective-permute-start(f32[1,3,1,2,128]{4,3,2,1,0:T(2,128)S(1)} %pad_maximum_fusion.21), channel_id=1, source_target_pairs={{0,4},{4,0},{1,5},{5,1},{2,6},{6,2},{3,7},{7,3},{8,12},{12,8},{9,1... | collective-permute-start | bytes 9224 | tf_op jit(solution)/shard_map/ppermute | solution.py:25
  119.6 3.0 %collective-permute-start.23 = (f32[1,3,3,1,128]{4,3,2,1,0:T(1,128)S(1)}, f32[1,3,3,1,128]{4,3,2,1,0:T(1,128)S(1)}, u32[]{:S(2)}, u32[]{:S(2)}) collective-permute-start(f32[1,3,3,1,128]{4,3,2,1,0:T(1,128)S(1)} %get-tuple-element.16), channel_id=1, source_target_pairs={{0,1},{1,2},{2,3},{4,5},{5,6},{6,7},{8,9},{9,10},{10,11},{12,13},{... | collective-permute-start | bytes 13832 | tf_op jit(solution)/shard_map/ppermute | solution.py:33
  121.3 5.2 %collective-permute-start.24 = (f32[1,3,3,1,128]{4,3,2,1,0:T(1,128)S(1)}, f32[1,3,3,1,128]{4,3,2,1,0:T(1,128)S(1)}, u32[]{:S(2)}, u32[]{:S(2)}) collective-permute-start(f32[1,3,3,1,128]{4,3,2,1,0:T(1,128)S(1)} %get-tuple-element.17), channel_id=1, source_target_pairs={{1,0},{2,1},{3,2},{5,4},{6,5},{7,6},{9,8},{10,9},{11,10},{13,12},{... | collective-permute-start | bytes 13832 | tf_op jit(solution)/shard_map/ppermute | solution.py:35
  130.9 3.6 %collective-permute-start.25 = (f32[3,4]{1,0:T(4,128)S(1)}, f32[3,4]{1,0:T(4,128)S(1)}, u32[]{:S(2)}, u32[]{:S(2)}) collective-permute-start(f32[3,4]{1,0:T(4,128)S(1)} %multiply_reduce_fusion.5), channel_id=1, source_target_pairs={{0,8},{8,0},{16,24},{24,16},{1,9},{9,1},{17,25},{25,17},{2,10},{10... | collective-permute-start | bytes 152 | tf_op jit(solution)/shard_map/ppermute | solution.py:50
  134.5 4.5 %collective-permute-start.26 = (f32[3,4]{1,0:T(4,128)S(1)}, f32[3,4]{1,0:T(4,128)S(1)}, u32[]{:S(2)}, u32[]{:S(2)}) collective-permute-start(f32[3,4]{1,0:T(4,128)S(1)} %add.87), channel_id=1, source_target_pairs={{0,16},{8,24},{16,0},{24,8},{1,17},{9,25},{17,1},{25,9},{2,18},{10... | collective-permute-start | bytes 152 | tf_op jit(solution)/shard_map/ppermute | solution.py:50
  139.0 3.6 %collective-permute-start.27 = (f32[3,4]{1,0:T(4,128)S(1)}, f32[3,4]{1,0:T(4,128)S(1)}, u32[]{:S(2)}, u32[]{:S(2)}) collective-permute-start(f32[3,4]{1,0:T(4,128)S(1)} %add.88), channel_id=1, source_target_pairs={{0,4},{4,0},{1,5},{5,1},{2,6},{6,2},{3,7},{7,3},{8,12},{12,8},{9,1... | collective-permute-start | bytes 152 | tf_op jit(solution)/shard_map/ppermute | solution.py:50
  142.6 1.2 collective-permute-start.28
  143.8 3.9 %collective-permute-start.29 = (f32[3,4]{1,0:T(4,128)S(1)}, f32[3,4]{1,0:T(4,128)S(1)}, u32[]{:S(2)}, u32[]{:S(2)}) collective-permute-start(f32[3,4]{1,0:T(4,128)S(1)} %add.90), channel_id=1, source_target_pairs={{0,2},{1,3},{2,0},{3,1},{4,6},{5,7},{6,4},{7,5},{8,10},{9,11},{10,... | collective-permute-start | bytes 152 | tf_op jit(solution)/shard_map/ppermute | solution.py:50
  (3 other events, 8.4 us)

commit v4 on v3

--- a/solution.py
+++ b/solution.py
@@ -150,10 +150,10 @@
     def spread_t(near_field):
         return jnp.broadcast_to(near_field, (near_field.shape[0], tiles, near_field.shape[2]))
 
+    later_weight = lax.optimization_barrier(weight)
     row = jnp.sum(weight, axis=-1)[None]
-    sums = wsum(weight, jnp.concatenate([spread_t(near_v), local_near], axis=0))
-    near_sums = sums[0:3]
-    lever = local_own * row - sums[3:6]
+    near_sums = wsum(weight, spread_t(near_v))
+    lever = local_own * row - wsum(later_weight, local_near)
 
     gravity_pull = jnp.array([0.0, 0.0, -GRAVITY], jnp.float32).reshape(3, 1, 1)
     predicted = own_valid[None] * (
@@ -177,13 +177,17 @@
     near_wx = []
     for _ in range(ITERS):
         near_u = rim_flat(shaped(basis[-1]))
-        out = wsum(weight, jnp.concatenate([spread_t(near_u), near_u * local_near], axis=0))
-        near_w.append(out[0:1])
-        near_wx.append(out[1:4])
-        basis.append(-(out[0:1] / width) / diagonal)
+        out = wsum(weight, spread_t(near_u))
+        near_w.append(out)
+        near_wx.append(wsum(later_weight, near_u * local_near))
+        basis.append(-(out / width) / diagonal)
     stacked = jnp.concatenate(basis, axis=0)
     weighted = stacked[:ITERS] * diagonal
-    gram = total(jnp.sum(weighted[:, None] * stacked[None, :], axis=(2, 3)))
+    gram = total(jnp.sum(weighted[:, None] * stacked[None, :], axis=2))
+    shift = width // 2
+    while shift >= 1:
+        gram = gram + jnp.roll(gram, shift, axis=-1)
+        shift //= 2
     coords = solve3(gram[:, :ITERS] + gram[:, 1:], gram[:, 0])
 
     pressure = coords[0] * basis[0]

time: 164 us -> 156 us (0.951)
  between operations: 14.3 us -> 1.19 us
  other arithmetic: 35.7 us -> 43.1 us
    reduce_sum x5 -> x7, other arithmetic: 21.1 us -> 26.5 us  [wsum(): return jnp.sum(weight[None] * near[:, :, None, :], axis=-1)]
  transfers between devices with their start and end apart: 30 -> 30, of which waited for: 20 -> 19; matrix products, arithmetic and copies ran while one was open for 1% -> 4% of each run, Pallas kernels for 0% -> 0%
where the time goes in v4:
time: 156 us; the launch traced here: 155 us
  waiting for transfers between devices  60.4 us (39%)
  starting transfers between devices  49.1 us (31%)
  other arithmetic  43.1 us (28%)
    ppermute x10, waiting for transfers between devices, with_halo(): lax.ppermute(head, axis, [((i + 1) % count, i) for i in range(ends)])  38.5 us
    reduce_sum x7, other arithmetic, wsum(): return jnp.sum(weight[None] * near[:, :, None, :], axis=-1)  26.5 us
    ppermute x10, starting transfers between devices, with_halo(): lax.ppermute(tail, axis, [(i, (i + 1) % count) for i in range(ends)])  24.4 us
    ppermute x10, starting transfers between devices, with_halo(): lax.ppermute(head, axis, [((i + 1) % count, i) for i in range(ends)])  13.1 us
    ppermute x5, waiting for transfers between devices, total(): lax.ppermute(values, axis, [(i, i ^ step) for i in range(count)])  11.3 us
    ppermute x5, waiting for transfers between devices, with_halo(): got = lax.ppermute(jnp.where(first, tail, head), axis, [(0, 1), (1, 0)])  10.6 us
    ppermute x5, starting transfers between devices, with_halo(): got = lax.ppermute(jnp.where(first, tail, head), axis, [(0, 1), (1, 0)])  7.66 us
    reduce_sum x1, other arithmetic, on_device(): row = jnp.sum(weight, axis=-1)[None]  4.18 us
  transfers between devices with their start and end apart: 30, of which 19 were waited for; matrix products, arithmetic and copies ran while one was open for 4% of the time, Pallas kernels for 0%

profile of v4, /device:TPU:0, one launch (start us, length us, event | category | flops | bytes accessed | tf_op | source)
XLA Modules:
  0.0 154.9 jit_solution(10415983017589983627)
XLA Ops:
  2.1 4.9 %collective-permute-start = (f32[7,1,1,2,128]{4,3,2,1,0:T(2,128)S(1)}, f32[7,1,1,2,128]{4,3,2,1,0:T(2,128)S(1)}, u32[]{:S(2)}, u32[]{:S(2)}) collective-permute-start(f32[7,1,1,2,128]{4,3,2,1,0:T(2,128)S(1)} %pad_maximum_fusion.13), channel_id=1, source_target_pairs={{0,8},{8,16},{16,24},{1,9},{9,17},{17,25},{2,10},{10,18},{18,26},{... | collective-permute-start | bytes 21512 | tf_op jit(solution)/shard_map/ppermute | solution.py:33
  8.3 4.2 %collective-permute-done.1 = f32[7,1,1,2,128]{4,3,2,1,0:T(2,128)S(1)} collective-permute-done((f32[7,1,1,2,128]{4,3,2,1,0:T(2,128)S(1)}, f32[7,1,1,2,128]{4,3,2,1,0:T(2,128)S(1)}, u32[]{:S(2)}, u32[]{:S(2)}) %collective-permute-start.1) | collective-permute-done | bytes 7200 | tf_op jit(solution)/shard_map/ppermute | solution.py:35
  14.8 2.3 %collective-permute-done.2 = f32[7,3,1,2,128]{4,3,2,1,0:T(2,128)S(1)} collective-permute-done((f32[7,3,1,2,128]{4,3,2,1,0:T(2,128)S(1)}, f32[7,3,1,2,128]{4,3,2,1,0:T(2,128)S(1)}, u32[]{:S(2)}, u32[]{:S(2)}) %collective-permute-start.2) | collective-permute-done | bytes 21536 | tf_op jit(solution)/shard_map/ppermute | solution.py:25
  21.2 2.8 %collective-permute-done.4 = f32[7,3,3,1,128]{4,3,2,1,0:T(1,128)S(1)} collective-permute-done((f32[7,3,3,1,128]{4,3,2,1,0:T(1,128)S(1)}, f32[7,3,3,1,128]{4,3,2,1,0:T(1,128)S(1)}, u32[]{:S(2)}, u32[]{:S(2)}) %collective-permute-start.4) | collective-permute-done | bytes 32288 | tf_op jit(solution)/shard_map/ppermute | solution.py:35
  24.9 2.4 %broadcast_subtract_fusion = f32[3,2,128,4608]{3,2,1,0:T(8,128)S(1)} fusion(f32[3,4608]{1,0:T(4,128)S(1)} %sub.186, f32[3,2,128]{2,1,0:T(2,128)} %bitcast.256), kind=kLoop, calls=%fused_computation.6 | loop fusion | flops 3538944 | bytes 14214144 | tf_op jit(solution)/shard_map/sub | solution.py:139
  27.4 4.2 %fusion.38 = (f32[2,128]{1,0:T(2,128)S(1)}, f32[2,128,4608]{2,1,0:T(8,128)}, f32[1,2,128,4608]{3,2,1,0:T(8,128)S(1)}) fusion(f32[2,4608]{1,0:T(2,128)S(1)} %copy-done.1, f32[4608]{0:T(1024)S(1)} %mul.541, f32[2,128]{1,0:T(2,128)S(1)} %compare_convert_fusion.1, f32[3,2,128,4608]{3,2,1,0:T(8,128)S(1)} %broadcast_subtract_fusion), kind=kLoop, calls=%fused_computation.146 | loop fusion | flops 14155520 | bytes 23650304 | tf_op jit(solution)/shard_map/reduce_sum | solution.py:154
  31.6 3.3 %fusion.7 = f32[2,128,4608]{2,1,0:T(8,128)} fusion(f32[2,4608]{1,0:T(2,128)S(1)} %copy-done.1, f32[4608]{0:T(1024)S(1)} %mul.541, f32[1,2,128,4608]{3,2,1,0:T(8,128)S(1)} %get-tuple-element.21, f32[2,128]{1,0:T(2,128)S(1)} %compare_convert_fusion.1), kind=kLoop, calls=%fused_computation.22 | loop fusion | flops 3538944 | bytes 9493504 | tf_op jit(solution)/shard_map/mul | solution.py:71
  35.2 3.4 %multiply_reduce_fusion.5 = f32[3,2,128]{2,1,0:T(2,128)S(1)} fusion(f32[3,4608]{1,0:T(4,128)S(1)} %slice.177, f32[2,128,4608]{2,1,0:T(8,128)} %fusion.7), kind=kLoop, calls=%fused_computation.5 | loop fusion | flops 7077120 | bytes 4776960 | tf_op jit(solution)/shard_map/reduce_sum | solution.py:71
  38.6 3.5 %collective-permute-start.5 = (f32[3,1,1,2,128]{4,3,0,2,1:T(2,128)S(1)}, f32[3,1,1,2,128]{4,3,0,2,1:T(2,128)S(1)}, u32[]{:S(2)}, u32[]{:S(2)}) collective-permute-start(f32[3,1,1,2,128]{4,3,0,2,1:T(2,128)S(1)} %fusion.23), channel_id=1, source_target_pairs={{0,8},{8,16},{16,24},{1,9},{9,17},{17,25},{2,10},{10,18},{18,26},{... | collective-permute-start | bytes 9224 | tf_op jit(solution)/shard_map/ppermute | solution.py:33
  43.4 4.2 %collective-permute-done.6 = f32[3,1,1,2,128]{4,3,0,2,1:T(2,128)S(1)} collective-permute-done((f32[3,1,1,2,128]{4,3,0,2,1:T(2,128)S(1)}, f32[3,1,1,2,128]{4,3,0,2,1:T(2,128)S(1)}, u32[]{:S(2)}, u32[]{:S(2)}) %collective-permute-start.6) | collective-permute-done | bytes 3104 | tf_op jit(solution)/shard_map/ppermute | solution.py:35
  49.2 2.1 %collective-permute-done.7 = f32[3,3,1,2,128]{4,3,0,2,1:T(2,128)S(1)} collective-permute-done((f32[3,3,1,2,128]{4,3,0,2,1:T(2,128)S(1)}, f32[3,3,1,2,128]{4,3,0,2,1:T(2,128)S(1)}, u32[]{:S(2)}, u32[]{:S(2)}) %collective-permute-start.7) | collective-permute-done | bytes 9248 | tf_op jit(solution)/shard_map/ppermute | solution.py:25
  54.8 3.7 %collective-permute-done.9 = f32[3,3,3,1,128]{4,3,0,2,1:T(1,128)S(1)} collective-permute-done((f32[3,3,3,1,128]{4,3,0,2,1:T(1,128)S(1)}, f32[3,3,3,1,128]{4,3,0,2,1:T(1,128)S(1)}, u32[]{:S(2)}, u32[]{:S(2)}) %collective-permute-start.9) | collective-permute-done | bytes 13856 | tf_op jit(solution)/shard_map/ppermute | solution.py:35
  58.9 4.1 %multiply_reduce_fusion = f32[4,2,128]{2,1,0:T(2,128)S(1)} fusion(f32[4,2,4608]{2,1,0:T(2,128)S(1)} %pad_maximum_fusion, f32[2,128,4608]{2,1,0:T(8,128)} %fusion.7), kind=kLoop, calls=%fused_computation | loop fusion | flops 9436160 | bytes 4870144 | tf_op jit(solution)/shard_map/reduce_sum | solution.py:71
  62.9 3.7 %multiply_reduce_fusion.4 = f32[3,2,128]{2,1,0:T(2,128)S(1)} fusion(f32[3,2,4608]{2,1,0:T(2,128)S(1)} %get-tuple-element.27, f32[2,128,4608]{2,1,0:T(8,128)} %get-tuple-element.20), kind=kLoop, calls=%fused_computation.4 | loop fusion | flops 7077120 | bytes 4832256 | tf_op jit(solution)/shard_map/reduce_sum | solution.py:71
  66.7 3.5 %collective-permute-start.10 = (f32[1,1,1,2,128]{4,3,2,1,0:T(2,128)S(1)}, f32[1,1,1,2,128]{4,3,2,1,0:T(2,128)S(1)}, u32[]{:S(2)}, u32[]{:S(2)}) collective-permute-start(f32[1,1,1,2,128]{4,3,2,1,0:T(2,128)S(1)} %bitcast.264), channel_id=1, source_target_pairs={{0,8},{8,16},{16,24},{1,9},{9,17},{17,25},{2,10},{10,18},{18,26},{... | collective-permute-start | bytes 3080 | tf_op jit(solution)/shard_map/ppermute | solution.py:33
  71.5 4.2 %collective-permute-done.11 = f32[1,1,1,2,128]{4,3,2,1,0:T(2,128)S(1)} collective-permute-done((f32[1,1,1,2,128]{4,3,2,1,0:T(2,128)S(1)}, f32[1,1,1,2,128]{4,3,2,1,0:T(2,128)S(1)}, u32[]{:S(2)}, u32[]{:S(2)}) %collective-permute-start.11) | collective-permute-done | bytes 1056 | tf_op jit(solution)/shard_map/ppermute | solution.py:35
  77.2 2.1 %collective-permute-done.12 = f32[1,3,1,2,128]{4,3,2,1,0:T(2,128)S(1)} collective-permute-done((f32[1,3,1,2,128]{4,3,2,1,0:T(2,128)S(1)}, f32[1,3,1,2,128]{4,3,2,1,0:T(2,128)S(1)}, u32[]{:S(2)}, u32[]{:S(2)}) %collective-permute-start.12) | collective-permute-done | bytes 3104 | tf_op jit(solution)/shard_map/ppermute | solution.py:25
  82.6 3.6 %collective-permute-done.14 = f32[1,3,3,1,128]{4,3,2,1,0:T(1,128)S(1)} collective-permute-done((f32[1,3,3,1,128]{4,3,2,1,0:T(1,128)S(1)}, f32[1,3,3,1,128]{4,3,2,1,0:T(1,128)S(1)}, u32[]{:S(2)}, u32[]{:S(2)}) %collective-permute-start.14) | collective-permute-done | bytes 4640 | tf_op jit(solution)/shard_map/ppermute | solution.py:35
  86.3 3.5 %multiply_reduce_fusion.8 = f32[2,128]{1,0:T(2,128)S(1)} fusion(f32[4608]{0:T(1024)S(1)} %reshape.498, f32[2,4608]{1,0:T(2,128)S(1)} %copy-done.1, f32[4608]{0:T(1024)S(1)} %mul.541, f32[1,2,128,4608]{3,2,1,0:T(8,128)} %copy-done, f32[2,128]{1,0:T(2,128)S(1)} %compare_convert_fusion.1), kind=kLoop, calls=%fused_computation.20 | loop fusion | flops 5897984 | bytes 4794368 | tf_op jit(solution)/shard_map/reduce_sum | solution.py:71
  93.0 4.2 %collective-permute-done.16 = f32[1,1,1,2,128]{4,3,2,1,0:T(2,128)S(1)} collective-permute-done((f32[1,1,1,2,128]{4,3,2,1,0:T(2,128)S(1)}, f32[1,1,1,2,128]{4,3,2,1,0:T(2,128)S(1)}, u32[]{:S(2)}, u32[]{:S(2)}) %collective-permute-start.16) | collective-permute-done | bytes 1056 | tf_op jit(solution)/shard_map/ppermute | solution.py:35
  98.7 2.1 %collective-permute-done.17 = f32[1,3,1,2,128]{4,3,2,1,0:T(2,128)S(1)} collective-permute-done((f32[1,3,1,2,128]{4,3,2,1,0:T(2,128)S(1)}, f32[1,3,1,2,128]{4,3,2,1,0:T(2,128)S(1)}, u32[]{:S(2)}, u32[]{:S(2)}) %collective-permute-start.17) | collective-permute-done | bytes 3104 | tf_op jit(solution)/shard_map/ppermute | solution.py:25
  103.8 3.9 %collective-permute-done.19 = f32[1,3,3,1,128]{4,3,2,1,0:T(1,128)S(1)} collective-permute-done((f32[1,3,3,1,128]{4,3,2,1,0:T(1,128)S(1)}, f32[1,3,3,1,128]{4,3,2,1,0:T(1,128)S(1)}, u32[]{:S(2)}, u32[]{:S(2)}) %collective-permute-start.19) | collective-permute-done | bytes 4640 | tf_op jit(solution)/shard_map/ppermute | solution.py:35
  107.7 3.5 %multiply_reduce_fusion.7 = f32[2,128]{1,0:T(2,128)S(1)} fusion(f32[4608]{0:T(1024)S(1)} %reshape.499, f32[2,4608]{1,0:T(2,128)S(1)} %copy-done.1, f32[4608]{0:T(1024)S(1)} %mul.541, f32[1,2,128,4608]{3,2,1,0:T(8,128)} %copy-done, f32[2,128]{1,0:T(2,128)S(1)} %compare_convert_fusion.1), kind=kLoop, calls=%fused_computation.19 | loop fusion | flops 5897984 | bytes 4794368 | tf_op jit(solution)/shard_map/reduce_sum | solution.py:71
  114.5 4.2 %collective-permute-done.21 = f32[1,1,1,2,128]{4,3,2,1,0:T(2,128)S(1)} collective-permute-done((f32[1,1,1,2,128]{4,3,2,1,0:T(2,128)S(1)}, f32[1,1,1,2,128]{4,3,2,1,0:T(2,128)S(1)}, u32[]{:S(2)}, u32[]{:S(2)}) %collective-permute-start.21) | collective-permute-done | bytes 1056 | tf_op jit(solution)/shard_map/ppermute | solution.py:35
  120.1 2.1 %collective-permute-done.22 = f32[1,3,1,2,128]{4,3,2,1,0:T(2,128)S(1)} collective-permute-done((f32[1,3,1,2,128]{4,3,2,1,0:T(2,128)S(1)}, f32[1,3,1,2,128]{4,3,2,1,0:T(2,128)S(1)}, u32[]{:S(2)}, u32[]{:S(2)}) %collective-permute-start.22) | collective-permute-done | bytes 3104 | tf_op jit(solution)/shard_map/ppermute | solution.py:25
  125.4 3.7 %collective-permute-done.24 = f32[1,3,3,1,128]{4,3,2,1,0:T(1,128)S(1)} collective-permute-done((f32[1,3,3,1,128]{4,3,2,1,0:T(1,128)S(1)}, f32[1,3,3,1,128]{4,3,2,1,0:T(1,128)S(1)}, u32[]{:S(2)}, u32[]{:S(2)}) %collective-permute-start.24) | collective-permute-done | bytes 4640 | tf_op jit(solution)/shard_map/ppermute | solution.py:35
  129.2 3.5 %multiply_reduce_fusion.6 = f32[2,128]{1,0:T(2,128)S(1)} fusion(f32[4608]{0:T(1024)S(1)} %reshape.500, f32[2,4608]{1,0:T(2,128)S(1)} %copy-done.1, f32[4608]{0:T(1024)S(1)} %mul.541, f32[1,2,128,4608]{3,2,1,0:T(8,128)} %copy-done, f32[2,128]{1,0:T(2,128)S(1)} %compare_convert_fusion.1), kind=kLoop, calls=%fused_computation.18 | loop fusion | flops 5897984 | bytes 4794368 | tf_op jit(solution)/shard_map/reduce_sum | solution.py:71
  132.8 3.6 %collective-permute-done.25 = f32[3,4,128]{2,1,0:T(4,128)S(1)} collective-permute-done((f32[3,4,128]{2,1,0:T(4,128)S(1)}, f32[3,4,128]{2,1,0:T(4,128)S(1)}, u32[]{:S(2)}, u32[]{:S(2)}) %collective-permute-start.25) | collective-permute-done | bytes 6176 | tf_op jit(solution)/shard_map/ppermute | solution.py:50
  136.5 4.6 %collective-permute-done.26 = f32[3,4,128]{2,1,0:T(4,128)S(1)} collective-permute-done((f32[3,4,128]{2,1,0:T(4,128)S(1)}, f32[3,4,128]{2,1,0:T(4,128)S(1)}, u32[]{:S(2)}, u32[]{:S(2)}) %collective-permute-start.26) | collective-permute-done | bytes 6176 | tf_op jit(solution)/shard_map/ppermute | solution.py:50
  142.5 2.1 %collective-permute-done.27 = f32[3,4,128]{2,1,0:T(4,128)S(1)} collective-permute-done((f32[3,4,128]{2,1,0:T(4,128)S(1)}, f32[3,4,128]{2,1,0:T(4,128)S(1)}, u32[]{:S(2)}, u32[]{:S(2)}) %collective-permute-start.27) | collective-permute-done | bytes 6176 | tf_op jit(solution)/shard_map/ppermute | solution.py:50
  145.8 2.3 %collective-permute-start.29 = (f32[3,4,128]{2,1,0:T(4,128)S(1)}, f32[3,4,128]{2,1,0:T(4,128)S(1)}, u32[]{:S(2)}, u32[]{:S(2)}) collective-permute-start(f32[3,4,128]{2,1,0:T(4,128)S(1)} %add.186), channel_id=1, source_target_pairs={{0,2},{1,3},{2,0},{3,1},{4,6},{5,7},{6,4},{7,5},{8,10},{9,11},{10,... | collective-permute-start | bytes 18440 | tf_op jit(solution)/shard_map/ppermute | solution.py:50
  148.1 4.9 %multiply_reduce_fusion.3 = (f32[3,2,128]{2,1,0:T(2,128)S(1)}, f32[3,2,128]{2,1,0:T(2,128)S(1)}, f32[3,2,128]{2,1,0:T(2,128)S(1)}) fusion(f32[3,2,4608]{2,1,0:T(2,128)S(1)} %get-tuple-element.26, f32[2,128,4608]{2,1,0:T(8,128)} %get-tuple-element.20, f32[3,2,4608]{2,1,0:T(2,128)S(1)} %get-tuple-element.25, f32[3,2,4608]{2,1,0:T(2,128)S(1)} %get-tuple-element.24), kind=kLoop, calls=%fused_computation.3 | loop fusion | flops 21231360 | bytes 5059584 | tf_op jit(solution)/shard_map/reduce_sum | solution.py:71
  (130 shorter events, 43.8 us)
Async XLA Ops:
  2.1 6.3 %collective-permute-start = (f32[7,1,1,2,128]{4,3,2,1,0:T(2,128)S(1)}, f32[7,1,1,2,128]{4,3,2,1,0:T(2,128)S(1)}, u32[]{:S(2)}, u32[]{:S(2)}) collective-permute-start(f32[7,1,1,2,128]{4,3,2,1,0:T(2,128)S(1)} %pad_maximum_fusion.13), channel_id=1, source_target_pairs={{0,8},{8,16},{16,24},{1,9},{9,17},{17,25},{2,10},{10,18},{18,26},{... | collective-permute-start | bytes 21512 | tf_op jit(solution)/shard_map/ppermute | solution.py:33
  7.0 5.5 %collective-permute-start.1 = (f32[7,1,1,2,128]{4,3,2,1,0:T(2,128)S(1)}, f32[7,1,1,2,128]{4,3,2,1,0:T(2,128)S(1)}, u32[]{:S(2)}, u32[]{:S(2)}) collective-permute-start(f32[7,1,1,2,128]{4,3,2,1,0:T(2,128)S(1)} %pad_maximum_fusion.13), channel_id=1, source_target_pairs={{8,0},{16,8},{24,16},{9,1},{17,9},{25,17},{10,2},{18,10},{26,18},{... | collective-permute-start | bytes 21512 | tf_op jit(solution)/shard_map/ppermute | solution.py:35
  13.2 3.9 %collective-permute-start.2 = (f32[7,3,1,2,128]{4,3,2,1,0:T(2,128)S(1)}, f32[7,3,1,2,128]{4,3,2,1,0:T(2,128)S(1)}, u32[]{:S(2)}, u32[]{:S(2)}) collective-permute-start(f32[7,3,1,2,128]{4,3,2,1,0:T(2,128)S(1)} %pad_maximum_fusion.5), channel_id=1, source_target_pairs={{0,4},{4,0},{1,5},{5,1},{2,6},{6,2},{3,7},{7,3},{8,12},{12,8},{9,1... | collective-permute-start | bytes 64520 | tf_op jit(solution)/shard_map/ppermute | solution.py:25
  17.9 3.3 %collective-permute-start.3 = (f32[7,3,3,1,128]{4,3,2,1,0:T(1,128)S(1)}, f32[7,3,3,1,128]{4,3,2,1,0:T(1,128)S(1)}, u32[]{:S(2)}, u32[]{:S(2)}) collective-permute-start(f32[7,3,3,1,128]{4,3,2,1,0:T(1,128)S(1)} %get-tuple-element.29), channel_id=1, source_target_pairs={{0,1},{1,2},{2,3},{4,5},{5,6},{6,7},{8,9},{9,10},{10,11},{12,13},{... | collective-permute-start | bytes 96776 | tf_op jit(solution)/shard_map/ppermute | solution.py:33
  19.2 4.8 %collective-permute-start.4 = (f32[7,3,3,1,128]{4,3,2,1,0:T(1,128)S(1)}, f32[7,3,3,1,128]{4,3,2,1,0:T(1,128)S(1)}, u32[]{:S(2)}, u32[]{:S(2)}) collective-permute-start(f32[7,3,3,1,128]{4,3,2,1,0:T(1,128)S(1)} %get-tuple-element.30), channel_id=1, source_target_pairs={{1,0},{2,1},{3,2},{5,4},{6,5},{7,6},{9,8},{10,9},{11,10},{13,12},{... | collective-permute-start | bytes 96776 | tf_op jit(solution)/shard_map/ppermute | solution.py:35
  31.6 3.6 %copy-start = (f32[1,2,128,4608]{3,2,1,0:T(8,128)}, f32[1,2,128,4608]{3,2,1,0:T(8,128)S(1)}, u32[]{:S(2)}) copy-start(f32[1,2,128,4608]{3,2,1,0:T(8,128)S(1)} %get-tuple-element.21) | copy-start | bytes 14155780
  38.6 4.8 %collective-permute-start.5 = (f32[3,1,1,2,128]{4,3,0,2,1:T(2,128)S(1)}, f32[3,1,1,2,128]{4,3,0,2,1:T(2,128)S(1)}, u32[]{:S(2)}, u32[]{:S(2)}) collective-permute-start(f32[3,1,1,2,128]{4,3,0,2,1:T(2,128)S(1)} %fusion.23), channel_id=1, source_target_pairs={{0,8},{8,16},{16,24},{1,9},{9,17},{17,25},{2,10},{10,18},{18,26},{... | collective-permute-start | bytes 9224 | tf_op jit(solution)/shard_map/ppermute | solution.py:33
  42.1 5.5 %collective-permute-start.6 = (f32[3,1,1,2,128]{4,3,0,2,1:T(2,128)S(1)}, f32[3,1,1,2,128]{4,3,0,2,1:T(2,128)S(1)}, u32[]{:S(2)}, u32[]{:S(2)}) collective-permute-start(f32[3,1,1,2,128]{4,3,0,2,1:T(2,128)S(1)} %fusion.23), channel_id=1, source_target_pairs={{8,0},{16,8},{24,16},{9,1},{17,9},{25,17},{10,2},{18,10},{26,18},{... | collective-permute-start | bytes 9224 | tf_op jit(solution)/shard_map/ppermute | solution.py:35
  47.6 3.7 %collective-permute-start.7 = (f32[3,3,1,2,128]{4,3,0,2,1:T(2,128)S(1)}, f32[3,3,1,2,128]{4,3,0,2,1:T(2,128)S(1)}, u32[]{:S(2)}, u32[]{:S(2)}) collective-permute-start(f32[3,3,1,2,128]{4,3,0,2,1:T(2,128)S(1)} %pad_maximum_fusion.9), channel_id=1, source_target_pairs={{0,4},{4,0},{1,5},{5,1},{2,6},{6,2},{3,7},{7,3},{8,12},{12,8},{9,1... | collective-permute-start | bytes 27656 | tf_op jit(solution)/shard_map/ppermute | solution.py:25
  51.3 3.4 %collective-permute-start.8 = (f32[3,3,3,1,128]{4,3,0,2,1:T(1,128)S(1)}, f32[3,3,3,1,128]{4,3,0,2,1:T(1,128)S(1)}, u32[]{:S(2)}, u32[]{:S(2)}) collective-permute-start(f32[3,3,3,1,128]{4,3,0,2,1:T(1,128)S(1)} %get-tuple-element.31), channel_id=1, source_target_pairs={{0,1},{1,2},{2,3},{4,5},{5,6},{6,7},{8,9},{9,10},{10,11},{12,13},{... | collective-permute-start | bytes 41480 | tf_op jit(solution)/shard_map/ppermute | solution.py:33
  53.4 5.1 %collective-permute-start.9 = (f32[3,3,3,1,128]{4,3,0,2,1:T(1,128)S(1)}, f32[3,3,3,1,128]{4,3,0,2,1:T(1,128)S(1)}, u32[]{:S(2)}, u32[]{:S(2)}) collective-permute-start(f32[3,3,3,1,128]{4,3,0,2,1:T(1,128)S(1)} %get-tuple-element.32), channel_id=1, source_target_pairs={{1,0},{2,1},{3,2},{5,4},{6,5},{7,6},{9,8},{10,9},{11,10},{13,12},{... | collective-permute-start | bytes 41480 | tf_op jit(solution)/shard_map/ppermute | solution.py:35
  58.9 7.7 %copy-start.2 = (f32[3,1,1,2,128]{4,3,2,1,0:T(2,128)S(1)}, f32[3,1,1,2,128]{4,3,2,1,0:T(2,128)}, u32[]{:S(2)}) copy-start(f32[3,1,1,2,128]{4,3,2,1,0:T(2,128)} %param.5) | copy-start | bytes 9220
  66.7 4.8 %collective-permute-start.10 = (f32[1,1,1,2,128]{4,3,2,1,0:T(2,128)S(1)}, f32[1,1,1,2,128]{4,3,2,1,0:T(2,128)S(1)}, u32[]{:S(2)}, u32[]{:S(2)}) collective-permute-start(f32[1,1,1,2,128]{4,3,2,1,0:T(2,128)S(1)} %bitcast.264), channel_id=1, source_target_pairs={{0,8},{8,16},{16,24},{1,9},{9,17},{17,25},{2,10},{10,18},{18,26},{... | collective-permute-start | bytes 3080 | tf_op jit(solution)/shard_map/ppermute | solution.py:33
  70.2 5.5 %collective-permute-start.11 = (f32[1,1,1,2,128]{4,3,2,1,0:T(2,128)S(1)}, f32[1,1,1,2,128]{4,3,2,1,0:T(2,128)S(1)}, u32[]{:S(2)}, u32[]{:S(2)}) collective-permute-start(f32[1,1,1,2,128]{4,3,2,1,0:T(2,128)S(1)} %bitcast.265), channel_id=1, source_target_pairs={{8,0},{16,8},{24,16},{9,1},{17,9},{25,17},{10,2},{18,10},{26,18},{... | collective-permute-start | bytes 3080 | tf_op jit(solution)/shard_map/ppermute | solution.py:35
  75.7 3.6 %collective-permute-start.12 = (f32[1,3,1,2,128]{4,3,2,1,0:T(2,128)S(1)}, f32[1,3,1,2,128]{4,3,2,1,0:T(2,128)S(1)}, u32[]{:S(2)}, u32[]{:S(2)}) collective-permute-start(f32[1,3,1,2,128]{4,3,2,1,0:T(2,128)S(1)} %pad_maximum_fusion.15), channel_id=1, source_target_pairs={{0,4},{4,0},{1,5},{5,1},{2,6},{6,2},{3,7},{7,3},{8,12},{12,8},{9,1... | collective-permute-start | bytes 9224 | tf_op jit(solution)/shard_map/ppermute | solution.py:25
  79.3 3.3 %collective-permute-start.13 = (f32[1,3,3,1,128]{4,3,2,1,0:T(1,128)S(1)}, f32[1,3,3,1,128]{4,3,2,1,0:T(1,128)S(1)}, u32[]{:S(2)}, u32[]{:S(2)}) collective-permute-start(f32[1,3,3,1,128]{4,3,2,1,0:T(1,128)S(1)} %get-tuple-element.39), channel_id=1, source_target_pairs={{0,1},{1,2},{2,3},{4,5},{5,6},{6,7},{8,9},{9,10},{10,11},{12,13},{... | collective-permute-start | bytes 13832 | tf_op jit(solution)/shard_map/ppermute | solution.py:33
  81.3 4.9 %collective-permute-start.14 = (f32[1,3,3,1,128]{4,3,2,1,0:T(1,128)S(1)}, f32[1,3,3,1,128]{4,3,2,1,0:T(1,128)S(1)}, u32[]{:S(2)}, u32[]{:S(2)}) collective-permute-start(f32[1,3,3,1,128]{4,3,2,1,0:T(1,128)S(1)} %get-tuple-element.40), channel_id=1, source_target_pairs={{1,0},{2,1},{3,2},{5,4},{6,5},{7,6},{9,8},{10,9},{11,10},{13,12},{... | collective-permute-start | bytes 13832 | tf_op jit(solution)/shard_map/ppermute | solution.py:35
  89.8 3.2 %collective-permute-start.15 = (f32[1,1,1,2,128]{4,3,2,1,0:T(2,128)S(1)}, f32[1,1,1,2,128]{4,3,2,1,0:T(2,128)S(1)}, u32[]{:S(2)}, u32[]{:S(2)}) collective-permute-start(f32[1,1,1,2,128]{4,3,2,1,0:T(2,128)S(1)} %get-tuple-element.52), channel_id=1, source_target_pairs={{0,8},{8,16},{16,24},{1,9},{9,17},{17,25},{2,10},{10,18},{18,26},{... | collective-permute-start | bytes 3080 | tf_op jit(solution)/shard_map/ppermute | solution.py:33
  91.7 5.5 %collective-permute-start.16 = (f32[1,1,1,2,128]{4,3,2,1,0:T(2,128)S(1)}, f32[1,1,1,2,128]{4,3,2,1,0:T(2,128)S(1)}, u32[]{:S(2)}, u32[]{:S(2)}) collective-permute-start(f32[1,1,1,2,128]{4,3,2,1,0:T(2,128)S(1)} %get-tuple-element.52), channel_id=1, source_target_pairs={{8,0},{16,8},{24,16},{9,1},{17,9},{25,17},{10,2},{18,10},{26,18},{... | collective-permute-start | bytes 3080 | tf_op jit(solution)/shard_map/ppermute | solution.py:35
  97.2 3.6 %collective-permute-start.17 = (f32[1,3,1,2,128]{4,3,2,1,0:T(2,128)S(1)}, f32[1,3,1,2,128]{4,3,2,1,0:T(2,128)S(1)}, u32[]{:S(2)}, u32[]{:S(2)}) collective-permute-start(f32[1,3,1,2,128]{4,3,2,1,0:T(2,128)S(1)} %pad_maximum_fusion.16), channel_id=1, source_target_pairs={{0,4},{4,0},{1,5},{5,1},{2,6},{6,2},{3,7},{7,3},{8,12},{12,8},{9,1... | collective-permute-start | bytes 9224 | tf_op jit(solution)/shard_map/ppermute | solution.py:25
  100.8 3.0 %collective-permute-start.18 = (f32[1,3,3,1,128]{4,3,2,1,0:T(1,128)S(1)}, f32[1,3,3,1,128]{4,3,2,1,0:T(1,128)S(1)}, u32[]{:S(2)}, u32[]{:S(2)}) collective-permute-start(f32[1,3,3,1,128]{4,3,2,1,0:T(1,128)S(1)} %get-tuple-element.37), channel_id=1, source_target_pairs={{0,1},{1,2},{2,3},{4,5},{5,6},{6,7},{8,9},{9,10},{10,11},{12,13},{... | collective-permute-start | bytes 13832 | tf_op jit(solution)/shard_map/ppermute | solution.py:33
  102.5 5.2 %collective-permute-start.19 = (f32[1,3,3,1,128]{4,3,2,1,0:T(1,128)S(1)}, f32[1,3,3,1,128]{4,3,2,1,0:T(1,128)S(1)}, u32[]{:S(2)}, u32[]{:S(2)}) collective-permute-start(f32[1,3,3,1,128]{4,3,2,1,0:T(1,128)S(1)} %get-tuple-element.38), channel_id=1, source_target_pairs={{1,0},{2,1},{3,2},{5,4},{6,5},{7,6},{9,8},{10,9},{11,10},{13,12},{... | collective-permute-start | bytes 13832 | tf_op jit(solution)/shard_map/ppermute | solution.py:35
  111.2 3.2 %collective-permute-start.20 = (f32[1,1,1,2,128]{4,3,2,1,0:T(2,128)S(1)}, f32[1,1,1,2,128]{4,3,2,1,0:T(2,128)S(1)}, u32[]{:S(2)}, u32[]{:S(2)}) collective-permute-start(f32[1,1,1,2,128]{4,3,2,1,0:T(2,128)S(1)} %divide_bitcast_fusion), channel_id=1, source_target_pairs={{0,8},{8,16},{16,24},{1,9},{9,17},{17,25},{2,10},{10,18},{18,26},{... | collective-permute-start | bytes 3080 | tf_op jit(solution)/shard_map/ppermute | solution.py:33
  113.2 5.5 %collective-permute-start.21 = (f32[1,1,1,2,128]{4,3,2,1,0:T(2,128)S(1)}, f32[1,1,1,2,128]{4,3,2,1,0:T(2,128)S(1)}, u32[]{:S(2)}, u32[]{:S(2)}) collective-permute-start(f32[1,1,1,2,128]{4,3,2,1,0:T(2,128)S(1)} %divide_bitcast_fusion), channel_id=1, source_target_pairs={{8,0},{16,8},{24,16},{9,1},{17,9},{25,17},{10,2},{18,10},{26,18},{... | collective-permute-start | bytes 3080 | tf_op jit(solution)/shard_map/ppermute | solution.py:35
  118.6 3.6 %collective-permute-start.22 = (f32[1,3,1,2,128]{4,3,2,1,0:T(2,128)S(1)}, f32[1,3,1,2,128]{4,3,2,1,0:T(2,128)S(1)}, u32[]{:S(2)}, u32[]{:S(2)}) collective-permute-start(f32[1,3,1,2,128]{4,3,2,1,0:T(2,128)S(1)} %pad_maximum_fusion.17), channel_id=1, source_target_pairs={{0,4},{4,0},{1,5},{5,1},{2,6},{6,2},{3,7},{7,3},{8,12},{12,8},{9,1... | collective-permute-start | bytes 9224 | tf_op jit(solution)/shard_map/ppermute | solution.py:25
  122.3 3.2 %collective-permute-start.23 = (f32[1,3,3,1,128]{4,3,2,1,0:T(1,128)S(1)}, f32[1,3,3,1,128]{4,3,2,1,0:T(1,128)S(1)}, u32[]{:S(2)}, u32[]{:S(2)}) collective-permute-start(f32[1,3,3,1,128]{4,3,2,1,0:T(1,128)S(1)} %get-tuple-element.35), channel_id=1, source_target_pairs={{0,1},{1,2},{2,3},{4,5},{5,6},{6,7},{8,9},{9,10},{10,11},{12,13},{... | collective-permute-start | bytes 13832 | tf_op jit(solution)/shard_map/ppermute | solution.py:33
  124.0 5.2 %collective-permute-start.24 = (f32[1,3,3,1,128]{4,3,2,1,0:T(1,128)S(1)}, f32[1,3,3,1,128]{4,3,2,1,0:T(1,128)S(1)}, u32[]{:S(2)}, u32[]{:S(2)}) collective-permute-start(f32[1,3,3,1,128]{4,3,2,1,0:T(1,128)S(1)} %get-tuple-element.36), channel_id=1, source_target_pairs={{1,0},{2,1},{3,2},{5,4},{6,5},{7,6},{9,8},{10,9},{11,10},{13,12},{... | collective-permute-start | bytes 13832 | tf_op jit(solution)/shard_map/ppermute | solution.py:35
  132.8 3.7 %collective-permute-start.25 = (f32[3,4,128]{2,1,0:T(4,128)S(1)}, f32[3,4,128]{2,1,0:T(4,128)S(1)}, u32[]{:S(2)}, u32[]{:S(2)}) collective-permute-start(f32[3,4,128]{2,1,0:T(4,128)S(1)} %multiply_reduce_fusion.9), channel_id=1, source_target_pairs={{0,8},{8,0},{16,24},{24,16},{1,9},{9,1},{17,25},{25,17},{2,10},{10... | collective-permute-start | bytes 18440 | tf_op jit(solution)/shard_map/ppermute | solution.py:50
  136.5 4.6 %collective-permute-start.26 = (f32[3,4,128]{2,1,0:T(4,128)S(1)}, f32[3,4,128]{2,1,0:T(4,128)S(1)}, u32[]{:S(2)}, u32[]{:S(2)}) collective-permute-start(f32[3,4,128]{2,1,0:T(4,128)S(1)} %add.183), channel_id=1, source_target_pairs={{0,16},{8,24},{16,0},{24,8},{1,17},{9,25},{17,1},{25,9},{2,18},{10... | collective-permute-start | bytes 18440 | tf_op jit(solution)/shard_map/ppermute | solution.py:50
  141.0 3.6 %collective-permute-start.27 = (f32[3,4,128]{2,1,0:T(4,128)S(1)}, f32[3,4,128]{2,1,0:T(4,128)S(1)}, u32[]{:S(2)}, u32[]{:S(2)}) collective-permute-start(f32[3,4,128]{2,1,0:T(4,128)S(1)} %add.184), channel_id=1, source_target_pairs={{0,4},{4,0},{1,5},{5,1},{2,6},{6,2},{3,7},{7,3},{8,12},{12,8},{9,1... | collective-permute-start | bytes 18440 | tf_op jit(solution)/shard_map/ppermute | solution.py:50
  144.7 1.2 collective-permute-start.28
  145.8 7.2 %collective-permute-start.29 = (f32[3,4,128]{2,1,0:T(4,128)S(1)}, f32[3,4,128]{2,1,0:T(4,128)S(1)}, u32[]{:S(2)}, u32[]{:S(2)}) collective-permute-start(f32[3,4,128]{2,1,0:T(4,128)S(1)} %add.186), channel_id=1, source_target_pairs={{0,2},{1,3},{2,0},{3,1},{4,6},{5,7},{6,4},{7,5},{8,10},{9,11},{10,... | collective-permute-start | bytes 18440 | tf_op jit(solution)/shard_map/ppermute | solution.py:50
  (4 other events, 10.0 us)

commit v5 on v3

--- a/solution.py
+++ b/solution.py
@@ -39,7 +39,36 @@
     return cells
 
 
+def gather_rim(cells):
+    comps, size_x, size_y, size_z, width = cells.shape
+    counts = [lax.axis_size(axis) for axis, _ in AXES]
+    devices = counts[0] * counts[1] * counts[2]
+    rows = jnp.broadcast_to(cells[None], (devices,) + cells.shape)
+    got = lax.all_to_all(rows, ("gx", "gy", "gz"), 0, 0, tiled=True)
+    grid = got.reshape(counts[0], counts[1], counts[2], comps, size_x, size_y, size_z, width)
+    grid = grid.transpose(3, 0, 4, 1, 5, 2, 6, 7).reshape(
+        comps, counts[0] * size_x, counts[1] * size_y, counts[2] * size_z, width
+    )
+    padded = jnp.pad(grid, ((0, 0), (1, 1), (1, 1), (1, 1), (0, 0)))
+    start = (
+        0,
+        lax.axis_index("gx") * size_x,
+        lax.axis_index("gy") * size_y,
+        lax.axis_index("gz") * size_z,
+        0,
+    )
+    return lax.dynamic_slice(padded, start, (comps, size_x + 2, size_y + 2, size_z + 2, width))
+
+
 def total(values):
+    counts = [lax.axis_size(axis) for axis, _ in AXES]
+    devices = counts[0] * counts[1] * counts[2]
+    rows = jnp.broadcast_to(values[None], (devices,) + values.shape)
+    got = lax.all_to_all(rows, ("gx", "gy", "gz"), 0, 0, tiled=True)
+    return jnp.sum(got, axis=0)
+
+
+def total_butterfly(values):
     for axis in ("gx", "gy", "gz"):
         count = lax.axis_size(axis)
         if count & (count - 1):
@@ -124,7 +153,7 @@
     packed = jnp.concatenate([positions, valid_mask, velocity], axis=0)
 
     def rim_flat(cells):
-        rim = with_halo(cells, AXES, 1)
+        rim = gather_rim(cells)
         return rim.reshape(rim.shape[0], 1, -1)
 
     near_all = rim_flat(packed)
@@ -183,7 +212,11 @@
         basis.append(-(out[0:1] / width) / diagonal)
     stacked = jnp.concatenate(basis, axis=0)
     weighted = stacked[:ITERS] * diagonal
-    gram = total(jnp.sum(weighted[:, None] * stacked[None, :], axis=(2, 3)))
+    gram = total(jnp.sum(weighted[:, None] * stacked[None, :], axis=2))
+    shift = width // 2
+    while shift >= 1:
+        gram = gram + jnp.roll(gram, shift, axis=-1)
+        shift //= 2
     coords = solve3(gram[:, :ITERS] + gram[:, 1:], gram[:, 0])
 
     pressure = coords[0] * basis[0]

time: 164 us -> 104 us (0.63)
  waiting for transfers between devices: 61.9 us -> 23.2 us
  starting transfers between devices: 49 us -> 12.6 us
  blocking collectives: 0 us -> 29.6 us
  between operations: 14.3 us -> 1.02 us
  other arithmetic: 35.7 us -> 33.7 us
    ppermute x30 -> x0, waiting for transfers between devices: 61.9 us -> none  [the longest x10 38.5 us: with_halo(): lax.ppermute(head, axis, [((i + 1) % count, i) for i in range(ends)])]
    ppermute x30 -> x0, starting transfers between devices: 49 us -> none  [the longest x10 24.4 us: with_halo(): lax.ppermute(tail, axis, [(i, (i + 1) % count) for i in range(ends)])]
    all_to_all x0 -> x3, blocking collectives: none -> 29.6 us  [the longest x2 19 us: gather_rim(): got = lax.all_to_all(rows, ('gx', 'gy', 'gz'), 0, 0, tiled=True)]
    all_to_all x0 -> x3, waiting for transfers between devices: none -> 23.2 us  [gather_rim(): got = lax.all_to_all(rows, ('gx', 'gy', 'gz'), 0, 0, tiled=True)]
    all_to_all x0 -> x3, starting transfers between devices: none -> 12.6 us  [gather_rim(): got = lax.all_to_all(rows, ('gx', 'gy', 'gz'), 0, 0, tiled=True)]
    concatenate x16 -> x0, other arithmetic: 3.1 us -> none  [the longest x10 1.62 us: with_halo(): jnp.concatenate([lax.ppermute(tail, axis, [(i, (i + 1) % count) for i in...]
    broadcast_in_dim x0 -> x6, local copies, waits for them, and re-layouts: none -> 2.03 us  [the longest x5 2 us: gather_rim(): rows = jnp.broadcast_to(cells[None], (devices,) + cells.shape)]
  transfers between devices with their start and end apart: 30 -> 3, of which waited for: 20 -> 3; matrix products, arithmetic and copies ran while one was open for 1% -> 1% of each run, Pallas kernels for 0% -> 0%
where the time goes in v5:
time: 104 us; the launch traced here: 103 us
  other arithmetic  33.7 us (32%)
  blocking collectives  29.6 us (28%)
  waiting for transfers between devices  23.2 us (22%)
  starting transfers between devices  12.6 us (12%)
  local copies, waits for them, and re-layouts  3.31 us (3%)
    all_to_all x3, waiting for transfers between devices, gather_rim(): got = lax.all_to_all(rows, ('gx', 'gy', 'gz'), 0, 0, tiled=True)  23.2 us
    reduce_sum x5, other arithmetic, wsum(): return jnp.sum(weight[None] * near[:, :, None, :], axis=-1)  21.1 us
    all_to_all x2, blocking collectives, gather_rim(): got = lax.all_to_all(rows, ('gx', 'gy', 'gz'), 0, 0, tiled=True)  19 us
    all_to_all x3, starting transfers between devices, gather_rim(): got = lax.all_to_all(rows, ('gx', 'gy', 'gz'), 0, 0, tiled=True)  12.6 us
    all_to_all x1, blocking collectives, total(): got = lax.all_to_all(rows, ('gx', 'gy', 'gz'), 0, 0, tiled=True)  10.6 us
    mul x1, other arithmetic, wsum(): return jnp.sum(weight[None] * near[:, :, None, :], axis=-1)  2.87 us
    reduce_sum x1, other arithmetic, on_device(): row = jnp.sum(weight, axis=-1)[None]  2.54 us
    sub x1, other arithmetic, on_device(): offset = own_x[:, :, :, None] - near_x[:, :, None, :]  2.43 us
  transfers between devices with their start and end apart: 3, of which 3 were waited for; matrix products, arithmetic and copies ran while one was open for 1% of the time, Pallas kernels for 0%

profile of v5, /device:TPU:0, one launch (start us, length us, event | category | flops | bytes accessed | tf_op | source)
XLA Modules:
  0.0 103.4 jit_solution(12153503830532529889)
XLA Ops:
  0.6 0.7 compare_convert_fusion
  1.4 0.7 maximum_bitcast_fusion
  2.1 0.7 broadcast_in_dim.47
  2.8 7.3 %all-to-all-start = ((f32[32,7,1,1,2,128]{5,4,1,3,2,0:T(2,128)}), f32[32,7,1,1,2,128]{5,4,1,3,2,0:T(2,128)S(1)}, u32[]{:S(2)}, u32[]{:S(2)}) async-start(f32[32,7,1,1,2,128]{5,4,1,3,2,0:T(2,128)} %broadcast_in_dim.47), calls=%async_computation | async-start | bytes 458752 | tf_op jit(solution)/shard_map/all_to_all | solution.py:47
  10.2 0.1 copy.22
  10.3 0.7 compare_convert_fusion.1
  11.0 8.9 %all-to-all-done = f32[32,7,1,1,2,128]{5,4,1,3,2,0:T(2,128)S(1)} async-done(((f32[32,7,1,1,2,128]{5,4,1,3,2,0:T(2,128)}), f32[32,7,1,1,2,128]{5,4,1,3,2,0:T(2,128)S(1)}, u32[]{:S(2)}, u32[]{:S(2)}) %all-to-all-start) | async-done | bytes 229408 | tf_op jit(solution)/shard_map/all_to_all | solution.py:47
  20.2 2.4 %broadcast_subtract_fusion = f32[3,2,128,4608]{3,2,1,0:T(8,128)S(1)} fusion(f32[3,4608]{1,0:T(4,128)S(1)} %sub.155, f32[3,2,128]{2,1,0:T(2,128)} %bitcast.223), kind=kLoop, calls=%fused_computation.5 | loop fusion | flops 3538944 | bytes 14214144 | tf_op jit(solution)/shard_map/sub | solution.py:168
  22.6 2.5 %fusion.7 = (f32[2,128]{1,0:T(2,128)S(1)}, f32[1,2,128,4608]{3,2,1,0:T(8,128)S(1)}) fusion(f32[2,4608]{1,0:T(2,128)S(1)} %copy-done, f32[4608]{0:T(1024)S(1)} %mul.411, f32[2,128]{1,0:T(2,128)S(1)} %compare_convert_fusion.1, f32[3,2,128,4608]{3,2,1,0:T(8,128)S(1)} %broadcast_subtract_fusion), kind=kLoop, calls=%fused_computation.17 | loop fusion | flops 14155520 | bytes 18931712 | tf_op jit(solution)/shard_map/reduce_sum | solution.py:182
  25.2 2.9 %multiply_bitcast_fusion = f32[2,128,4608]{2,1,0:T(8,128)} fusion(f32[1,2,128,4608]{3,2,1,0:T(8,128)S(1)} %get-tuple-element.15, f32[2,4608]{1,0:T(2,128)S(1)} %copy-done, f32[4608]{0:T(1024)S(1)} %mul.411, f32[2,128]{1,0:T(2,128)S(1)} %compare_convert_fusion.1), kind=kLoop, calls=%fused_computation.18 | loop fusion | flops 3538944 | bytes 9493504 | tf_op jit(solution)/shard_map/mul | solution.py:100
  28.1 0.1 broadcast_subtract_fusion.1
  28.3 0.1 pad_maximum_fusion
  28.4 4.9 %multiply_reduce_fusion = f32[6,2,128]{2,1,0:T(2,128)S(1)} fusion(f32[6,2,4608]{2,1,0:T(2,128)S(1)} %pad_maximum_fusion, f32[2,128,4608]{2,1,0:T(8,128)} %multiply_bitcast_fusion), kind=kLoop, calls=%fused_computation | loop fusion | flops 14154240 | bytes 4945920 | tf_op jit(solution)/shard_map/reduce_sum | solution.py:100
  33.4 10.1 %all_to_all.30 = f32[32,3,1,1,2,128]{5,4,1,3,2,0:T(2,128)S(1)} all-to-all(f32[32,3,1,1,2,128]{5,4,1,3,2,0:T(2,128)S(1)} %broadcast_in_dim.51), channel_id=1, replica_groups=mesh['gx'=4,'gy'=2,'gz'=4] {'gx','gy','gz'}, dimensions={0} | all-to-all | bytes 196608 | tf_op jit(solution)/shard_map/all_to_all | solution.py:47
  43.7 0.1 fusion.8
  43.9 4.1 %multiply_reduce_fusion.4 = f32[4,2,128]{2,1,0:T(2,128)S(1)} fusion(f32[4,2,4608]{2,1,0:T(2,128)S(1)} %pad_maximum_fusion.1, f32[2,128,4608]{2,1,0:T(8,128)} %multiply_bitcast_fusion), kind=kLoop, calls=%fused_computation.4 | loop fusion | flops 9436160 | bytes 4870144 | tf_op jit(solution)/shard_map/reduce_sum | solution.py:100
  48.0 0.1 multiply_reduce_fusion.6
  48.1 8.9 %all_to_all.31 = f32[32,1,1,1,2,128]{5,4,3,2,1,0:T(2,128)S(1)} all-to-all(f32[32,1,1,1,2,128]{5,4,3,2,1,0:T(2,128)S(1)} %broadcast_in_dim.57), channel_id=1, replica_groups=mesh['gx'=4,'gy'=2,'gz'=4] {'gx','gy','gz'}, dimensions={0} | all-to-all | bytes 65536 | tf_op jit(solution)/shard_map/all_to_all | solution.py:47
  57.1 0.1 subtract_multiply_fusion.2
  57.3 4.1 %multiply_reduce_fusion.3 = f32[4,2,128]{2,1,0:T(2,128)S(1)} fusion(f32[4,2,4608]{2,1,0:T(2,128)S(1)} %pad_maximum_fusion.2, f32[2,128,4608]{2,1,0:T(8,128)} %multiply_bitcast_fusion), kind=kLoop, calls=%fused_computation.3 | loop fusion | flops 9436160 | bytes 4870144 | tf_op jit(solution)/shard_map/reduce_sum | solution.py:100
  61.4 0.6 broadcast_in_dim.61
  62.0 2.7 %all-to-all-start.3 = ((f32[32,1,1,1,2,128]{5,4,3,2,1,0:T(2,128)}), f32[32,1,1,1,2,128]{5,4,3,2,1,0:T(2,128)S(1)}, u32[]{:S(2)}, u32[]{:S(2)}) async-start(f32[32,1,1,1,2,128]{5,4,3,2,1,0:T(2,128)} %broadcast_in_dim.61), calls=%async_computation.3 | async-start | bytes 65536 | tf_op jit(solution)/shard_map/all_to_all | solution.py:47
  64.7 7.1 %all-to-all-done.3 = f32[32,1,1,1,2,128]{5,4,3,2,1,0:T(2,128)S(1)} async-done(((f32[32,1,1,1,2,128]{5,4,3,2,1,0:T(2,128)}), f32[32,1,1,1,2,128]{5,4,3,2,1,0:T(2,128)S(1)}, u32[]{:S(2)}, u32[]{:S(2)}) %all-to-all-start.3) | async-done | bytes 32800 | tf_op jit(solution)/shard_map/all_to_all | solution.py:47
  71.8 0.1 subtract_multiply_fusion.1
  72.0 4.1 %multiply_reduce_fusion.2 = f32[4,2,128]{2,1,0:T(2,128)S(1)} fusion(f32[4,2,4608]{2,1,0:T(2,128)S(1)} %pad_maximum_fusion.3, f32[2,128,4608]{2,1,0:T(8,128)} %multiply_bitcast_fusion), kind=kLoop, calls=%fused_computation.2 | loop fusion | flops 9436160 | bytes 4870144 | tf_op jit(solution)/shard_map/reduce_sum | solution.py:100
  76.1 0.6 broadcast_in_dim.65
  76.7 2.5 %all-to-all-start.4 = ((f32[32,1,1,1,2,128]{5,4,3,2,1,0:T(2,128)}), f32[32,1,1,1,2,128]{5,4,3,2,1,0:T(2,128)S(1)}, u32[]{:S(2)}, u32[]{:S(2)}) async-start(f32[32,1,1,1,2,128]{5,4,3,2,1,0:T(2,128)} %broadcast_in_dim.65), calls=%async_computation.4 | async-start | bytes 65536 | tf_op jit(solution)/shard_map/all_to_all | solution.py:47
  79.3 7.2 %all-to-all-done.4 = f32[32,1,1,1,2,128]{5,4,3,2,1,0:T(2,128)S(1)} async-done(((f32[32,1,1,1,2,128]{5,4,3,2,1,0:T(2,128)}), f32[32,1,1,1,2,128]{5,4,3,2,1,0:T(2,128)S(1)}, u32[]{:S(2)}, u32[]{:S(2)}) %all-to-all-start.4) | async-done | bytes 32800 | tf_op jit(solution)/shard_map/all_to_all | solution.py:47
  86.6 0.1 subtract_multiply_fusion
  86.8 4.1 %multiply_reduce_fusion.1 = f32[4,2,128]{2,1,0:T(2,128)S(1)} fusion(f32[4,2,4608]{2,1,0:T(2,128)S(1)} %pad_maximum_fusion.4, f32[2,128,4608]{2,1,0:T(8,128)} %multiply_bitcast_fusion), kind=kLoop, calls=%fused_computation.1 | loop fusion | flops 9436160 | bytes 4870144 | tf_op jit(solution)/shard_map/reduce_sum | solution.py:100
  90.9 10.6 %all_to_all.32 = f32[32,3,4,128]{3,2,1,0:T(4,128)S(1)} all-to-all(f32[32,3,4,128]{3,2,1,0:T(4,128)S(1)} %broadcast_in_dim.134), channel_id=1, replica_groups=mesh['gx'=4,'gy'=2,'gz'=4] {'gx','gy','gz'}, dimensions={0} | all-to-all | bytes 393216 | tf_op jit(solution)/shard_map/all_to_all | solution.py:67
  102.8 0.7 subtract_bitcast_fusion
  (68 shorter events, 2.4 us)
Async XLA Ops:
  2.8 17.1 %all-to-all-start = ((f32[32,7,1,1,2,128]{5,4,1,3,2,0:T(2,128)}), f32[32,7,1,1,2,128]{5,4,1,3,2,0:T(2,128)S(1)}, u32[]{:S(2)}, u32[]{:S(2)}) async-start(f32[32,7,1,1,2,128]{5,4,1,3,2,0:T(2,128)} %broadcast_in_dim.47), calls=%async_computation | async-start | bytes 458752 | tf_op jit(solution)/shard_map/all_to_all | solution.py:47
  20.2 2.5 %copy-start = (f32[2,4608]{1,0:T(2,128)S(1)}, f32[2,4608]{1,0:T(2,128)}, u32[]{:S(2)}) copy-start(f32[2,4608]{1,0:T(2,128)} %constant.48.clone) | copy-start | bytes 110596
  28.1 5.2 %copy-start.2 = (f32[3,1,1,2,128]{4,3,2,1,0:T(2,128)S(1)}, f32[3,1,1,2,128]{4,3,2,1,0:T(2,128)}, u32[]{:S(2)}) copy-start(f32[3,1,1,2,128]{4,3,2,1,0:T(2,128)} %param.6) | copy-start | bytes 9220
  28.1 5.2 %copy-start.4 = (f32[3]{0:T(128)S(1)}, f32[3]{0:T(128)}, u32[]{:S(2)}) copy-start(f32[3]{0:T(128)} %constant.49.clone) | copy-start | bytes 40
  28.4 19.6 %copy-start.1 = (f32[3,1,1,2,128]{4,3,2,1,0:T(2,128)S(1)}, f32[3,1,1,2,128]{4,3,2,1,0:T(2,128)}, u32[]{:S(2)}) copy-start(f32[3,1,1,2,128]{4,3,2,1,0:T(2,128)} %param.5) | copy-start | bytes 9220
  62.0 9.8 %all-to-all-start.3 = ((f32[32,1,1,1,2,128]{5,4,3,2,1,0:T(2,128)}), f32[32,1,1,1,2,128]{5,4,3,2,1,0:T(2,128)S(1)}, u32[]{:S(2)}, u32[]{:S(2)}) async-start(f32[32,1,1,1,2,128]{5,4,3,2,1,0:T(2,128)} %broadcast_in_dim.61), calls=%async_computation.3 | async-start | bytes 65536 | tf_op jit(solution)/shard_map/all_to_all | solution.py:47
  76.7 9.8 %all-to-all-start.4 = ((f32[32,1,1,1,2,128]{5,4,3,2,1,0:T(2,128)}), f32[32,1,1,1,2,128]{5,4,3,2,1,0:T(2,128)S(1)}, u32[]{:S(2)}, u32[]{:S(2)}) async-start(f32[32,1,1,1,2,128]{5,4,3,2,1,0:T(2,128)} %broadcast_in_dim.65), calls=%async_computation.4 | async-start | bytes 65536 | tf_op jit(solution)/shard_map/all_to_all | solution.py:47
  102.8 0.7 copy-start.3

commit v6 on v5

--- a/solution.py
+++ b/solution.py
@@ -165,8 +165,8 @@
     own_v = flat(velocity)
     tiles = own_x.shape[1]
 
-    offset = own_x[:, :, :, None] - near_x[:, :, None, :]
-    distance = offset[0] * offset[0] + offset[1] * offset[1] + offset[2] * offset[2]
+    gaps = [own_x[k][:, :, None] - near_x[k][:, None, :] for k in range(3)]
+    distance = gaps[0] * gaps[0] + gaps[1] * gaps[1] + gaps[2] * gaps[2]
     closeness = jnp.maximum(1.0 - distance, 0.0)
     weight = (
         closeness * closeness * own_valid[:, :, None] * near_valid[:, None, :]

time: 104 us -> 99.6 us (0.958)
  other arithmetic: 33.7 us -> 26.9 us
  local copies, waits for them, and re-layouts: 3.31 us -> 6.19 us
    mul x1 -> x0, other arithmetic: 2.87 us -> none  [wsum(): return jnp.sum(weight[None] * near[:, :, None, :], axis=-1)]
    sub x1 -> x0, other arithmetic: 2.43 us -> none  [on_device(): offset = own_x[:, :, :, None] - near_x[:, :, None, :]]
    reduce_sum x5, other arithmetic: 21.1 us -> 18.9 us  [wsum(): return jnp.sum(weight[None] * near[:, :, None, :], axis=-1)]
    unnamed x10, local copies, waits for them, and re-layouts: 0.03 us -> 2.15 us
  transfers between devices with their start and end apart: 3 -> 3, of which waited for: 3 -> 3; matrix products, arithmetic and copies ran while one was open for 1% -> 2% of each run, Pallas kernels for 0% -> 0%
where the time goes in v6:
time: 99.6 us; the launch traced here: 98.8 us
  blocking collectives  29.6 us (30%)
  other arithmetic  26.9 us (27%)
  waiting for transfers between devices  22.5 us (23%)
  starting transfers between devices  12.6 us (13%)
  local copies, waits for them, and re-layouts  6.19 us (6%)
  between operations  1.02 us (1%)
    all_to_all x3, waiting for transfers between devices, gather_rim(): got = lax.all_to_all(rows, ('gx', 'gy', 'gz'), 0, 0, tiled=True)  22.5 us
    all_to_all x2, blocking collectives, gather_rim(): got = lax.all_to_all(rows, ('gx', 'gy', 'gz'), 0, 0, tiled=True)  19 us
    reduce_sum x5, other arithmetic, wsum(): return jnp.sum(weight[None] * near[:, :, None, :], axis=-1)  18.9 us
    all_to_all x3, starting transfers between devices, gather_rim(): got = lax.all_to_all(rows, ('gx', 'gy', 'gz'), 0, 0, tiled=True)  12.6 us
    all_to_all x1, blocking collectives, total(): got = lax.all_to_all(rows, ('gx', 'gy', 'gz'), 0, 0, tiled=True)  10.6 us
    reduce_sum x1, other arithmetic, on_device(): row = jnp.sum(weight, axis=-1)[None]  3.34 us
    unnamed x10, local copies, waits for them, and re-layouts  2.15 us
    broadcast_in_dim x5, local copies, waits for them, and re-layouts, gather_rim(): rows = jnp.broadcast_to(cells[None], (devices,) + cells.shape)  2 us
  transfers between devices with their start and end apart: 3, of which 3 were waited for; matrix products, arithmetic and copies ran while one was open for 2% of the time, Pallas kernels for 0%

profile of v6, /device:TPU:0, one launch (start us, length us, event | category | flops | bytes accessed | tf_op | source)
XLA Modules:
  0.0 98.8 jit_solution(3490601490097431222)
XLA Ops:
  0.6 0.7 compare_convert_fusion
  1.4 0.7 maximum_bitcast_fusion
  2.1 0.7 broadcast_in_dim.47
  2.8 7.3 %all-to-all-start = ((f32[32,7,1,1,2,128]{5,4,1,3,2,0:T(2,128)}), f32[32,7,1,1,2,128]{5,4,1,3,2,0:T(2,128)S(1)}, u32[]{:S(2)}, u32[]{:S(2)}) async-start(f32[32,7,1,1,2,128]{5,4,1,3,2,0:T(2,128)} %broadcast_in_dim.47), calls=%async_computation | async-start | bytes 458752 | tf_op jit(solution)/shard_map/all_to_all | solution.py:47
  10.2 0.1 copy.25
  10.3 0.7 compare_convert_fusion.1
  11.0 0.7 slice_bitcast_fusion.2
  11.7 8.2 %all-to-all-done = f32[32,7,1,1,2,128]{5,4,1,3,2,0:T(2,128)S(1)} async-done(((f32[32,7,1,1,2,128]{5,4,1,3,2,0:T(2,128)}), f32[32,7,1,1,2,128]{5,4,1,3,2,0:T(2,128)S(1)}, u32[]{:S(2)}, u32[]{:S(2)}) %all-to-all-start) | async-done | bytes 229408 | tf_op jit(solution)/shard_map/all_to_all | solution.py:47
  20.3 0.1 broadcast_subtract_fusion
  20.4 0.1 pad_maximum_fusion
  20.6 3.3 %fusion.22 = (f32[2,128]{1,0:T(2,128)S(1)}, f32[2,128,4608]{2,1,0:T(8,128)S(1)}) fusion(f32[2,4608]{1,0:T(2,128)} %constant.48.clone, f32[4608]{0:T(1024)S(1)} %mul.413, f32[2,128]{1,0:T(2,128)S(1)} %compare_convert_fusion.1, f32[4608]{0:T(1024)S(1)} %sub.213, f32[2,128]{1,0:T(2,128)S(1)} %get-tuple-element.26, f32[4608]{0:T(1024)S(1)} %sub.208, ...), kind=kLoop, calls=%fused_computation.109 | loop fusion | flops 17694464 | bytes 4834304 | tf_op jit(solution)/shard_map/reduce_sum | solution.py:182
  23.9 2.1 %copy-done = f32[2,128,4608]{2,1,0:T(8,128)} copy-done((f32[2,128,4608]{2,1,0:T(8,128)}, f32[2,128,4608]{2,1,0:T(8,128)S(1)}, u32[]{:S(2)}) %copy-start) | copy-done | bytes 4718616
  26.1 2.6 %multiply_reduce_fusion = f32[6,2,128]{2,1,0:T(2,128)S(1)} fusion(f32[6,2,4608]{2,1,0:T(2,128)S(1)} %pad_maximum_fusion, f32[2,128,4608]{2,1,0:T(8,128)S(1)} %get-tuple-element.21), kind=kLoop, calls=%fused_computation | loop fusion | flops 14154240 | bytes 4945920 | tf_op jit(solution)/shard_map/reduce_sum | solution.py:100
  28.8 10.1 %all_to_all.30 = f32[32,3,1,1,2,128]{5,4,1,3,2,0:T(2,128)S(1)} all-to-all(f32[32,3,1,1,2,128]{5,4,1,3,2,0:T(2,128)S(1)} %broadcast_in_dim.51), channel_id=1, replica_groups=mesh['gx'=4,'gy'=2,'gz'=4] {'gx','gy','gz'}, dimensions={0} | all-to-all | bytes 196608 | tf_op jit(solution)/shard_map/all_to_all | solution.py:47
  39.1 0.1 fusion
  39.3 4.1 %multiply_reduce_fusion.4 = f32[4,2,128]{2,1,0:T(2,128)S(1)} fusion(f32[4,2,4608]{2,1,0:T(2,128)S(1)} %pad_maximum_fusion.1, f32[2,128,4608]{2,1,0:T(8,128)} %copy-done), kind=kLoop, calls=%fused_computation.4 | loop fusion | flops 9436160 | bytes 4870144 | tf_op jit(solution)/shard_map/reduce_sum | solution.py:100
  43.4 0.1 multiply_reduce_fusion.6
  43.5 8.9 %all_to_all.31 = f32[32,1,1,1,2,128]{5,4,3,2,1,0:T(2,128)S(1)} all-to-all(f32[32,1,1,1,2,128]{5,4,3,2,1,0:T(2,128)S(1)} %broadcast_in_dim.57), channel_id=1, replica_groups=mesh['gx'=4,'gy'=2,'gz'=4] {'gx','gy','gz'}, dimensions={0} | all-to-all | bytes 65536 | tf_op jit(solution)/shard_map/all_to_all | solution.py:47
  52.5 0.1 subtract_multiply_fusion.2
  52.7 4.1 %multiply_reduce_fusion.3 = f32[4,2,128]{2,1,0:T(2,128)S(1)} fusion(f32[4,2,4608]{2,1,0:T(2,128)S(1)} %pad_maximum_fusion.2, f32[2,128,4608]{2,1,0:T(8,128)} %copy-done), kind=kLoop, calls=%fused_computation.3 | loop fusion | flops 9436160 | bytes 4870144 | tf_op jit(solution)/shard_map/reduce_sum | solution.py:100
  56.8 0.6 broadcast_in_dim.61
  57.4 2.7 %all-to-all-start.3 = ((f32[32,1,1,1,2,128]{5,4,3,2,1,0:T(2,128)}), f32[32,1,1,1,2,128]{5,4,3,2,1,0:T(2,128)S(1)}, u32[]{:S(2)}, u32[]{:S(2)}) async-start(f32[32,1,1,1,2,128]{5,4,3,2,1,0:T(2,128)} %broadcast_in_dim.61), calls=%async_computation.3 | async-start | bytes 65536 | tf_op jit(solution)/shard_map/all_to_all | solution.py:47
  60.1 7.1 %all-to-all-done.3 = f32[32,1,1,1,2,128]{5,4,3,2,1,0:T(2,128)S(1)} async-done(((f32[32,1,1,1,2,128]{5,4,3,2,1,0:T(2,128)}), f32[32,1,1,1,2,128]{5,4,3,2,1,0:T(2,128)S(1)}, u32[]{:S(2)}, u32[]{:S(2)}) %all-to-all-start.3) | async-done | bytes 32800 | tf_op jit(solution)/shard_map/all_to_all | solution.py:47
  67.2 0.1 subtract_multiply_fusion.1
  67.4 4.1 %multiply_reduce_fusion.2 = f32[4,2,128]{2,1,0:T(2,128)S(1)} fusion(f32[4,2,4608]{2,1,0:T(2,128)S(1)} %pad_maximum_fusion.3, f32[2,128,4608]{2,1,0:T(8,128)} %copy-done), kind=kLoop, calls=%fused_computation.2 | loop fusion | flops 9436160 | bytes 4870144 | tf_op jit(solution)/shard_map/reduce_sum | solution.py:100
  71.5 0.6 broadcast_in_dim.130
  72.1 2.5 %all-to-all-start.4 = ((f32[32,1,1,1,2,128]{5,4,3,2,1,0:T(2,128)}), f32[32,1,1,1,2,128]{5,4,3,2,1,0:T(2,128)S(1)}, u32[]{:S(2)}, u32[]{:S(2)}) async-start(f32[32,1,1,1,2,128]{5,4,3,2,1,0:T(2,128)} %broadcast_in_dim.130), calls=%async_computation.4 | async-start | bytes 65536 | tf_op jit(solution)/shard_map/all_to_all | solution.py:47
  74.7 7.2 %all-to-all-done.4 = f32[32,1,1,1,2,128]{5,4,3,2,1,0:T(2,128)S(1)} async-done(((f32[32,1,1,1,2,128]{5,4,3,2,1,0:T(2,128)}), f32[32,1,1,1,2,128]{5,4,3,2,1,0:T(2,128)S(1)}, u32[]{:S(2)}, u32[]{:S(2)}) %all-to-all-start.4) | async-done | bytes 32800 | tf_op jit(solution)/shard_map/all_to_all | solution.py:47
  82.0 0.1 subtract_multiply_fusion
  82.2 4.1 %multiply_reduce_fusion.1 = f32[4,2,128]{2,1,0:T(2,128)S(1)} fusion(f32[4,2,4608]{2,1,0:T(2,128)S(1)} %pad_maximum_fusion.4, f32[2,128,4608]{2,1,0:T(8,128)} %copy-done), kind=kLoop, calls=%fused_computation.1 | loop fusion | flops 9436160 | bytes 4870144 | tf_op jit(solution)/shard_map/reduce_sum | solution.py:100
  86.3 10.6 %all_to_all.32 = f32[32,3,4,128]{3,2,1,0:T(4,128)S(1)} all-to-all(f32[32,3,4,128]{3,2,1,0:T(4,128)S(1)} %broadcast_in_dim.133), channel_id=1, replica_groups=mesh['gx'=4,'gy'=2,'gz'=4] {'gx','gy','gz'}, dimensions={0} | all-to-all | bytes 393216 | tf_op jit(solution)/shard_map/all_to_all | solution.py:67
  98.2 0.7 subtract_bitcast_fusion
  (70 shorter events, 2.5 us)
Async XLA Ops:
  2.8 17.1 %all-to-all-start = ((f32[32,7,1,1,2,128]{5,4,1,3,2,0:T(2,128)}), f32[32,7,1,1,2,128]{5,4,1,3,2,0:T(2,128)S(1)}, u32[]{:S(2)}, u32[]{:S(2)}) async-start(f32[32,7,1,1,2,128]{5,4,1,3,2,0:T(2,128)} %broadcast_in_dim.47), calls=%async_computation | async-start | bytes 458752 | tf_op jit(solution)/shard_map/all_to_all | solution.py:47
  20.6 8.1 %copy-start.2 = (f32[3,1,1,2,128]{4,3,2,1,0:T(2,128)S(1)}, f32[3,1,1,2,128]{4,3,2,1,0:T(2,128)}, u32[]{:S(2)}) copy-start(f32[3,1,1,2,128]{4,3,2,1,0:T(2,128)} %param.6) | copy-start | bytes 9220
  20.6 8.1 %copy-start.4 = (f32[3]{0:T(128)S(1)}, f32[3]{0:T(128)}, u32[]{:S(2)}) copy-start(f32[3]{0:T(128)} %constant.49.clone) | copy-start | bytes 40
  23.9 2.1 %copy-start = (f32[2,128,4608]{2,1,0:T(8,128)}, f32[2,128,4608]{2,1,0:T(8,128)S(1)}, u32[]{:S(2)}) copy-start(f32[2,128,4608]{2,1,0:T(8,128)S(1)} %get-tuple-element.21) | copy-start | bytes 14155780
  26.1 17.3 %copy-start.1 = (f32[3,1,1,2,128]{4,3,2,1,0:T(2,128)S(1)}, f32[3,1,1,2,128]{4,3,2,1,0:T(2,128)}, u32[]{:S(2)}) copy-start(f32[3,1,1,2,128]{4,3,2,1,0:T(2,128)} %param.5) | copy-start | bytes 9220
  57.4 9.8 %all-to-all-start.3 = ((f32[32,1,1,1,2,128]{5,4,3,2,1,0:T(2,128)}), f32[32,1,1,1,2,128]{5,4,3,2,1,0:T(2,128)S(1)}, u32[]{:S(2)}, u32[]{:S(2)}) async-start(f32[32,1,1,1,2,128]{5,4,3,2,1,0:T(2,128)} %broadcast_in_dim.61), calls=%async_computation.3 | async-start | bytes 65536 | tf_op jit(solution)/shard_map/all_to_all | solution.py:47
  72.1 9.8 %all-to-all-start.4 = ((f32[32,1,1,1,2,128]{5,4,3,2,1,0:T(2,128)}), f32[32,1,1,1,2,128]{5,4,3,2,1,0:T(2,128)S(1)}, u32[]{:S(2)}, u32[]{:S(2)}) async-start(f32[32,1,1,1,2,128]{5,4,3,2,1,0:T(2,128)} %broadcast_in_dim.130), calls=%async_computation.4 | async-start | bytes 65536 | tf_op jit(solution)/shard_map/all_to_all | solution.py:47
  98.2 0.7 copy-start.3

commit v7 on v6

--- a/solution.py
+++ b/solution.py
@@ -1,5 +1,4 @@
 import jax
-import numpy as np
 import jax.numpy as jnp
 from jax import lax
 from jax.sharding import PartitionSpec as P
@@ -46,18 +45,18 @@
     rows = jnp.broadcast_to(cells[None], (devices,) + cells.shape)
     got = lax.all_to_all(rows, ("gx", "gy", "gz"), 0, 0, tiled=True)
     grid = got.reshape(counts[0], counts[1], counts[2], comps, size_x, size_y, size_z, width)
-    grid = grid.transpose(3, 0, 4, 1, 5, 2, 6, 7).reshape(
-        comps, counts[0] * size_x, counts[1] * size_y, counts[2] * size_z, width
+    grid = grid.transpose(3, 2, 6, 0, 4, 1, 5, 7).reshape(
+        comps, counts[2] * size_z, counts[0] * size_x, counts[1] * size_y, width
     )
     padded = jnp.pad(grid, ((0, 0), (1, 1), (1, 1), (1, 1), (0, 0)))
     start = (
         0,
+        lax.axis_index("gz") * size_z,
         lax.axis_index("gx") * size_x,
         lax.axis_index("gy") * size_y,
-        lax.axis_index("gz") * size_z,
         0,
     )
-    return lax.dynamic_slice(padded, start, (comps, size_x + 2, size_y + 2, size_z + 2, width))
+    return lax.dynamic_slice(padded, start, (comps, size_z + 2, size_x + 2, size_y + 2, width))
 
 
 def total(values):
@@ -82,12 +81,12 @@
 
 
 def neighbours(rim):
-    comps, size_x, size_y, size_z, width = rim.shape
+    comps, size_z, size_x, size_y, width = rim.shape
     blocks = []
     for ax in range(size_x - 2):
         for ay in range(size_y - 2):
             for az in range(size_z - 2):
-                window = rim[:, ax:ax + 3, ay:ay + 3, az:az + 3, :]
+                window = rim[:, az:az + 3, ax:ax + 3, ay:ay + 3, :]
                 blocks.append(window.reshape(comps, 27 * width))
     return jnp.stack(blocks, axis=1)
 
@@ -113,18 +112,6 @@
             for az in range(size_z):
                 corners.append(jnp.stack([base[0] + ax, base[1] + ay, base[2] + az]))
     return jnp.stack(corners, axis=1).astype(jnp.float32)
-
-
-def adjacency(block_shape):
-    _, size_x, size_y, size_z, width = block_shape
-    rows = []
-    for ax in range(size_x):
-        for ay in range(size_y):
-            for az in range(size_z):
-                near = np.zeros((size_x + 2, size_y + 2, size_z + 2), np.float32)
-                near[ax:ax + 3, ay:ay + 3, az:az + 3] = 1.0
-                rows.append(np.repeat(near.reshape(-1), width))
-    return np.stack(rows)
 
 
 def solve3(matrix, rhs):
@@ -153,8 +140,7 @@
     packed = jnp.concatenate([positions, valid_mask, velocity], axis=0)
 
     def rim_flat(cells):
-        rim = gather_rim(cells)
-        return rim.reshape(rim.shape[0], 1, -1)
+        return neighbours(gather_rim(cells))
 
     near_all = rim_flat(packed)
     near_x = near_all[0:3]
@@ -163,24 +149,18 @@
     own_x = flat(positions)
     own_valid = flat(valid_mask)[0]
     own_v = flat(velocity)
-    tiles = own_x.shape[1]
 
     gaps = [own_x[k][:, :, None] - near_x[k][:, None, :] for k in range(3)]
     distance = gaps[0] * gaps[0] + gaps[1] * gaps[1] + gaps[2] * gaps[2]
     closeness = jnp.maximum(1.0 - distance, 0.0)
-    weight = (
-        closeness * closeness * own_valid[:, :, None] * near_valid[:, None, :]
-    ) * jnp.asarray(adjacency(block_shape))[:, None, :]
+    weight = closeness * closeness * own_valid[:, :, None] * near_valid[:, None, :]
 
     corner = tile_corners(block_shape)[:, :, None]
     local_own = own_x - corner
     local_near = near_x - corner
 
-    def spread_t(near_field):
-        return jnp.broadcast_to(near_field, (near_field.shape[0], tiles, near_field.shape[2]))
-
     row = jnp.sum(weight, axis=-1)[None]
-    sums = wsum(weight, jnp.concatenate([spread_t(near_v), local_near], axis=0))
+    sums = wsum(weight, jnp.concatenate([near_v, local_near], axis=0))
     near_sums = sums[0:3]
     lever = local_own * row - sums[3:6]
 
@@ -195,7 +175,7 @@
 
     near_pred = rim_flat(shaped(predicted))
     dotted = jnp.sum(near_pred * local_near, axis=0, keepdims=True)
-    psums = wsum(weight, jnp.concatenate([spread_t(near_pred), dotted], axis=0))
+    psums = wsum(weight, jnp.concatenate([near_pred, dotted], axis=0))
     flux = jnp.sum(local_own * psums[0:3], axis=0, keepdims=True) - psums[3:4]
     source = -(GRADIENT_GAIN / width) * (
         jnp.sum(predicted * lever, axis=0, keepdims=True) - flux
@@ -206,7 +186,7 @@
     near_wx = []
     for _ in range(ITERS):
         near_u = rim_flat(shaped(basis[-1]))
-        out = wsum(weight, jnp.concatenate([spread_t(near_u), near_u * local_near], axis=0))
+        out = wsum(weight, jnp.concatenate([near_u, near_u * local_near], axis=0))
         near_w.append(out[0:1])
         near_wx.append(out[1:4])
         basis.append(-(out[0:1] / width) / diagonal)

time: 99.6 us -> 129 us (1.30); the launches traced: 98.8 us -> 127 us
  local copies, waits for them, and re-layouts: 6.19 us -> 34.5 us
  blocking collectives: 29.6 us -> 19.5 us
  waiting for transfers between devices: 22.5 us -> 27.4 us
  starting transfers between devices: 12.6 us -> 17.1 us
    reduce_sum x5, other arithmetic: 18.9 us -> 6.9 us  [wsum(): return jnp.sum(weight[None] * near[:, :, None, :], axis=-1)]
    another operation x0 -> x9, local copies, waits for them, and re-layouts: none -> 10.6 us  [neighbours(): return jnp.stack(blocks, axis=1)]
    slice x2 -> x15, local copies, waits for them, and re-layouts: 0.11 us -> 10.6 us  [neighbours(): window = rim[:, az:az + 3, ax:ax + 3, ay:ay + 3, :]]
    all_to_all x2 -> x1, blocking collectives: 19 us -> 8.95 us  [gather_rim(): got = lax.all_to_all(rows, ('gx', 'gy', 'gz'), 0, 0, tiled=True)]
    all_to_all x3 -> x4, waiting for transfers between devices: 22.5 us -> 27.4 us  [gather_rim(): got = lax.all_to_all(rows, ('gx', 'gy', 'gz'), 0, 0, tiled=True)]
    all_to_all x3 -> x4, starting transfers between devices: 12.6 us -> 17.1 us  [gather_rim(): got = lax.all_to_all(rows, ('gx', 'gy', 'gz'), 0, 0, tiled=True)]
    concatenate x5, other arithmetic: 0.37 us -> 3.3 us  [the longest x3 2.3 us: on_device(): out = wsum(weight, jnp.concatenate([near_u, near_u * local_near], axis=0))]
    unnamed x10 -> x60, local copies, waits for them, and re-layouts: 2.15 us -> 4.87 us
  transfers between devices with their start and end apart: 3 -> 4, of which waited for: 3 -> 4; matrix products, arithmetic and copies ran while one was open for 2% -> 4% of each run, Pallas kernels for 0% -> 0%
where the time goes in v7:
time: 129 us; the launch traced here: 127 us
  local copies, waits for them, and re-layouts  34.5 us (27%)
  waiting for transfers between devices  27.4 us (21%)
  other arithmetic  27.2 us (21%)
  blocking collectives  19.5 us (15%)
  starting transfers between devices  17.1 us (13%)
    all_to_all x4, waiting for transfers between devices, gather_rim(): got = lax.all_to_all(rows, ('gx', 'gy', 'gz'), 0, 0, tiled=True)  27.4 us
    all_to_all x4, starting transfers between devices, gather_rim(): got = lax.all_to_all(rows, ('gx', 'gy', 'gz'), 0, 0, tiled=True)  17.1 us
    slice x15, local copies, waits for them, and re-layouts, neighbours(): window = rim[:, az:az + 3, ax:ax + 3, ay:ay + 3, :]  10.6 us
    another operation x9, local copies, waits for them, and re-layouts, neighbours(): return jnp.stack(blocks, axis=1)  10.6 us
    all_to_all x1, blocking collectives, total(): got = lax.all_to_all(rows, ('gx', 'gy', 'gz'), 0, 0, tiled=True)  10.6 us
    all_to_all x1, blocking collectives, gather_rim(): got = lax.all_to_all(rows, ('gx', 'gy', 'gz'), 0, 0, tiled=True)  8.95 us
    reduce_sum x5, other arithmetic, wsum(): return jnp.sum(weight[None] * near[:, :, None, :], axis=-1)  6.9 us
    unnamed x60, local copies, waits for them, and re-layouts  4.87 us
  transfers between devices with their start and end apart: 4, of which 4 were waited for; matrix products, arithmetic and copies ran while one was open for 4% of the time, Pallas kernels for 0%

profile of v7, /device:TPU:0, one launch (start us, length us, event | category | flops | bytes accessed | tf_op | source)
XLA Modules:
  0.0 126.9 jit_solution(7970955733391573920)
XLA Ops:
  2.8 7.3 %all-to-all-start = ((f32[32,7,1,1,2,128]{5,4,1,3,2,0:T(2,128)}), f32[32,7,1,1,2,128]{5,4,1,3,2,0:T(2,128)S(1)}, u32[]{:S(2)}, u32[]{:S(2)}) async-start(f32[32,7,1,1,2,128]{5,4,1,3,2,0:T(2,128)} %broadcast_in_dim.27), calls=%async_computation | async-start | bytes 458752 | tf_op jit(solution)/shard_map/all_to_all | solution.py:46
  10.9 1.3 %slice_bitcast_fusion.2 = (f32[2,128]{1,0:T(2,128)S(1)}, f32[2,128]{1,0:T(2,128)S(1)}, f32[2,128]{1,0:T(2,128)}) fusion(f32[3,1,1,2,128]{4,3,2,1,0:T(2,128)} %param.4), kind=kLoop, calls=%fused_computation.92 | loop fusion | bytes 6144 | tf_op jit(solution)/shard_map/sub | solution.py:153
  12.2 7.7 %all-to-all-done = f32[32,7,1,1,2,128]{5,4,1,3,2,0:T(2,128)S(1)} async-done(((f32[32,7,1,1,2,128]{5,4,1,3,2,0:T(2,128)}), f32[32,7,1,1,2,128]{5,4,1,3,2,0:T(2,128)S(1)}, u32[]{:S(2)}, u32[]{:S(2)}) %all-to-all-start) | async-done | bytes 229408 | tf_op jit(solution)/shard_map/all_to_all | solution.py:46
  21.1 1.9 %fusion.23 = (f32[2,128]{1,0:T(2,128)S(1)}, f32[2,128,3456]{2,1,0:T(8,128)S(1)}) fusion(f32[2,3456]{1,0:T(2,128)S(1)} %get-tuple-element.41, f32[2,128]{1,0:T(2,128)S(1)} %compare_convert_fusion.1, f32[2,3456]{1,0:T(2,128)S(1)} %get-tuple-element.42, f32[2,128]{1,0:T(2,128)S(1)} %copy-done.25, f32[2,3456]{1,0:T(2,128)S(1)} %get-tuple-element.43, ...), kind=kLoop, calls=%fused_computation.128 | loop fusion | flops 12386048 | bytes 3654656 | tf_op jit(solution)/shard_map/reduce_sum | solution.py:162
  23.0 1.9 %multiply_reduce_fusion = f32[6,2,128]{2,1,0:T(2,128)S(1)} fusion(f32[6,2,3456]{2,1,0:T(2,128)S(1)} %copy.117, f32[2,128,3456]{2,1,0:T(8,128)S(1)} %get-tuple-element.23), kind=kLoop, calls=%fused_computation | loop fusion | flops 10615296 | bytes 3710976 | tf_op jit(solution)/shard_map/reduce_sum | solution.py:99
  26.2 3.3 %all-to-all-start.1 = ((f32[32,3,1,1,2,128]{5,4,1,3,2,0:T(2,128)}), f32[32,3,1,1,2,128]{5,4,1,3,2,0:T(2,128)}, u32[]{:S(2)}, u32[]{:S(2)}) async-start(f32[32,3,1,1,2,128]{5,4,1,3,2,0:T(2,128)} %broadcast_in_dim.29), calls=%async_computation.1 | async-start | bytes 196608 | tf_op jit(solution)/shard_map/all_to_all | solution.py:46
  30.2 7.1 %all-to-all-done.1 = f32[32,3,1,1,2,128]{5,4,1,3,2,0:T(2,128)} async-done(((f32[32,3,1,1,2,128]{5,4,1,3,2,0:T(2,128)}), f32[32,3,1,1,2,128]{5,4,1,3,2,0:T(2,128)}, u32[]{:S(2)}, u32[]{:S(2)}) %all-to-all-start.1) | async-done | bytes 98336 | tf_op jit(solution)/shard_map/all_to_all | solution.py:46
  39.6 1.5 %stack_reshape.32 = f32[3,1,3456]{2,0,1:T(4,128)} reshape(f32[3,3,3,3,128]{4,3,2,1,0:T(4,128)} %copy.121) | data formatting | bytes 82944 | tf_op jit(solution)/shard_map/stack;reshape | solution.py:91
  41.0 1.4 %constant_dynamic-update-slice_fusion.1 = f32[3,2,3456]{2,0,1:T(4,128)} fusion(f32[3,1,3456]{2,0,1:T(4,128)} %stack_reshape.32), kind=kLoop, calls=%fused_computation.48 | loop fusion | bytes 96768
  42.5 1.4 %copy.122 = f32[3,3,3,3,128]{4,3,2,1,0:T(4,128)} copy(f32[3,3,3,3,128]{4,1,3,2,0:T(4,128)} %get-tuple-element.24) | data formatting | bytes 82944 | tf_op jit(solution)/shard_map/slice | solution.py:89
  43.9 1.5 %stack_reshape.33 = f32[3,1,3456]{2,0,1:T(4,128)} reshape(f32[3,3,3,3,128]{4,3,2,1,0:T(4,128)} %copy.122) | data formatting | bytes 82944 | tf_op jit(solution)/shard_map/stack;reshape | solution.py:91
  45.4 1.4 %constant_dynamic-update-slice_fusion = f32[3,2,3456]{2,0,1:T(4,128)} fusion(f32[3,2,3456]{2,0,1:T(4,128)} %constant_dynamic-update-slice_fusion.1, f32[3,1,3456]{2,0,1:T(4,128)} %stack_reshape.33), kind=kLoop, calls=%fused_computation.47 | loop fusion | bytes 110592 | tf_op jit(solution)/shard_map/stack | solution.py:91
  46.8 1.0 multiply_reduce_fusion.5
  47.9 1.0 pad_maximum_fusion.2
  48.9 1.3 multiply_reduce_fusion.4
  50.9 8.9 %all_to_all.30 = f32[32,1,1,1,2,128]{5,4,3,2,1,0:T(2,128)S(1)} all-to-all(f32[32,1,1,1,2,128]{5,4,3,2,1,0:T(2,128)S(1)} %broadcast_in_dim.33), channel_id=1, replica_groups=mesh['gx'=4,'gy'=2,'gz'=4] {'gx','gy','gz'}, dimensions={0} | all-to-all | bytes 65536 | tf_op jit(solution)/shard_map/all_to_all | solution.py:46
  61.9 1.3 %copy.126 = f32[1,3,3,3,128]{4,3,2,1,0:T(4,128)} copy(f32[1,3,3,3,128]{4,1,3,2,0:T(4,128)} %get-tuple-element.30) | data formatting | bytes 27648 | tf_op jit(solution)/shard_map/slice | solution.py:89
  63.2 1.3 %stack_reshape.34 = f32[1,1,3456]{2,1,0:T(1,128)} reshape(f32[1,3,3,3,128]{4,3,2,1,0:T(4,128)} %copy.126) | data formatting | bytes 27648 | tf_op jit(solution)/shard_map/stack;reshape | solution.py:91
  67.1 1.3 multiply_reduce_fusion.3
  70.1 3.3 %all-to-all-start.3 = ((f32[32,1,1,1,2,128]{5,4,3,2,1,0:T(2,128)}), f32[32,1,1,1,2,128]{5,4,3,2,1,0:T(2,128)}, u32[]{:S(2)}, u32[]{:S(2)}) async-start(f32[32,1,1,1,2,128]{5,4,3,2,1,0:T(2,128)} %broadcast_in_dim.35), calls=%async_computation.3 | async-start | bytes 65536 | tf_op jit(solution)/shard_map/all_to_all | solution.py:46
  74.0 6.7 %all-to-all-done.3 = f32[32,1,1,1,2,128]{5,4,3,2,1,0:T(2,128)} async-done(((f32[32,1,1,1,2,128]{5,4,3,2,1,0:T(2,128)}), f32[32,1,1,1,2,128]{5,4,3,2,1,0:T(2,128)}, u32[]{:S(2)}, u32[]{:S(2)}) %all-to-all-start.3) | async-done | bytes 32800 | tf_op jit(solution)/shard_map/all_to_all | solution.py:46
  83.4 1.3 %copy.133 = f32[1,3,3,3,128]{4,3,2,1,0:T(4,128)} copy(f32[1,3,3,3,128]{4,1,3,2,0:T(4,128)} %get-tuple-element.28) | data formatting | bytes 27648 | tf_op jit(solution)/shard_map/slice | solution.py:89
  84.7 1.3 %stack_reshape.36 = f32[1,1,3456]{2,1,0:T(1,128)} reshape(f32[1,3,3,3,128]{4,3,2,1,0:T(4,128)} %copy.133) | data formatting | bytes 27648 | tf_op jit(solution)/shard_map/stack;reshape | solution.py:91
  88.6 1.3 multiply_reduce_fusion.2
  91.8 3.3 %all-to-all-start.4 = ((f32[32,1,1,1,2,128]{5,4,3,2,1,0:T(2,128)}), f32[32,1,1,1,2,128]{5,4,3,2,1,0:T(2,128)}, u32[]{:S(2)}, u32[]{:S(2)}) async-start(f32[32,1,1,1,2,128]{5,4,3,2,1,0:T(2,128)} %broadcast_in_dim.37), calls=%async_computation.4 | async-start | bytes 65536 | tf_op jit(solution)/shard_map/all_to_all | solution.py:46
  95.1 1.2 maximum_multiply_fusion
  96.3 6.0 %all-to-all-done.4 = f32[32,1,1,1,2,128]{5,4,3,2,1,0:T(2,128)} async-done(((f32[32,1,1,1,2,128]{5,4,3,2,1,0:T(2,128)}), f32[32,1,1,1,2,128]{5,4,3,2,1,0:T(2,128)}, u32[]{:S(2)}, u32[]{:S(2)}) %all-to-all-start.4) | async-done | bytes 32800 | tf_op jit(solution)/shard_map/all_to_all | solution.py:46
  105.1 1.3 %copy.140 = f32[1,3,3,3,128]{4,3,2,1,0:T(4,128)} copy(f32[1,3,3,3,128]{4,1,3,2,0:T(4,128)} %get-tuple-element.26) | data formatting | bytes 27648 | tf_op jit(solution)/shard_map/slice | solution.py:89
  106.4 1.3 %stack_reshape.38 = f32[1,1,3456]{2,1,0:T(1,128)} reshape(f32[1,3,3,3,128]{4,3,2,1,0:T(4,128)} %copy.140) | data formatting | bytes 27648 | tf_op jit(solution)/shard_map/stack;reshape | solution.py:91
  110.3 1.3 multiply_reduce_fusion.1
  113.0 10.6 %all_to_all.31 = f32[32,3,4,128]{3,2,1,0:T(4,128)S(1)} all-to-all(f32[32,3,4,128]{3,2,1,0:T(4,128)S(1)} %broadcast_in_dim.38), channel_id=1, replica_groups=mesh['gx'=4,'gy'=2,'gz'=4] {'gx','gy','gz'}, dimensions={0} | all-to-all | bytes 393216 | tf_op jit(solution)/shard_map/all_to_all | solution.py:66
  125.6 1.4 %subtract_bitcast_fusion = f32[3,1,1,2,128]{4,3,2,1,0:T(2,128)} fusion(f32[3,2,128]{2,1,0:T(2,128)S(1)} %copy-done.5, f32[4,2,128]{2,1,0:T(2,128)} %copy-done.18, f32[4,2,128]{2,1,0:T(2,128)} %copy-done.17, f32[4,2,128]{2,1,0:T(2,128)} %copy-done.16, f32[3,1,1,2,128]{4,3,2,1,0:T(2,128)S(1)} %copy-done.7, f32[128]{0:T(128)S(1)} %get-tuple-element.13, ...), kind=kLoop, calls=%fused_computation.74 | loop fusion | flops 10752 | bytes 26136
  (142 shorter events, 31.8 us)
Async XLA Ops:
  2.8 17.1 %all-to-all-start = ((f32[32,7,1,1,2,128]{5,4,1,3,2,0:T(2,128)}), f32[32,7,1,1,2,128]{5,4,1,3,2,0:T(2,128)S(1)}, u32[]{:S(2)}, u32[]{:S(2)}) async-start(f32[32,7,1,1,2,128]{5,4,1,3,2,0:T(2,128)} %broadcast_in_dim.27), calls=%async_computation | async-start | bytes 458752 | tf_op jit(solution)/shard_map/all_to_all | solution.py:46
  10.2 10.5 %copy-start.22 = (f32[3,2]{0,1:T(2,128)}, f32[3,2]{0,1:T(2,128)S(1)}, u32[]{:S(2)}) copy-start(f32[3,2]{0,1:T(2,128)S(1)} %add_convert_fusion) | copy-start | bytes 76
  19.9 1.2 copy-start.25
  20.5 0.7 copy-start
  21.1 4.3 %copy-start.20 = (f32[3,1,1,2,128]{4,3,2,1,0:T(2,128)S(1)}, f32[3,1,1,2,128]{4,3,2,1,0:T(2,128)}, u32[]{:S(2)}) copy-start(f32[3,1,1,2,128]{4,3,2,1,0:T(2,128)} %param.5) | copy-start | bytes 9220
  21.1 4.3 %copy-start.26 = (f32[3]{0:T(128)S(1)}, f32[3]{0:T(128)}, u32[]{:S(2)}) copy-start(f32[3]{0:T(128)} %constant.46.clone) | copy-start | bytes 40
  23.0 27.3 %copy-start.1 = (f32[2,128]{1,0:T(2,128)}, f32[2,128]{1,0:T(2,128)S(1)}, u32[]{:S(2)}) copy-start(f32[2,128]{1,0:T(2,128)S(1)} %get-tuple-element.22) | copy-start | bytes 3076
  24.9 0.6 copy-start.8
  24.9 25.3 %copy-start.6 = (f32[3,1,1,2,128]{4,3,2,1,0:T(2,128)S(1)}, f32[3,1,1,2,128]{4,3,2,1,0:T(2,128)}, u32[]{:S(2)}) copy-start(f32[3,1,1,2,128]{4,3,2,1,0:T(2,128)} %param.4) | copy-start | bytes 9220
  25.5 35.0 %copy-start.4 = (f32[3,2,128]{2,1,0:T(2,128)}, f32[3,2,128]{2,1,0:T(2,128)S(1)}, u32[]{:S(2)}) copy-start(f32[3,2,128]{2,1,0:T(2,128)S(1)} %fusion.10) | copy-start | bytes 9220
  26.2 11.1 %all-to-all-start.1 = ((f32[32,3,1,1,2,128]{5,4,1,3,2,0:T(2,128)}), f32[32,3,1,1,2,128]{5,4,1,3,2,0:T(2,128)}, u32[]{:S(2)}, u32[]{:S(2)}) async-start(f32[32,3,1,1,2,128]{5,4,1,3,2,0:T(2,128)} %broadcast_in_dim.29), calls=%async_computation.1 | async-start | bytes 196608 | tf_op jit(solution)/shard_map/all_to_all | solution.py:46
  30.2 30.3 %copy-start.19 = (f32[3,2]{1,0:T(4,128)}, f32[3,2]{1,0:T(4,128)S(1)}, u32[]{:S(2)}) copy-start(f32[3,2]{1,0:T(4,128)S(1)} %copy.118) | copy-start | bytes 76
  45.4 4.8 %copy-start.9 = (f32[6,2,128]{2,1,0:T(2,128)S(1)}, f32[6,2,128]{2,1,0:T(2,128)}, u32[]{:S(2)}) copy-start(f32[6,2,128]{2,1,0:T(2,128)} %copy-done.8) | copy-start | bytes 18436
  50.3 0.5 copy-start.11
  64.5 3.8 %copy-start.2 = (f32[2,128]{1,0:T(2,128)S(1)}, f32[2,128]{1,0:T(2,128)}, u32[]{:S(2)}) copy-start(f32[2,128]{1,0:T(2,128)} %copy-done.1) | copy-start | bytes 3076
  67.0 6.4 %copy-start.3 = (f32[2,128]{1,0:T(2,128)S(1)}, f32[2,128]{1,0:T(2,128)}, u32[]{:S(2)}) copy-start(f32[2,128]{1,0:T(2,128)} %copy-done.1) | copy-start | bytes 3076
  68.3 0.6 copy-start.16
  68.9 0.6 copy-start.12
  70.1 10.5 %all-to-all-start.3 = ((f32[32,1,1,1,2,128]{5,4,3,2,1,0:T(2,128)}), f32[32,1,1,1,2,128]{5,4,3,2,1,0:T(2,128)}, u32[]{:S(2)}, u32[]{:S(2)}) async-start(f32[32,1,1,1,2,128]{5,4,3,2,1,0:T(2,128)} %broadcast_in_dim.35), calls=%async_computation.3 | async-start | bytes 65536 | tf_op jit(solution)/shard_map/all_to_all | solution.py:46
  88.6 6.5 %copy-start.13 = (f32[1,2,128]{2,1,0:T(2,128)S(1)}, f32[1,2,128]{2,1,0:T(2,128)}, u32[]{:S(2)}) copy-start(f32[1,2,128]{2,1,0:T(2,128)} %copy-done.12) | copy-start | bytes 3076
  88.6 6.5 %copy-start.24 = (f32[2,128]{1,0:T(2,128)S(1)}, f32[2,128]{1,0:T(2,128)}, u32[]{:S(2)}) copy-start(f32[2,128]{1,0:T(2,128)} %multiply_add_fusion.1) | copy-start | bytes 3076
  89.9 0.6 copy-start.17
  91.1 12.6 %copy-start.14 = (f32[1,2,128]{2,1,0:T(2,128)}, f32[1,2,128]{2,1,0:T(2,128)S(1)}, u32[]{:S(2)}) copy-start(f32[1,2,128]{2,1,0:T(2,128)S(1)} %bitcast_divide_fusion.1) | copy-start | bytes 3076
  91.8 10.5 %all-to-all-start.4 = ((f32[32,1,1,1,2,128]{5,4,3,2,1,0:T(2,128)}), f32[32,1,1,1,2,128]{5,4,3,2,1,0:T(2,128)}, u32[]{:S(2)}, u32[]{:S(2)}) async-start(f32[32,1,1,1,2,128]{5,4,3,2,1,0:T(2,128)} %broadcast_in_dim.37), calls=%async_computation.4 | async-start | bytes 65536 | tf_op jit(solution)/shard_map/all_to_all | solution.py:46
  107.7 4.5 %copy-start.15 = (f32[1,2,128]{2,1,0:T(2,128)S(1)}, f32[1,2,128]{2,1,0:T(2,128)}, u32[]{:S(2)}) copy-start(f32[1,2,128]{2,1,0:T(2,128)} %copy-done.14) | copy-start | bytes 3076
  107.7 5.2 %copy-start.21 = (f32[3,2,128]{2,1,0:T(2,128)S(1)}, f32[3,2,128]{2,1,0:T(2,128)}, u32[]{:S(2)}) copy-start(f32[3,2,128]{2,1,0:T(2,128)} %maximum_multiply_fusion) | copy-start | bytes 9220
  110.2 15.3 %copy-start.5 = (f32[3,2,128]{2,1,0:T(2,128)S(1)}, f32[3,2,128]{2,1,0:T(2,128)}, u32[]{:S(2)}) copy-start(f32[3,2,128]{2,1,0:T(2,128)} %copy-done.4) | copy-start | bytes 9220
  110.2 15.3 %copy-start.7 = (f32[3,1,1,2,128]{4,3,2,1,0:T(2,128)S(1)}, f32[3,1,1,2,128]{4,3,2,1,0:T(2,128)}, u32[]{:S(2)}) copy-start(f32[3,1,1,2,128]{4,3,2,1,0:T(2,128)} %param.4) | copy-start | bytes 9220
  110.2 15.3 %copy-start.10 = (f32[6,2,128]{2,1,0:T(2,128)S(1)}, f32[6,2,128]{2,1,0:T(2,128)}, u32[]{:S(2)}) copy-start(f32[6,2,128]{2,1,0:T(2,128)} %copy-done.8) | copy-start | bytes 18436
  111.6 1.4 %copy-start.18 = (f32[4,2,128]{2,1,0:T(2,128)}, f32[4,2,128]{2,1,0:T(2,128)S(1)}, u32[]{:S(2)}) copy-start(f32[4,2,128]{2,1,0:T(2,128)S(1)} %multiply_reduce_fusion.1) | copy-start | bytes 12292
  125.5 1.4 %copy-start.23 = (f32[1,2,128]{2,1,0:T(2,128)}, f32[1,2,128]{2,1,0:T(2,128)S(1)}, u32[]{:S(2)}) copy-start(f32[1,2,128]{2,1,0:T(2,128)S(1)} %get-tuple-element.37) | copy-start | bytes 3076

commit v8 on v7

--- a/solution.py
+++ b/solution.py
@@ -88,7 +88,7 @@
             for az in range(size_z - 2):
                 window = rim[:, az:az + 3, ax:ax + 3, ay:ay + 3, :]
                 blocks.append(window.reshape(comps, 27 * width))
-    return jnp.stack(blocks, axis=1)
+    return blocks
 
 
 def flat(cells):
@@ -96,7 +96,10 @@
 
 
 def wsum(weight, near):
-    return jnp.sum(weight[None] * near[:, :, None, :], axis=-1)
+    return jnp.stack(
+        [jnp.sum(tile_weight[None] * tile_near[:, None, :], axis=-1) for tile_weight, tile_near in zip(weight, near)],
+        axis=1,
+    )
 
 
 def tile_corners(block_shape):
@@ -143,24 +146,23 @@
         return neighbours(gather_rim(cells))
 
     near_all = rim_flat(packed)
-    near_x = near_all[0:3]
-    near_valid = near_all[3]
-    near_v = near_all[4:7]
     own_x = flat(positions)
     own_valid = flat(valid_mask)[0]
     own_v = flat(velocity)
-
-    gaps = [own_x[k][:, :, None] - near_x[k][:, None, :] for k in range(3)]
-    distance = gaps[0] * gaps[0] + gaps[1] * gaps[1] + gaps[2] * gaps[2]
-    closeness = jnp.maximum(1.0 - distance, 0.0)
-    weight = closeness * closeness * own_valid[:, :, None] * near_valid[:, None, :]
-
-    corner = tile_corners(block_shape)[:, :, None]
-    local_own = own_x - corner
-    local_near = near_x - corner
-
-    row = jnp.sum(weight, axis=-1)[None]
-    sums = wsum(weight, jnp.concatenate([near_v, local_near], axis=0))
+    corner = tile_corners(block_shape)
+
+    weight = []
+    local_near = []
+    for t, tile in enumerate(near_all):
+        gaps = [own_x[k, t][:, None] - tile[k][None, :] for k in range(3)]
+        distance = gaps[0] * gaps[0] + gaps[1] * gaps[1] + gaps[2] * gaps[2]
+        closeness = jnp.maximum(1.0 - distance, 0.0)
+        weight.append(closeness * closeness * own_valid[t][:, None] * tile[3][None, :])
+        local_near.append(tile[0:3] - corner[:, t][:, None])
+    local_own = own_x - corner[:, :, None]
+
+    row = jnp.stack([jnp.sum(tile_weight, axis=-1) for tile_weight in weight])[None]
+    sums = wsum(weight, [jnp.concatenate([tile[4:7], near], axis=0) for tile, near in zip(near_all, local_near)])
     near_sums = sums[0:3]
     lever = local_own * row - sums[3:6]
 
@@ -174,8 +176,13 @@
         return values.reshape(values.shape[0], *block_shape[1:])
 
     near_pred = rim_flat(shaped(predicted))
-    dotted = jnp.sum(near_pred * local_near, axis=0, keepdims=True)
-    psums = wsum(weight, jnp.concatenate([near_pred, dotted], axis=0))
+    psums = wsum(
+        weight,
+        [
+            jnp.concatenate([tile, jnp.sum(tile * near, axis=0, keepdims=True)], axis=0)
+            for tile, near in zip(near_pred, local_near)
+        ],
+    )
     flux = jnp.sum(local_own * psums[0:3], axis=0, keepdims=True) - psums[3:4]
     source = -(GRADIENT_GAIN / width) * (
         jnp.sum(predicted * lever, axis=0, keepdims=True) - flux
@@ -186,7 +193,7 @@
     near_wx = []
     for _ in range(ITERS):
         near_u = rim_flat(shaped(basis[-1]))
-        out = wsum(weight, jnp.concatenate([near_u, near_u * local_near], axis=0))
+        out = wsum(weight, [jnp.concatenate([tile, tile * near], axis=0) for tile, near in zip(near_u, local_near)])
         near_w.append(out[0:1])
         near_wx.append(out[1:4])
         basis.append(-(out[0:1] / width) / diagonal)

time: 129 us -> 143 us (1.11)
  blocking collectives: 19.5 us -> 38.6 us
  waiting for transfers between devices: 27.4 us -> 10.6 us
  local copies, waits for them, and re-layouts: 34.5 us -> 50.1 us
  starting transfers between devices: 17.1 us -> 10.5 us
  other arithmetic: 27.2 us -> 29 us
    all_to_all x1 -> x3, blocking collectives: 8.95 us -> 28 us  [gather_rim(): got = lax.all_to_all(rows, ('gx', 'gy', 'gz'), 0, 0, tiled=True)]
    all_to_all x4 -> x2, waiting for transfers between devices: 27.4 us -> 10.6 us  [gather_rim(): got = lax.all_to_all(rows, ('gx', 'gy', 'gz'), 0, 0, tiled=True)]
    reshape x0 -> x9, local copies, waits for them, and re-layouts: none -> 11.1 us  [the longest x8 11 us: neighbours(): blocks.append(window.reshape(comps, 27 * width))]
    another operation x9 -> x0, local copies, waits for them, and re-layouts: 10.6 us -> none  [neighbours(): return jnp.stack(blocks, axis=1)]
    mul x0 -> x11, local copies, waits for them, and re-layouts: none -> 9.75 us  [the longest x6 7.96 us: on_device(): tile * near]
    all_to_all x4 -> x2, starting transfers between devices: 17.1 us -> 10.5 us  [gather_rim(): got = lax.all_to_all(rows, ('gx', 'gy', 'gz'), 0, 0, tiled=True)]
    sub x1 -> x8, local copies, waits for them, and re-layouts: 1.27 us -> 4.82 us  [the longest x7 4.28 us: on_device(): gaps = [own_x[k, t][:, None] - tile[k][None, :] for k in range(3)]]
    slice x0 -> x18, local copies, waits for them, and re-layouts: none -> 2.87 us  [the longest x5 1.41 us: on_device(): tile[4:7]]
  transfers between devices with their start and end apart: 4 -> 2, of which waited for: 4 -> 2; matrix products, arithmetic and copies ran while one was open for 4% -> 4% of each run, Pallas kernels for 0% -> 0%
where the time goes in v8:
time: 143 us; the launch traced here: 140 us
  local copies, waits for them, and re-layouts  50.1 us (35%)
  blocking collectives  38.6 us (27%)
  other arithmetic  29 us (20%)
  waiting for transfers between devices  10.6 us (7%)
  starting transfers between devices  10.5 us (7%)
  between operations  1.62 us (1%)
    all_to_all x3, blocking collectives, gather_rim(): got = lax.all_to_all(rows, ('gx', 'gy', 'gz'), 0, 0, tiled=True)  28 us
    reshape x8, local copies, waits for them, and re-layouts, neighbours(): blocks.append(window.reshape(comps, 27 * width))  11 us
    all_to_all x2, waiting for transfers between devices, gather_rim(): got = lax.all_to_all(rows, ('gx', 'gy', 'gz'), 0, 0, tiled=True)  10.6 us
    all_to_all x1, blocking collectives, total(): got = lax.all_to_all(rows, ('gx', 'gy', 'gz'), 0, 0, tiled=True)  10.6 us
    all_to_all x2, starting transfers between devices, gather_rim(): got = lax.all_to_all(rows, ('gx', 'gy', 'gz'), 0, 0, tiled=True)  10.5 us
    slice x11, local copies, waits for them, and re-layouts, neighbours(): window = rim[:, az:az + 3, ax:ax + 3, ay:ay + 3, :]  9.02 us
    mul x6, local copies, waits for them, and re-layouts, on_device(): tile * near  7.96 us
    reduce_sum x10, other arithmetic, wsum(): jnp.sum(tile_weight[None] * tile_near[:, None, :], axis=-1)  7.11 us
  transfers between devices with their start and end apart: 2, of which 2 were waited for; matrix products, arithmetic and copies ran while one was open for 4% of the time, Pallas kernels for 0%

profile of v8, /device:TPU:0, one launch (start us, length us, event | category | flops | bytes accessed | tf_op | source)
XLA Modules:
  0.0 140.4 jit_solution(12686375367357039282)
XLA Ops:
  2.8 7.3 %all-to-all-start = ((f32[32,7,1,1,2,128]{5,4,1,3,2,0:T(2,128)}), f32[32,7,1,1,2,128]{5,4,1,3,2,0:T(2,128)S(1)}, u32[]{:S(2)}, u32[]{:S(2)}) async-start(f32[32,7,1,1,2,128]{5,4,1,3,2,0:T(2,128)} %broadcast_in_dim.29), calls=%async_computation | async-start | bytes 458752 | tf_op jit(solution)/shard_map/all_to_all | solution.py:46
  13.3 1.3 compare_convert_fusion.2
  15.2 4.7 %all-to-all-done = f32[32,7,1,1,2,128]{5,4,1,3,2,0:T(2,128)S(1)} async-done(((f32[32,7,1,1,2,128]{5,4,1,3,2,0:T(2,128)}), f32[32,7,1,1,2,128]{5,4,1,3,2,0:T(2,128)S(1)}, u32[]{:S(2)}, u32[]{:S(2)}) %all-to-all-start) | async-done | bytes 229408 | tf_op jit(solution)/shard_map/all_to_all | solution.py:46
  27.9 2.6 %fusion.30 = (f32[128]{0:T(128)S(1)}, f32[128,3456]{1,0:T(8,128)S(1)}, f32[128,3456]{1,0:T(8,128)S(1)}, f32[128]{0:T(128)S(1)}) fusion(f32[3456]{0:T(1024)S(1)} %mul.557, f32[128]{0:T(128)} %get-tuple-element.71, f32[3456]{0:T(1024)} %sub.294, f32[128]{0:T(128)} %get-tuple-element.63, f32[3456]{0:T(1024)} %sub.289, f32[128]{0:T(128)} %get-tuple-element.64, ...), kind=kLoop, calls=%fused_computation.157 | loop fusion | flops 12386048 | bytes 3654656 | tf_op jit(solution)/shard_map/reduce_sum | solution.py:164
  33.3 10.1 %all_to_all.30 = f32[32,3,1,1,2,128]{5,4,1,3,2,0:T(2,128)S(1)} all-to-all(f32[32,3,1,1,2,128]{5,4,1,3,2,0:T(2,128)S(1)} %broadcast_in_dim.31), channel_id=1, replica_groups=mesh['gx'=4,'gy'=2,'gz'=4] {'gx','gy','gz'}, dimensions={0} | all-to-all | bytes 196608 | tf_op jit(solution)/shard_map/all_to_all | solution.py:46
  43.6 1.3 multiply_reduce_fusion.11
  45.5 1.5 %reshape.593 = f32[3,3456]{1,0:T(4,128)} reshape(f32[3,3,3,3,128]{4,3,2,1,0:T(4,128)} %copy.189) | data formatting | bytes 82944 | tf_op jit(solution)/shard_map/reshape | solution.py:90
  47.0 1.3 copy.190
  48.3 1.3 broadcast_in_dim.32
  52.3 1.5 %reshape.594 = f32[3,3456]{1,0:T(4,128)} reshape(f32[3,3,3,3,128]{4,3,2,1,0:T(4,128)} %copy.191) | data formatting | bytes 82944 | tf_op jit(solution)/shard_map/reshape | solution.py:90
  53.8 1.3 copy.192
  55.1 1.3 broadcast_in_dim.33
  60.0 8.9 %all_to_all.31 = f32[32,1,1,1,2,128]{5,4,3,2,1,0:T(2,128)S(1)} all-to-all(f32[32,1,1,1,2,128]{5,4,3,2,1,0:T(2,128)S(1)} %broadcast_in_dim.36), channel_id=1, replica_groups=mesh['gx'=4,'gy'=2,'gz'=4] {'gx','gy','gz'}, dimensions={0} | all-to-all | bytes 65536 | tf_op jit(solution)/shard_map/all_to_all | solution.py:46
  70.2 1.3 mul.594
  71.6 1.3 reshape.597
  72.9 1.3 copy.199
  74.2 1.3 mul.599
  75.6 1.3 reshape.598
  81.7 8.9 %all_to_all.32 = f32[32,1,1,1,2,128]{5,4,3,2,1,0:T(2,128)S(1)} all-to-all(f32[32,1,1,1,2,128]{5,4,3,2,1,0:T(2,128)S(1)} %broadcast_in_dim.38), channel_id=1, replica_groups=mesh['gx'=4,'gy'=2,'gz'=4] {'gx','gy','gz'}, dimensions={0} | all-to-all | bytes 65536 | tf_op jit(solution)/shard_map/all_to_all | solution.py:46
  92.0 1.3 mul.604
  93.3 1.3 reshape.601
  94.6 1.3 copy.205
  95.9 1.3 mul.609
  97.3 1.3 reshape.602
  104.1 3.2 %all-to-all-start.4 = ((f32[32,1,1,1,2,128]{5,4,3,2,1,0:T(2,128)}), f32[32,1,1,1,2,128]{5,4,3,2,1,0:T(2,128)}, u32[]{:S(2)}, u32[]{:S(2)}) async-start(f32[32,1,1,1,2,128]{5,4,3,2,1,0:T(2,128)} %broadcast_in_dim.40), calls=%async_computation.4 | async-start | bytes 65536 | tf_op jit(solution)/shard_map/all_to_all | solution.py:46
  108.5 5.9 %all-to-all-done.4 = f32[32,1,1,1,2,128]{5,4,3,2,1,0:T(2,128)} async-done(((f32[32,1,1,1,2,128]{5,4,3,2,1,0:T(2,128)}), f32[32,1,1,1,2,128]{5,4,3,2,1,0:T(2,128)}, u32[]{:S(2)}, u32[]{:S(2)}) %all-to-all-start.4) | async-done | bytes 32800 | tf_op jit(solution)/shard_map/all_to_all | solution.py:46
  116.5 1.3 mul.617
  117.8 1.3 reshape.605
  119.2 1.3 copy.212
  120.5 1.3 mul.622
  121.8 1.3 reshape.606
  127.1 10.6 %all_to_all.33 = f32[32,3,4,128]{3,2,1,0:T(4,128)S(1)} all-to-all(f32[32,3,4,128]{3,2,1,0:T(4,128)S(1)} %broadcast_in_dim.41), channel_id=1, replica_groups=mesh['gx'=4,'gy'=2,'gz'=4] {'gx','gy','gz'}, dimensions={0} | all-to-all | bytes 393216 | tf_op jit(solution)/shard_map/all_to_all | solution.py:66
  (241 shorter events, 45.7 us)
Async XLA Ops:
  2.8 17.1 %all-to-all-start = ((f32[32,7,1,1,2,128]{5,4,1,3,2,0:T(2,128)}), f32[32,7,1,1,2,128]{5,4,1,3,2,0:T(2,128)S(1)}, u32[]{:S(2)}, u32[]{:S(2)}) async-start(f32[32,7,1,1,2,128]{5,4,1,3,2,0:T(2,128)} %broadcast_in_dim.29), calls=%async_computation | async-start | bytes 458752 | tf_op jit(solution)/shard_map/all_to_all | solution.py:46
  24.6 3.3 %copy-start.5 = (f32[3,3,3,3,128]{4,1,3,2,0:T(4,128)}, f32[3,3,3,3,128]{4,1,3,2,0:T(4,128)S(1)}, u32[]{:S(2)}) copy-start(f32[3,3,3,3,128]{4,1,3,2,0:T(4,128)S(1)} %get-tuple-element.43) | copy-start | bytes 124420
  27.9 3.3 %copy-start = (f32[3,3456]{1,0:T(4,128)S(1)}, f32[3,3456]{1,0:T(4,128)}, u32[]{:S(2)}) copy-start(f32[3,3456]{1,0:T(4,128)} %slice.290) | copy-start | bytes 124420
  27.9 3.3 %copy-start.29 = (f32[3]{0:T(128)S(1)}, f32[3]{0:T(128)}, u32[]{:S(2)}) copy-start(f32[3]{0:T(128)} %get-tuple-element.72) | copy-start | bytes 40
  27.9 3.3 %copy-start.9 = (f32[3,3456]{1,0:T(4,128)S(1)}, f32[3,3456]{1,0:T(4,128)}, u32[]{:S(2)}) copy-start(f32[3,3456]{1,0:T(4,128)} %slice.288) | copy-start | bytes 124420
  32.1 11.4 %copy-start.6 = (f32[3,3,3,3,128]{4,1,3,2,0:T(4,128)S(1)}, f32[3,3,3,3,128]{4,1,3,2,0:T(4,128)}, u32[]{:S(2)}) copy-start(f32[3,3,3,3,128]{4,1,3,2,0:T(4,128)} %copy-done.5) | copy-start | bytes 124420
  32.1 11.4 %copy-start.8 = (f32[3,3,3,3,128]{4,1,3,2,0:T(4,128)S(1)}, f32[3,3,3,3,128]{4,1,3,2,0:T(4,128)}, u32[]{:S(2)}) copy-start(f32[3,3,3,3,128]{4,1,3,2,0:T(4,128)} %copy-done.7) | copy-start | bytes 124420
  50.5 7.4 %copy-start.19 = (f32[3,1,1,2,128]{4,3,2,1,0:T(2,128)S(1)}, f32[3,1,1,2,128]{4,3,2,1,0:T(2,128)}, u32[]{:S(2)}) copy-start(f32[3,1,1,2,128]{4,3,2,1,0:T(2,128)} %param.4) | copy-start | bytes 9220
  76.9 2.3 %copy-start.1 = (f32[3,3456]{1,0:T(4,128)S(1)}, f32[3,3456]{1,0:T(4,128)}, u32[]{:S(2)}) copy-start(f32[3,3456]{1,0:T(4,128)} %slice.290) | copy-start | bytes 124420
  76.9 2.3 %copy-start.13 = (f32[3456]{0:T(1024)S(1)}, f32[3456]{0:T(1024)}, u32[]{:S(2)}) copy-start(f32[3456]{0:T(1024)} %mul.599) | copy-start | bytes 41476
  76.9 3.0 %copy-start.16 = (f32[1,3456]{1,0:T(1,128)S(1)}, f32[1,3456]{1,0:T(1,128)}, u32[]{:S(2)}) copy-start(f32[1,3456]{1,0:T(1,128)} %reshape.598) | copy-start | bytes 41476
  79.2 12.2 %copy-start.31 = (f32[4,128]{1,0:T(4,128)}, f32[4,128]{1,0:T(4,128)S(1)}, u32[]{:S(2)}) copy-start(f32[4,128]{1,0:T(4,128)S(1)} %multiply_reduce_fusion.7) | copy-start | bytes 6148
  80.5 10.8 %copy-start.33 = (f32[4,128]{1,0:T(4,128)}, f32[4,128]{1,0:T(4,128)S(1)}, u32[]{:S(2)}) copy-start(f32[4,128]{1,0:T(4,128)S(1)} %multiply_reduce_fusion.6) | copy-start | bytes 6148
  98.6 2.3 %copy-start.14 = (f32[3456]{0:T(1024)S(1)}, f32[3456]{0:T(1024)}, u32[]{:S(2)}) copy-start(f32[3456]{0:T(1024)} %mul.609) | copy-start | bytes 41476
  98.6 3.0 %copy-start.17 = (f32[1,3456]{1,0:T(1,128)S(1)}, f32[1,3456]{1,0:T(1,128)}, u32[]{:S(2)}) copy-start(f32[1,3456]{1,0:T(1,128)} %reshape.602) | copy-start | bytes 41476
  104.1 10.4 %all-to-all-start.4 = ((f32[32,1,1,1,2,128]{5,4,3,2,1,0:T(2,128)}), f32[32,1,1,1,2,128]{5,4,3,2,1,0:T(2,128)}, u32[]{:S(2)}, u32[]{:S(2)}) async-start(f32[32,1,1,1,2,128]{5,4,3,2,1,0:T(2,128)} %broadcast_in_dim.40), calls=%async_computation.4 | async-start | bytes 65536 | tf_op jit(solution)/shard_map/all_to_all | solution.py:46
  123.2 2.3 %copy-start.3 = (f32[3,3456]{1,0:T(4,128)S(1)}, f32[3,3456]{1,0:T(4,128)}, u32[]{:S(2)}) copy-start(f32[3,3456]{1,0:T(4,128)} %slice.290) | copy-start | bytes 124420
  123.2 2.3 %copy-start.12 = (f32[3456]{0:T(1024)S(1)}, f32[3456]{0:T(1024)}, u32[]{:S(2)}) copy-start(f32[3456]{0:T(1024)} %mul.622) | copy-start | bytes 41476
  123.2 3.2 %copy-start.15 = (f32[1,3456]{1,0:T(1,128)S(1)}, f32[1,3456]{1,0:T(1,128)}, u32[]{:S(2)}) copy-start(f32[1,3456]{1,0:T(1,128)} %reshape.606) | copy-start | bytes 41476
  125.5 13.4 %copy-start.22 = (f32[1,2,128]{2,0,1:T(1,128)S(1)}, f32[1,2,128]{2,0,1:T(1,128)}, u32[]{:S(2)}) copy-start(f32[1,2,128]{2,0,1:T(1,128)} %copy-done.20) | copy-start | bytes 3076
  125.5 13.4 %copy-start.25 = (f32[1,2,128]{2,0,1:T(1,128)S(1)}, f32[1,2,128]{2,0,1:T(1,128)}, u32[]{:S(2)}) copy-start(f32[1,2,128]{2,0,1:T(1,128)} %copy-done.23) | copy-start | bytes 3076
  125.5 13.4 %copy-start.28 = (f32[1,2,128]{2,0,1:T(1,128)S(1)}, f32[1,2,128]{2,0,1:T(1,128)}, u32[]{:S(2)}) copy-start(f32[1,2,128]{2,0,1:T(1,128)} %copy-done.26) | copy-start | bytes 3076
  125.5 13.4 %copy-start.58 = (f32[1,2,128]{2,0,1:T(1,128)S(1)}, f32[1,2,128]{2,0,1:T(1,128)}, u32[]{:S(2)}) copy-start(f32[1,2,128]{2,0,1:T(1,128)} %get-tuple-element.29) | copy-start | bytes 3076
  125.6 13.4 %copy-start.59 = (f32[1,2,128]{2,0,1:T(1,128)S(1)}, f32[1,2,128]{2,0,1:T(1,128)}, u32[]{:S(2)}) copy-start(f32[1,2,128]{2,0,1:T(1,128)} %get-tuple-element.27) | copy-start | bytes 3076
  125.6 13.5 %copy-start.32 = (f32[4,128]{1,0:T(4,128)S(1)}, f32[4,128]{1,0:T(4,128)}, u32[]{:S(2)}) copy-start(f32[4,128]{1,0:T(4,128)} %copy-done.31) | copy-start | bytes 6148
  125.6 13.5 %copy-start.34 = (f32[4,128]{1,0:T(4,128)S(1)}, f32[4,128]{1,0:T(4,128)}, u32[]{:S(2)}) copy-start(f32[4,128]{1,0:T(4,128)} %copy-done.33) | copy-start | bytes 6148
  125.6 13.5 %copy-start.36 = (f32[4,128]{1,0:T(4,128)S(1)}, f32[4,128]{1,0:T(4,128)}, u32[]{:S(2)}) copy-start(f32[4,128]{1,0:T(4,128)} %copy-done.35) | copy-start | bytes 6148
  125.6 13.5 %copy-start.38 = (f32[4,128]{1,0:T(4,128)S(1)}, f32[4,128]{1,0:T(4,128)}, u32[]{:S(2)}) copy-start(f32[4,128]{1,0:T(4,128)} %copy-done.37) | copy-start | bytes 6148
  125.6 13.5 %copy-start.50 = (f32[2,128]{1,0:T(2,128)S(1)}, f32[2,128]{1,0:T(2,128)}, u32[]{:S(2)}) copy-start(f32[2,128]{1,0:T(2,128)} %copy-done.49) | copy-start | bytes 3076
  125.6 13.5 %copy-start.52 = (f32[3,2]{0,1:T(2,128)S(1)}, f32[3,2]{0,1:T(2,128)}, u32[]{:S(2)}) copy-start(f32[3,2]{0,1:T(2,128)} %copy-done.51) | copy-start | bytes 76
  125.6 13.5 %copy-start.55 = (f32[2,128]{1,0:T(2,128)S(1)}, f32[2,128]{1,0:T(2,128)}, u32[]{:S(2)}) copy-start(f32[2,128]{1,0:T(2,128)} %compare_convert_fusion.2) | copy-start | bytes 3076
  125.6 13.5 %copy-start.57 = (f32[3]{0:T(128)S(1)}, f32[3]{0:T(128)}, u32[]{:S(2)}) copy-start(f32[3]{0:T(128)} %constant.46.clone) | copy-start | bytes 40
  (31 other events, 50.9 us)

commit v9 on v8

--- a/solution.py
+++ b/solution.py
@@ -82,6 +82,10 @@
 
 def neighbours(rim):
     comps, size_z, size_x, size_y, width = rim.shape
+    if size_x == 3 and size_y == 3:
+        slab = 9 * width
+        flat_rim = rim.reshape(comps, size_z * slab)
+        return [flat_rim[:, az * slab:(az + 3) * slab] for az in range(size_z - 2)]
     blocks = []
     for ax in range(size_x - 2):
         for ay in range(size_y - 2):

time: 143 us -> 105 us (0.73)
  local copies, waits for them, and re-layouts: 50.1 us -> 20.8 us
  other arithmetic: 29 us -> 20.1 us
    slice x22 -> x3, local copies, waits for them, and re-layouts: 11.8 us -> 2.6 us  [neighbours(): return [flat_rim[:, az * slab:(az + 3) * slab] for az in range(size_z - 2)]]
    mul x6 -> x0, local copies, waits for them, and re-layouts: 7.96 us -> none  [on_device(): tile * near]
    reshape x8 -> x5, local copies, waits for them, and re-layouts: 11 us -> 5.73 us  [neighbours(): flat_rim = rim.reshape(comps, size_z * slab)]
    sub x7 -> x1, local copies, waits for them, and re-layouts: 4.28 us -> 0.52 us  [on_device(): gaps = [own_x[k, t][:, None] - tile[k][None, :] for k in range(3)]]
    dynamic_slice x0 -> x10, local copies, waits for them, and re-layouts: none -> 2.76 us  [gather_rim(): lax.dynamic_slice(padded, start, (comps, size_z + 2, size_x + 2, size_y +...]
    broadcast_in_dim x2, local copies, waits for them, and re-layouts: 2.68 us -> 0.02 us  [on_device(): jnp.sum(tile * near, axis=0, keepdims=True)]
    reduce_sum x2 -> x0, local copies, waits for them, and re-layouts: 2.65 us -> none  [on_device(): jnp.sum(tile * near, axis=0, keepdims=True)]
    mul x6, other arithmetic: 4.76 us -> 2.55 us  [on_device(): tile * near]
where the time goes in v9:
time: 105 us; the launch traced here: 103 us
  blocking collectives  38.6 us (37%)
  local copies, waits for them, and re-layouts  20.8 us (20%)
  other arithmetic  20.1 us (19%)
  waiting for transfers between devices  11.8 us (11%)
  starting transfers between devices  10.5 us (10%)
  between operations  1.61 us (2%)
    all_to_all x3, blocking collectives, gather_rim(): got = lax.all_to_all(rows, ('gx', 'gy', 'gz'), 0, 0, tiled=True)  28 us
    all_to_all x2, waiting for transfers between devices, gather_rim(): got = lax.all_to_all(rows, ('gx', 'gy', 'gz'), 0, 0, tiled=True)  11.8 us
    all_to_all x1, blocking collectives, total(): got = lax.all_to_all(rows, ('gx', 'gy', 'gz'), 0, 0, tiled=True)  10.6 us
    all_to_all x2, starting transfers between devices, gather_rim(): got = lax.all_to_all(rows, ('gx', 'gy', 'gz'), 0, 0, tiled=True)  10.5 us
    reduce_sum x10, other arithmetic, wsum(): jnp.sum(tile_weight[None] * tile_near[:, None, :], axis=-1)  6.61 us
    reshape x5, local copies, waits for them, and re-layouts, neighbours(): flat_rim = rim.reshape(comps, size_z * slab)  5.73 us
    unnamed x104, local copies, waits for them, and re-layouts  4.79 us
    dynamic_slice x10, local copies, waits for them, and re-layouts, gather_rim(): lax.dynamic_slice(padded, start, (comps, size_z + 2, size_x + 2, size_y +...  2.76 us
  transfers between devices with their start and end apart: 2, of which 2 were waited for; matrix products, arithmetic and copies ran while one was open for 4% of the time, Pallas kernels for 0%

profile of v9, /device:TPU:0, one launch (start us, length us, event | category | flops | bytes accessed | tf_op | source)
XLA Modules:
  0.0 103.4 jit_solution(3460841398078486537)
XLA Ops:
  0.6 0.7 compare_convert_fusion.1
  1.4 0.7 maximum_bitcast_fusion
  2.1 0.7 broadcast_in_dim.29
  2.8 7.3 %all-to-all-start = ((f32[32,7,1,1,2,128]{5,4,1,3,2,0:T(2,128)}), f32[32,7,1,1,2,128]{5,4,1,3,2,0:T(2,128)S(1)}, u32[]{:S(2)}, u32[]{:S(2)}) async-start(f32[32,7,1,1,2,128]{5,4,1,3,2,0:T(2,128)} %broadcast_in_dim.29), calls=%async_computation | async-start | bytes 458752 | tf_op jit(solution)/shard_map/all_to_all | solution.py:46
  10.1 0.7 compare_convert_fusion
  10.8 0.7 copy.98
  12.8 0.7 compare_convert_fusion.2
  14.0 5.9 %all-to-all-done = f32[32,7,1,1,2,128]{5,4,1,3,2,0:T(2,128)S(1)} async-done(((f32[32,7,1,1,2,128]{5,4,1,3,2,0:T(2,128)}), f32[32,7,1,1,2,128]{5,4,1,3,2,0:T(2,128)S(1)}, u32[]{:S(2)}, u32[]{:S(2)}) %all-to-all-start) | async-done | bytes 229408 | tf_op jit(solution)/shard_map/all_to_all | solution.py:46
  21.2 2.5 %fusion.30 = (f32[128]{0:T(128)S(1)}, f32[128,3456]{1,0:T(8,128)S(1)}, f32[128,3456]{1,0:T(8,128)S(1)}, f32[128]{0:T(128)S(1)}) fusion(f32[3456]{0:T(1024)S(1)} %get-tuple-element.18, f32[128]{0:T(128)} %get-tuple-element.73, f32[3456]{0:T(1024)S(1)} %get-tuple-element.19, f32[128]{0:T(128)} %get-tuple-element.65, f32[3456]{0:T(1024)S(1)} %get-tuple-element.20, ...), kind=kLoop, calls=%fused_computation.156 | loop fusion | flops 12386048 | bytes 3654656 | tf_op jit(solution)/shard_map/reduce_sum | solution.py:168
  23.7 0.9 multiply_reduce_fusion.1
  24.6 0.9 multiply_reduce_fusion
  26.7 10.1 %all_to_all.30 = f32[32,3,1,1,2,128]{5,4,1,3,2,0:T(2,128)S(1)} all-to-all(f32[32,3,1,1,2,128]{5,4,1,3,2,0:T(2,128)S(1)} %broadcast_in_dim.31), channel_id=1, replica_groups=mesh['gx'=4,'gy'=2,'gz'=4] {'gx','gy','gz'}, dimensions={0} | all-to-all | bytes 196608 | tf_op jit(solution)/shard_map/all_to_all | solution.py:46
  37.0 0.7 copy.66
  37.6 1.6 %reshape.535 = f32[3,4608]{1,0:T(4,128)} reshape(f32[3,4,3,3,128]{4,3,2,1,0:T(4,128)} %copy.66) | data formatting | bytes 110592 | tf_op jit(solution)/shard_map/reshape | solution.py:87
  39.2 1.0 multiply_reduce_fusion.11
  42.3 8.9 %all_to_all.31 = f32[32,1,1,1,2,128]{5,4,3,2,1,0:T(2,128)S(1)} all-to-all(f32[32,1,1,1,2,128]{5,4,3,2,1,0:T(2,128)S(1)} %broadcast_in_dim.36), channel_id=1, replica_groups=mesh['gx'=4,'gy'=2,'gz'=4] {'gx','gy','gz'}, dimensions={0} | all-to-all | bytes 65536 | tf_op jit(solution)/shard_map/all_to_all | solution.py:46
  51.9 1.4 %reshape.538 = f32[1,4608]{1,0:T(1,128)} reshape(f32[1,4,3,3,128]{4,3,2,1,0:T(4,128)} %copy.71) | data formatting | bytes 36864 | tf_op jit(solution)/shard_map/reshape | solution.py:87
  53.3 0.9 slice_reduce_fusion.13
  54.1 0.8 broadcast_multiply_fusion.4
  57.5 8.9 %all_to_all.32 = f32[32,1,1,1,2,128]{5,4,3,2,1,0:T(2,128)S(1)} all-to-all(f32[32,1,1,1,2,128]{5,4,3,2,1,0:T(2,128)S(1)} %broadcast_in_dim.38), channel_id=1, replica_groups=mesh['gx'=4,'gy'=2,'gz'=4] {'gx','gy','gz'}, dimensions={0} | all-to-all | bytes 65536 | tf_op jit(solution)/shard_map/all_to_all | solution.py:46
  67.2 1.4 %reshape.541 = f32[1,4608]{1,0:T(1,128)} reshape(f32[1,4,3,3,128]{4,3,2,1,0:T(4,128)} %copy.74) | data formatting | bytes 36864 | tf_op jit(solution)/shard_map/reshape | solution.py:87
  68.6 0.9 slice_reduce_fusion.11
  69.4 0.8 broadcast_multiply_fusion.2
  73.4 3.2 %all-to-all-start.4 = ((f32[32,1,1,1,2,128]{5,4,3,2,1,0:T(2,128)}), f32[32,1,1,1,2,128]{5,4,3,2,1,0:T(2,128)}, u32[]{:S(2)}, u32[]{:S(2)}) async-start(f32[32,1,1,1,2,128]{5,4,3,2,1,0:T(2,128)} %broadcast_in_dim.40), calls=%async_computation.4 | async-start | bytes 65536 | tf_op jit(solution)/shard_map/all_to_all | solution.py:46
  76.7 0.7 maximum_multiply_fusion.1
  78.0 5.9 %all-to-all-done.4 = f32[32,1,1,1,2,128]{5,4,3,2,1,0:T(2,128)} async-done(((f32[32,1,1,1,2,128]{5,4,3,2,1,0:T(2,128)}), f32[32,1,1,1,2,128]{5,4,3,2,1,0:T(2,128)}, u32[]{:S(2)}, u32[]{:S(2)}) %all-to-all-start.4) | async-done | bytes 32800 | tf_op jit(solution)/shard_map/all_to_all | solution.py:46
  83.9 0.8 copy.76
  85.3 1.4 %reshape.544 = f32[1,4608]{1,0:T(1,128)} reshape(f32[1,4,3,3,128]{4,3,2,1,0:T(4,128)} %copy.78) | data formatting | bytes 36864 | tf_op jit(solution)/shard_map/reshape | solution.py:87
  86.7 0.9 slice_reduce_fusion.9
  87.6 0.8 broadcast_multiply_fusion
  90.1 10.6 %all_to_all.33 = f32[32,3,4,128]{3,2,1,0:T(4,128)S(1)} all-to-all(f32[32,3,4,128]{3,2,1,0:T(4,128)S(1)} %broadcast_in_dim.41), channel_id=1, replica_groups=mesh['gx'=4,'gy'=2,'gz'=4] {'gx','gy','gz'}, dimensions={0} | all-to-all | bytes 393216 | tf_op jit(solution)/shard_map/all_to_all | solution.py:66
  102.1 0.8 fusion.12
  (186 shorter events, 17.7 us)
Async XLA Ops:
  2.8 17.1 %all-to-all-start = ((f32[32,7,1,1,2,128]{5,4,1,3,2,0:T(2,128)}), f32[32,7,1,1,2,128]{5,4,1,3,2,0:T(2,128)S(1)}, u32[]{:S(2)}, u32[]{:S(2)}) async-start(f32[32,7,1,1,2,128]{5,4,1,3,2,0:T(2,128)} %broadcast_in_dim.29), calls=%async_computation | async-start | bytes 458752 | tf_op jit(solution)/shard_map/all_to_all | solution.py:46
  13.5 12.6 %copy-start.42 = (f32[2,128]{1,0:T(2,128)}, f32[2,128]{1,0:T(2,128)S(1)}, u32[]{:S(2)}) copy-start(f32[2,128]{1,0:T(2,128)S(1)} %compare_convert_fusion.2) | copy-start | bytes 3076
  20.5 4.0 %copy-start.4 = (f32[3,3456]{1,0:T(4,128)}, f32[3,3456]{1,0:T(4,128)S(1)}, u32[]{:S(2)}) copy-start(f32[3,3456]{1,0:T(4,128)S(1)} %get-tuple-element.46) | copy-start | bytes 124420
  23.6 1.9 %copy-start.25 = (f32[128]{0:T(128)}, f32[128]{0:T(128)S(1)}, u32[]{:S(2)}) copy-start(f32[128]{0:T(128)S(1)} %get-tuple-element.50) | copy-start | bytes 1540
  23.7 1.9 %copy-start.30 = (f32[128]{0:T(128)}, f32[128]{0:T(128)S(1)}, u32[]{:S(2)}) copy-start(f32[128]{0:T(128)S(1)} %get-tuple-element.79) | copy-start | bytes 1540
  23.7 2.5 %copy-start.5 = (f32[3,1,1,2,128]{4,3,2,1,0:T(2,128)S(1)}, f32[3,1,1,2,128]{4,3,2,1,0:T(2,128)}, u32[]{:S(2)}) copy-start(f32[3,1,1,2,128]{4,3,2,1,0:T(2,128)} %param.5) | copy-start | bytes 9220
  23.7 2.5 %copy-start.45 = (f32[3]{0:T(128)S(1)}, f32[3]{0:T(128)}, u32[]{:S(2)}) copy-start(f32[3]{0:T(128)} %constant.46.clone) | copy-start | bytes 40
  53.3 2.4 %copy-start.1 = (f32[3,3456]{1,0:T(4,128)S(1)}, f32[3,3456]{1,0:T(4,128)}, u32[]{:S(2)}) copy-start(f32[3,3456]{1,0:T(4,128)} %copy-done) | copy-start | bytes 124420
  55.6 10.9 %copy-start.16 = (f32[4,128]{1,0:T(4,128)}, f32[4,128]{1,0:T(4,128)S(1)}, u32[]{:S(2)}) copy-start(f32[4,128]{1,0:T(4,128)S(1)} %multiply_reduce_fusion.6) | copy-start | bytes 6148
  56.3 10.2 %copy-start.18 = (f32[4,128]{1,0:T(4,128)}, f32[4,128]{1,0:T(4,128)S(1)}, u32[]{:S(2)}) copy-start(f32[4,128]{1,0:T(4,128)S(1)} %multiply_reduce_fusion.7) | copy-start | bytes 6148
  68.6 2.4 %copy-start.2 = (f32[3,3456]{1,0:T(4,128)S(1)}, f32[3,3456]{1,0:T(4,128)}, u32[]{:S(2)}) copy-start(f32[3,3456]{1,0:T(4,128)} %copy-done) | copy-start | bytes 124420
  73.4 10.5 %all-to-all-start.4 = ((f32[32,1,1,1,2,128]{5,4,3,2,1,0:T(2,128)}), f32[32,1,1,1,2,128]{5,4,3,2,1,0:T(2,128)}, u32[]{:S(2)}, u32[]{:S(2)}) async-start(f32[32,1,1,1,2,128]{5,4,3,2,1,0:T(2,128)} %broadcast_in_dim.40), calls=%async_computation.4 | async-start | bytes 65536 | tf_op jit(solution)/shard_map/all_to_all | solution.py:46
  86.7 2.5 %copy-start.3 = (f32[3,3456]{1,0:T(4,128)S(1)}, f32[3,3456]{1,0:T(4,128)}, u32[]{:S(2)}) copy-start(f32[3,3456]{1,0:T(4,128)} %copy-done) | copy-start | bytes 124420
  88.5 1.5 %copy-start.29 = (f32[128]{0:T(128)S(1)}, f32[128]{0:T(128)}, u32[]{:S(2)}) copy-start(f32[128]{0:T(128)} %copy-done.25) | copy-start | bytes 1540
  88.5 1.5 %copy-start.34 = (f32[128]{0:T(128)S(1)}, f32[128]{0:T(128)}, u32[]{:S(2)}) copy-start(f32[128]{0:T(128)} %copy-done.30) | copy-start | bytes 1540
  88.5 1.5 %copy-start.8 = (f32[1,2,128]{2,0,1:T(1,128)S(1)}, f32[1,2,128]{2,0,1:T(1,128)}, u32[]{:S(2)}) copy-start(f32[1,2,128]{2,0,1:T(1,128)} %copy-done.7) | copy-start | bytes 3076
  88.5 1.5 %copy-start.11 = (f32[1,2,128]{2,0,1:T(1,128)S(1)}, f32[1,2,128]{2,0,1:T(1,128)}, u32[]{:S(2)}) copy-start(f32[1,2,128]{2,0,1:T(1,128)} %copy-done.10) | copy-start | bytes 3076
  88.5 1.5 %copy-start.14 = (f32[1,2,128]{2,0,1:T(1,128)S(1)}, f32[1,2,128]{2,0,1:T(1,128)}, u32[]{:S(2)}) copy-start(f32[1,2,128]{2,0,1:T(1,128)} %copy-done.13) | copy-start | bytes 3076
  88.5 1.5 %copy-start.41 = (f32[3,2,128]{2,1,0:T(2,128)S(1)}, f32[3,2,128]{2,1,0:T(2,128)}, u32[]{:S(2)}) copy-start(f32[3,2,128]{2,1,0:T(2,128)} %copy.75) | copy-start | bytes 9220
  89.1 12.8 %copy-start.9 = (f32[1,2,128]{2,0,1:T(1,128)S(1)}, f32[1,2,128]{2,0,1:T(1,128)}, u32[]{:S(2)}) copy-start(f32[1,2,128]{2,0,1:T(1,128)} %copy-done.7) | copy-start | bytes 3076
  89.1 12.8 %copy-start.12 = (f32[1,2,128]{2,0,1:T(1,128)S(1)}, f32[1,2,128]{2,0,1:T(1,128)}, u32[]{:S(2)}) copy-start(f32[1,2,128]{2,0,1:T(1,128)} %copy-done.10) | copy-start | bytes 3076
  89.1 12.8 %copy-start.15 = (f32[1,2,128]{2,0,1:T(1,128)S(1)}, f32[1,2,128]{2,0,1:T(1,128)}, u32[]{:S(2)}) copy-start(f32[1,2,128]{2,0,1:T(1,128)} %copy-done.13) | copy-start | bytes 3076
  89.2 12.8 %copy-start.48 = (f32[1,2,128]{2,0,1:T(1,128)S(1)}, f32[1,2,128]{2,0,1:T(1,128)}, u32[]{:S(2)}) copy-start(f32[1,2,128]{2,0,1:T(1,128)} %get-tuple-element.43) | copy-start | bytes 3076
  89.2 12.8 %copy-start.49 = (f32[1,2,128]{2,0,1:T(1,128)S(1)}, f32[1,2,128]{2,0,1:T(1,128)}, u32[]{:S(2)}) copy-start(f32[1,2,128]{2,0,1:T(1,128)} %get-tuple-element.41) | copy-start | bytes 3076
  89.2 12.8 %copy-start.17 = (f32[4,128]{1,0:T(4,128)S(1)}, f32[4,128]{1,0:T(4,128)}, u32[]{:S(2)}) copy-start(f32[4,128]{1,0:T(4,128)} %copy-done.16) | copy-start | bytes 6148
  89.2 12.8 %copy-start.19 = (f32[4,128]{1,0:T(4,128)S(1)}, f32[4,128]{1,0:T(4,128)}, u32[]{:S(2)}) copy-start(f32[4,128]{1,0:T(4,128)} %copy-done.18) | copy-start | bytes 6148
  89.2 12.8 %copy-start.21 = (f32[4,128]{1,0:T(4,128)S(1)}, f32[4,128]{1,0:T(4,128)}, u32[]{:S(2)}) copy-start(f32[4,128]{1,0:T(4,128)} %copy-done.20) | copy-start | bytes 6148
  89.2 12.8 %copy-start.23 = (f32[4,128]{1,0:T(4,128)S(1)}, f32[4,128]{1,0:T(4,128)}, u32[]{:S(2)}) copy-start(f32[4,128]{1,0:T(4,128)} %copy-done.22) | copy-start | bytes 6148
  89.2 12.8 %copy-start.37 = (f32[2,128]{1,0:T(2,128)S(1)}, f32[2,128]{1,0:T(2,128)}, u32[]{:S(2)}) copy-start(f32[2,128]{1,0:T(2,128)} %copy-done.35) | copy-start | bytes 3076
  89.2 12.8 %copy-start.40 = (f32[3,2]{0,1:T(2,128)S(1)}, f32[3,2]{0,1:T(2,128)}, u32[]{:S(2)}) copy-start(f32[3,2]{0,1:T(2,128)} %copy-done.38) | copy-start | bytes 76
  89.2 12.8 %copy-start.44 = (f32[2,128]{1,0:T(2,128)S(1)}, f32[2,128]{1,0:T(2,128)}, u32[]{:S(2)}) copy-start(f32[2,128]{1,0:T(2,128)} %copy-done.42) | copy-start | bytes 3076
  89.2 12.8 %copy-start.47 = (f32[3]{0:T(128)S(1)}, f32[3]{0:T(128)}, u32[]{:S(2)}) copy-start(f32[3]{0:T(128)} %constant.46.clone) | copy-start | bytes 40
  (21 other events, 21.9 us)

commit v10 on v6

--- a/solution.py
+++ b/solution.py
@@ -180,7 +180,8 @@
         return jnp.broadcast_to(near_field, (near_field.shape[0], tiles, near_field.shape[2]))
 
     row = jnp.sum(weight, axis=-1)[None]
-    sums = wsum(weight, jnp.concatenate([spread_t(near_v), local_near], axis=0))
+    fields = [near_v[k] for k in range(3)] + [local_near[k] for k in range(3)]
+    sums = jnp.stack([jnp.sum(weight * field[:, None, :], axis=-1) for field in fields])
     near_sums = sums[0:3]
     lever = local_own * row - sums[3:6]
 

time: 99.6 us -> 98.7 us (level)
  local copies, waits for them, and re-layouts: 6.19 us -> 4.04 us
  other arithmetic: 26.9 us -> 28.2 us
    reduce_sum x1, other arithmetic: 3.34 us -> 7.35 us  [on_device(): jnp.sum(weight * field[:, None, :], axis=-1)]
    reduce_sum x5 -> x4, other arithmetic: 18.9 us -> 16.2 us  [wsum(): return jnp.sum(weight[None] * near[:, :, None, :], axis=-1)]
    unnamed x10 -> x8, local copies, waits for them, and re-layouts: 2.15 us -> 0.03 us
where the time goes in v10:
time: 98.7 us; the launch traced here: 98 us
  blocking collectives  29.6 us (30%)
  other arithmetic  28.2 us (29%)
  waiting for transfers between devices  22.7 us (23%)
  starting transfers between devices  12.4 us (13%)
  local copies, waits for them, and re-layouts  4.04 us (4%)
  between operations  1.02 us (1%)
    all_to_all x3, waiting for transfers between devices, gather_rim(): got = lax.all_to_all(rows, ('gx', 'gy', 'gz'), 0, 0, tiled=True)  22.7 us
    all_to_all x2, blocking collectives, gather_rim(): got = lax.all_to_all(rows, ('gx', 'gy', 'gz'), 0, 0, tiled=True)  19 us
    reduce_sum x4, other arithmetic, wsum(): return jnp.sum(weight[None] * near[:, :, None, :], axis=-1)  16.2 us
    all_to_all x3, starting transfers between devices, gather_rim(): got = lax.all_to_all(rows, ('gx', 'gy', 'gz'), 0, 0, tiled=True)  12.4 us
    all_to_all x1, blocking collectives, total(): got = lax.all_to_all(rows, ('gx', 'gy', 'gz'), 0, 0, tiled=True)  10.6 us
    reduce_sum x1, other arithmetic, on_device(): jnp.sum(weight * field[:, None, :], axis=-1)  7.35 us
    broadcast_in_dim x5, local copies, waits for them, and re-layouts, gather_rim(): rows = jnp.broadcast_to(cells[None], (devices,) + cells.shape)  2 us
  transfers between devices with their start and end apart: 3, of which 3 were waited for; matrix products, arithmetic and copies ran while one was open for 2% of the time, Pallas kernels for 0%

profile of v10, /device:TPU:0, one launch (start us, length us, event | category | flops | bytes accessed | tf_op | source)
XLA Modules:
  0.0 98.0 jit_solution(220585890298896149)
XLA Ops:
  0.7 0.7 compare_convert_fusion
  1.4 0.7 maximum_bitcast_fusion
  2.1 0.7 broadcast_in_dim.43
  2.8 7.3 %all-to-all-start = ((f32[32,7,1,1,2,128]{5,4,1,3,2,0:T(2,128)}), f32[32,7,1,1,2,128]{5,4,1,3,2,0:T(2,128)S(1)}, u32[]{:S(2)}, u32[]{:S(2)}) async-start(f32[32,7,1,1,2,128]{5,4,1,3,2,0:T(2,128)} %broadcast_in_dim.43), calls=%async_computation | async-start | bytes 458752 | tf_op jit(solution)/shard_map/all_to_all | solution.py:47
  10.1 0.1 add_bitcast_fusion.1
  10.2 0.1 copy.22
  10.3 0.7 compare_convert_fusion.1
  11.1 0.7 slice_bitcast_fusion.5
  11.8 8.2 %all-to-all-done = f32[32,7,1,1,2,128]{5,4,1,3,2,0:T(2,128)S(1)} async-done(((f32[32,7,1,1,2,128]{5,4,1,3,2,0:T(2,128)}), f32[32,7,1,1,2,128]{5,4,1,3,2,0:T(2,128)S(1)}, u32[]{:S(2)}, u32[]{:S(2)}) %all-to-all-start) | async-done | bytes 229408 | tf_op jit(solution)/shard_map/all_to_all | solution.py:47
  20.0 0.1 copy.21
  20.1 0.1 broadcast_subtract_fusion
  20.3 0.1 pad_dynamic-slice_fusion
  20.5 7.3 %multiply_reduce_fusion.6 = (f32[2,128]{1,0:T(2,128)S(1)}, f32[2,128]{1,0:T(2,128)S(1)}, f32[2,128]{1,0:T(2,128)S(1)}, f32[2,128]{1,0:T(2,128)S(1)}, f32[2,128]{...) fusion(f32[2,4608]{1,0:T(2,128)S(1)} %get-tuple-element.31, ...), kind=kLoop, calls=%fused_computation.14 | loop fusion | flops 31848704 | bytes 5006336 | tf_op jit(solution)/shard_map/reduce_sum | solution.py:184
  27.9 10.1 %all_to_all.30 = f32[32,3,1,1,2,128]{5,4,1,3,2,0:T(2,128)S(1)} all-to-all(f32[32,3,1,1,2,128]{5,4,1,3,2,0:T(2,128)S(1)} %broadcast_in_dim.45), channel_id=1, replica_groups=mesh['gx'=4,'gy'=2,'gz'=4] {'gx','gy','gz'}, dimensions={0} | all-to-all | bytes 196608 | tf_op jit(solution)/shard_map/all_to_all | solution.py:47
  38.2 0.1 fusion
  38.4 4.1 %multiply_reduce_fusion.3 = f32[4,2,128]{2,1,0:T(2,128)S(1)} fusion(f32[4,2,4608]{2,1,0:T(2,128)S(1)} %pad_maximum_fusion, f32[2,128,4608]{2,1,0:T(8,128)} %get-tuple-element.28), kind=kLoop, calls=%fused_computation.3 | loop fusion | flops 9436160 | bytes 4870144 | tf_op jit(solution)/shard_map/reduce_sum | solution.py:100
  42.5 0.1 multiply_reduce_fusion.11
  42.6 8.9 %all_to_all.31 = f32[32,1,1,1,2,128]{5,4,3,2,1,0:T(2,128)S(1)} all-to-all(f32[32,1,1,1,2,128]{5,4,3,2,1,0:T(2,128)S(1)} %broadcast_in_dim.51), channel_id=1, replica_groups=mesh['gx'=4,'gy'=2,'gz'=4] {'gx','gy','gz'}, dimensions={0} | all-to-all | bytes 65536 | tf_op jit(solution)/shard_map/all_to_all | solution.py:47
  51.6 0.1 subtract_multiply_fusion.2
  51.8 4.1 %multiply_reduce_fusion.2 = f32[4,2,128]{2,1,0:T(2,128)S(1)} fusion(f32[4,2,4608]{2,1,0:T(2,128)S(1)} %pad_maximum_fusion.1, f32[2,128,4608]{2,1,0:T(8,128)} %get-tuple-element.28), kind=kLoop, calls=%fused_computation.2 | loop fusion | flops 9436160 | bytes 4870144 | tf_op jit(solution)/shard_map/reduce_sum | solution.py:100
  55.9 0.6 broadcast_in_dim.55
  56.5 2.5 %all-to-all-start.3 = ((f32[32,1,1,1,2,128]{5,4,3,2,1,0:T(2,128)}), f32[32,1,1,1,2,128]{5,4,3,2,1,0:T(2,128)S(1)}, u32[]{:S(2)}, u32[]{:S(2)}) async-start(f32[32,1,1,1,2,128]{5,4,3,2,1,0:T(2,128)} %broadcast_in_dim.55), calls=%async_computation.3 | async-start | bytes 65536 | tf_op jit(solution)/shard_map/all_to_all | solution.py:47
  59.1 7.2 %all-to-all-done.3 = f32[32,1,1,1,2,128]{5,4,3,2,1,0:T(2,128)S(1)} async-done(((f32[32,1,1,1,2,128]{5,4,3,2,1,0:T(2,128)}), f32[32,1,1,1,2,128]{5,4,3,2,1,0:T(2,128)S(1)}, u32[]{:S(2)}, u32[]{:S(2)}) %all-to-all-start.3) | async-done | bytes 32800 | tf_op jit(solution)/shard_map/all_to_all | solution.py:47
  66.4 0.1 subtract_multiply_fusion.1
  66.6 4.1 %multiply_reduce_fusion.1 = f32[4,2,128]{2,1,0:T(2,128)S(1)} fusion(f32[4,2,4608]{2,1,0:T(2,128)S(1)} %pad_maximum_fusion.2, f32[2,128,4608]{2,1,0:T(8,128)} %get-tuple-element.28), kind=kLoop, calls=%fused_computation.1 | loop fusion | flops 9436160 | bytes 4870144 | tf_op jit(solution)/shard_map/reduce_sum | solution.py:100
  70.6 0.6 broadcast_in_dim.59
  71.2 2.5 %all-to-all-start.4 = ((f32[32,1,1,1,2,128]{5,4,3,2,1,0:T(2,128)}), f32[32,1,1,1,2,128]{5,4,3,2,1,0:T(2,128)S(1)}, u32[]{:S(2)}, u32[]{:S(2)}) async-start(f32[32,1,1,1,2,128]{5,4,3,2,1,0:T(2,128)} %broadcast_in_dim.59), calls=%async_computation.4 | async-start | bytes 65536 | tf_op jit(solution)/shard_map/all_to_all | solution.py:47
  73.8 7.2 %all-to-all-done.4 = f32[32,1,1,1,2,128]{5,4,3,2,1,0:T(2,128)S(1)} async-done(((f32[32,1,1,1,2,128]{5,4,3,2,1,0:T(2,128)}), f32[32,1,1,1,2,128]{5,4,3,2,1,0:T(2,128)S(1)}, u32[]{:S(2)}, u32[]{:S(2)}) %all-to-all-start.4) | async-done | bytes 32800 | tf_op jit(solution)/shard_map/all_to_all | solution.py:47
  81.1 0.1 subtract_multiply_fusion
  81.3 4.1 %multiply_reduce_fusion = f32[4,2,128]{2,1,0:T(2,128)S(1)} fusion(f32[4,2,4608]{2,1,0:T(2,128)S(1)} %pad_maximum_fusion.3, f32[2,128,4608]{2,1,0:T(8,128)} %get-tuple-element.28), kind=kLoop, calls=%fused_computation | loop fusion | flops 9436160 | bytes 4870144 | tf_op jit(solution)/shard_map/reduce_sum | solution.py:100
  85.4 10.6 %all_to_all.32 = f32[32,3,4,128]{3,2,1,0:T(4,128)S(1)} all-to-all(f32[32,3,4,128]{3,2,1,0:T(4,128)S(1)} %broadcast_in_dim.122), channel_id=1, replica_groups=mesh['gx'=4,'gy'=2,'gz'=4] {'gx','gy','gz'}, dimensions={0} | all-to-all | bytes 393216 | tf_op jit(solution)/shard_map/all_to_all | solution.py:67
  97.3 0.7 subtract_bitcast_fusion
  (68 shorter events, 2.2 us)
Async XLA Ops:
  0.6 27.2 %copy-start.2 = (f32[3]{0:T(128)S(1)}, f32[3]{0:T(128)}, u32[]{:S(2)}) copy-start(f32[3]{0:T(128)} %constant.49.clone) | copy-start | bytes 40
  0.6 27.2 %copy-start.1 = (f32[3,1,1,2,128]{4,3,2,1,0:T(2,128)S(1)}, f32[3,1,1,2,128]{4,3,2,1,0:T(2,128)}, u32[]{:S(2)}) copy-start(f32[3,1,1,2,128]{4,3,2,1,0:T(2,128)} %param.6) | copy-start | bytes 9220
  2.8 17.1 %all-to-all-start = ((f32[32,7,1,1,2,128]{5,4,1,3,2,0:T(2,128)}), f32[32,7,1,1,2,128]{5,4,1,3,2,0:T(2,128)S(1)}, u32[]{:S(2)}, u32[]{:S(2)}) async-start(f32[32,7,1,1,2,128]{5,4,1,3,2,0:T(2,128)} %broadcast_in_dim.43), calls=%async_computation | async-start | bytes 458752 | tf_op jit(solution)/shard_map/all_to_all | solution.py:47
  20.5 22.0 %copy-start = (f32[3,1,1,2,128]{4,3,2,1,0:T(2,128)S(1)}, f32[3,1,1,2,128]{4,3,2,1,0:T(2,128)}, u32[]{:S(2)}) copy-start(f32[3,1,1,2,128]{4,3,2,1,0:T(2,128)} %param.5) | copy-start | bytes 9220
  56.5 9.8 %all-to-all-start.3 = ((f32[32,1,1,1,2,128]{5,4,3,2,1,0:T(2,128)}), f32[32,1,1,1,2,128]{5,4,3,2,1,0:T(2,128)S(1)}, u32[]{:S(2)}, u32[]{:S(2)}) async-start(f32[32,1,1,1,2,128]{5,4,3,2,1,0:T(2,128)} %broadcast_in_dim.55), calls=%async_computation.3 | async-start | bytes 65536 | tf_op jit(solution)/shard_map/all_to_all | solution.py:47
  71.2 9.8 %all-to-all-start.4 = ((f32[32,1,1,1,2,128]{5,4,3,2,1,0:T(2,128)}), f32[32,1,1,1,2,128]{5,4,3,2,1,0:T(2,128)S(1)}, u32[]{:S(2)}, u32[]{:S(2)}) async-start(f32[32,1,1,1,2,128]{5,4,3,2,1,0:T(2,128)} %broadcast_in_dim.59), calls=%async_computation.4 | async-start | bytes 65536 | tf_op jit(solution)/shard_map/all_to_all | solution.py:47
  97.3 0.7 copy-start.3

commit v11 on v6

--- a/solution.py
+++ b/solution.py
@@ -97,7 +97,13 @@
 
 
 def wsum(weight, near):
-    return jnp.sum(weight[None] * near[:, :, None, :], axis=-1)
+    return jnp.stack(
+        [
+            jnp.sum(tile_weight[None] * near[:, min(t, near.shape[1] - 1), None, :], axis=-1)
+            for t, tile_weight in enumerate(weight)
+        ],
+        axis=1,
+    )
 
 
 def tile_corners(block_shape):
@@ -165,24 +171,32 @@
     own_v = flat(velocity)
     tiles = own_x.shape[1]
 
-    gaps = [own_x[k][:, :, None] - near_x[k][:, None, :] for k in range(3)]
-    distance = gaps[0] * gaps[0] + gaps[1] * gaps[1] + gaps[2] * gaps[2]
-    closeness = jnp.maximum(1.0 - distance, 0.0)
-    weight = (
-        closeness * closeness * own_valid[:, :, None] * near_valid[:, None, :]
-    ) * jnp.asarray(adjacency(block_shape))[:, None, :]
-
     corner = tile_corners(block_shape)[:, :, None]
     local_own = own_x - corner
     local_near = near_x - corner
+    adjacent = adjacency(block_shape)
 
     def spread_t(near_field):
         return jnp.broadcast_to(near_field, (near_field.shape[0], tiles, near_field.shape[2]))
 
-    row = jnp.sum(weight, axis=-1)[None]
-    sums = wsum(weight, jnp.concatenate([spread_t(near_v), local_near], axis=0))
-    near_sums = sums[0:3]
-    lever = local_own * row - sums[3:6]
+    weight = []
+    tile_sums = []
+    for t in range(tiles):
+        gaps = [own_x[k, t][:, None] - near_x[k, 0][None, :] for k in range(3)]
+        distance = gaps[0] * gaps[0] + gaps[1] * gaps[1] + gaps[2] * gaps[2]
+        closeness = jnp.maximum(1.0 - distance, 0.0)
+        tile_weight = (
+            closeness * closeness * own_valid[t][:, None] * near_valid[0][None, :]
+        ) * jnp.asarray(adjacent[t])[None, :]
+        weight.append(tile_weight)
+        fields = [near_v[k, 0] for k in range(3)] + [local_near[k, t] for k in range(3)]
+        tile_sums.append(
+            jnp.stack([jnp.sum(tile_weight, axis=-1)] + [jnp.sum(tile_weight * field[None, :], axis=-1) for field in fields])
+        )
+    sums = jnp.stack(tile_sums, axis=1)
+    row = sums[0:1]
+    near_sums = sums[1:4]
+    lever = local_own * row - sums[4:7]
 
     gravity_pull = jnp.array([0.0, 0.0, -GRAVITY], jnp.float32).reshape(3, 1, 1)
     predicted = own_valid[None] * (

time: 99.6 us -> 93.6 us (0.940)
  blocking collectives: 29.6 us -> 38.6 us
  waiting for transfers between devices: 22.5 us -> 14.7 us
  starting transfers between devices: 12.6 us -> 9.79 us
  other arithmetic: 26.9 us -> 24.2 us
  local copies, waits for them, and re-layouts: 6.19 us -> 4.51 us
    all_to_all x2 -> x3, blocking collectives: 19 us -> 28 us  [gather_rim(): got = lax.all_to_all(rows, ('gx', 'gy', 'gz'), 0, 0, tiled=True)]
    all_to_all x3 -> x2, waiting for transfers between devices: 22.5 us -> 14.7 us  [gather_rim(): got = lax.all_to_all(rows, ('gx', 'gy', 'gz'), 0, 0, tiled=True)]
    reduce_sum x7 -> x11, other arithmetic: 22.3 us -> 19.3 us  [the longest x8 12.6 us: wsum(): jnp.sum(tile_weight[None] * near[:, min(t, near.shape[1] - 1), None, :],...]
    all_to_all x3 -> x2, starting transfers between devices: 12.6 us -> 9.79 us  [gather_rim(): got = lax.all_to_all(rows, ('gx', 'gy', 'gz'), 0, 0, tiled=True)]
    convert_element_type x2 -> x3, other arithmetic: 1.45 us -> 2.18 us  [on_device(): (slot_ids[None, None, None, :] < counts[:, :, :, None]).astype(jnp.float32)]
    unnamed x10 -> x22, local copies, waits for them, and re-layouts: 2.15 us -> 1.47 us
  transfers between devices with their start and end apart: 3 -> 2, of which waited for: 3 -> 2; matrix products, arithmetic and copies ran while one was open for 2% -> 3% of each run, Pallas kernels for 0% -> 0%
where the time goes in v11:
time: 93.6 us; the launch traced here: 92.9 us
  blocking collectives  38.6 us (41%)
  other arithmetic  24.2 us (26%)
  waiting for transfers between devices  14.7 us (16%)
  starting transfers between devices  9.79 us (10%)
  local copies, waits for them, and re-layouts  4.51 us (5%)
  between operations  1.1 us (1%)
    all_to_all x3, blocking collectives, gather_rim(): got = lax.all_to_all(rows, ('gx', 'gy', 'gz'), 0, 0, tiled=True)  28 us
    all_to_all x2, waiting for transfers between devices, gather_rim(): got = lax.all_to_all(rows, ('gx', 'gy', 'gz'), 0, 0, tiled=True)  14.7 us
    reduce_sum x8, other arithmetic, wsum(): jnp.sum(tile_weight[None] * near[:, min(t, near.shape[1] - 1), None, :],...  12.6 us
    all_to_all x1, blocking collectives, total(): got = lax.all_to_all(rows, ('gx', 'gy', 'gz'), 0, 0, tiled=True)  10.6 us
    all_to_all x2, starting transfers between devices, gather_rim(): got = lax.all_to_all(rows, ('gx', 'gy', 'gz'), 0, 0, tiled=True)  9.79 us
    reduce_sum x2, other arithmetic, on_device(): jnp.sum(tile_weight * field[None, :], axis=-1)  6.6 us
    convert_element_type x3, other arithmetic, on_device(): (slot_ids[None, None, None, :] < counts[:, :, :, None]).astype(jnp.float32)  2.18 us
  transfers between devices with their start and end apart: 2, of which 2 were waited for; matrix products, arithmetic and copies ran while one was open for 3% of the time, Pallas kernels for 0%

profile of v11, /device:TPU:0, one launch (start us, length us, event | category | flops | bytes accessed | tf_op | source)
XLA Modules:
  0.0 92.9 jit_solution(6104235529933502292)
XLA Ops:
  0.6 0.7 compare_convert_fusion.1
  1.4 0.7 maximum_bitcast_fusion
  2.1 0.7 broadcast_in_dim.43
  2.8 7.3 %all-to-all-start = ((f32[32,7,1,1,2,128]{5,4,1,3,2,0:T(2,128)}), f32[32,7,1,1,2,128]{5,4,1,3,2,0:T(2,128)S(1)}, u32[]{:S(2)}, u32[]{:S(2)}) async-start(f32[32,7,1,1,2,128]{5,4,1,3,2,0:T(2,128)} %broadcast_in_dim.43), calls=%async_computation | async-start | bytes 458752 | tf_op jit(solution)/shard_map/all_to_all | solution.py:47
  10.1 0.7 compare_convert_fusion
  10.9 0.7 copy.117
  11.7 0.7 compare_convert_fusion.2
  12.5 7.5 %all-to-all-done = f32[32,7,1,1,2,128]{5,4,1,3,2,0:T(2,128)S(1)} async-done(((f32[32,7,1,1,2,128]{5,4,1,3,2,0:T(2,128)}), f32[32,7,1,1,2,128]{5,4,1,3,2,0:T(2,128)S(1)}, u32[]{:S(2)}, u32[]{:S(2)}) %all-to-all-start) | async-done | bytes 229408 | tf_op jit(solution)/shard_map/all_to_all | solution.py:47
  20.4 0.3 slice_reduce_fusion
  20.8 2.5 %multiply_reduce_fusion.8 = (f32[128]{0:T(128)S(1)}, f32[128]{0:T(128)S(1)}, f32[128]{0:T(128)S(1)}, f32[128]{0:T(128)S(1)}, f32[128]{0:T(128)S(1)}, /*index=5*/...) fusion(f32[4608]{0:T(1024)S(1)} %get-tuple-element.14, f32[4608]{0:T(1024)S(1)} %copy-done.3, f32[4608]{0:T(1024)S(1)} %mul.641, ...), kind=kLoop, calls=%fused_computation.16 | loop fusion | flops 15924352 | bytes 2567680 | tf_op jit(solution)/shard_map/reduce_sum | solution.py:194
  23.3 4.1 %multiply_reduce_fusion.14 = (f32[128]{0:T(128)S(1)}, f32[128]{0:T(128)S(1)}, f32[128]{0:T(128)S(1)}, f32[128]{0:T(128)S(1)}, f32[128]{0:T(128)S(1)}, /*index=5*...) fusion(f32[4608]{0:T(1024)S(1)} %get-tuple-element.17, f32[4608]{0:T(1024)S(1)} %copy-done.2, f32[4608]{0:T(1024)S(1)} %mul.641, ...), kind=kLoop, calls=%fused_computation.23 | loop fusion | flops 15924352 | bytes 2567680 | tf_op jit(solution)/shard_map/reduce_sum | solution.py:194
  27.6 10.1 %all_to_all.30 = f32[32,3,1,1,2,128]{5,4,1,3,2,0:T(2,128)S(1)} all-to-all(f32[32,3,1,1,2,128]{5,4,1,3,2,0:T(2,128)S(1)} %broadcast_in_dim.45), channel_id=1, replica_groups=mesh['gx'=4,'gy'=2,'gz'=4] {'gx','gy','gz'}, dimensions={0} | all-to-all | bytes 196608 | tf_op jit(solution)/shard_map/all_to_all | solution.py:47
  37.8 0.1 fusion
  38.0 0.1 fusion.4
  38.2 2.4 %multiply_reduce_fusion.7 = f32[4,128]{1,0:T(4,128)S(1)} fusion(f32[4,4608]{1,0:T(4,128)S(1)} %bitcast.278, f32[128,4608]{1,0:T(8,128)} %get-tuple-element.65), kind=kLoop, calls=%fused_computation.7 | loop fusion | flops 4718080 | bytes 2435072 | tf_op jit(solution)/shard_map/reduce_sum | solution.py:102
  40.6 0.8 multiply_reduce_fusion.6
  41.5 8.9 %all_to_all.31 = f32[32,1,1,1,2,128]{5,4,3,2,1,0:T(2,128)S(1)} all-to-all(f32[32,1,1,1,2,128]{5,4,3,2,1,0:T(2,128)S(1)} %broadcast_in_dim.51), channel_id=1, replica_groups=mesh['gx'=4,'gy'=2,'gz'=4] {'gx','gy','gz'}, dimensions={0} | all-to-all | bytes 65536 | tf_op jit(solution)/shard_map/all_to_all | solution.py:47
  50.7 0.1 fusion.3
  50.8 2.4 %multiply_reduce_fusion.5 = f32[4,128]{1,0:T(4,128)S(1)} fusion(f32[4,4608]{1,0:T(4,128)S(1)} %bitcast.282, f32[128,4608]{1,0:T(8,128)} %get-tuple-element.65), kind=kLoop, calls=%fused_computation.5 | loop fusion | flops 4718080 | bytes 2435072 | tf_op jit(solution)/shard_map/reduce_sum | solution.py:102
  53.2 0.7 multiply_reduce_fusion.4
  54.0 8.9 %all_to_all.32 = f32[32,1,1,1,2,128]{5,4,3,2,1,0:T(2,128)S(1)} all-to-all(f32[32,1,1,1,2,128]{5,4,3,2,1,0:T(2,128)S(1)} %broadcast_in_dim.55), channel_id=1, replica_groups=mesh['gx'=4,'gy'=2,'gz'=4] {'gx','gy','gz'}, dimensions={0} | all-to-all | bytes 65536 | tf_op jit(solution)/shard_map/all_to_all | solution.py:47
  63.1 0.1 fusion.2
  63.3 2.4 %multiply_reduce_fusion.3 = f32[4,128]{1,0:T(4,128)S(1)} fusion(f32[4,4608]{1,0:T(4,128)S(1)} %bitcast.284, f32[128,4608]{1,0:T(8,128)} %get-tuple-element.65), kind=kLoop, calls=%fused_computation.3 | loop fusion | flops 4718080 | bytes 2435072 | tf_op jit(solution)/shard_map/reduce_sum | solution.py:102
  65.7 0.7 multiply_reduce_fusion.2
  66.5 0.6 broadcast_in_dim.59
  67.1 2.5 %all-to-all-start.4 = ((f32[32,1,1,1,2,128]{5,4,3,2,1,0:T(2,128)}), f32[32,1,1,1,2,128]{5,4,3,2,1,0:T(2,128)S(1)}, u32[]{:S(2)}, u32[]{:S(2)}) async-start(f32[32,1,1,1,2,128]{5,4,3,2,1,0:T(2,128)} %broadcast_in_dim.59), calls=%async_computation.4 | async-start | bytes 65536 | tf_op jit(solution)/shard_map/all_to_all | solution.py:47
  69.6 7.2 %all-to-all-done.4 = f32[32,1,1,1,2,128]{5,4,3,2,1,0:T(2,128)S(1)} async-done(((f32[32,1,1,1,2,128]{5,4,3,2,1,0:T(2,128)}), f32[32,1,1,1,2,128]{5,4,3,2,1,0:T(2,128)S(1)}, u32[]{:S(2)}, u32[]{:S(2)}) %all-to-all-start.4) | async-done | bytes 32800 | tf_op jit(solution)/shard_map/all_to_all | solution.py:47
  77.0 0.1 fusion.1
  77.1 2.4 %multiply_reduce_fusion.1 = f32[4,128]{1,0:T(4,128)S(1)} fusion(f32[4,4608]{1,0:T(4,128)S(1)} %bitcast.280, f32[128,4608]{1,0:T(8,128)} %get-tuple-element.65), kind=kLoop, calls=%fused_computation.1 | loop fusion | flops 4718080 | bytes 2435072 | tf_op jit(solution)/shard_map/reduce_sum | solution.py:102
  79.6 0.7 multiply_reduce_fusion
  80.4 10.6 %all_to_all.33 = f32[32,3,4,128]{3,2,1,0:T(4,128)S(1)} all-to-all(f32[32,3,4,128]{3,2,1,0:T(4,128)S(1)} %broadcast_in_dim.122), channel_id=1, replica_groups=mesh['gx'=4,'gy'=2,'gz'=4] {'gx','gy','gz'}, dimensions={0} | all-to-all | bytes 393216 | tf_op jit(solution)/shard_map/all_to_all | solution.py:67
  92.3 0.6 copy.55
  (91 shorter events, 3.2 us)
Async XLA Ops:
  0.6 20.1 %copy-start.3 = (f32[4608]{0:T(1024)S(1)}, f32[4608]{0:T(1024)}, u32[]{:S(2)}) copy-start(f32[4608]{0:T(1024)} %constant.51.clone) | copy-start | bytes 55300
  2.8 17.1 %all-to-all-start = ((f32[32,7,1,1,2,128]{5,4,1,3,2,0:T(2,128)}), f32[32,7,1,1,2,128]{5,4,1,3,2,0:T(2,128)S(1)}, u32[]{:S(2)}, u32[]{:S(2)}) async-start(f32[32,7,1,1,2,128]{5,4,1,3,2,0:T(2,128)} %broadcast_in_dim.43), calls=%async_computation | async-start | bytes 458752 | tf_op jit(solution)/shard_map/all_to_all | solution.py:47
  10.1 13.2 %copy-start.2 = (f32[4608]{0:T(1024)S(1)}, f32[4608]{0:T(1024)}, u32[]{:S(2)}) copy-start(f32[4608]{0:T(1024)} %constant.50.clone) | copy-start | bytes 55300
  20.7 6.7 %copy-start = (f32[3,1,1,2,128]{4,3,2,1,0:T(2,128)S(1)}, f32[3,1,1,2,128]{4,3,2,1,0:T(2,128)}, u32[]{:S(2)}) copy-start(f32[3,1,1,2,128]{4,3,2,1,0:T(2,128)} %param.7) | copy-start | bytes 9220
  20.7 6.7 %copy-start.4 = (f32[3]{0:T(128)S(1)}, f32[3]{0:T(128)}, u32[]{:S(2)}) copy-start(f32[3]{0:T(128)} %constant.52.clone) | copy-start | bytes 40
  38.2 3.2 %copy-start.1 = (f32[3,1,1,2,128]{4,3,2,1,0:T(2,128)S(1)}, f32[3,1,1,2,128]{4,3,2,1,0:T(2,128)}, u32[]{:S(2)}) copy-start(f32[3,1,1,2,128]{4,3,2,1,0:T(2,128)} %param.6) | copy-start | bytes 9220
  67.1 9.7 %all-to-all-start.4 = ((f32[32,1,1,1,2,128]{5,4,3,2,1,0:T(2,128)}), f32[32,1,1,1,2,128]{5,4,3,2,1,0:T(2,128)S(1)}, u32[]{:S(2)}, u32[]{:S(2)}) async-start(f32[32,1,1,1,2,128]{5,4,3,2,1,0:T(2,128)} %broadcast_in_dim.59), calls=%async_computation.4 | async-start | bytes 65536 | tf_op jit(solution)/shard_map/all_to_all | solution.py:47
  92.2 0.7 copy-start.5

commit v12 on v11

--- a/solution.py
+++ b/solution.py
@@ -39,7 +39,7 @@
     return cells
 
 
-def gather_rim(cells):
+def gather_rim(cells, outside=0.0):
     comps, size_x, size_y, size_z, width = cells.shape
     counts = [lax.axis_size(axis) for axis, _ in AXES]
     devices = counts[0] * counts[1] * counts[2]
@@ -49,7 +49,7 @@
     grid = grid.transpose(3, 0, 4, 1, 5, 2, 6, 7).reshape(
         comps, counts[0] * size_x, counts[1] * size_y, counts[2] * size_z, width
     )
-    padded = jnp.pad(grid, ((0, 0), (1, 1), (1, 1), (1, 1), (0, 0)))
+    padded = jnp.pad(grid, ((0, 0), (1, 1), (1, 1), (1, 1), (0, 0)), constant_values=outside)
     start = (
         0,
         lax.axis_index("gx") * size_x,
@@ -156,16 +156,17 @@
     width = positions.shape[4]
     slot_ids = jnp.arange(width, dtype=jnp.int32)
     valid_mask = (slot_ids[None, None, None, :] < counts[:, :, :, None]).astype(jnp.float32)[None]
-    packed = jnp.concatenate([positions, valid_mask, velocity], axis=0)
-
-    def rim_flat(cells):
-        rim = gather_rim(cells)
+    coded = jnp.where(valid_mask[0] > 0, positions[0], -1.0)[None]
+    packed = jnp.concatenate([coded, positions[1:3], velocity], axis=0)
+
+    def rim_flat(cells, outside=0.0):
+        rim = gather_rim(cells, outside)
         return rim.reshape(rim.shape[0], 1, -1)
 
-    near_all = rim_flat(packed)
+    near_all = rim_flat(packed, -1.0)
     near_x = near_all[0:3]
-    near_valid = near_all[3]
-    near_v = near_all[4:7]
+    near_valid = (near_all[0] >= 0.0).astype(jnp.float32)
+    near_v = near_all[3:6]
     own_x = flat(positions)
     own_valid = flat(valid_mask)[0]
     own_v = flat(velocity)

time: 93.6 us -> 93.6 us (level)
  waiting for transfers between devices: 14.7 us -> 13.7 us
    convert_element_type x3 -> x2, other arithmetic: 2.18 us -> 1.45 us  [on_device(): (slot_ids[None, None, None, :] < counts[:, :, :, None]).astype(jnp.float32)]
where the time goes in v12:
time: 93.6 us; the launch traced here: 92.9 us
  blocking collectives  38.8 us (41%)
  other arithmetic  24.3 us (26%)
  waiting for transfers between devices  13.7 us (15%)
  starting transfers between devices  9.79 us (10%)
  local copies, waits for them, and re-layouts  5.16 us (6%)
  between operations  1.11 us (1%)
    all_to_all x3, blocking collectives, gather_rim(): got = lax.all_to_all(rows, ('gx', 'gy', 'gz'), 0, 0, tiled=True)  28.2 us
    all_to_all x2, waiting for transfers between devices, gather_rim(): got = lax.all_to_all(rows, ('gx', 'gy', 'gz'), 0, 0, tiled=True)  13.7 us
    reduce_sum x8, other arithmetic, wsum(): jnp.sum(tile_weight[None] * near[:, min(t, near.shape[1] - 1), None, :],...  12.6 us
    all_to_all x1, blocking collectives, total(): got = lax.all_to_all(rows, ('gx', 'gy', 'gz'), 0, 0, tiled=True)  10.6 us
    all_to_all x2, starting transfers between devices, gather_rim(): got = lax.all_to_all(rows, ('gx', 'gy', 'gz'), 0, 0, tiled=True)  9.79 us
    reduce_sum x2, other arithmetic, on_device(): jnp.sum(tile_weight * field[None, :], axis=-1)  6.61 us
  transfers between devices with their start and end apart: 2, of which 2 were waited for; matrix products, arithmetic and copies ran while one was open for 3% of the time, Pallas kernels for 0%

profile of v12, /device:TPU:0, one launch (start us, length us, event | category | flops | bytes accessed | tf_op | source)
XLA Modules:
  0.0 92.9 jit_solution(1528036228413863927)
XLA Ops:
  0.6 0.7 slice.263
  1.3 0.8 compare_select_fusion
  2.1 0.7 maximum_bitcast_fusion
  2.8 0.7 broadcast_in_dim.48
  3.5 7.3 %all-to-all-start = ((f32[32,6,1,1,2,128]{5,4,1,3,2,0:T(2,128)}), f32[32,6,1,1,2,128]{5,4,1,3,2,0:T(2,128)S(1)}, u32[]{:S(2)}, u32[]{:S(2)}) async-start(f32[32,6,1,1,2,128]{5,4,1,3,2,0:T(2,128)} %broadcast_in_dim.48), calls=%async_computation | async-start | bytes 393216 | tf_op jit(solution)/shard_map/all_to_all | solution.py:47
  10.8 0.7 compare_convert_fusion.1
  11.5 0.7 copy.115
  12.4 0.7 compare_convert_fusion.3
  13.2 6.5 %all-to-all-done = f32[32,6,1,1,2,128]{5,4,1,3,2,0:T(2,128)S(1)} async-done(((f32[32,6,1,1,2,128]{5,4,1,3,2,0:T(2,128)}), f32[32,6,1,1,2,128]{5,4,1,3,2,0:T(2,128)S(1)}, u32[]{:S(2)}, u32[]{:S(2)}) %all-to-all-start) | async-done | bytes 196640 | tf_op jit(solution)/shard_map/all_to_all | solution.py:47
  20.2 0.3 slice_reduce_fusion
  20.5 2.6 %multiply_reduce_fusion.8 = (f32[128]{0:T(128)S(1)}, f32[128]{0:T(128)S(1)}, f32[128]{0:T(128)S(1)}, f32[128]{0:T(128)S(1)}, f32[128]{0:T(128)S(1)}, /*index=5*/...) fusion(f32[4608]{0:T(1024)S(1)} %get-tuple-element.14, f32[4608]{0:T(1024)S(1)} %copy-done.3, ...), kind=kLoop, calls=%fused_computation.15 | loop fusion | flops 15924352 | bytes 2567680 | tf_op jit(solution)/shard_map/reduce_sum | solution.py:195
  23.1 4.1 %multiply_reduce_fusion.14 = (f32[128]{0:T(128)S(1)}, f32[128]{0:T(128)S(1)}, f32[128]{0:T(128)S(1)}, f32[128]{0:T(128)S(1)}, f32[128]{0:T(128)S(1)}, /*index=5*...) fusion(f32[4608]{0:T(1024)S(1)} %get-tuple-element.17, f32[4608]{0:T(1024)S(1)} %copy-done.2, ...), kind=kLoop, calls=%fused_computation.22 | loop fusion | flops 15924352 | bytes 2567680 | tf_op jit(solution)/shard_map/reduce_sum | solution.py:195
  27.3 10.3 %all_to_all.30 = f32[32,3,1,1,2,128]{5,4,1,3,2,0:T(2,128)S(1)} all-to-all(f32[32,3,1,1,2,128]{5,4,1,3,2,0:T(2,128)S(1)} %broadcast_in_dim.50), channel_id=1, replica_groups=mesh['gx'=4,'gy'=2,'gz'=4] {'gx','gy','gz'}, dimensions={0} | all-to-all | bytes 196608 | tf_op jit(solution)/shard_map/all_to_all | solution.py:47
  37.8 0.1 fusion
  38.1 2.4 %multiply_reduce_fusion.7 = f32[4,128]{1,0:T(4,128)S(1)} fusion(f32[4,4608]{1,0:T(4,128)S(1)} %bitcast.276, f32[128,4608]{1,0:T(8,128)} %get-tuple-element.64), kind=kLoop, calls=%fused_computation.7 | loop fusion | flops 4718080 | bytes 2435072 | tf_op jit(solution)/shard_map/reduce_sum | solution.py:102
  40.5 0.8 multiply_reduce_fusion.6
  41.5 8.9 %all_to_all.31 = f32[32,1,1,1,2,128]{5,4,3,2,1,0:T(2,128)S(1)} all-to-all(f32[32,1,1,1,2,128]{5,4,3,2,1,0:T(2,128)S(1)} %broadcast_in_dim.56), channel_id=1, replica_groups=mesh['gx'=4,'gy'=2,'gz'=4] {'gx','gy','gz'}, dimensions={0} | all-to-all | bytes 65536 | tf_op jit(solution)/shard_map/all_to_all | solution.py:47
  50.6 0.1 fusion.3
  50.8 2.4 %multiply_reduce_fusion.5 = f32[4,128]{1,0:T(4,128)S(1)} fusion(f32[4,4608]{1,0:T(4,128)S(1)} %bitcast.280, f32[128,4608]{1,0:T(8,128)} %get-tuple-element.64), kind=kLoop, calls=%fused_computation.5 | loop fusion | flops 4718080 | bytes 2435072 | tf_op jit(solution)/shard_map/reduce_sum | solution.py:102
  53.2 0.7 multiply_reduce_fusion.4
  54.0 8.9 %all_to_all.32 = f32[32,1,1,1,2,128]{5,4,3,2,1,0:T(2,128)S(1)} all-to-all(f32[32,1,1,1,2,128]{5,4,3,2,1,0:T(2,128)S(1)} %broadcast_in_dim.60), channel_id=1, replica_groups=mesh['gx'=4,'gy'=2,'gz'=4] {'gx','gy','gz'}, dimensions={0} | all-to-all | bytes 65536 | tf_op jit(solution)/shard_map/all_to_all | solution.py:47
  63.1 0.1 fusion.2
  63.3 2.4 %multiply_reduce_fusion.3 = f32[4,128]{1,0:T(4,128)S(1)} fusion(f32[4,4608]{1,0:T(4,128)S(1)} %bitcast.282, f32[128,4608]{1,0:T(8,128)} %get-tuple-element.64), kind=kLoop, calls=%fused_computation.3 | loop fusion | flops 4718080 | bytes 2435072 | tf_op jit(solution)/shard_map/reduce_sum | solution.py:102
  65.7 0.7 multiply_reduce_fusion.2
  66.4 0.6 broadcast_in_dim.124
  67.0 2.5 %all-to-all-start.4 = ((f32[32,1,1,1,2,128]{5,4,3,2,1,0:T(2,128)}), f32[32,1,1,1,2,128]{5,4,3,2,1,0:T(2,128)S(1)}, u32[]{:S(2)}, u32[]{:S(2)}) async-start(f32[32,1,1,1,2,128]{5,4,3,2,1,0:T(2,128)} %broadcast_in_dim.124), calls=%async_computation.4 | async-start | bytes 65536 | tf_op jit(solution)/shard_map/all_to_all | solution.py:47
  69.6 7.2 %all-to-all-done.4 = f32[32,1,1,1,2,128]{5,4,3,2,1,0:T(2,128)S(1)} async-done(((f32[32,1,1,1,2,128]{5,4,3,2,1,0:T(2,128)}), f32[32,1,1,1,2,128]{5,4,3,2,1,0:T(2,128)S(1)}, u32[]{:S(2)}, u32[]{:S(2)}) %all-to-all-start.4) | async-done | bytes 32800 | tf_op jit(solution)/shard_map/all_to_all | solution.py:47
  77.0 0.1 fusion.1
  77.1 2.4 %multiply_reduce_fusion.1 = f32[4,128]{1,0:T(4,128)S(1)} fusion(f32[4,4608]{1,0:T(4,128)S(1)} %bitcast.278, f32[128,4608]{1,0:T(8,128)} %get-tuple-element.64), kind=kLoop, calls=%fused_computation.1 | loop fusion | flops 4718080 | bytes 2435072 | tf_op jit(solution)/shard_map/reduce_sum | solution.py:102
  79.5 0.7 multiply_reduce_fusion
  80.3 10.6 %all_to_all.33 = f32[32,3,4,128]{3,2,1,0:T(4,128)S(1)} all-to-all(f32[32,3,4,128]{3,2,1,0:T(4,128)S(1)} %broadcast_in_dim.127), channel_id=1, replica_groups=mesh['gx'=4,'gy'=2,'gz'=4] {'gx','gy','gz'}, dimensions={0} | all-to-all | bytes 393216 | tf_op jit(solution)/shard_map/all_to_all | solution.py:67
  92.3 0.6 copy.55
  (92 shorter events, 3.2 us)
Async XLA Ops:
  0.6 19.8 %copy-start.3 = (f32[4608]{0:T(1024)S(1)}, f32[4608]{0:T(1024)}, u32[]{:S(2)}) copy-start(f32[4608]{0:T(1024)} %constant.54.clone) | copy-start | bytes 55300
  3.5 16.2 %all-to-all-start = ((f32[32,6,1,1,2,128]{5,4,1,3,2,0:T(2,128)}), f32[32,6,1,1,2,128]{5,4,1,3,2,0:T(2,128)S(1)}, u32[]{:S(2)}, u32[]{:S(2)}) async-start(f32[32,6,1,1,2,128]{5,4,1,3,2,0:T(2,128)} %broadcast_in_dim.48), calls=%async_computation | async-start | bytes 393216 | tf_op jit(solution)/shard_map/all_to_all | solution.py:47
  10.8 12.3 %copy-start.2 = (f32[4608]{0:T(1024)S(1)}, f32[4608]{0:T(1024)}, u32[]{:S(2)}) copy-start(f32[4608]{0:T(1024)} %constant.53.clone) | copy-start | bytes 55300
  20.5 6.7 %copy-start = (f32[3,1,1,2,128]{4,3,2,1,0:T(2,128)S(1)}, f32[3,1,1,2,128]{4,3,2,1,0:T(2,128)}, u32[]{:S(2)}) copy-start(f32[3,1,1,2,128]{4,3,2,1,0:T(2,128)} %param.7) | copy-start | bytes 9220
  20.5 6.7 %copy-start.4 = (f32[3]{0:T(128)S(1)}, f32[3]{0:T(128)}, u32[]{:S(2)}) copy-start(f32[3]{0:T(128)} %constant.55.clone) | copy-start | bytes 40
  38.1 3.2 %copy-start.1 = (f32[3,1,1,2,128]{4,3,2,1,0:T(2,128)S(1)}, f32[3,1,1,2,128]{4,3,2,1,0:T(2,128)}, u32[]{:S(2)}) copy-start(f32[3,1,1,2,128]{4,3,2,1,0:T(2,128)} %param.6) | copy-start | bytes 9220
  67.0 9.7 %all-to-all-start.4 = ((f32[32,1,1,1,2,128]{5,4,3,2,1,0:T(2,128)}), f32[32,1,1,1,2,128]{5,4,3,2,1,0:T(2,128)S(1)}, u32[]{:S(2)}, u32[]{:S(2)}) async-start(f32[32,1,1,1,2,128]{5,4,3,2,1,0:T(2,128)} %broadcast_in_dim.124), calls=%async_computation.4 | async-start | bytes 65536 | tf_op jit(solution)/shard_map/all_to_all | solution.py:47
  92.2 0.7 copy-start.5

commit v13 on v12

--- a/solution.py
+++ b/solution.py
@@ -227,11 +227,9 @@
         basis.append(-(out[0:1] / width) / diagonal)
     stacked = jnp.concatenate(basis, axis=0)
     weighted = stacked[:ITERS] * diagonal
-    gram = total(jnp.sum(weighted[:, None] * stacked[None, :], axis=2))
-    shift = width // 2
-    while shift >= 1:
-        gram = gram + jnp.roll(gram, shift, axis=-1)
-        shift //= 2
+    gram = total(jnp.sum(weighted[:, None] * stacked[None, :], axis=(2, 3)))
+    lane_zero = 0.0 * diagonal[0, 0]
+    gram = gram[:, :, None] + lane_zero
     coords = solve3(gram[:, :ITERS] + gram[:, 1:], gram[:, 0])
 
     pressure = coords[0] * basis[0]

time: 93.6 us -> 88.3 us (0.943)
  blocking collectives: 38.8 us -> 28.2 us
  waiting for transfers between devices: 13.7 us -> 21.1 us
  other arithmetic: 24.3 us -> 17.2 us
  starting transfers between devices: 9.79 us -> 12.4 us
  local copies, waits for them, and re-layouts: 5.16 us -> 7.62 us
    all_to_all x1 -> x0, blocking collectives: 10.6 us -> none  [total(): got = lax.all_to_all(rows, ('gx', 'gy', 'gz'), 0, 0, tiled=True)]
    all_to_all x0 -> x1, waiting for transfers between devices: none -> 7.4 us  [total(): got = lax.all_to_all(rows, ('gx', 'gy', 'gz'), 0, 0, tiled=True)]
    reduce_sum x8, other arithmetic: 12.6 us -> 5.93 us  [wsum(): jnp.sum(tile_weight[None] * near[:, min(t, near.shape[1] - 1), None, :],...]
    all_to_all x0 -> x1, starting transfers between devices: none -> 2.57 us  [total(): got = lax.all_to_all(rows, ('gx', 'gy', 'gz'), 0, 0, tiled=True)]
    unnamed x22 -> x30, local copies, waits for them, and re-layouts: 1.47 us -> 3.85 us
  transfers between devices with their start and end apart: 2 -> 3, of which waited for: 2 -> 3; matrix products, arithmetic and copies ran while one was open for 3% -> 3% of each run, Pallas kernels for 0% -> 0%
where the time goes in v13:
time: 88.3 us; the launch traced here: 87.6 us
  blocking collectives  28.2 us (32%)
  waiting for transfers between devices  21.1 us (24%)
  other arithmetic  17.2 us (19%)
  starting transfers between devices  12.4 us (14%)
  local copies, waits for them, and re-layouts  7.62 us (9%)
  between operations  1.13 us (1%)
    all_to_all x3, blocking collectives, gather_rim(): got = lax.all_to_all(rows, ('gx', 'gy', 'gz'), 0, 0, tiled=True)  28.2 us
    all_to_all x2, waiting for transfers between devices, gather_rim(): got = lax.all_to_all(rows, ('gx', 'gy', 'gz'), 0, 0, tiled=True)  13.7 us
    all_to_all x2, starting transfers between devices, gather_rim(): got = lax.all_to_all(rows, ('gx', 'gy', 'gz'), 0, 0, tiled=True)  9.79 us
    all_to_all x1, waiting for transfers between devices, total(): got = lax.all_to_all(rows, ('gx', 'gy', 'gz'), 0, 0, tiled=True)  7.4 us
    reduce_sum x2, other arithmetic, on_device(): jnp.sum(tile_weight * field[None, :], axis=-1)  6.61 us
    reduce_sum x8, other arithmetic, wsum(): jnp.sum(tile_weight[None] * near[:, min(t, near.shape[1] - 1), None, :],...  5.93 us
    unnamed x30, local copies, waits for them, and re-layouts  3.85 us
    all_to_all x1, starting transfers between devices, total(): got = lax.all_to_all(rows, ('gx', 'gy', 'gz'), 0, 0, tiled=True)  2.57 us
  transfers between devices with their start and end apart: 3, of which 3 were waited for; matrix products, arithmetic and copies ran while one was open for 3% of the time, Pallas kernels for 0%

profile of v13, /device:TPU:0, one launch (start us, length us, event | category | flops | bytes accessed | tf_op | source)
XLA Modules:
  0.0 87.6 jit_solution(2712603798499078290)
XLA Ops:
  0.6 0.7 slice.210
  1.3 0.8 compare_select_fusion
  2.1 0.7 maximum_bitcast_fusion
  2.8 0.7 broadcast_in_dim.48
  3.5 7.3 %all-to-all-start = ((f32[32,6,1,1,2,128]{5,4,1,3,2,0:T(2,128)}), f32[32,6,1,1,2,128]{5,4,1,3,2,0:T(2,128)S(1)}, u32[]{:S(2)}, u32[]{:S(2)}) async-start(f32[32,6,1,1,2,128]{5,4,1,3,2,0:T(2,128)} %broadcast_in_dim.48), calls=%async_computation | async-start | bytes 393216 | tf_op jit(solution)/shard_map/all_to_all | solution.py:47
  10.8 0.7 copy.115
  11.5 0.7 compare_convert_fusion.1
  12.4 0.7 compare_convert_fusion.3
  13.2 6.5 %all-to-all-done = f32[32,6,1,1,2,128]{5,4,1,3,2,0:T(2,128)S(1)} async-done(((f32[32,6,1,1,2,128]{5,4,1,3,2,0:T(2,128)}), f32[32,6,1,1,2,128]{5,4,1,3,2,0:T(2,128)S(1)}, u32[]{:S(2)}, u32[]{:S(2)}) %all-to-all-start) | async-done | bytes 196640 | tf_op jit(solution)/shard_map/all_to_all | solution.py:47
  20.5 2.6 %multiply_reduce_fusion.14 = (f32[128]{0:T(128)S(1)}, f32[128]{0:T(128)S(1)}, f32[128]{0:T(128)S(1)}, f32[128]{0:T(128)S(1)}, f32[128]{0:T(128)S(1)}, /*index=5*...) fusion(f32[4608]{0:T(1024)S(1)} %get-tuple-element.17, f32[4608]{0:T(1024)S(1)} %copy-done.7, ...), kind=kLoop, calls=%fused_computation.22 | loop fusion | flops 15924352 | bytes 2567680 | tf_op jit(solution)/shard_map/reduce_sum | solution.py:195
  23.1 4.1 %multiply_reduce_fusion.8 = (f32[128]{0:T(128)S(1)}, f32[128]{0:T(128)S(1)}, f32[128]{0:T(128)S(1)}, f32[128]{0:T(128)S(1)}, f32[128]{0:T(128)S(1)}, /*index=5*/...) fusion(f32[4608]{0:T(1024)S(1)} %get-tuple-element.14, f32[4608]{0:T(1024)S(1)} %copy-done.6, ...), kind=kLoop, calls=%fused_computation.15 | loop fusion | flops 15924352 | bytes 2567680 | tf_op jit(solution)/shard_map/reduce_sum | solution.py:195
  27.3 10.3 %all_to_all.30 = f32[32,3,1,1,2,128]{5,4,1,3,2,0:T(2,128)S(1)} all-to-all(f32[32,3,1,1,2,128]{5,4,1,3,2,0:T(2,128)S(1)} %broadcast_in_dim.50), channel_id=1, replica_groups=mesh['gx'=4,'gy'=2,'gz'=4] {'gx','gy','gz'}, dimensions={0} | all-to-all | bytes 196608 | tf_op jit(solution)/shard_map/all_to_all | solution.py:47
  38.2 0.7 multiply_reduce_fusion.7
  39.4 0.8 multiply_reduce_fusion.6
  40.4 8.9 %all_to_all.31 = f32[32,1,1,1,2,128]{5,4,3,2,1,0:T(2,128)S(1)} all-to-all(f32[32,1,1,1,2,128]{5,4,3,2,1,0:T(2,128)S(1)} %broadcast_in_dim.56), channel_id=1, replica_groups=mesh['gx'=4,'gy'=2,'gz'=4] {'gx','gy','gz'}, dimensions={0} | all-to-all | bytes 65536 | tf_op jit(solution)/shard_map/all_to_all | solution.py:47
  49.7 0.7 multiply_reduce_fusion.5
  50.4 0.6 copy-done.1
  51.1 0.7 multiply_reduce_fusion.4
  51.8 8.9 %all_to_all.32 = f32[32,1,1,1,2,128]{5,4,3,2,1,0:T(2,128)S(1)} all-to-all(f32[32,1,1,1,2,128]{5,4,3,2,1,0:T(2,128)S(1)} %broadcast_in_dim.60), channel_id=1, replica_groups=mesh['gx'=4,'gy'=2,'gz'=4] {'gx','gy','gz'}, dimensions={0} | all-to-all | bytes 65536 | tf_op jit(solution)/shard_map/all_to_all | solution.py:47
  61.1 0.7 multiply_reduce_fusion.3
  61.9 0.6 copy-done.2
  62.5 0.7 multiply_reduce_fusion.2
  63.2 0.6 broadcast_in_dim.126
  63.8 2.5 %all-to-all-start.4 = ((f32[32,1,1,1,2,128]{5,4,3,2,1,0:T(2,128)}), f32[32,1,1,1,2,128]{5,4,3,2,1,0:T(2,128)S(1)}, u32[]{:S(2)}, u32[]{:S(2)}) async-start(f32[32,1,1,1,2,128]{5,4,3,2,1,0:T(2,128)} %broadcast_in_dim.126), calls=%async_computation.4 | async-start | bytes 65536 | tf_op jit(solution)/shard_map/all_to_all | solution.py:47
  66.4 7.2 %all-to-all-done.4 = f32[32,1,1,1,2,128]{5,4,3,2,1,0:T(2,128)S(1)} async-done(((f32[32,1,1,1,2,128]{5,4,3,2,1,0:T(2,128)}), f32[32,1,1,1,2,128]{5,4,3,2,1,0:T(2,128)S(1)}, u32[]{:S(2)}, u32[]{:S(2)}) %all-to-all-start.4) | async-done | bytes 32800 | tf_op jit(solution)/shard_map/all_to_all | solution.py:47
  73.9 0.7 multiply_reduce_fusion.1
  74.7 0.6 copy-done.3
  75.3 0.7 multiply_reduce_fusion
  76.1 0.6 broadcast_in_dim.129
  76.8 2.6 %all-to-all-start.5 = ((f32[32,3,4]{2,1,0:T(4,128)}), f32[32,3,4]{2,1,0:T(4,128)S(1)}, u32[]{:S(2)}, u32[]{:S(2)}) async-start(f32[32,3,4]{2,1,0:T(4,128)} %broadcast_in_dim.129), calls=%async_computation.5 | async-start | bytes 131072 | tf_op jit(solution)/shard_map/all_to_all | solution.py:67
  79.4 7.4 %all-to-all-done.5 = f32[32,3,4]{2,1,0:T(4,128)S(1)} async-done(((f32[32,3,4]{2,1,0:T(4,128)}), f32[32,3,4]{2,1,0:T(4,128)S(1)}, u32[]{:S(2)}, u32[]{:S(2)}) %all-to-all-start.5) | async-done | bytes 1568 | tf_op jit(solution)/shard_map/all_to_all | solution.py:67
  87.1 0.6 copy.55
  (89 shorter events, 3.6 us)
Async XLA Ops:
  0.6 19.8 %copy-start.7 = (f32[4608]{0:T(1024)S(1)}, f32[4608]{0:T(1024)}, u32[]{:S(2)}) copy-start(f32[4608]{0:T(1024)} %constant.54.clone) | copy-start | bytes 55300
  3.5 16.2 %all-to-all-start = ((f32[32,6,1,1,2,128]{5,4,1,3,2,0:T(2,128)}), f32[32,6,1,1,2,128]{5,4,1,3,2,0:T(2,128)S(1)}, u32[]{:S(2)}, u32[]{:S(2)}) async-start(f32[32,6,1,1,2,128]{5,4,1,3,2,0:T(2,128)} %broadcast_in_dim.48), calls=%async_computation | async-start | bytes 393216 | tf_op jit(solution)/shard_map/all_to_all | solution.py:47
  10.8 12.3 %copy-start.6 = (f32[4608]{0:T(1024)S(1)}, f32[4608]{0:T(1024)}, u32[]{:S(2)}) copy-start(f32[4608]{0:T(1024)} %constant.55.clone) | copy-start | bytes 55300
  20.5 6.7 %copy-start.4 = (f32[3,1,1,2,128]{4,3,2,1,0:T(2,128)S(1)}, f32[3,1,1,2,128]{4,3,2,1,0:T(2,128)}, u32[]{:S(2)}) copy-start(f32[3,1,1,2,128]{4,3,2,1,0:T(2,128)} %param.7) | copy-start | bytes 9220
  20.5 6.7 %copy-start.8 = (f32[3]{0:T(128)S(1)}, f32[3]{0:T(128)}, u32[]{:S(2)}) copy-start(f32[3]{0:T(128)} %constant.56.clone) | copy-start | bytes 40
  37.8 1.7 %copy-start = (f32[128,4608]{1,0:T(8,128)S(1)}, f32[128,4608]{1,0:T(8,128)}, u32[]{:S(2)}) copy-start(f32[128,4608]{1,0:T(8,128)} %get-tuple-element.65) | copy-start | bytes 7077892
  38.1 2.1 %copy-start.5 = (f32[3,1,1,2,128]{4,3,2,1,0:T(2,128)S(1)}, f32[3,1,1,2,128]{4,3,2,1,0:T(2,128)}, u32[]{:S(2)}) copy-start(f32[3,1,1,2,128]{4,3,2,1,0:T(2,128)} %param.6) | copy-start | bytes 9220
  49.4 1.7 %copy-start.1 = (f32[128,4608]{1,0:T(8,128)S(1)}, f32[128,4608]{1,0:T(8,128)}, u32[]{:S(2)}) copy-start(f32[128,4608]{1,0:T(8,128)} %get-tuple-element.65) | copy-start | bytes 7077892
  60.8 1.7 %copy-start.2 = (f32[128,4608]{1,0:T(8,128)S(1)}, f32[128,4608]{1,0:T(8,128)}, u32[]{:S(2)}) copy-start(f32[128,4608]{1,0:T(8,128)} %get-tuple-element.65) | copy-start | bytes 7077892
  63.8 9.7 %all-to-all-start.4 = ((f32[32,1,1,1,2,128]{5,4,3,2,1,0:T(2,128)}), f32[32,1,1,1,2,128]{5,4,3,2,1,0:T(2,128)S(1)}, u32[]{:S(2)}, u32[]{:S(2)}) async-start(f32[32,1,1,1,2,128]{5,4,3,2,1,0:T(2,128)} %broadcast_in_dim.126), calls=%async_computation.4 | async-start | bytes 65536 | tf_op jit(solution)/shard_map/all_to_all | solution.py:47
  73.6 1.7 %copy-start.3 = (f32[128,4608]{1,0:T(8,128)S(1)}, f32[128,4608]{1,0:T(8,128)}, u32[]{:S(2)}) copy-start(f32[128,4608]{1,0:T(8,128)} %get-tuple-element.65) | copy-start | bytes 7077892
  76.8 10.0 %all-to-all-start.5 = ((f32[32,3,4]{2,1,0:T(4,128)}), f32[32,3,4]{2,1,0:T(4,128)S(1)}, u32[]{:S(2)}, u32[]{:S(2)}) async-start(f32[32,3,4]{2,1,0:T(4,128)} %broadcast_in_dim.129), calls=%async_computation.5 | async-start | bytes 131072 | tf_op jit(solution)/shard_map/all_to_all | solution.py:67
  87.0 0.7 copy-start.9

commit v14 on v13

--- a/solution.py
+++ b/solution.py
@@ -221,10 +221,10 @@
     near_wx = []
     for _ in range(ITERS):
         near_u = rim_flat(shaped(basis[-1]))
-        out = wsum(weight, jnp.concatenate([spread_t(near_u), near_u * local_near], axis=0))
-        near_w.append(out[0:1])
-        near_wx.append(out[1:4])
-        basis.append(-(out[0:1] / width) / diagonal)
+        out = wsum(weight, spread_t(near_u))
+        near_w.append(out)
+        near_wx.append(wsum(weight, near_u * local_near))
+        basis.append(-(out / width) / diagonal)
     stacked = jnp.concatenate(basis, axis=0)
     weighted = stacked[:ITERS] * diagonal
     gram = total(jnp.sum(weighted[:, None] * stacked[None, :], axis=(2, 3)))

time: 88.3 us -> 91.8 us (1.040)
  other arithmetic: 17.2 us -> 27 us
  blocking collectives: 28.2 us -> 19.3 us
  starting transfers between devices: 12.4 us -> 15 us
  waiting for transfers between devices: 21.1 us -> 22.8 us
  local copies, waits for them, and re-layouts: 7.62 us -> 6.07 us
    reduce_sum x8 -> x7, other arithmetic: 5.93 us -> 16.2 us  [wsum(): jnp.sum(tile_weight[None] * near[:, min(t, near.shape[1] - 1), None, :],...]
    all_to_all x3 -> x2, blocking collectives: 28.2 us -> 19.3 us  [gather_rim(): got = lax.all_to_all(rows, ('gx', 'gy', 'gz'), 0, 0, tiled=True)]
    all_to_all x2 -> x3, waiting for transfers between devices: 13.7 us -> 20.8 us  [gather_rim(): got = lax.all_to_all(rows, ('gx', 'gy', 'gz'), 0, 0, tiled=True)]
    all_to_all x1, waiting for transfers between devices: 7.4 us -> 2.04 us  [total(): got = lax.all_to_all(rows, ('gx', 'gy', 'gz'), 0, 0, tiled=True)]
    all_to_all x2 -> x3, starting transfers between devices: 9.79 us -> 12.5 us  [gather_rim(): got = lax.all_to_all(rows, ('gx', 'gy', 'gz'), 0, 0, tiled=True)]
    unnamed x30 -> x22, local copies, waits for them, and re-layouts: 3.85 us -> 1.48 us
  transfers between devices with their start and end apart: 3 -> 4, of which waited for: 3 -> 4; matrix products, arithmetic and copies ran while one was open for 3% -> 8% of each run, Pallas kernels for 0% -> 0%
where the time goes in v14:
time: 91.8 us; the launch traced here: 91.3 us
  other arithmetic  27 us (29%)
  waiting for transfers between devices  22.8 us (25%)
  blocking collectives  19.3 us (21%)
  starting transfers between devices  15 us (16%)
  local copies, waits for them, and re-layouts  6.07 us (7%)
  between operations  1.1 us (1%)
    all_to_all x3, waiting for transfers between devices, gather_rim(): got = lax.all_to_all(rows, ('gx', 'gy', 'gz'), 0, 0, tiled=True)  20.8 us
    all_to_all x2, blocking collectives, gather_rim(): got = lax.all_to_all(rows, ('gx', 'gy', 'gz'), 0, 0, tiled=True)  19.3 us
    reduce_sum x7, other arithmetic, wsum(): jnp.sum(tile_weight[None] * near[:, min(t, near.shape[1] - 1), None, :],...  16.2 us
    all_to_all x3, starting transfers between devices, gather_rim(): got = lax.all_to_all(rows, ('gx', 'gy', 'gz'), 0, 0, tiled=True)  12.5 us
    reduce_sum x2, other arithmetic, on_device(): jnp.sum(tile_weight * field[None, :], axis=-1)  6.6 us
    all_to_all x1, starting transfers between devices, total(): got = lax.all_to_all(rows, ('gx', 'gy', 'gz'), 0, 0, tiled=True)  2.57 us
    all_to_all x1, waiting for transfers between devices, total(): got = lax.all_to_all(rows, ('gx', 'gy', 'gz'), 0, 0, tiled=True)  2.04 us
    broadcast_in_dim x5, local copies, waits for them, and re-layouts, gather_rim(): rows = jnp.broadcast_to(cells[None], (devices,) + cells.shape)  2 us
  transfers between devices with their start and end apart: 4, of which 4 were waited for; matrix products, arithmetic and copies ran while one was open for 8% of the time, Pallas kernels for 0%

profile of v14, /device:TPU:0, one launch (start us, length us, event | category | flops | bytes accessed | tf_op | source)
XLA Modules:
  0.0 91.3 jit_solution(8683104074809077239)
XLA Ops:
  0.6 0.7 slice.195
  1.3 0.8 compare_select_fusion
  2.1 0.7 maximum_bitcast_fusion
  2.8 0.7 broadcast_in_dim.36
  3.5 7.3 %all-to-all-start = ((f32[32,6,1,1,2,128]{5,4,1,3,2,0:T(2,128)}), f32[32,6,1,1,2,128]{5,4,1,3,2,0:T(2,128)S(1)}, u32[]{:S(2)}, u32[]{:S(2)}) async-start(f32[32,6,1,1,2,128]{5,4,1,3,2,0:T(2,128)} %broadcast_in_dim.36), calls=%async_computation | async-start | bytes 393216 | tf_op jit(solution)/shard_map/all_to_all | solution.py:47
  10.8 0.7 copy.151
  11.5 0.7 compare_convert_fusion.1
  12.4 0.7 compare_convert_fusion.3
  13.2 6.5 %all-to-all-done = f32[32,6,1,1,2,128]{5,4,1,3,2,0:T(2,128)S(1)} async-done(((f32[32,6,1,1,2,128]{5,4,1,3,2,0:T(2,128)}), f32[32,6,1,1,2,128]{5,4,1,3,2,0:T(2,128)S(1)}, u32[]{:S(2)}, u32[]{:S(2)}) %all-to-all-start) | async-done | bytes 196640 | tf_op jit(solution)/shard_map/all_to_all | solution.py:47
  20.0 0.3 slice_reduce_fusion
  20.5 2.6 %multiply_reduce_fusion.14 = (f32[128]{0:T(128)S(1)}, f32[128]{0:T(128)S(1)}, f32[128]{0:T(128)S(1)}, f32[128]{0:T(128)S(1)}, f32[128]{0:T(128)S(1)}, /*index=5*...) fusion(f32[4608]{0:T(1024)S(1)} %get-tuple-element.20, f32[4608]{0:T(1024)S(1)} %copy-done, ...), kind=kLoop, calls=%fused_computation.23 | loop fusion | flops 15924352 | bytes 2567680 | tf_op jit(solution)/shard_map/reduce_sum | solution.py:195
  23.1 4.1 %multiply_reduce_fusion.20 = (f32[128]{0:T(128)S(1)}, f32[128]{0:T(128)S(1)}, f32[128]{0:T(128)S(1)}, f32[128]{0:T(128)S(1)}, f32[128]{0:T(128)S(1)}, /*index=5*...) fusion(f32[4608]{0:T(1024)S(1)} %get-tuple-element.23, f32[4608]{0:T(1024)S(1)} %copy-done.1, ...), kind=kLoop, calls=%fused_computation.30 | loop fusion | flops 15924352 | bytes 2567680 | tf_op jit(solution)/shard_map/reduce_sum | solution.py:195
  27.3 10.3 %all_to_all.30 = f32[32,3,1,1,2,128]{5,4,1,3,2,0:T(2,128)S(1)} all-to-all(f32[32,3,1,1,2,128]{5,4,1,3,2,0:T(2,128)S(1)} %broadcast_in_dim.38), channel_id=1, replica_groups=mesh['gx'=4,'gy'=2,'gz'=4] {'gx','gy','gz'}, dimensions={0} | all-to-all | bytes 196608 | tf_op jit(solution)/shard_map/all_to_all | solution.py:47
  38.1 2.5 %multiply_reduce_fusion.1 = f32[4,128]{1,0:T(4,128)S(1)} fusion(f32[4,4608]{1,0:T(4,128)S(1)} %bitcast.295, f32[128,4608]{1,0:T(8,128)} %get-tuple-element.70), kind=kLoop, calls=%fused_computation.1 | loop fusion | flops 4718080 | bytes 2435072 | tf_op jit(solution)/shard_map/reduce_sum | solution.py:102
  40.6 0.7 multiply_reduce_fusion
  41.5 8.9 %all_to_all.31 = f32[32,1,1,1,2,128]{5,4,3,2,1,0:T(2,128)S(1)} all-to-all(f32[32,1,1,1,2,128]{5,4,3,2,1,0:T(2,128)S(1)} %broadcast_in_dim.44), channel_id=1, replica_groups=mesh['gx'=4,'gy'=2,'gz'=4] {'gx','gy','gz'}, dimensions={0} | all-to-all | bytes 65536 | tf_op jit(solution)/shard_map/all_to_all | solution.py:47
  50.5 2.7 %multiply_reduce_fusion.13 = (f32[128]{0:T(128)S(1)}, f32[128]{0:T(128)S(1)}) fusion(f32[4608]{0:T(1024)S(1)} %mul.1073, f32[4608]{0:T(1024)S(1)} %copy-done.1, f32[4608]{0:T(1024)S(1)} %compare_convert_fusion, f32[128]{0:T(128)S(1)} %get-tuple-element.82, f32[4608]{0:T(1024)S(1)} %sub.413, f32[128]{0:T(128)S(1)} %get-tuple-element.78, f32[4608]{0:T(1024)S(1)} %sub.408, ...), kind=kLoop, calls=%fused_computation.21 | loop fusion | flops 18874112 | bytes 134144 | tf_op jit(solution)/shard_map/reduce_sum | solution.py:102
  53.2 0.6 broadcast_in_dim.46
  53.8 2.7 %all-to-all-start.3 = ((f32[32,1,1,1,2,128]{5,4,3,2,1,0:T(2,128)}), f32[32,1,1,1,2,128]{5,4,3,2,1,0:T(2,128)S(1)}, u32[]{:S(2)}, u32[]{:S(2)}) async-start(f32[32,1,1,1,2,128]{5,4,3,2,1,0:T(2,128)} %broadcast_in_dim.46), calls=%async_computation.3 | async-start | bytes 65536 | tf_op jit(solution)/shard_map/all_to_all | solution.py:47
  56.5 7.0 %all-to-all-done.3 = f32[32,1,1,1,2,128]{5,4,3,2,1,0:T(2,128)S(1)} async-done(((f32[32,1,1,1,2,128]{5,4,3,2,1,0:T(2,128)}), f32[32,1,1,1,2,128]{5,4,3,2,1,0:T(2,128)S(1)}, u32[]{:S(2)}, u32[]{:S(2)}) %all-to-all-start.3) | async-done | bytes 32800 | tf_op jit(solution)/shard_map/all_to_all | solution.py:47
  63.6 2.7 %multiply_reduce_fusion.11 = (f32[128]{0:T(128)S(1)}, f32[128]{0:T(128)S(1)}) fusion(f32[4608]{0:T(1024)S(1)} %mul.1086, f32[4608]{0:T(1024)S(1)} %copy-done.1, f32[4608]{0:T(1024)S(1)} %compare_convert_fusion, f32[128]{0:T(128)S(1)} %get-tuple-element.82, f32[4608]{0:T(1024)S(1)} %sub.413, f32[128]{0:T(128)S(1)} %get-tuple-element.78, f32[4608]{0:T(1024)S(1)} %sub.408, ...), kind=kLoop, calls=%fused_computation.18 | loop fusion | flops 18874112 | bytes 134144 | tf_op jit(solution)/shard_map/reduce_sum | solution.py:102
  66.3 0.6 broadcast_in_dim.48
  66.9 2.5 %all-to-all-start.4 = ((f32[32,1,1,1,2,128]{5,4,3,2,1,0:T(2,128)}), f32[32,1,1,1,2,128]{5,4,3,2,1,0:T(2,128)S(1)}, u32[]{:S(2)}, u32[]{:S(2)}) async-start(f32[32,1,1,1,2,128]{5,4,3,2,1,0:T(2,128)} %broadcast_in_dim.48), calls=%async_computation.4 | async-start | bytes 65536 | tf_op jit(solution)/shard_map/all_to_all | solution.py:47
  69.5 7.2 %all-to-all-done.4 = f32[32,1,1,1,2,128]{5,4,3,2,1,0:T(2,128)S(1)} async-done(((f32[32,1,1,1,2,128]{5,4,3,2,1,0:T(2,128)}), f32[32,1,1,1,2,128]{5,4,3,2,1,0:T(2,128)S(1)}, u32[]{:S(2)}, u32[]{:S(2)}) %all-to-all-start.4) | async-done | bytes 32800 | tf_op jit(solution)/shard_map/all_to_all | solution.py:47
  76.7 2.7 %multiply_reduce_fusion.9 = (f32[128]{0:T(128)S(1)}, f32[128]{0:T(128)S(1)}) fusion(f32[4608]{0:T(1024)S(1)} %mul.1094, f32[4608]{0:T(1024)S(1)} %copy-done.1, f32[4608]{0:T(1024)S(1)} %compare_convert_fusion, f32[128]{0:T(128)S(1)} %get-tuple-element.82, f32[4608]{0:T(1024)S(1)} %sub.413, f32[128]{0:T(128)S(1)} %get-tuple-element.78, f32[4608]{0:T(1024)S(1)} %sub.408, ...), kind=kLoop, calls=%fused_computation.16 | loop fusion | flops 18874112 | bytes 134144 | tf_op jit(solution)/shard_map/reduce_sum | solution.py:102
  79.4 0.2 subtract_multiply_fusion.2
  79.7 0.6 broadcast_in_dim.49
  80.4 2.6 %all-to-all-start.5 = ((f32[32,3,4]{2,1,0:T(4,128)}), f32[32,3,4]{2,1,0:T(4,128)S(1)}, u32[]{:S(2)}, u32[]{:S(2)}) async-start(f32[32,3,4]{2,1,0:T(4,128)} %broadcast_in_dim.49), calls=%async_computation.5 | async-start | bytes 131072 | tf_op jit(solution)/shard_map/all_to_all | solution.py:67
  83.4 3.1 %multiply_reduce_fusion.3 = (f32[3,128]{1,0:T(4,128)S(1)}, f32[3,128]{1,0:T(4,128)S(1)}, f32[3,128]{1,0:T(4,128)S(1)}) fusion(f32[3,4608]{1,0:T(4,128)S(1)} %bitcast.297, f32[128,4608]{1,0:T(8,128)} %get-tuple-element.70, f32[3,4608]{1,0:T(4,128)S(1)} %bitcast.298, f32[3,4608]{1,0:T(4,128)S(1)} %bitcast.301), kind=kLoop, calls=%fused_computation.3 | loop fusion | flops 10615680 | bytes 2529792 | tf_op jit(solution)/shard_map/reduce_sum | solution.py:102
  86.5 1.9 %multiply_reduce_fusion.2 = (f32[3,128]{1,0:T(4,128)S(1)}, f32[3,128]{1,0:T(4,128)S(1)}, f32[3,128]{1,0:T(4,128)S(1)}) fusion(f32[3,4608]{1,0:T(4,128)S(1)} %bitcast.299, f32[128,4608]{1,0:T(8,128)S(1)} %get-tuple-element.71, f32[3,4608]{1,0:T(4,128)S(1)} %bitcast.300, f32[3,4608]{1,0:T(4,128)S(1)} %bitcast.302), kind=kLoop, calls=%fused_computation.2 | loop fusion | flops 10615680 | bytes 2529792 | tf_op jit(solution)/shard_map/reduce_sum | solution.py:102
  88.3 2.0 %all-to-all-done.5 = f32[32,3,4]{2,1,0:T(4,128)S(1)} async-done(((f32[32,3,4]{2,1,0:T(4,128)}), f32[32,3,4]{2,1,0:T(4,128)S(1)}, u32[]{:S(2)}, u32[]{:S(2)}) %all-to-all-start.5) | async-done | bytes 1568 | tf_op jit(solution)/shard_map/all_to_all | solution.py:67
  90.7 0.6 copy.91
  (77 shorter events, 2.3 us)
Async XLA Ops:
  0.6 19.8 %copy-start = (f32[4608]{0:T(1024)S(1)}, f32[4608]{0:T(1024)}, u32[]{:S(2)}) copy-start(f32[4608]{0:T(1024)} %constant.55.clone) | copy-start | bytes 55300
  3.5 16.2 %all-to-all-start = ((f32[32,6,1,1,2,128]{5,4,1,3,2,0:T(2,128)}), f32[32,6,1,1,2,128]{5,4,1,3,2,0:T(2,128)S(1)}, u32[]{:S(2)}, u32[]{:S(2)}) async-start(f32[32,6,1,1,2,128]{5,4,1,3,2,0:T(2,128)} %broadcast_in_dim.36), calls=%async_computation | async-start | bytes 393216 | tf_op jit(solution)/shard_map/all_to_all | solution.py:47
  10.8 12.3 %copy-start.1 = (f32[4608]{0:T(1024)S(1)}, f32[4608]{0:T(1024)}, u32[]{:S(2)}) copy-start(f32[4608]{0:T(1024)} %constant.54.clone) | copy-start | bytes 55300
  20.5 6.7 %copy-start.2 = (f32[3,1,1,2,128]{4,3,2,1,0:T(2,128)S(1)}, f32[3,1,1,2,128]{4,3,2,1,0:T(2,128)}, u32[]{:S(2)}) copy-start(f32[3,1,1,2,128]{4,3,2,1,0:T(2,128)} %param.7) | copy-start | bytes 9220
  20.5 6.7 %copy-start.4 = (f32[3]{0:T(128)S(1)}, f32[3]{0:T(128)}, u32[]{:S(2)}) copy-start(f32[3]{0:T(128)} %constant.56.clone) | copy-start | bytes 40
  38.1 3.2 %copy-start.3 = (f32[3,1,1,2,128]{4,3,2,1,0:T(2,128)S(1)}, f32[3,1,1,2,128]{4,3,2,1,0:T(2,128)}, u32[]{:S(2)}) copy-start(f32[3,1,1,2,128]{4,3,2,1,0:T(2,128)} %param.6) | copy-start | bytes 9220
  53.8 9.7 %all-to-all-start.3 = ((f32[32,1,1,1,2,128]{5,4,3,2,1,0:T(2,128)}), f32[32,1,1,1,2,128]{5,4,3,2,1,0:T(2,128)S(1)}, u32[]{:S(2)}, u32[]{:S(2)}) async-start(f32[32,1,1,1,2,128]{5,4,3,2,1,0:T(2,128)} %broadcast_in_dim.46), calls=%async_computation.3 | async-start | bytes 65536 | tf_op jit(solution)/shard_map/all_to_all | solution.py:47
  66.9 9.7 %all-to-all-start.4 = ((f32[32,1,1,1,2,128]{5,4,3,2,1,0:T(2,128)}), f32[32,1,1,1,2,128]{5,4,3,2,1,0:T(2,128)S(1)}, u32[]{:S(2)}, u32[]{:S(2)}) async-start(f32[32,1,1,1,2,128]{5,4,3,2,1,0:T(2,128)} %broadcast_in_dim.48), calls=%async_computation.4 | async-start | bytes 65536 | tf_op jit(solution)/shard_map/all_to_all | solution.py:47
  80.4 10.0 %all-to-all-start.5 = ((f32[32,3,4]{2,1,0:T(4,128)}), f32[32,3,4]{2,1,0:T(4,128)S(1)}, u32[]{:S(2)}, u32[]{:S(2)}) async-start(f32[32,3,4]{2,1,0:T(4,128)} %broadcast_in_dim.49), calls=%async_computation.5 | async-start | bytes 131072 | tf_op jit(solution)/shard_map/all_to_all | solution.py:67
  90.6 0.7 copy-start.5
